TPU v7x, 32 devices: a whole 2x2x4 slice. The times are simulated.
32 devices in a mesh: ep: 8 (over z, x), tp: 4 (over y, core).
Axes of the slice: x: 2, y: 2, z: 4, core: 2. Of those that a mesh axis runs over, the one named last changes fastest.
Arguments:
- features: bfloat16 [2048, 1024], P('ep'), may hold values from -6 to 6
- cotangent: bfloat16 [2048, 2048], P('ep'), may hold values from -6 to 6
- expert_ids: int32 [2048, 2], P('ep'), may hold values from 0 to 7, all different within a row; in each aligned block of 256 rows (0 to 255, 256 to 511, ...) at most 96 rows name the same one
- gate_levels: int32 [2048, 2], P('ep'), may hold values from 1 to 15
- w_in: bfloat16 [8, 1024, 4096], P('ep', None, 'tp'), may hold values from -0.1875 to 0.1875
- w_out: bfloat16 [8, 4096, 2048], P('ep', 'tp'), may hold values from -0.09375 to 0.09375
Outputs:
- grad_in: bfloat16 [2048, 1024], P('ep', 'tp')
- grad_w_in: bfloat16 [8, 1024, 4096], P('ep', None, 'tp')
- grad_w_out: bfloat16 [8, 4096, 2048], P('ep', 'tp')
Inputs may be any that keep to these rules, and one draw needn't show every extreme that they name: `expert_ids`: each row names two different experts. In each aligned block of 256 rows no expert is named by more than 96 rows, and some expert reaches 96 rows in some block.
All inputs are finite; a program needn't handle non-finite values.
Results may differ from a plain program's by a relative error of at most 0.0065.
Values may be sent and summed in bfloat16 or wider, within the bound.
No kernel may reach another device: no remote copies, remote signals or barrier semaphores. Data moves between devices by JAX's collectives and lax.ppermute only.
A program may use at most 128 MiB of HBM per device.

v0:
```python
import math

import jax
import jax.numpy as jnp
from jax import lax
from jax.sharding import PartitionSpec as P

E = 8


def shifted(value, axis, by):
    peers = lax.axis_size(axis)
    return lax.ppermute(value, axis, [(i, (i + by) % peers) for i in range(peers)])


def slot_positions(expert_ids, blocks, experts, capacity):
    flattened = expert_ids.reshape(blocks, -1)
    one_hot = (flattened[:, :, None] == jnp.arange(experts, dtype=jnp.int32)[None, None, :]).astype(
        jnp.int32
    )
    earlier = jnp.cumsum(one_hot, axis=1) - one_hot
    within = jnp.sum(one_hot * earlier, axis=2)
    block_ids = jnp.arange(blocks, dtype=jnp.int32)[:, None]
    return ((block_ids * experts + flattened) * capacity + within).reshape(-1)


def shards(features, cotangent, expert_ids, gate_levels, w_in, w_out):
    device_count = lax.axis_size("ep")
    replicas = device_count // E
    replica = lax.axis_index("ep") // E
    tokens_here = expert_ids.shape[0]
    sub_rows = tokens_here // replicas
    capacity = 3 * sub_rows // 8
    slot_count = device_count * capacity
    pair_count = 2 * tokens_here
    positions = slot_positions(expert_ids, replicas, E, capacity)
    owner = (
        jnp.full((slot_count,), pair_count, jnp.int32)
        .at[positions]
        .set(jnp.arange(pair_count, dtype=jnp.int32))
    )
    filled = owner < pair_count
    pair_ids = jnp.minimum(owner, pair_count - 1)
    token_ids = pair_ids // 2
    gate_values = gate_levels.reshape(-1).astype(jnp.float32) / 16.0
    slot_gates = jnp.where(filled, gate_values[pair_ids], 0.0)
    slot_mask = filled.astype(jnp.bfloat16)[:, None]
    packed_x = features[token_ids] * slot_mask
    packed_dy = (cotangent[token_ids].astype(jnp.float32) * slot_gates[:, None]).astype(
        jnp.bfloat16
    )
    rows_x, rows_dy = (
        lax.all_to_all(packed_x, "ep", split_axis=0, concat_axis=0, tiled=True),
        lax.all_to_all(packed_dy, "ep", split_axis=0, concat_axis=0, tiled=True),
    )
    piece_in = w_in[0]
    piece_out = w_out[0]
    span = piece_in.shape[1]
    weight_in = jnp.zeros((piece_in.shape[0], span * replicas), jnp.bfloat16)
    weight_out = jnp.zeros((span * replicas, piece_out.shape[1]), jnp.bfloat16)
    weight_in = lax.dynamic_update_slice_in_dim(weight_in, piece_in, replica * span, 1)
    weight_out = lax.dynamic_update_slice_in_dim(weight_out, piece_out, replica * span, 0)
    moving = (piece_in, piece_out)
    for turn_index in range(1, replicas):
        moving = shifted((moving[0], moving[1]), "ep", E)
        anchor = (replica - turn_index) % replicas
        weight_in = lax.dynamic_update_slice_in_dim(weight_in, moving[0], anchor * span, 1)
        weight_out = lax.dynamic_update_slice_in_dim(weight_out, moving[1], anchor * span, 0)
    pre = jnp.dot(rows_x, weight_in, preferred_element_type=jnp.float32)
    activated, gelu_back = jax.vjp(jax.nn.gelu, pre)
    act_rows = activated.astype(jnp.bfloat16)
    back_act = lax.dot_general(
        rows_dy, weight_out, (((1,), (1,)), ((), ())), preferred_element_type=jnp.float32
    )
    back_pre = gelu_back(back_act)[0].astype(jnp.bfloat16)
    summed = lax.psum_scatter(
        lax.dot_general(
            weight_in, back_pre, (((1,), (1,)), ((), ())), preferred_element_type=jnp.float32
        ),
        "tp",
        scatter_dimension=0,
        tiled=True,
    )
    returned = lax.all_to_all(
        summed.astype(jnp.bfloat16), "ep", split_axis=1, concat_axis=1, tiled=True
    )
    picked = returned[:, positions].astype(jnp.float32)
    grad_in = jnp.sum(picked.reshape(picked.shape[0], tokens_here, 2), axis=2).T.astype(
        jnp.bfloat16
    )

    def span_grads(first_span, span_total):
        width = span_total * span
        act_cols = lax.dynamic_slice_in_dim(act_rows, first_span * span, width, 1)
        pre_cols = lax.dynamic_slice_in_dim(back_pre, first_span * span, width, 1)
        grad_first = lax.dot_general(
            pre_cols, rows_x, (((0,), (0,)), ((), ())), preferred_element_type=jnp.float32
        )
        grad_second = lax.dot_general(
            act_cols, rows_dy, (((0,), (0,)), ((), ())), preferred_element_type=jnp.float32
        )
        return (grad_first, grad_second)

    summed_grads = span_grads((replica - 1) % replicas, 1)
    for turn_index in range(1, replicas):
        summed_grads = shifted((summed_grads[0], summed_grads[1]), "ep", E)
        own_grads = span_grads((replica - turn_index - 1) % replicas, 1)
        summed_grads = (summed_grads[0] + own_grads[0], summed_grads[1] + own_grads[1])
    grad_scale = 1.0 / math.sqrt(2.0 * tokens_here * device_count / E)
    grad_w_in = (summed_grads[0] * grad_scale).T.astype(jnp.bfloat16)[None]
    grad_w_out = (summed_grads[1] * grad_scale).astype(jnp.bfloat16)[None]
    return (grad_in, grad_w_in, grad_w_out)


def solution(mesh):
    return jax.shard_map(
        shards,
        mesh=mesh,
        in_specs=(
            P("ep", None),
            P("ep", None),
            P("ep", None),
            P("ep", None),
            P("ep", None, "tp"),
            P("ep", "tp", None),
        ),
        out_specs=(P("ep", "tp"), P("ep", None, "tp"), P("ep", "tp", None)),
        check_vma=False,
    )
```

profile of v0, /device:TPU:0, one launch (start us, length us, event | category | flops | bytes accessed | tf_op | source)
XLA Modules:
  0.0 224.9 jit_solution(1685540654432374637)
XLA Ops:
  7.2 0.0 copy-start
  7.2 0.0 copy-start.2
  7.2 1.0 copy.10
  8.2 0.7 broadcast_multiply_fusion.1
  8.9 0.1 eq.29
  9.0 1.1 reduce-window.6
  10.2 0.2 slice_reduce_fusion
  10.4 0.1 fusion.26
  10.5 0.1 copy.9
  10.6 0.1 mul.109
  10.8 2.4 %scatter_custom_fusion = s32[768]{0:T(1024)S(1)} fusion(s32[512]{0:T(512)S(1)} %bitcast.57, s32[512]{0:T(512)S(1)} %iota.15, s32[]{:T(128)} %constant.26.clone.1), kind=kCustom, calls=%fused_computation.57 | custom fusion | bytes 3076 | tf_op jit(solution)/shard_map/scatter | solution.py:40
  13.3 0.7 convert_multiply_fusion.1
  14.0 0.1 copy.11
  14.1 0.1 div.25
  14.3 5.0 %gather_fusion.1 = f32[768]{0:T(1024)S(1)} fusion(f32[512]{0:T(512)S(1)} %div.25, s32[1024]{0:T(1024)S(1)} %get-tuple-element.7), kind=kCustom, calls=%fused_computation.1 | custom fusion | bytes 9216 | tf_op jit(solution)/shard_map/gather | solution.py:46
  19.3 0.1 reshape.196
  19.4 0.0 copy-done.2
  19.4 3.5 %gather_fusion.2 = bf16[768,1024]{1,0:T(8,128)(2,1)} fusion(bf16[256,1024]{1,0:T(8,128)(2,1)S(1)} %copy-done.2, s32[1024]{0:T(1024)S(1)} %get-tuple-element.8), kind=kCustom, calls=%fused_computation.2 | custom fusion | bytes 3148800 | tf_op jit(solution)/shard_map/gather | solution.py:48
  23.0 0.0 copy-start.1
  23.0 2.8 %broadcast_multiply_fusion = bf16[8,96,1024]{2,1,0:T(8,128)(2,1)} fusion(bf16[8,96,1024]{2,1,0:T(8,128)(2,1)} %bitcast.54, bf16[8,96]{1,0:T(8,128)(2,1)S(1)} %reshape.196), kind=kLoop, calls=%fused_computation.32 | loop fusion | flops 786432 | bytes 3147264 | tf_op jit(solution)/shard_map/mul | solution.py:48
  25.8 7.3 %all-to-all-start.1 = ((bf16[8,96,1024]{2,1,0:T(8,128)(2,1)}), bf16[8,96,1024]{2,1,0:T(8,128)(2,1)}, u32[]{:S(2)}, u32[]{:S(2)}) async-start(bf16[8,96,1024]{2,1,0:T(8,128)(2,1)} %broadcast_multiply_fusion), calls=%async_computation.1 | async-start | bytes 3145728 | tf_op jit(solution)/shard_map/all_to_all | solution.py:53
  33.1 0.1 mul.111
  33.1 0.0 copy-done.1
  33.1 4.2 %gather_fusion = bf16[768,2048]{1,0:T(8,128)(2,1)} fusion(bf16[256,2048]{1,0:T(8,128)(2,1)S(1)} %copy-done.1, s32[1024]{0:T(1024)S(1)} %get-tuple-element.8), kind=kCustom, calls=%fused_computation | custom fusion | bytes 6294528 | tf_op jit(solution)/shard_map/gather | solution.py:49
  37.4 4.1 %fusion = bf16[8,96,2048]{2,1,0:T(8,128)(2,1)} fusion(bf16[8,96,2048]{2,1,0:T(8,128)(2,1)} %bitcast.53, f32[8,96]{1,0:T(8,128)S(1)} %mul.111), kind=kLoop, calls=%fused_computation.7 | loop fusion | flops 4718592 | bytes 6294528 | tf_op jit(solution)/shard_map/convert_element_type | solution.py:49
  41.5 28.7 %all-to-all-done.1 = bf16[8,96,1024]{2,1,0:T(8,128)(2,1)} async-done(((bf16[8,96,1024]{2,1,0:T(8,128)(2,1)}), bf16[8,96,1024]{2,1,0:T(8,128)(2,1)}, u32[]{:S(2)}, u32[]{:S(2)}) %all-to-all-start.1) | async-done | bytes 1572896 | tf_op jit(solution)/shard_map/all_to_all | solution.py:53
  70.2 4.4 %all-to-all-start = ((bf16[8,96,2048]{2,1,0:T(8,128)(2,1)}), bf16[8,96,2048]{2,1,0:T(8,128)(2,1)}, u32[]{:S(2)}, u32[]{:S(2)}) async-start(bf16[8,96,2048]{2,1,0:T(8,128)(2,1)} %fusion), calls=%async_computation | async-start | bytes 6291456 | tf_op jit(solution)/shard_map/all_to_all | solution.py:54
  74.6 0.2 reduce-scatter.2.cloned.1.call-start
  74.8 0.0 copy-done
  74.9 4.9 %fusion.15 = f32[768,1024]{1,0:T(8,128)} fusion(bf16[768,1024]{1,0:T(8,128)(2,1)} %bitcast.12, bf16[1,1024,1024]{2,1,0:T(8,128)(2,1)S(1)} %copy-done), kind=kOutput, calls=%fused_computation.24 | convolution fusion | flops 1610612736 | bytes 6815744 | tf_op jit(solution)/shard_map/dot_general | solution.py:69
  79.8 65.1 %all-to-all-done = bf16[8,96,2048]{2,1,0:T(8,128)(2,1)} async-done(((bf16[8,96,2048]{2,1,0:T(8,128)(2,1)}), bf16[8,96,2048]{2,1,0:T(8,128)(2,1)}, u32[]{:S(2)}, u32[]{:S(2)}) %all-to-all-start) | async-done | bytes 3145760 | tf_op jit(solution)/shard_map/all_to_all | solution.py:54
  144.8 9.1 %fusion.10 = bf16[768,1024]{1,0:T(8,128)(2,1)S(1)} fusion(f32[768,1024]{1,0:T(8,128)} %fusion.15, bf16[768,2048]{1,0:T(8,128)(2,1)} %bitcast.9, bf16[1,1024,2048]{2,1,0:T(8,128)(2,1)} %param.11), kind=kOutput, calls=%fused_computation.20 | convolution fusion | flops 3236954112 | bytes 12058624 | tf_op jit(solution)/shard_map/dot_general | solution.py:72
  153.9 0.0 copy-start.3
  153.9 1.2 copy-done.3
  155.2 3.5 %fusion.17 = f32[1024,768]{0,1:T(8,128)} fusion(bf16[768,1024]{1,0:T(8,128)(2,1)S(1)} %fusion.10, bf16[1,1024,1024]{2,1,0:T(8,128)(2,1)S(1)} %copy-done), kind=kOutput, calls=%fused_computation.26 | convolution fusion | flops 1610612736 | bytes 6815744 | tf_op jit(solution)/shard_map/dot_general | solution.py:77
  158.7 0.0 reduce-scatter.2.cloned.1.call-update
  158.7 5.0 %fusion.20 = bf16[1,1024,1024]{2,1,0:T(8,128)(2,1)} fusion(bf16[768,1024]{1,0:T(8,128)(2,1)} %bitcast.12, bf16[768,1024]{1,0:T(8,128)(2,1)} %copy-done.3), kind=kOutput, calls=%fused_computation.27 | convolution fusion | flops 1612709888 | bytes 5242880 | tf_op jit(solution)/shard_map/dot_general | solution.py:96
  163.7 31.9 %reduce-scatter.2.cloned.1.call-done = f32[256,768]{0,1:T(8,128)} async-done(((f32[1024,768]{0,1:T(8,128)}), f32[256,768]{0,1:T(8,128)}) %reduce-scatter.2.cloned.1.call-update) | async-done | bytes 786448 | tf_op jit(solution)/shard_map/reduce_scatter | solution.py:76
  195.7 1.9 convert_element_type.61
  197.6 5.5 %all-to-all-start.2 = ((bf16[256,8,96]{0,2,1:T(8,128)(2,1)}), bf16[256,8,96]{0,2,1:T(8,128)(2,1)S(1)}, u32[]{:S(2)}, u32[]{:S(2)}) async-start(bf16[256,8,96]{0,2,1:T(8,128)(2,1)} %bitcast.15), calls=%async_computation.3 | async-start | bytes 786432 | tf_op jit(solution)/shard_map/all_to_all | solution.py:84
  203.1 8.6 %fusion.3 = bf16[1,1024,2048]{2,1,0:T(8,128)(2,1)} fusion(bf16[768,2048]{1,0:T(8,128)(2,1)} %bitcast.9, f32[768,1024]{1,0:T(8,128)} %fusion.15), kind=kOutput, calls=%fused_computation.13 | convolution fusion | flops 3232497664 | bytes 10485760 | tf_op jit(solution)/shard_map/dot_general | solution.py:99
  211.7 2.9 %all-to-all-done.2 = bf16[256,8,96]{0,2,1:T(8,128)(2,1)S(1)} async-done(((bf16[256,8,96]{0,2,1:T(8,128)(2,1)}), bf16[256,8,96]{0,2,1:T(8,128)(2,1)S(1)}, u32[]{:S(2)}, u32[]{:S(2)}) %all-to-all-start.2) | async-done | bytes 393248 | tf_op jit(solution)/shard_map/all_to_all | solution.py:84
  214.6 1.9 gather_fusion.3
  216.6 0.1 convert_element_type.62
  216.7 1.3 reduce.1
  (10 shorter events, 0.1 us)
Async XLA Ops:
  7.2 67.7 %copy-start = (bf16[1,1024,1024]{2,1,0:T(8,128)(2,1)S(1)}, bf16[1,1024,1024]{2,1,0:T(8,128)(2,1)}, u32[]{:S(2)}) copy-start(bf16[1,1024,1024]{2,1,0:T(8,128)(2,1)} %param.10) | copy-start | bytes 6291460
  7.2 12.2 %copy-start.2 = (bf16[256,1024]{1,0:T(8,128)(2,1)S(1)}, bf16[256,1024]{1,0:T(8,128)(2,1)}, u32[]{:S(2)}) copy-start(bf16[256,1024]{1,0:T(8,128)(2,1)} %param.6) | copy-start | bytes 1572868
  23.0 10.2 %copy-start.1 = (bf16[256,2048]{1,0:T(8,128)(2,1)S(1)}, bf16[256,2048]{1,0:T(8,128)(2,1)}, u32[]{:S(2)}) copy-start(bf16[256,2048]{1,0:T(8,128)(2,1)} %param.7) | copy-start | bytes 3145732
  25.8 44.4 %all-to-all-start.1 = ((bf16[8,96,1024]{2,1,0:T(8,128)(2,1)}), bf16[8,96,1024]{2,1,0:T(8,128)(2,1)}, u32[]{:S(2)}, u32[]{:S(2)}) async-start(bf16[8,96,1024]{2,1,0:T(8,128)(2,1)} %broadcast_multiply_fusion), calls=%async_computation.1 | async-start | bytes 3145728 | tf_op jit(solution)/shard_map/all_to_all | solution.py:53
  70.2 74.6 %all-to-all-start = ((bf16[8,96,2048]{2,1,0:T(8,128)(2,1)}), bf16[8,96,2048]{2,1,0:T(8,128)(2,1)}, u32[]{:S(2)}, u32[]{:S(2)}) async-start(bf16[8,96,2048]{2,1,0:T(8,128)(2,1)} %fusion), calls=%async_computation | async-start | bytes 6291456 | tf_op jit(solution)/shard_map/all_to_all | solution.py:54
  74.6 121.0 %reduce-scatter.2.cloned.1.call-start = ((), (), s32[]{:S(2)}) async-start(), calls=%async_computation.4 | async-start | bytes 3932160 | tf_op jit(solution)/shard_map/reduce_scatter | solution.py:76
  153.9 1.2 copy-start.3
  197.6 17.0 %all-to-all-start.2 = ((bf16[256,8,96]{0,2,1:T(8,128)(2,1)}), bf16[256,8,96]{0,2,1:T(8,128)(2,1)S(1)}, u32[]{:S(2)}, u32[]{:S(2)}) async-start(bf16[256,8,96]{0,2,1:T(8,128)(2,1)} %bitcast.15), calls=%async_computation.3 | async-start | bytes 786432 | tf_op jit(solution)/shard_map/all_to_all | solution.py:84
Sparse Core Ops, SparseCore 0:
  158.8 36.8 reduce-scatter.1
where the time goes:
time: 225 us
  waiting for transfers between devices  129 us (57%)
  matrix products  31.2 us (14%)
  local copies, waits for them, and re-layouts  20.6 us (9%)
  starting transfers between devices  17.4 us (8%)
  between operations  14.2 us (6%)
  other arithmetic  12.9 us (6%)
    all_to_all x1, waiting for transfers between devices, shards(): lax.all_to_all(packed_dy, 'ep', split_axis=0, concat_axis=0, tiled=True)  65.1 us
    reduce_scatter x1, waiting for transfers between devices, shards(): lax.psum_scatter(lax.dot_general(weight_in, back_pre, (((1,), (1,)), ((),...  31.9 us
    all_to_all x1, waiting for transfers between devices, shards(): lax.all_to_all(packed_x, 'ep', split_axis=0, concat_axis=0, tiled=True)  28.7 us
    dot_general x1, matrix products, shards(): lax.dot_general(rows_dy, weight_out, (((1,), (1,)), ((), ())), preferred_...  9.11 us
    dot_general x1, matrix products, span_grads(): lax.dot_general(act_cols, rows_dy, (((0,), (0,)), ((), ())), preferred_el...  8.64 us
    all_to_all x1, starting transfers between devices, shards(): lax.all_to_all(packed_x, 'ep', split_axis=0, concat_axis=0, tiled=True)  7.28 us
    all_to_all x1, starting transfers between devices, shards(): lax.all_to_all(summed.astype(jnp.bfloat16), 'ep', split_axis=1, concat_ax...  5.49 us
    dot_general x1, matrix products, span_grads(): lax.dot_general(pre_cols, rows_x, (((0,), (0,)), ((), ())), preferred_ele...  5.04 us
  transfers between devices with their start and end apart: 4, of which 4 were waited for; matrix products, arithmetic and copies ran while one was open for 12% of the time, Pallas kernels for 0%

commit v1 on v0

--- a/solution.py
+++ b/solution.py
@@ -24,6 +24,19 @@
     return ((block_ids * experts + flattened) * capacity + within).reshape(-1)
 
 
+def chip_then_link_sum(partial, j):
+    quarter = partial.shape[0] // 4
+
+    def rows(q):
+        return lax.dynamic_slice_in_dim(partial, q * quarter, quarter, 0)
+
+    keep = jnp.concatenate([rows(j), rows(j ^ 2)], axis=0)
+    give = jnp.concatenate([rows(j ^ 1), rows(j ^ 3)], axis=0)
+    keep = keep + lax.ppermute(give, "tp", [(i, i ^ 1) for i in range(4)])
+    mine, send = keep[:quarter], keep[quarter:]
+    return mine + lax.ppermute(send, "tp", [(i, i ^ 2) for i in range(4)])
+
+
 def shards(features, cotangent, expert_ids, gate_levels, w_in, w_out):
     device_count = lax.axis_size("ep")
     replicas = device_count // E
@@ -45,14 +58,25 @@
     gate_values = gate_levels.reshape(-1).astype(jnp.float32) / 16.0
     slot_gates = jnp.where(filled, gate_values[pair_ids], 0.0)
     slot_mask = filled.astype(jnp.bfloat16)[:, None]
-    packed_x = features[token_ids] * slot_mask
-    packed_dy = (cotangent[token_ids].astype(jnp.float32) * slot_gates[:, None]).astype(
-        jnp.bfloat16
-    )
-    rows_x, rows_dy = (
-        lax.all_to_all(packed_x, "ep", split_axis=0, concat_axis=0, tiled=True),
-        lax.all_to_all(packed_dy, "ep", split_axis=0, concat_axis=0, tiled=True),
-    )
+    tp_size = lax.axis_size("tp")
+    tp_index = lax.axis_index("tp")
+    split = 2 if tp_size % 2 == 0 else 1
+    half = tp_index % split
+
+    def dispatched(table, scale):
+        width = table.shape[1] // split
+        mine = lax.dynamic_slice_in_dim(table, half * width, width, 1)[token_ids]
+        mine = (mine.astype(jnp.float32) * scale).astype(jnp.bfloat16)
+        mine = lax.all_to_all(mine, "ep", split_axis=0, concat_axis=0, tiled=True)
+        if split == 1:
+            return mine
+        other = lax.ppermute(mine, "tp", [(i, i ^ 1) for i in range(tp_size)])
+        whole = jnp.zeros((mine.shape[0], table.shape[1]), jnp.bfloat16)
+        whole = lax.dynamic_update_slice_in_dim(whole, mine, half * width, 1)
+        return lax.dynamic_update_slice_in_dim(whole, other, (1 - half) * width, 1)
+
+    rows_x = dispatched(features, slot_mask.astype(jnp.float32))
+    rows_dy = dispatched(cotangent, slot_gates[:, None])
     piece_in = w_in[0]
     piece_out = w_out[0]
     span = piece_in.shape[1]
@@ -73,14 +97,13 @@
         rows_dy, weight_out, (((1,), (1,)), ((), ())), preferred_element_type=jnp.float32
     )
     back_pre = gelu_back(back_act)[0].astype(jnp.bfloat16)
-    summed = lax.psum_scatter(
-        lax.dot_general(
-            weight_in, back_pre, (((1,), (1,)), ((), ())), preferred_element_type=jnp.float32
-        ),
-        "tp",
-        scatter_dimension=0,
-        tiled=True,
+    partial = lax.dot_general(
+        weight_in, back_pre, (((1,), (1,)), ((), ())), preferred_element_type=jnp.float32
     )
+    if tp_size == 4:
+        summed = chip_then_link_sum(partial, tp_index)
+    else:
+        summed = lax.psum_scatter(partial, "tp", scatter_dimension=0, tiled=True)
     returned = lax.all_to_all(
         summed.astype(jnp.bfloat16), "ep", split_axis=1, concat_axis=1, tiled=True
     )

time: 225 us -> 149 us (0.66)
  waiting for transfers between devices: 129 us -> 76.2 us
  between operations: 14.2 us -> 0.98 us
  matrix products: 31.2 us -> 20.5 us
  local copies, waits for them, and re-layouts: 20.6 us -> 25.1 us
  other arithmetic: 12.9 us -> 9.5 us
    all_to_all x2, waiting for transfers between devices: 93.7 us -> 53.4 us  [dispatched(): mine = lax.all_to_all(mine, 'ep', split_axis=0, concat_axis=0, tiled=True)]
    reduce_scatter x1 -> x0, waiting for transfers between devices: 31.9 us -> none  [shards(): lax.psum_scatter(lax.dot_general(weight_in, back_pre, (((1,), (1,)), ((),...]
    ppermute x0 -> x4, waiting for transfers between devices: none -> 20.3 us  [the longest x1 14.9 us: chip_then_link_sum(): return mine + lax.ppermute(send, 'tp', [(i, i ^ 2) for i in range(4)])]
    dynamic_update_slice x0 -> x4, local copies, waits for them, and re-layouts: none -> 5.37 us  [the longest x2 2.9 us: dispatched(): return lax.dynamic_update_slice_in_dim(whole, other, (1 - half) * width, 1)]
    dot_general x1, matrix products: 9.11 us -> 5.08 us  [shards(): lax.dot_general(rows_dy, weight_out, (((1,), (1,)), ((), ())), preferred_...]
    dot_general x1, matrix products: 4.9 us -> 1.8 us  [shards(): pre = jnp.dot(rows_x, weight_in, preferred_element_type=jnp.float32)]
    mul x2 -> x1, other arithmetic: 2.82 us -> 0.01 us  [dispatched(): mine = (mine.astype(jnp.float32) * scale).astype(jnp.bfloat16)]
  transfers between devices with their start and end apart: 4 -> 7, of which waited for: 4 -> 6; matrix products, arithmetic and copies ran while one was open for 12% -> 15% of each run, Pallas kernels for 0% -> 0%
where the time goes in v1:
time: 149 us
  waiting for transfers between devices  76.2 us (51%)
  local copies, waits for them, and re-layouts  25.1 us (17%)
  matrix products  20.5 us (14%)
  starting transfers between devices  16.5 us (11%)
  other arithmetic  9.5 us (6%)
    all_to_all x2, waiting for transfers between devices, dispatched(): mine = lax.all_to_all(mine, 'ep', split_axis=0, concat_axis=0, tiled=True)  53.4 us
    ppermute x1, waiting for transfers between devices, chip_then_link_sum(): return mine + lax.ppermute(send, 'tp', [(i, i ^ 2) for i in range(4)])  14.9 us
    all_to_all x2, starting transfers between devices, dispatched(): mine = lax.all_to_all(mine, 'ep', split_axis=0, concat_axis=0, tiled=True)  11 us
    dot_general x1, matrix products, span_grads(): lax.dot_general(act_cols, rows_dy, (((0,), (0,)), ((), ())), preferred_el...  8.64 us
    gather x2, local copies, waits for them, and re-layouts, dispatched(): mine = lax.dynamic_slice_in_dim(table, half * width, width, 1)[token_ids]  6.24 us
    dot_general x1, matrix products, shards(): lax.dot_general(rows_dy, weight_out, (((1,), (1,)), ((), ())), preferred_...  5.08 us
    gather x1, local copies, waits for them, and re-layouts, shards(): slot_gates = jnp.where(filled, gate_values[pair_ids], 0.0)  5.01 us
    convert_element_type x2, other arithmetic, dispatched(): mine = (mine.astype(jnp.float32) * scale).astype(jnp.bfloat16)  4.05 us
  transfers between devices with their start and end apart: 7, of which 6 were waited for; matrix products, arithmetic and copies ran while one was open for 15% of the time, Pallas kernels for 0%

profile of v1, /device:TPU:0, one launch (start us, length us, event | category | flops | bytes accessed | tf_op | source)
XLA Modules:
  0.0 148.8 jit_solution(2680846008494431200)
XLA Ops:
  0.7 0.8 broadcast_multiply_fusion
  1.5 0.8 copy.10
  2.3 0.7 convert_multiply_fusion.2
  3.0 0.1 copy.9
  3.1 0.1 mul.138
  3.3 0.1 copy.11
  3.4 0.1 div.25
  3.6 0.1 eq.30
  3.7 1.1 reduce-window.6
  4.9 0.2 slice_reduce_fusion
  5.1 0.1 fusion.25
  5.3 2.4 %scatter_custom_fusion = s32[768]{0:T(1024)S(1)} fusion(s32[512]{0:T(512)S(1)} %bitcast.65, s32[512]{0:T(512)S(1)} %iota.15, s32[]{:T(128)} %constant.80.clone.1), kind=kCustom, calls=%fused_computation.72 | custom fusion | bytes 3076 | tf_op jit(solution)/shard_map/scatter | solution.py:53
  7.7 5.0 %gather_fusion.1 = f32[768]{0:T(1024)S(1)} fusion(f32[512]{0:T(512)S(1)} %div.25, s32[1024]{0:T(1024)S(1)} %get-tuple-element.11), kind=kCustom, calls=%fused_computation.1 | custom fusion | bytes 9216 | tf_op jit(solution)/shard_map/gather | solution.py:59
  12.8 1.1 constant_dynamic-slice_fusion.1
  13.9 3.6 %gather_fusion = bf16[768,1024]{1,0:T(8,128)(2,1)} fusion(bf16[256,1024]{1,0:T(8,128)(2,1)S(1)} %constant_dynamic-slice_fusion.1, s32[1024]{0:T(1024)S(1)} %get-tuple-element.12), kind=kCustom, calls=%fused_computation | custom fusion | bytes 3148800 | tf_op jit(solution)/shard_map/gather | solution.py:68
  17.5 2.9 %fusion.10 = bf16[8,96,1024]{2,1,0:T(8,128)(2,1)} fusion(bf16[8,96,1024]{2,1,0:T(8,128)(2,1)} %bitcast.59, f32[8,96]{1,0:T(8,128)S(1)} %mul.140), kind=kLoop, calls=%fused_computation.20 | loop fusion | flops 2359296 | bytes 3148800 | tf_op jit(solution)/shard_map/convert_element_type | solution.py:69
  20.4 7.3 %all-to-all-start = ((bf16[8,96,1024]{2,1,0:T(8,128)(2,1)}), bf16[8,96,1024]{2,1,0:T(8,128)(2,1)}, u32[]{:S(2)}, u32[]{:S(2)}) async-start(bf16[8,96,1024]{2,1,0:T(8,128)(2,1)} %fusion.10), calls=%async_computation | async-start | bytes 3145728 | tf_op jit(solution)/shard_map/all_to_all | solution.py:70
  27.7 0.1 reshape.202
  27.8 2.7 %gather_fusion.2 = bf16[768,512]{1,0:T(8,128)(2,1)S(1)} fusion(bf16[256,512]{1,0:T(8,128)(2,1)S(1)} %constant_dynamic-slice_fusion, s32[1024]{0:T(1024)S(1)} %get-tuple-element.12), kind=kCustom, calls=%fused_computation.2 | custom fusion | bytes 1575936 | tf_op jit(solution)/shard_map/gather | solution.py:68
  30.5 1.1 fusion.18
  31.6 33.2 %all-to-all-done = bf16[8,96,1024]{2,1,0:T(8,128)(2,1)} async-done(((bf16[8,96,1024]{2,1,0:T(8,128)(2,1)}), bf16[8,96,1024]{2,1,0:T(8,128)(2,1)}, u32[]{:S(2)}, u32[]{:S(2)}) %all-to-all-start) | async-done | bytes 1572896 | tf_op jit(solution)/shard_map/all_to_all | solution.py:70
  64.8 3.7 %all-to-all-start.1 = ((bf16[8,96,512]{2,1,0:T(8,128)(2,1)}), bf16[8,96,512]{2,1,0:T(8,128)(2,1)S(1)}, u32[]{:S(2)}, u32[]{:S(2)}) async-start(bf16[8,96,512]{2,1,0:T(8,128)(2,1)} %fusion.18), calls=%async_computation.1 | async-start | bytes 1572864 | tf_op jit(solution)/shard_map/all_to_all | solution.py:70
  68.6 20.2 %all-to-all-done.1 = bf16[8,96,512]{2,1,0:T(8,128)(2,1)S(1)} async-done(((bf16[8,96,512]{2,1,0:T(8,128)(2,1)}), bf16[8,96,512]{2,1,0:T(8,128)(2,1)S(1)}, u32[]{:S(2)}, u32[]{:S(2)}) %all-to-all-start.1) | async-done | bytes 786464 | tf_op jit(solution)/shard_map/all_to_all | solution.py:70
  88.8 0.2 broadcast_in_dim.34
  89.0 0.1 constant_dynamic-update-slice_fusion.1
  89.1 2.1 %collective-permute-done.1 = bf16[768,512]{1,0:T(8,128)(2,1)} collective-permute-done((bf16[768,512]{1,0:T(8,128)(2,1)S(1)}, bf16[768,512]{1,0:T(8,128)(2,1)}, u32[]{:S(2)}, u32[]{:S(2)}) %collective-permute-start.1) | collective-permute-done | bytes 786464 | tf_op jit(solution)/shard_map/ppermute | solution.py:73
  91.2 1.2 constant_dynamic-update-slice_fusion
  92.5 1.8 %fusion.15 = f32[768,1024]{1,0:T(8,128)S(1)} fusion(bf16[768,1024]{1,0:T(8,128)(2,1)S(1)} %constant_dynamic-update-slice_fusion, bf16[1,1024,1024]{2,1,0:T(8,128)(2,1)S(1)} %copy-done), kind=kOutput, calls=%fused_computation.24 | convolution fusion | flops 1610612736 | bytes 6815744 | tf_op jit(solution)/shard_map/dot_general | solution.py:93
  94.3 0.4 broadcast_in_dim.30
  94.7 2.4 %constant_dynamic-update-slice_fusion.3 = bf16[768,2048]{1,0:T(8,128)(2,1)S(1)} fusion(bf16[768,2048]{1,0:T(8,128)(2,1)S(1)} %broadcast_in_dim.30, bf16[768,1024]{1,0:T(8,128)(2,1)} %bitcast.9, s32[]{:T(128)S(6)} %select_n.69), kind=kLoop, calls=%fused_computation.65 | loop fusion | bytes 3145732 | tf_op jit(solution)/shard_map/dynamic_update_slice | solution.py:75
  97.1 1.7 %constant_dynamic-update-slice_fusion.2 = bf16[768,2048]{1,0:T(8,128)(2,1)S(1)} fusion(bf16[768,2048]{1,0:T(8,128)(2,1)S(1)} %constant_dynamic-update-slice_fusion.3, bf16[768,1024]{1,0:T(8,128)(2,1)} %collective-permute-done, s32[]{:T(128)S(6)} %select_n.75), kind=kLoop, calls=%fused_computation.64 | loop fusion | bytes 3145732 | tf_op jit(solution)/shard_map/dynamic_update_slice | solution.py:76
  98.8 5.1 %fusion.9 = bf16[768,1024]{1,0:T(8,128)(2,1)S(1)} fusion(f32[768,1024]{1,0:T(8,128)S(1)} %fusion.15, bf16[768,2048]{1,0:T(8,128)(2,1)S(1)} %constant_dynamic-update-slice_fusion.2, bf16[1,1024,2048]{2,1,0:T(8,128)(2,1)S(1)} %copy-done.3), kind=kOutput, calls=%fused_computation.18 | convolution fusion | flops 3236954112 | bytes 12058624 | tf_op jit(solution)/shard_map/dot_general | solution.py:96
  103.9 1.8 %fusion.13 = f32[768,1024]{1,0:T(8,128)S(1)} fusion(bf16[768,1024]{1,0:T(8,128)(2,1)S(1)} %fusion.9, bf16[1,1024,1024]{2,1,0:T(8,128)(2,1)S(1)} %copy-done), kind=kOutput, calls=%fused_computation.22 | convolution fusion | flops 1610612736 | bytes 6815744 | tf_op jit(solution)/shard_map/dot_general | solution.py:100
  105.7 0.4 dynamic-slice_bitcast_fusion.3
  106.1 0.2 pad_maximum_fusion
  106.3 0.2 collective-permute-start.2
  106.5 3.3 %collective-permute-done.2 = f32[512,768]{0,1:T(8,128)S(1)} collective-permute-done((f32[512,768]{0,1:T(8,128)S(1)}, f32[512,768]{0,1:T(8,128)S(1)}, u32[]{:S(2)}, u32[]{:S(2)}) %collective-permute-start.2) | collective-permute-done | bytes 1572896 | tf_op jit(solution)/shard_map/ppermute | solution.py:35
  109.8 0.3 maximum_add_fusion
  110.1 1.6 %collective-permute-start.3 = (f32[256,768]{0,1:T(8,128)S(1)}, f32[256,768]{0,1:T(8,128)S(1)}, u32[]{:S(2)}, u32[]{:S(2)}) collective-permute-start(f32[256,768]{0,1:T(8,128)S(1)} %slice.26), channel_id=1, source_target_pairs={{0,2},{1,3},{2,0},{3,1},{4,6},{5,7},{6,4},{7,5},{8,10},{9,11},{10,... | collective-permute-start | bytes 2359304 | tf_op jit(solution)/shard_map/ppermute | solution.py:37
  111.7 3.2 %fusion.17 = bf16[1,1024,1024]{2,1,0:T(8,128)(2,1)} fusion(bf16[768,1024]{1,0:T(8,128)(2,1)S(1)} %constant_dynamic-update-slice_fusion, bf16[768,1024]{1,0:T(8,128)(2,1)S(1)} %fusion.9), kind=kOutput, calls=%fused_computation.26 | convolution fusion | flops 1612709888 | bytes 5242880 | tf_op jit(solution)/shard_map/dot_general | solution.py:119
  114.9 14.9 %collective-permute-done.3 = f32[256,768]{0,1:T(8,128)S(1)} collective-permute-done((f32[256,768]{0,1:T(8,128)S(1)}, f32[256,768]{0,1:T(8,128)S(1)}, u32[]{:S(2)}, u32[]{:S(2)}) %collective-permute-start.3) | collective-permute-done | bytes 786464 | tf_op jit(solution)/shard_map/ppermute | solution.py:37
  129.8 0.8 fusion.23
  130.6 3.7 %all-to-all-start.2 = ((bf16[256,8,96]{0,2,1:T(8,128)(2,1)}), bf16[256,8,96]{0,2,1:T(8,128)(2,1)S(1)}, u32[]{:S(2)}, u32[]{:S(2)}) async-start(bf16[256,8,96]{0,2,1:T(8,128)(2,1)} %bitcast.18), calls=%async_computation.2 | async-start | bytes 786432 | tf_op jit(solution)/shard_map/all_to_all | solution.py:107
  134.3 8.6 %fusion.2 = bf16[1,1024,2048]{2,1,0:T(8,128)(2,1)} fusion(bf16[768,2048]{1,0:T(8,128)(2,1)} %copy-done.1, f32[768,1024]{1,0:T(8,128)} %copy-done.4), kind=kOutput, calls=%fused_computation.11 | convolution fusion | flops 3232497664 | bytes 10485760 | tf_op jit(solution)/shard_map/dot_general | solution.py:122
  142.9 2.5 %all-to-all-done.2 = bf16[256,8,96]{0,2,1:T(8,128)(2,1)S(1)} async-done(((bf16[256,8,96]{0,2,1:T(8,128)(2,1)}), bf16[256,8,96]{0,2,1:T(8,128)(2,1)S(1)}, u32[]{:S(2)}, u32[]{:S(2)}) %all-to-all-start.2) | async-done | bytes 393248 | tf_op jit(solution)/shard_map/all_to_all | solution.py:107
  145.4 1.9 %gather_fusion.3 = bf16[512,256]{1,0:T(8,128)(2,1)S(1)} fusion(bf16[256,768]{0,1:T(8,128)(2,1)S(1)} %bitcast.58, s32[1024]{0:T(1024)S(1)} %pad_clamp_fusion), kind=kCustom, calls=%fused_computation.3 | custom fusion | bytes 526336 | tf_op jit(solution)/shard_map/gather | solution.py:110
  147.4 0.1 convert_element_type.78
  147.5 1.3 reduce.1
  (26 shorter events, 0.4 us)
Async XLA Ops:
  0.6 91.9 %copy-start = (bf16[1,1024,1024]{2,1,0:T(8,128)(2,1)S(1)}, bf16[1,1024,1024]{2,1,0:T(8,128)(2,1)}, u32[]{:S(2)}) copy-start(bf16[1,1024,1024]{2,1,0:T(8,128)(2,1)} %param.10) | copy-start | bytes 6291460
  17.5 10.3 %copy-start.2 = (bf16[256,1024]{1,0:T(8,128)(2,1)S(1)}, bf16[256,1024]{1,0:T(8,128)(2,1)}, u32[]{:S(2)}) copy-start(bf16[256,1024]{1,0:T(8,128)(2,1)} %param.6) | copy-start | bytes 1572868
  20.4 44.4 %all-to-all-start = ((bf16[8,96,1024]{2,1,0:T(8,128)(2,1)}), bf16[8,96,1024]{2,1,0:T(8,128)(2,1)}, u32[]{:S(2)}, u32[]{:S(2)}) async-start(bf16[8,96,1024]{2,1,0:T(8,128)(2,1)} %fusion.10), calls=%async_computation | async-start | bytes 3145728 | tf_op jit(solution)/shard_map/all_to_all | solution.py:70
  64.8 24.0 %all-to-all-start.1 = ((bf16[8,96,512]{2,1,0:T(8,128)(2,1)}), bf16[8,96,512]{2,1,0:T(8,128)(2,1)S(1)}, u32[]{:S(2)}, u32[]{:S(2)}) async-start(bf16[8,96,512]{2,1,0:T(8,128)(2,1)} %fusion.18), calls=%async_computation.1 | async-start | bytes 1572864 | tf_op jit(solution)/shard_map/all_to_all | solution.py:70
  68.5 28.5 %collective-permute-start = (bf16[768,1024]{1,0:T(8,128)(2,1)}, bf16[768,1024]{1,0:T(8,128)(2,1)}, u32[]{:S(2)}, u32[]{:S(2)}) collective-permute-start(bf16[768,1024]{1,0:T(8,128)(2,1)} %bitcast.9), channel_id=1, source_target_pairs={{0,1},{1,0},{2,3},{3,2},{4,5},{5,4},{6,7},{7,6},{8,9},{9,8},{10,11... | collective-permute-start | bytes 4718600 | tf_op jit(solution)/shard_map/ppermute | solution.py:73
  88.8 2.4 %collective-permute-start.1 = (bf16[768,512]{1,0:T(8,128)(2,1)S(1)}, bf16[768,512]{1,0:T(8,128)(2,1)}, u32[]{:S(2)}, u32[]{:S(2)}) collective-permute-start(bf16[768,512]{1,0:T(8,128)(2,1)S(1)} %bitcast.61), channel_id=1, source_target_pairs={{0,1},{1,0},{2,3},{3,2},{4,5},{5,4},{6,7},{7,6},{8,9},{9,8},{10,11... | collective-permute-start | bytes 2359304 | tf_op jit(solution)/shard_map/ppermute | solution.py:73
  94.3 4.5 %copy-start.4 = (f32[768,1024]{1,0:T(8,128)}, f32[768,1024]{1,0:T(8,128)S(1)}, u32[]{:S(2)}) copy-start(f32[768,1024]{1,0:T(8,128)S(1)} %fusion.15) | copy-start | bytes 9437188
  94.7 4.1 %copy-start.3 = (bf16[1,1024,2048]{2,1,0:T(8,128)(2,1)S(1)}, bf16[1,1024,2048]{2,1,0:T(8,128)(2,1)}, u32[]{:S(2)}) copy-start(bf16[1,1024,2048]{2,1,0:T(8,128)(2,1)} %param.11) | copy-start | bytes 12582916
  98.8 5.1 %copy-start.1 = (bf16[768,2048]{1,0:T(8,128)(2,1)}, bf16[768,2048]{1,0:T(8,128)(2,1)S(1)}, u32[]{:S(2)}) copy-start(bf16[768,2048]{1,0:T(8,128)(2,1)S(1)} %constant_dynamic-update-slice_fusion.2) | copy-start | bytes 9437188
  106.3 3.5 %collective-permute-start.2 = (f32[512,768]{0,1:T(8,128)S(1)}, f32[512,768]{0,1:T(8,128)S(1)}, u32[]{:S(2)}, u32[]{:S(2)}) collective-permute-start(f32[512,768]{0,1:T(8,128)S(1)} %pad_maximum_fusion), channel_id=1, source_target_pairs={{0,1},{1,0},{2,3},{3,2},{4,5},{5,4},{6,7},{7,6},{8,9},{9,8},{10,11... | collective-permute-start | bytes 4718600 | tf_op jit(solution)/shard_map/ppermute | solution.py:35
  110.1 19.6 %collective-permute-start.3 = (f32[256,768]{0,1:T(8,128)S(1)}, f32[256,768]{0,1:T(8,128)S(1)}, u32[]{:S(2)}, u32[]{:S(2)}) collective-permute-start(f32[256,768]{0,1:T(8,128)S(1)} %slice.26), channel_id=1, source_target_pairs={{0,2},{1,3},{2,0},{3,1},{4,6},{5,7},{6,4},{7,5},{8,10},{9,11},{10,... | collective-permute-start | bytes 2359304 | tf_op jit(solution)/shard_map/ppermute | solution.py:37
  130.6 14.8 %all-to-all-start.2 = ((bf16[256,8,96]{0,2,1:T(8,128)(2,1)}), bf16[256,8,96]{0,2,1:T(8,128)(2,1)S(1)}, u32[]{:S(2)}, u32[]{:S(2)}) async-start(bf16[256,8,96]{0,2,1:T(8,128)(2,1)} %bitcast.18), calls=%async_computation.2 | async-start | bytes 786432 | tf_op jit(solution)/shard_map/all_to_all | solution.py:107

commit v2 on v1

--- a/solution.py
+++ b/solution.py
@@ -47,26 +47,24 @@
     slot_count = device_count * capacity
     pair_count = 2 * tokens_here
     positions = slot_positions(expert_ids, replicas, E, capacity)
-    owner = (
-        jnp.full((slot_count,), pair_count, jnp.int32)
-        .at[positions]
-        .set(jnp.arange(pair_count, dtype=jnp.int32))
-    )
-    filled = owner < pair_count
-    pair_ids = jnp.minimum(owner, pair_count - 1)
-    token_ids = pair_ids // 2
-    gate_values = gate_levels.reshape(-1).astype(jnp.float32) / 16.0
-    slot_gates = jnp.where(filled, gate_values[pair_ids], 0.0)
-    slot_mask = filled.astype(jnp.bfloat16)[:, None]
+    slot_ids = jnp.arange(slot_count, dtype=jnp.int32)[:, None]
+    choices = positions.reshape(tokens_here, 2)
+    first_hit = choices[None, :, 0] == slot_ids
+    second_hit = choices[None, :, 1] == slot_ids
+    gates = gate_levels.astype(jnp.float32) / 16.0
+    pick = (first_hit | second_hit).astype(jnp.bfloat16)
+    pick_scaled = jnp.where(
+        first_hit, gates[None, :, 0], jnp.where(second_hit, gates[None, :, 1], 0.0)
+    ).astype(jnp.bfloat16)
     tp_size = lax.axis_size("tp")
     tp_index = lax.axis_index("tp")
     split = 2 if tp_size % 2 == 0 else 1
     half = tp_index % split
 
-    def dispatched(table, scale):
+    def dispatched(table, selection):
         width = table.shape[1] // split
-        mine = lax.dynamic_slice_in_dim(table, half * width, width, 1)[token_ids]
-        mine = (mine.astype(jnp.float32) * scale).astype(jnp.bfloat16)
+        mine = lax.dynamic_slice_in_dim(table, half * width, width, 1)
+        mine = jnp.dot(selection, mine, preferred_element_type=jnp.float32).astype(jnp.bfloat16)
         mine = lax.all_to_all(mine, "ep", split_axis=0, concat_axis=0, tiled=True)
         if split == 1:
             return mine
@@ -75,8 +73,8 @@
         whole = lax.dynamic_update_slice_in_dim(whole, mine, half * width, 1)
         return lax.dynamic_update_slice_in_dim(whole, other, (1 - half) * width, 1)
 
-    rows_x = dispatched(features, slot_mask.astype(jnp.float32))
-    rows_dy = dispatched(cotangent, slot_gates[:, None])
+    rows_x = dispatched(features, pick)
+    rows_dy = dispatched(cotangent, pick_scaled)
     piece_in = w_in[0]
     piece_out = w_out[0]
     span = piece_in.shape[1]
@@ -107,10 +105,9 @@
     returned = lax.all_to_all(
         summed.astype(jnp.bfloat16), "ep", split_axis=1, concat_axis=1, tiled=True
     )
-    picked = returned[:, positions].astype(jnp.float32)
-    grad_in = jnp.sum(picked.reshape(picked.shape[0], tokens_here, 2), axis=2).T.astype(
-        jnp.bfloat16
-    )
+    grad_in = lax.dot_general(
+        pick, returned, (((0,), (1,)), ((), ())), preferred_element_type=jnp.float32
+    ).astype(jnp.bfloat16)
 
     def span_grads(first_span, span_total):
         width = span_total * span

time: 149 us -> 134 us (0.90)
  local copies, waits for them, and re-layouts: 25.1 us -> 7.82 us
  other arithmetic: 9.5 us -> 4.1 us
  matrix products: 20.5 us -> 25.6 us
  waiting for transfers between devices: 76.2 us -> 79 us
    gather x4 -> x0, local copies, waits for them, and re-layouts: 13.2 us -> none  [the longest x2 6.24 us: dispatched(): mine = lax.dynamic_slice_in_dim(table, half * width, width, 1)[token_ids]]
    dot_general x0 -> x3, matrix products: none -> 5.12 us  [the longest x2 4.03 us: dispatched(): jnp.dot(selection, mine, preferred_element_type=jnp.float32)]
    convert_element_type x2 -> x0, other arithmetic: 4.05 us -> none  [dispatched(): mine = (mine.astype(jnp.float32) * scale).astype(jnp.bfloat16)]
    all_to_all x2, waiting for transfers between devices: 53.4 us -> 56.2 us  [dispatched(): mine = lax.all_to_all(mine, 'ep', split_axis=0, concat_axis=0, tiled=True)]
    scatter x1 -> x0, local copies, waits for them, and re-layouts: 2.45 us -> none  [shards(): owner = jnp.full((slot_count,), pair_count, jnp.int32).at[positions].set(...]
  transfers between devices with their start and end apart: 7 -> 7, of which waited for: 6 -> 6; matrix products, arithmetic and copies ran while one was open for 15% -> 14% of each run, Pallas kernels for 0% -> 0%
where the time goes in v2:
time: 134 us
  waiting for transfers between devices  79 us (59%)
  matrix products  25.6 us (19%)
  starting transfers between devices  16.4 us (12%)
  local copies, waits for them, and re-layouts  7.82 us (6%)
  other arithmetic  4.1 us (3%)
    all_to_all x2, waiting for transfers between devices, dispatched(): mine = lax.all_to_all(mine, 'ep', split_axis=0, concat_axis=0, tiled=True)  56.2 us
    ppermute x1, waiting for transfers between devices, chip_then_link_sum(): return mine + lax.ppermute(send, 'tp', [(i, i ^ 2) for i in range(4)])  14.9 us
    all_to_all x2, starting transfers between devices, dispatched(): mine = lax.all_to_all(mine, 'ep', split_axis=0, concat_axis=0, tiled=True)  10.9 us
    dot_general x1, matrix products, span_grads(): lax.dot_general(act_cols, rows_dy, (((0,), (0,)), ((), ())), preferred_el...  8.64 us
    dot_general x1, matrix products, shards(): lax.dot_general(rows_dy, weight_out, (((1,), (1,)), ((), ())), preferred_...  5.04 us
    dot_general x2, matrix products, dispatched(): jnp.dot(selection, mine, preferred_element_type=jnp.float32)  4.03 us
    all_to_all x1, starting transfers between devices, shards(): lax.all_to_all(summed.astype(jnp.bfloat16), 'ep', split_axis=1, concat_ax...  3.63 us
    ppermute x1, waiting for transfers between devices, chip_then_link_sum(): keep = keep + lax.ppermute(give, 'tp', [(i, i ^ 1) for i in range(4)])  3.26 us
  transfers between devices with their start and end apart: 7, of which 6 were waited for; matrix products, arithmetic and copies ran while one was open for 14% of the time, Pallas kernels for 0%

profile of v2, /device:TPU:0, one launch (start us, length us, event | category | flops | bytes accessed | tf_op | source)
XLA Modules:
  0.0 133.8 jit_solution(4079419662471943943)
XLA Ops:
  0.6 0.0 copy-start
  0.7 0.8 convert_multiply_fusion
  1.5 0.8 copy.15
  2.3 0.0 copy-start.3
  2.3 0.1 eq.60
  2.5 1.1 reduce-window.6
  3.6 0.2 slice_reduce_fusion
  3.9 0.1 fusion.37
  4.0 0.1 reduce_sum.12
  4.1 0.1 copy.16
  4.2 0.7 multiply_add_fusion
  4.9 2.8 %convolution_convert_fusion = bf16[768,1024]{1,0:T(8,128)(2,1)} fusion(bf16[256,2048]{1,0:T(8,128)(2,1)} %param.7, s32[]{:T(128)S(6)} %select_n.52, f32[256]{0:T(256)S(1)} %bitcast.67, f32[256]{0:T(256)S(1)} %bitcast.66, s32[256]{0:T(256)S(1)} %bitcast.63, s32[256]{0:T(256)S(1)} %bitcast.60), kind=kOutput, calls=%fused_computation.19 | convolution fusion | flops 404226048 | bytes 2101252 | tf_op jit(solution)/shard_map/dot_general | solution.py:67
  7.7 7.3 %all-to-all-start = ((bf16[8,96,1024]{2,1,0:T(8,128)(2,1)}), bf16[8,96,1024]{2,1,0:T(8,128)(2,1)}, u32[]{:S(2)}, u32[]{:S(2)}) async-start(bf16[8,96,1024]{2,1,0:T(8,128)(2,1)} %bitcast.56), calls=%async_computation | async-start | bytes 3145728 | tf_op jit(solution)/shard_map/all_to_all | solution.py:68
  15.0 0.0 copy-done.3
  15.0 1.3 convolution_convert_fusion.1
  16.2 35.8 %all-to-all-done = bf16[8,96,1024]{2,1,0:T(8,128)(2,1)} async-done(((bf16[8,96,1024]{2,1,0:T(8,128)(2,1)}), bf16[8,96,1024]{2,1,0:T(8,128)(2,1)}, u32[]{:S(2)}, u32[]{:S(2)}) %all-to-all-start) | async-done | bytes 1572896 | tf_op jit(solution)/shard_map/all_to_all | solution.py:68
  52.1 3.6 %all-to-all-start.1 = ((bf16[8,96,512]{2,1,0:T(8,128)(2,1)}), bf16[8,96,512]{2,1,0:T(8,128)(2,1)S(1)}, u32[]{:S(2)}, u32[]{:S(2)}) async-start(bf16[8,96,512]{2,1,0:T(8,128)(2,1)} %bitcast.57), calls=%async_computation.1 | async-start | bytes 1572864 | tf_op jit(solution)/shard_map/all_to_all | solution.py:68
  55.7 0.0 collective-permute-start
  55.7 20.3 %all-to-all-done.1 = bf16[8,96,512]{2,1,0:T(8,128)(2,1)S(1)} async-done(((bf16[8,96,512]{2,1,0:T(8,128)(2,1)}), bf16[8,96,512]{2,1,0:T(8,128)(2,1)S(1)}, u32[]{:S(2)}, u32[]{:S(2)}) %all-to-all-start.1) | async-done | bytes 786464 | tf_op jit(solution)/shard_map/all_to_all | solution.py:68
  76.1 0.0 collective-permute-start.1
  76.1 0.2 broadcast_in_dim.46
  76.3 0.1 constant_dynamic-update-slice_fusion.1
  76.4 2.1 %collective-permute-done.1 = bf16[768,512]{1,0:T(8,128)(2,1)} collective-permute-done((bf16[768,512]{1,0:T(8,128)(2,1)S(1)}, bf16[768,512]{1,0:T(8,128)(2,1)}, u32[]{:S(2)}, u32[]{:S(2)}) %collective-permute-start.1) | collective-permute-done | bytes 786464 | tf_op jit(solution)/shard_map/ppermute | solution.py:71
  78.5 1.2 constant_dynamic-update-slice_fusion
  79.7 0.0 copy-done
  79.8 1.8 %fusion.14 = f32[768,1024]{1,0:T(8,128)S(1)} fusion(bf16[768,1024]{1,0:T(8,128)(2,1)S(1)} %constant_dynamic-update-slice_fusion, bf16[1,1024,1024]{2,1,0:T(8,128)(2,1)S(1)} %copy-done), kind=kOutput, calls=%fused_computation.17 | convolution fusion | flops 1610612736 | bytes 6815744 | tf_op jit(solution)/shard_map/dot_general | solution.py:91
  81.5 0.0 copy-start.4
  81.6 0.4 broadcast_in_dim.40
  81.9 0.0 copy-start.2
  82.0 2.4 %constant_dynamic-update-slice_fusion.3 = bf16[768,2048]{1,0:T(8,128)(2,1)S(1)} fusion(bf16[768,2048]{1,0:T(8,128)(2,1)S(1)} %broadcast_in_dim.40, bf16[768,1024]{1,0:T(8,128)(2,1)} %bitcast.11, s32[]{:T(128)S(6)} %select_n.52), kind=kLoop, calls=%fused_computation.61 | loop fusion | bytes 3145732 | tf_op jit(solution)/shard_map/dynamic_update_slice | solution.py:73
  84.3 0.0 collective-permute-done
  84.3 1.7 %constant_dynamic-update-slice_fusion.2 = bf16[768,2048]{1,0:T(8,128)(2,1)S(1)} fusion(bf16[768,2048]{1,0:T(8,128)(2,1)S(1)} %constant_dynamic-update-slice_fusion.3, bf16[768,1024]{1,0:T(8,128)(2,1)} %collective-permute-done, s32[]{:T(128)S(6)} %select_n.53), kind=kLoop, calls=%fused_computation.60 | loop fusion | bytes 3145732 | tf_op jit(solution)/shard_map/dynamic_update_slice | solution.py:74
  86.0 5.0 %fusion.9 = bf16[768,1024]{1,0:T(8,128)(2,1)S(1)} fusion(f32[768,1024]{1,0:T(8,128)S(1)} %fusion.14, bf16[768,2048]{1,0:T(8,128)(2,1)S(1)} %constant_dynamic-update-slice_fusion.2, bf16[1,1024,2048]{2,1,0:T(8,128)(2,1)S(1)} %copy-done.2), kind=kOutput, calls=%fused_computation.13 | convolution fusion | flops 3236954112 | bytes 12058624 | tf_op jit(solution)/shard_map/dot_general | solution.py:94
  91.1 1.8 %fusion.12 = f32[768,1024]{1,0:T(8,128)S(1)} fusion(bf16[768,1024]{1,0:T(8,128)(2,1)S(1)} %fusion.9, bf16[1,1024,1024]{2,1,0:T(8,128)(2,1)S(1)} %copy-done), kind=kOutput, calls=%fused_computation.15 | convolution fusion | flops 1610612736 | bytes 6815744 | tf_op jit(solution)/shard_map/dot_general | solution.py:98
  92.9 0.4 dynamic-slice_bitcast_fusion.3
  93.3 0.2 pad_maximum_fusion
  93.5 0.2 collective-permute-start.2
  93.7 3.3 %collective-permute-done.2 = f32[512,768]{0,1:T(8,128)S(1)} collective-permute-done((f32[512,768]{0,1:T(8,128)S(1)}, f32[512,768]{0,1:T(8,128)S(1)}, u32[]{:S(2)}, u32[]{:S(2)}) %collective-permute-start.2) | collective-permute-done | bytes 1572896 | tf_op jit(solution)/shard_map/ppermute | solution.py:35
  97.0 0.3 maximum_add_fusion
  97.3 0.1 slice.38
  97.3 1.6 %collective-permute-start.3 = (f32[256,768]{0,1:T(8,128)S(1)}, f32[256,768]{0,1:T(8,128)S(1)}, u32[]{:S(2)}, u32[]{:S(2)}) collective-permute-start(f32[256,768]{0,1:T(8,128)S(1)} %slice.38), channel_id=1, source_target_pairs={{0,2},{1,3},{2,0},{3,1},{4,6},{5,7},{6,4},{7,5},{8,10},{9,11},{10,... | collective-permute-start | bytes 2359304 | tf_op jit(solution)/shard_map/ppermute | solution.py:37
  98.9 3.2 %fusion.16 = bf16[1,1024,1024]{2,1,0:T(8,128)(2,1)} fusion(bf16[768,1024]{1,0:T(8,128)(2,1)S(1)} %constant_dynamic-update-slice_fusion, bf16[768,1024]{1,0:T(8,128)(2,1)S(1)} %fusion.9), kind=kOutput, calls=%fused_computation.20 | convolution fusion | flops 1612709888 | bytes 5242880 | tf_op jit(solution)/shard_map/dot_general | solution.py:116
  102.1 14.9 %collective-permute-done.3 = f32[256,768]{0,1:T(8,128)S(1)} collective-permute-done((f32[256,768]{0,1:T(8,128)S(1)}, f32[256,768]{0,1:T(8,128)S(1)}, u32[]{:S(2)}, u32[]{:S(2)}) %collective-permute-start.3) | collective-permute-done | bytes 786464 | tf_op jit(solution)/shard_map/ppermute | solution.py:37
  117.0 0.8 fusion.21
  117.8 3.6 %all-to-all-start.2 = ((bf16[256,8,96]{0,2,1:T(8,128)(2,1)}), bf16[256,8,96]{0,2,1:T(8,128)(2,1)S(1)}, u32[]{:S(2)}, u32[]{:S(2)}) async-start(bf16[256,8,96]{0,2,1:T(8,128)(2,1)} %bitcast.20), calls=%async_computation.2 | async-start | bytes 786432 | tf_op jit(solution)/shard_map/all_to_all | solution.py:105
  121.5 8.6 %fusion.2 = bf16[1,1024,2048]{2,1,0:T(8,128)(2,1)} fusion(bf16[768,2048]{1,0:T(8,128)(2,1)} %copy-done.1, f32[768,1024]{1,0:T(8,128)} %copy-done.4), kind=kOutput, calls=%fused_computation.6 | convolution fusion | flops 3232497664 | bytes 10485760 | tf_op jit(solution)/shard_map/dot_general | solution.py:119
  130.1 2.5 %all-to-all-done.2 = bf16[256,8,96]{0,2,1:T(8,128)(2,1)S(1)} async-done(((bf16[256,8,96]{0,2,1:T(8,128)(2,1)}), bf16[256,8,96]{0,2,1:T(8,128)(2,1)S(1)}, u32[]{:S(2)}, u32[]{:S(2)}) %all-to-all-start.2) | async-done | bytes 393248 | tf_op jit(solution)/shard_map/all_to_all | solution.py:105
  132.7 1.1 convolution_convert_fusion.2
  (9 shorter events, 0.1 us)
Async XLA Ops:
  0.6 79.1 %copy-start = (bf16[1,1024,1024]{2,1,0:T(8,128)(2,1)S(1)}, bf16[1,1024,1024]{2,1,0:T(8,128)(2,1)}, u32[]{:S(2)}) copy-start(bf16[1,1024,1024]{2,1,0:T(8,128)(2,1)} %param.10) | copy-start | bytes 6291460
  2.3 12.6 %copy-start.3 = (bf16[256,1024]{1,0:T(8,128)(2,1)S(1)}, bf16[256,1024]{1,0:T(8,128)(2,1)}, u32[]{:S(2)}) copy-start(bf16[256,1024]{1,0:T(8,128)(2,1)} %param.6) | copy-start | bytes 1572868
  7.7 44.4 %all-to-all-start = ((bf16[8,96,1024]{2,1,0:T(8,128)(2,1)}), bf16[8,96,1024]{2,1,0:T(8,128)(2,1)}, u32[]{:S(2)}, u32[]{:S(2)}) async-start(bf16[8,96,1024]{2,1,0:T(8,128)(2,1)} %bitcast.56), calls=%async_computation | async-start | bytes 3145728 | tf_op jit(solution)/shard_map/all_to_all | solution.py:68
  52.1 24.0 %all-to-all-start.1 = ((bf16[8,96,512]{2,1,0:T(8,128)(2,1)}), bf16[8,96,512]{2,1,0:T(8,128)(2,1)S(1)}, u32[]{:S(2)}, u32[]{:S(2)}) async-start(bf16[8,96,512]{2,1,0:T(8,128)(2,1)} %bitcast.57), calls=%async_computation.1 | async-start | bytes 1572864 | tf_op jit(solution)/shard_map/all_to_all | solution.py:68
  55.7 28.6 %collective-permute-start = (bf16[768,1024]{1,0:T(8,128)(2,1)}, bf16[768,1024]{1,0:T(8,128)(2,1)}, u32[]{:S(2)}, u32[]{:S(2)}) collective-permute-start(bf16[768,1024]{1,0:T(8,128)(2,1)} %bitcast.11), channel_id=1, source_target_pairs={{0,1},{1,0},{2,3},{3,2},{4,5},{5,4},{6,7},{7,6},{8,9},{9,8},{10,11... | collective-permute-start | bytes 4718600 | tf_op jit(solution)/shard_map/ppermute | solution.py:71
  76.1 2.4 %collective-permute-start.1 = (bf16[768,512]{1,0:T(8,128)(2,1)S(1)}, bf16[768,512]{1,0:T(8,128)(2,1)}, u32[]{:S(2)}, u32[]{:S(2)}) collective-permute-start(bf16[768,512]{1,0:T(8,128)(2,1)S(1)} %bitcast.54), channel_id=1, source_target_pairs={{0,1},{1,0},{2,3},{3,2},{4,5},{5,4},{6,7},{7,6},{8,9},{9,8},{10,11... | collective-permute-start | bytes 2359304 | tf_op jit(solution)/shard_map/ppermute | solution.py:71
  81.5 4.5 %copy-start.4 = (f32[768,1024]{1,0:T(8,128)}, f32[768,1024]{1,0:T(8,128)S(1)}, u32[]{:S(2)}) copy-start(f32[768,1024]{1,0:T(8,128)S(1)} %fusion.14) | copy-start | bytes 9437188
  81.9 4.1 %copy-start.2 = (bf16[1,1024,2048]{2,1,0:T(8,128)(2,1)S(1)}, bf16[1,1024,2048]{2,1,0:T(8,128)(2,1)}, u32[]{:S(2)}) copy-start(bf16[1,1024,2048]{2,1,0:T(8,128)(2,1)} %param.11) | copy-start | bytes 12582916
  86.0 5.1 %copy-start.1 = (bf16[768,2048]{1,0:T(8,128)(2,1)}, bf16[768,2048]{1,0:T(8,128)(2,1)S(1)}, u32[]{:S(2)}) copy-start(bf16[768,2048]{1,0:T(8,128)(2,1)S(1)} %constant_dynamic-update-slice_fusion.2) | copy-start | bytes 9437188
  93.5 3.5 %collective-permute-start.2 = (f32[512,768]{0,1:T(8,128)S(1)}, f32[512,768]{0,1:T(8,128)S(1)}, u32[]{:S(2)}, u32[]{:S(2)}) collective-permute-start(f32[512,768]{0,1:T(8,128)S(1)} %pad_maximum_fusion), channel_id=1, source_target_pairs={{0,1},{1,0},{2,3},{3,2},{4,5},{5,4},{6,7},{7,6},{8,9},{9,8},{10,11... | collective-permute-start | bytes 4718600 | tf_op jit(solution)/shard_map/ppermute | solution.py:35
  97.3 19.7 %collective-permute-start.3 = (f32[256,768]{0,1:T(8,128)S(1)}, f32[256,768]{0,1:T(8,128)S(1)}, u32[]{:S(2)}, u32[]{:S(2)}) collective-permute-start(f32[256,768]{0,1:T(8,128)S(1)} %slice.38), channel_id=1, source_target_pairs={{0,2},{1,3},{2,0},{3,1},{4,6},{5,7},{6,4},{7,5},{8,10},{9,11},{10,... | collective-permute-start | bytes 2359304 | tf_op jit(solution)/shard_map/ppermute | solution.py:37
  117.8 14.8 %all-to-all-start.2 = ((bf16[256,8,96]{0,2,1:T(8,128)(2,1)}), bf16[256,8,96]{0,2,1:T(8,128)(2,1)S(1)}, u32[]{:S(2)}, u32[]{:S(2)}) async-start(bf16[256,8,96]{0,2,1:T(8,128)(2,1)} %bitcast.20), calls=%async_computation.2 | async-start | bytes 786432 | tf_op jit(solution)/shard_map/all_to_all | solution.py:105

commit v3 on v2

--- a/solution.py
+++ b/solution.py
@@ -58,20 +58,29 @@
     ).astype(jnp.bfloat16)
     tp_size = lax.axis_size("tp")
     tp_index = lax.axis_index("tp")
-    split = 2 if tp_size % 2 == 0 else 1
-    half = tp_index % split
+    split = 4 if tp_size == 4 else (2 if tp_size % 2 == 0 else 1)
 
     def dispatched(table, selection):
         width = table.shape[1] // split
-        mine = lax.dynamic_slice_in_dim(table, half * width, width, 1)
+        part = tp_index % split
+        mine = lax.dynamic_slice_in_dim(table, part * width, width, 1)
         mine = jnp.dot(selection, mine, preferred_element_type=jnp.float32).astype(jnp.bfloat16)
         mine = lax.all_to_all(mine, "ep", split_axis=0, concat_axis=0, tiled=True)
+        pieces = [(mine, part)]
+        if split == 4:
+            across = lax.ppermute(mine, "tp", [(i, i ^ 2) for i in range(tp_size)])
+            pieces.append((across, part ^ 2))
+        if split >= 2:
+            pieces += [
+                (lax.ppermute(piece, "tp", [(i, i ^ 1) for i in range(tp_size)]), where ^ 1)
+                for piece, where in pieces
+            ]
         if split == 1:
             return mine
-        other = lax.ppermute(mine, "tp", [(i, i ^ 1) for i in range(tp_size)])
         whole = jnp.zeros((mine.shape[0], table.shape[1]), jnp.bfloat16)
-        whole = lax.dynamic_update_slice_in_dim(whole, mine, half * width, 1)
-        return lax.dynamic_update_slice_in_dim(whole, other, (1 - half) * width, 1)
+        for piece, where in pieces:
+            whole = lax.dynamic_update_slice_in_dim(whole, piece, where * width, 1)
+        return whole
 
     rows_x = dispatched(features, pick)
     rows_dy = dispatched(cotangent, pick_scaled)

time: 134 us -> 123 us (0.918)
  waiting for transfers between devices: 79 us -> 61.2 us
  starting transfers between devices: 16.4 us -> 22 us
    all_to_all x2, waiting for transfers between devices: 56.2 us -> 27.4 us  [dispatched(): mine = lax.all_to_all(mine, 'ep', split_axis=0, concat_axis=0, tiled=True)]
    ppermute x2 -> x6, waiting for transfers between devices: 2.11 us -> 12.9 us  [the longest x2 12.9 us: dispatched(): across = lax.ppermute(mine, 'tp', [(i, i ^ 2) for i in range(tp_size)])]
    ppermute x2 -> x6, starting transfers between devices: 0.03 us -> 3.77 us  [the longest x2 3.06 us: dispatched(): across = lax.ppermute(mine, 'tp', [(i, i ^ 2) for i in range(tp_size)])]
    unnamed x11 -> x9, local copies, waits for them, and re-layouts: 0.84 us -> 2.32 us
    all_to_all x1, starting transfers between devices: 3.63 us -> 5.11 us  [shards(): lax.all_to_all(summed.astype(jnp.bfloat16), 'ep', split_axis=1, concat_ax...]
    dynamic_update_slice x4 -> x8, local copies, waits for them, and re-layouts: 5.37 us -> 4.44 us  [dispatched(): whole = lax.dynamic_update_slice_in_dim(whole, piece, where * width, 1)]
  transfers between devices with their start and end apart: 7 -> 11, of which waited for: 6 -> 6; matrix products, arithmetic and copies ran while one was open for 14% -> 18% of each run, Pallas kernels for 0% -> 0%
where the time goes in v3:
time: 123 us; the launch traced here: 122 us
  waiting for transfers between devices  61.2 us (50%)
  matrix products  25.7 us (21%)
  starting transfers between devices  22 us (18%)
  local copies, waits for them, and re-layouts  8.38 us (7%)
  other arithmetic  3.95 us (3%)
    all_to_all x2, waiting for transfers between devices, dispatched(): mine = lax.all_to_all(mine, 'ep', split_axis=0, concat_axis=0, tiled=True)  27.4 us
    ppermute x1, waiting for transfers between devices, chip_then_link_sum(): return mine + lax.ppermute(send, 'tp', [(i, i ^ 2) for i in range(4)])  15.1 us
    ppermute x2, waiting for transfers between devices, dispatched(): across = lax.ppermute(mine, 'tp', [(i, i ^ 2) for i in range(tp_size)])  12.9 us
    all_to_all x2, starting transfers between devices, dispatched(): mine = lax.all_to_all(mine, 'ep', split_axis=0, concat_axis=0, tiled=True)  10.9 us
    dot_general x1, matrix products, span_grads(): lax.dot_general(act_cols, rows_dy, (((0,), (0,)), ((), ())), preferred_el...  8.64 us
    all_to_all x1, starting transfers between devices, shards(): lax.all_to_all(summed.astype(jnp.bfloat16), 'ep', split_axis=1, concat_ax...  5.11 us
    dot_general x1, matrix products, shards(): lax.dot_general(rows_dy, weight_out, (((1,), (1,)), ((), ())), preferred_...  5.04 us
    dynamic_update_slice x8, local copies, waits for them, and re-layouts, dispatched(): whole = lax.dynamic_update_slice_in_dim(whole, piece, where * width, 1)  4.44 us
  transfers between devices with their start and end apart: 11, of which 6 were waited for; matrix products, arithmetic and copies ran while one was open for 18% of the time, Pallas kernels for 0%

profile of v3, /device:TPU:0, one launch (start us, length us, event | category | flops | bytes accessed | tf_op | source)
XLA Modules:
  0.0 122.1 jit_solution(6085035181139207299)
XLA Ops:
  0.6 0.0 copy-start
  0.7 1.0 copy.15
  1.6 0.1 eq.61
  1.8 1.1 reduce-window.6
  2.9 0.2 slice_reduce_fusion
  3.2 0.1 fusion.37
  3.3 0.1 reduce_sum.12
  3.4 0.1 copy.16
  3.5 0.7 multiply_add_fusion
  4.2 1.9 %convolution_convert_fusion.1 = bf16[768,256]{1,0:T(8,128)(2,1)} fusion(s32[256]{0:T(256)S(1)} %bitcast.66, s32[256]{0:T(256)S(1)} %bitcast.63, bf16[256,1024]{1,0:T(8,128)(2,1)} %param.6, s32[]{:T(128)S(6)} %select_n.70), kind=kOutput, calls=%fused_computation.27 | convolution fusion | flops 101449728 | bytes 526340 | tf_op jit(solution)/shard_map/dot_general | solution.py:67
  6.2 7.3 %all-to-all-start.1 = ((bf16[8,96,256]{2,1,0:T(8,128)(2,1)}), bf16[8,96,256]{2,1,0:T(8,128)(2,1)S(1)}, u32[]{:S(2)}, u32[]{:S(2)}) async-start(bf16[8,96,256]{2,1,0:T(8,128)(2,1)} %bitcast.13), calls=%async_computation.1 | async-start | bytes 786432 | tf_op jit(solution)/shard_map/all_to_all | solution.py:68
  13.4 0.7 convert_multiply_fusion
  14.1 2.2 %convolution_convert_fusion = bf16[768,512]{1,0:T(8,128)(2,1)} fusion(f32[256]{0:T(256)S(1)} %bitcast.70, f32[256]{0:T(256)S(1)} %bitcast.69, s32[256]{0:T(256)S(1)} %bitcast.67, s32[256]{0:T(256)S(1)} %bitcast.64, bf16[256,2048]{1,0:T(8,128)(2,1)} %param.7, s32[]{:T(128)S(6)} %select_n.66), kind=kOutput, calls=%fused_computation.26 | convolution fusion | flops 202506240 | bytes 1052676 | tf_op jit(solution)/shard_map/dot_general | solution.py:67
  16.3 8.8 %all-to-all-done.1 = bf16[8,96,256]{2,1,0:T(8,128)(2,1)S(1)} async-done(((bf16[8,96,256]{2,1,0:T(8,128)(2,1)}), bf16[8,96,256]{2,1,0:T(8,128)(2,1)S(1)}, u32[]{:S(2)}, u32[]{:S(2)}) %all-to-all-start.1) | async-done | bytes 393248 | tf_op jit(solution)/shard_map/all_to_all | solution.py:68
  25.1 3.6 %all-to-all-start = ((bf16[8,96,512]{2,1,0:T(8,128)(2,1)}), bf16[8,96,512]{2,1,0:T(8,128)(2,1)S(1)}, u32[]{:S(2)}, u32[]{:S(2)}) async-start(bf16[8,96,512]{2,1,0:T(8,128)(2,1)} %bitcast.60), calls=%async_computation | async-start | bytes 1572864 | tf_op jit(solution)/shard_map/all_to_all | solution.py:68
  28.8 1.5 %collective-permute-start.3 = (bf16[768,256]{1,0:T(8,128)(2,1)S(1)}, bf16[768,256]{1,0:T(8,128)(2,1)}, u32[]{:S(2)}, u32[]{:S(2)}) collective-permute-start(bf16[768,256]{1,0:T(8,128)(2,1)S(1)} %bitcast.57), channel_id=1, source_target_pairs={{0,2},{1,3},{2,0},{3,1},{4,6},{5,7},{6,4},{7,5},{8,10},{9,11},{10,... | collective-permute-start | bytes 1179656 | tf_op jit(solution)/shard_map/ppermute | solution.py:71
  30.3 18.6 %all-to-all-done = bf16[8,96,512]{2,1,0:T(8,128)(2,1)S(1)} async-done(((bf16[8,96,512]{2,1,0:T(8,128)(2,1)}), bf16[8,96,512]{2,1,0:T(8,128)(2,1)S(1)}, u32[]{:S(2)}, u32[]{:S(2)}) %all-to-all-start) | async-done | bytes 786464 | tf_op jit(solution)/shard_map/all_to_all | solution.py:68
  48.9 1.5 %collective-permute-start = (bf16[768,512]{1,0:T(8,128)(2,1)S(1)}, bf16[768,512]{1,0:T(8,128)(2,1)}, u32[]{:S(2)}, u32[]{:S(2)}) collective-permute-start(bf16[768,512]{1,0:T(8,128)(2,1)S(1)} %bitcast.54), channel_id=1, source_target_pairs={{0,2},{1,3},{2,0},{3,1},{4,6},{5,7},{6,4},{7,5},{8,10},{9,11},{10,... | collective-permute-start | bytes 2359304 | tf_op jit(solution)/shard_map/ppermute | solution.py:71
  50.4 0.5 collective-permute-start.5
  50.9 0.2 broadcast_in_dim.46
  51.2 1.0 constant_dynamic-update-slice_fusion.2
  52.2 0.0 collective-permute-done.4
  52.3 1.0 constant_dynamic-update-slice_fusion.1
  53.3 0.2 collective-permute-start.1
  53.5 0.4 broadcast_in_dim.40
  53.9 0.1 constant_dynamic-update-slice_fusion.7
  54.0 12.9 %collective-permute-done = bf16[768,512]{1,0:T(8,128)(2,1)} collective-permute-done((bf16[768,512]{1,0:T(8,128)(2,1)S(1)}, bf16[768,512]{1,0:T(8,128)(2,1)}, u32[]{:S(2)}, u32[]{:S(2)}) %collective-permute-start) | collective-permute-done | bytes 786464 | tf_op jit(solution)/shard_map/ppermute | solution.py:71
  66.9 1.8 %fusion.14 = f32[768,1024]{1,0:T(8,128)S(1)} fusion(bf16[768,1024]{1,0:T(8,128)(2,1)S(1)} %constant_dynamic-update-slice_fusion, bf16[1,1024,1024]{2,1,0:T(8,128)(2,1)S(1)} %copy-done), kind=kOutput, calls=%fused_computation.17 | convolution fusion | flops 1610612736 | bytes 6815744 | tf_op jit(solution)/shard_map/dot_general | solution.py:100
  68.8 2.0 %constant_dynamic-update-slice_fusion.6 = bf16[768,2048]{1,0:T(8,128)(2,1)S(1)} fusion(bf16[768,2048]{1,0:T(8,128)(2,1)S(1)} %constant_dynamic-update-slice_fusion.7, bf16[768,512]{1,0:T(8,128)(2,1)} %collective-permute-done, s32[]{:T(128)S(6)} %select_n.67), kind=kLoop, calls=%fused_computation.64 | loop fusion | bytes 1572868 | tf_op jit(solution)/shard_map/dynamic_update_slice | solution.py:82
  70.7 0.1 constant_dynamic-update-slice_fusion.5
  70.9 0.1 constant_dynamic-update-slice_fusion.4
  71.0 1.3 %copy-done.2 = bf16[1,1024,2048]{2,1,0:T(8,128)(2,1)S(1)} copy-done((bf16[1,1024,2048]{2,1,0:T(8,128)(2,1)S(1)}, bf16[1,1024,2048]{2,1,0:T(8,128)(2,1)}, u32[]{:S(2)}) %copy-start.2) | copy-done | bytes 4194328
  72.3 5.0 %fusion.9 = bf16[768,1024]{1,0:T(8,128)(2,1)S(1)} fusion(f32[768,1024]{1,0:T(8,128)S(1)} %fusion.14, bf16[768,2048]{1,0:T(8,128)(2,1)S(1)} %constant_dynamic-update-slice_fusion.4, bf16[1,1024,2048]{2,1,0:T(8,128)(2,1)S(1)} %copy-done.2), kind=kOutput, calls=%fused_computation.13 | convolution fusion | flops 3236954112 | bytes 12058624 | tf_op jit(solution)/shard_map/dot_general | solution.py:103
  77.4 1.8 %fusion.12 = f32[768,1024]{1,0:T(8,128)S(1)} fusion(bf16[768,1024]{1,0:T(8,128)(2,1)S(1)} %fusion.9, bf16[1,1024,1024]{2,1,0:T(8,128)(2,1)S(1)} %copy-done), kind=kOutput, calls=%fused_computation.15 | convolution fusion | flops 1610612736 | bytes 6815744 | tf_op jit(solution)/shard_map/dot_general | solution.py:107
  79.2 0.4 dynamic-slice_bitcast_fusion.3
  79.6 0.2 pad_maximum_fusion
  79.8 0.6 collective-permute-start.6
  80.4 3.0 %collective-permute-done.6 = f32[512,768]{0,1:T(8,128)S(1)} collective-permute-done((f32[512,768]{0,1:T(8,128)S(1)}, f32[512,768]{0,1:T(8,128)S(1)}, u32[]{:S(2)}, u32[]{:S(2)}) %collective-permute-start.6) | collective-permute-done | bytes 1572896 | tf_op jit(solution)/shard_map/ppermute | solution.py:35
  83.4 0.3 maximum_add_fusion
  83.7 0.1 slice.38
  83.7 1.6 %collective-permute-start.7 = (f32[256,768]{0,1:T(8,128)S(1)}, f32[256,768]{0,1:T(8,128)S(1)}, u32[]{:S(2)}, u32[]{:S(2)}) collective-permute-start(f32[256,768]{0,1:T(8,128)S(1)} %slice.38), channel_id=1, source_target_pairs={{0,2},{1,3},{2,0},{3,1},{4,6},{5,7},{6,4},{7,5},{8,10},{9,11},{10,... | collective-permute-start | bytes 2359304 | tf_op jit(solution)/shard_map/ppermute | solution.py:37
  85.3 3.2 %fusion.16 = bf16[1,1024,1024]{2,1,0:T(8,128)(2,1)} fusion(bf16[768,1024]{1,0:T(8,128)(2,1)S(1)} %constant_dynamic-update-slice_fusion, bf16[768,1024]{1,0:T(8,128)(2,1)S(1)} %fusion.9), kind=kOutput, calls=%fused_computation.19 | convolution fusion | flops 1612709888 | bytes 5242880 | tf_op jit(solution)/shard_map/dot_general | solution.py:125
  88.5 15.1 %collective-permute-done.7 = f32[256,768]{0,1:T(8,128)S(1)} collective-permute-done((f32[256,768]{0,1:T(8,128)S(1)}, f32[256,768]{0,1:T(8,128)S(1)}, u32[]{:S(2)}, u32[]{:S(2)}) %collective-permute-start.7) | collective-permute-done | bytes 786464 | tf_op jit(solution)/shard_map/ppermute | solution.py:37
  103.6 0.9 fusion.21
  104.5 5.1 %all-to-all-start.2 = ((bf16[256,8,96]{0,2,1:T(8,128)(2,1)}), bf16[256,8,96]{0,2,1:T(8,128)(2,1)S(1)}, u32[]{:S(2)}, u32[]{:S(2)}) async-start(bf16[256,8,96]{0,2,1:T(8,128)(2,1)} %bitcast.20), calls=%async_computation.2 | async-start | bytes 786432 | tf_op jit(solution)/shard_map/all_to_all | solution.py:114
  109.6 8.6 %fusion.2 = bf16[1,1024,2048]{2,1,0:T(8,128)(2,1)} fusion(bf16[768,2048]{1,0:T(8,128)(2,1)} %copy-done.1, f32[768,1024]{1,0:T(8,128)} %copy-done.3), kind=kOutput, calls=%fused_computation.6 | convolution fusion | flops 3232497664 | bytes 10485760 | tf_op jit(solution)/shard_map/dot_general | solution.py:128
  118.2 2.8 %all-to-all-done.2 = bf16[256,8,96]{0,2,1:T(8,128)(2,1)S(1)} async-done(((bf16[256,8,96]{0,2,1:T(8,128)(2,1)}), bf16[256,8,96]{0,2,1:T(8,128)(2,1)S(1)}, u32[]{:S(2)}, u32[]{:S(2)}) %all-to-all-start.2) | async-done | bytes 393248 | tf_op jit(solution)/shard_map/all_to_all | solution.py:114
  121.0 1.1 convolution_convert_fusion.2
  (19 shorter events, 0.2 us)
Async XLA Ops:
  0.6 66.3 %copy-start = (bf16[1,1024,1024]{2,1,0:T(8,128)(2,1)S(1)}, bf16[1,1024,1024]{2,1,0:T(8,128)(2,1)}, u32[]{:S(2)}) copy-start(bf16[1,1024,1024]{2,1,0:T(8,128)(2,1)} %param.10) | copy-start | bytes 6291460
  6.2 19.0 %all-to-all-start.1 = ((bf16[8,96,256]{2,1,0:T(8,128)(2,1)}), bf16[8,96,256]{2,1,0:T(8,128)(2,1)S(1)}, u32[]{:S(2)}, u32[]{:S(2)}) async-start(bf16[8,96,256]{2,1,0:T(8,128)(2,1)} %bitcast.13), calls=%async_computation.1 | async-start | bytes 786432 | tf_op jit(solution)/shard_map/all_to_all | solution.py:68
  25.1 23.8 %all-to-all-start = ((bf16[8,96,512]{2,1,0:T(8,128)(2,1)}), bf16[8,96,512]{2,1,0:T(8,128)(2,1)S(1)}, u32[]{:S(2)}, u32[]{:S(2)}) async-start(bf16[8,96,512]{2,1,0:T(8,128)(2,1)} %bitcast.60), calls=%async_computation | async-start | bytes 1572864 | tf_op jit(solution)/shard_map/all_to_all | solution.py:68
  28.8 21.7 %collective-permute-start.3 = (bf16[768,256]{1,0:T(8,128)(2,1)S(1)}, bf16[768,256]{1,0:T(8,128)(2,1)}, u32[]{:S(2)}, u32[]{:S(2)}) collective-permute-start(bf16[768,256]{1,0:T(8,128)(2,1)S(1)} %bitcast.57), channel_id=1, source_target_pairs={{0,2},{1,3},{2,0},{3,1},{4,6},{5,7},{6,4},{7,5},{8,10},{9,11},{10,... | collective-permute-start | bytes 1179656 | tf_op jit(solution)/shard_map/ppermute | solution.py:71
  48.9 18.0 %collective-permute-start = (bf16[768,512]{1,0:T(8,128)(2,1)S(1)}, bf16[768,512]{1,0:T(8,128)(2,1)}, u32[]{:S(2)}, u32[]{:S(2)}) collective-permute-start(bf16[768,512]{1,0:T(8,128)(2,1)S(1)} %bitcast.54), channel_id=1, source_target_pairs={{0,2},{1,3},{2,0},{3,1},{4,6},{5,7},{6,4},{7,5},{8,10},{9,11},{10,... | collective-permute-start | bytes 2359304 | tf_op jit(solution)/shard_map/ppermute | solution.py:71
  50.4 1.9 %collective-permute-start.4 = (bf16[768,256]{1,0:T(8,128)(2,1)S(1)}, bf16[768,256]{1,0:T(8,128)(2,1)}, u32[]{:S(2)}, u32[]{:S(2)}) collective-permute-start(bf16[768,256]{1,0:T(8,128)(2,1)S(1)} %bitcast.58), channel_id=1, source_target_pairs={{0,1},{1,0},{2,3},{3,2},{4,5},{5,4},{6,7},{7,6},{8,9},{9,8},{10,11... | collective-permute-start | bytes 1179656 | tf_op jit(solution)/shard_map/ppermute | solution.py:75
  50.4 16.5 %collective-permute-start.5 = (bf16[768,256]{1,0:T(8,128)(2,1)}, bf16[768,256]{1,0:T(8,128)(2,1)S(1)}, u32[]{:S(2)}, u32[]{:S(2)}) collective-permute-start(bf16[768,256]{1,0:T(8,128)(2,1)} %collective-permute-done.3), channel_id=1, source_target_pairs={{0,1},{1,0},{2,3},{3,2},{4,5},{5,4},{6,7},{7,6},{8,9},{9,8},{10,11... | collective-permute-start | bytes 1179656 | tf_op jit(solution)/shard_map/ppermute | solution.py:75
  53.3 17.4 %collective-permute-start.1 = (bf16[768,512]{1,0:T(8,128)(2,1)S(1)}, bf16[768,512]{1,0:T(8,128)(2,1)S(1)}, u32[]{:S(2)}, u32[]{:S(2)}) collective-permute-start(bf16[768,512]{1,0:T(8,128)(2,1)S(1)} %bitcast.55), channel_id=1, source_target_pairs={{0,1},{1,0},{2,3},{3,2},{4,5},{5,4},{6,7},{7,6},{8,9},{9,8},{10,11... | collective-permute-start | bytes 2359304 | tf_op jit(solution)/shard_map/ppermute | solution.py:75
  66.9 4.0 %collective-permute-start.2 = (bf16[768,512]{1,0:T(8,128)(2,1)}, bf16[768,512]{1,0:T(8,128)(2,1)S(1)}, u32[]{:S(2)}, u32[]{:S(2)}) collective-permute-start(bf16[768,512]{1,0:T(8,128)(2,1)} %collective-permute-done), channel_id=1, source_target_pairs={{0,1},{1,0},{2,3},{3,2},{4,5},{5,4},{6,7},{7,6},{8,9},{9,8},{10,11... | collective-permute-start | bytes 2359304 | tf_op jit(solution)/shard_map/ppermute | solution.py:75
  68.7 8.6 %copy-start.3 = (f32[768,1024]{1,0:T(8,128)}, f32[768,1024]{1,0:T(8,128)S(1)}, u32[]{:S(2)}) copy-start(f32[768,1024]{1,0:T(8,128)S(1)} %fusion.14) | copy-start | bytes 9437188
  68.7 3.6 %copy-start.2 = (bf16[1,1024,2048]{2,1,0:T(8,128)(2,1)S(1)}, bf16[1,1024,2048]{2,1,0:T(8,128)(2,1)}, u32[]{:S(2)}) copy-start(bf16[1,1024,2048]{2,1,0:T(8,128)(2,1)} %param.11) | copy-start | bytes 12582916
  72.3 5.1 %copy-start.1 = (bf16[768,2048]{1,0:T(8,128)(2,1)}, bf16[768,2048]{1,0:T(8,128)(2,1)S(1)}, u32[]{:S(2)}) copy-start(bf16[768,2048]{1,0:T(8,128)(2,1)S(1)} %constant_dynamic-update-slice_fusion.4) | copy-start | bytes 9437188
  79.8 3.6 %collective-permute-start.6 = (f32[512,768]{0,1:T(8,128)S(1)}, f32[512,768]{0,1:T(8,128)S(1)}, u32[]{:S(2)}, u32[]{:S(2)}) collective-permute-start(f32[512,768]{0,1:T(8,128)S(1)} %pad_maximum_fusion), channel_id=1, source_target_pairs={{0,1},{1,0},{2,3},{3,2},{4,5},{5,4},{6,7},{7,6},{8,9},{9,8},{10,11... | collective-permute-start | bytes 4718600 | tf_op jit(solution)/shard_map/ppermute | solution.py:35
  83.7 19.9 %collective-permute-start.7 = (f32[256,768]{0,1:T(8,128)S(1)}, f32[256,768]{0,1:T(8,128)S(1)}, u32[]{:S(2)}, u32[]{:S(2)}) collective-permute-start(f32[256,768]{0,1:T(8,128)S(1)} %slice.38), channel_id=1, source_target_pairs={{0,2},{1,3},{2,0},{3,1},{4,6},{5,7},{6,4},{7,5},{8,10},{9,11},{10,... | collective-permute-start | bytes 2359304 | tf_op jit(solution)/shard_map/ppermute | solution.py:37
  104.5 16.5 %all-to-all-start.2 = ((bf16[256,8,96]{0,2,1:T(8,128)(2,1)}), bf16[256,8,96]{0,2,1:T(8,128)(2,1)S(1)}, u32[]{:S(2)}, u32[]{:S(2)}) async-start(bf16[256,8,96]{0,2,1:T(8,128)(2,1)} %bitcast.20), calls=%async_computation.2 | async-start | bytes 786432 | tf_op jit(solution)/shard_map/all_to_all | solution.py:114

commit v4 on v3

--- a/solution.py
+++ b/solution.py
@@ -34,7 +34,8 @@
     give = jnp.concatenate([rows(j ^ 1), rows(j ^ 3)], axis=0)
     keep = keep + lax.ppermute(give, "tp", [(i, i ^ 1) for i in range(4)])
     mine, send = keep[:quarter], keep[quarter:]
-    return mine + lax.ppermute(send, "tp", [(i, i ^ 2) for i in range(4)])
+    moved = lax.ppermute(send.astype(jnp.bfloat16), "tp", [(i, i ^ 2) for i in range(4)])
+    return mine + moved.astype(jnp.float32)
 
 
 def shards(features, cotangent, expert_ids, gate_levels, w_in, w_out):
@@ -99,7 +100,7 @@
         weight_out = lax.dynamic_update_slice_in_dim(weight_out, moving[1], anchor * span, 0)
     pre = jnp.dot(rows_x, weight_in, preferred_element_type=jnp.float32)
     activated, gelu_back = jax.vjp(jax.nn.gelu, pre)
-    act_rows = activated.astype(jnp.bfloat16)
+    act_rows = lax.optimization_barrier(activated.astype(jnp.bfloat16))
     back_act = lax.dot_general(
         rows_dy, weight_out, (((1,), (1,)), ((), ())), preferred_element_type=jnp.float32
     )

time: 123 us -> 115 us (0.935)
  waiting for transfers between devices: 61.2 us -> 53.5 us
    ppermute x1, waiting for transfers between devices: 15.1 us -> 6.71 us  [chip_then_link_sum(): lax.ppermute(send.astype(jnp.bfloat16), 'tp', [(i, i ^ 2) for i in range(...]
    dot_general x1, matrix products: 1.79 us -> 3.49 us  [shards(): pre = jnp.dot(rows_x, weight_in, preferred_element_type=jnp.float32)]
  transfers between devices with their start and end apart: 11 -> 11, of which waited for: 6 -> 6; matrix products, arithmetic and copies ran while one was open for 18% -> 19% of each run, Pallas kernels for 0% -> 0%
where the time goes in v4:
time: 115 us; the launch traced here: 114 us
  waiting for transfers between devices  53.5 us (47%)
  matrix products  26.6 us (23%)
  starting transfers between devices  22 us (19%)
  local copies, waits for them, and re-layouts  7.22 us (6%)
  other arithmetic  4.03 us (4%)
    all_to_all x2, waiting for transfers between devices, dispatched(): mine = lax.all_to_all(mine, 'ep', split_axis=0, concat_axis=0, tiled=True)  27.4 us
    ppermute x2, waiting for transfers between devices, dispatched(): across = lax.ppermute(mine, 'tp', [(i, i ^ 2) for i in range(tp_size)])  12.8 us
    all_to_all x2, starting transfers between devices, dispatched(): mine = lax.all_to_all(mine, 'ep', split_axis=0, concat_axis=0, tiled=True)  10.9 us
    dot_general x1, matrix products, span_grads(): lax.dot_general(act_cols, rows_dy, (((0,), (0,)), ((), ())), preferred_el...  7.86 us
    ppermute x1, waiting for transfers between devices, chip_then_link_sum(): lax.ppermute(send.astype(jnp.bfloat16), 'tp', [(i, i ^ 2) for i in range(...  6.71 us
    all_to_all x1, starting transfers between devices, shards(): lax.all_to_all(summed.astype(jnp.bfloat16), 'ep', split_axis=1, concat_ax...  5.11 us
    dot_general x1, matrix products, shards(): lax.dot_general(rows_dy, weight_out, (((1,), (1,)), ((), ())), preferred_...  5.04 us
    dot_general x2, matrix products, dispatched(): jnp.dot(selection, mine, preferred_element_type=jnp.float32)  4.14 us
  transfers between devices with their start and end apart: 11, of which 6 were waited for; matrix products, arithmetic and copies ran while one was open for 19% of the time, Pallas kernels for 0%

profile of v4, /device:TPU:0, one launch (start us, length us, event | category | flops | bytes accessed | tf_op | source)
XLA Modules:
  0.0 114.2 jit_solution(2538549996480562133)
XLA Ops:
  0.6 0.0 copy-start
  0.7 1.0 copy.15
  1.6 0.1 eq.61
  1.8 1.1 %reduce-window.6 = s32[1,8,4,128]{3,1,2,0:T(8,128)S(1)} reduce-window(s32[1,8,4,128]{3,1,2,0:T(8,128)S(1)} %convert_bitcast_fusion, s32[]{:T(128)} %constant.31.clone.1), window={size=1x1x1x128 pad=0_0x0_0x0_0x127_0}, to_apply=%region_0.1 | reduce-window | flops 520192 | bytes 32772 | tf_op jit(solution)/shard_map/reduce-window
  2.9 0.2 slice_reduce_fusion
  3.2 0.1 fusion.33
  3.3 0.1 reduce_sum.12
  3.4 0.1 copy.16
  3.5 0.7 multiply_add_fusion
  4.2 1.9 %convolution_convert_fusion.1 = bf16[768,256]{1,0:T(8,128)(2,1)} fusion(s32[256]{0:T(256)S(1)} %bitcast.69, s32[256]{0:T(256)S(1)} %bitcast.66, bf16[256,1024]{1,0:T(8,128)(2,1)} %param.6, s32[]{:T(128)S(6)} %select_n.70), kind=kOutput, calls=%fused_computation.23 | convolution fusion | flops 101449728 | bytes 526340 | tf_op jit(solution)/shard_map/dot_general | solution.py:68
  6.2 7.3 %all-to-all-start.1 = ((bf16[8,96,256]{2,1,0:T(8,128)(2,1)}), bf16[8,96,256]{2,1,0:T(8,128)(2,1)S(1)}, u32[]{:S(2)}, u32[]{:S(2)}) async-start(bf16[8,96,256]{2,1,0:T(8,128)(2,1)} %bitcast.13), calls=%async_computation.1 | async-start | bytes 786432 | tf_op jit(solution)/shard_map/all_to_all | solution.py:69
  13.4 0.7 convert_multiply_fusion
  14.1 2.2 %convolution_convert_fusion = bf16[768,512]{1,0:T(8,128)(2,1)} fusion(f32[256]{0:T(256)S(1)} %bitcast.73, f32[256]{0:T(256)S(1)} %bitcast.72, s32[256]{0:T(256)S(1)} %bitcast.70, s32[256]{0:T(256)S(1)} %bitcast.67, bf16[256,2048]{1,0:T(8,128)(2,1)} %param.7, s32[]{:T(128)S(6)} %select_n.66), kind=kOutput, calls=%fused_computation.22 | convolution fusion | flops 202506240 | bytes 1052676 | tf_op jit(solution)/shard_map/dot_general | solution.py:68
  16.3 8.8 %all-to-all-done.1 = bf16[8,96,256]{2,1,0:T(8,128)(2,1)S(1)} async-done(((bf16[8,96,256]{2,1,0:T(8,128)(2,1)}), bf16[8,96,256]{2,1,0:T(8,128)(2,1)S(1)}, u32[]{:S(2)}, u32[]{:S(2)}) %all-to-all-start.1) | async-done | bytes 393248 | tf_op jit(solution)/shard_map/all_to_all | solution.py:69
  25.1 3.6 %all-to-all-start = ((bf16[8,96,512]{2,1,0:T(8,128)(2,1)}), bf16[8,96,512]{2,1,0:T(8,128)(2,1)S(1)}, u32[]{:S(2)}, u32[]{:S(2)}) async-start(bf16[8,96,512]{2,1,0:T(8,128)(2,1)} %bitcast.63), calls=%async_computation | async-start | bytes 1572864 | tf_op jit(solution)/shard_map/all_to_all | solution.py:69
  28.8 1.5 %collective-permute-start.3 = (bf16[768,256]{1,0:T(8,128)(2,1)S(1)}, bf16[768,256]{1,0:T(8,128)(2,1)}, u32[]{:S(2)}, u32[]{:S(2)}) collective-permute-start(bf16[768,256]{1,0:T(8,128)(2,1)S(1)} %bitcast.60), channel_id=1, source_target_pairs={{0,2},{1,3},{2,0},{3,1},{4,6},{5,7},{6,4},{7,5},{8,10},{9,11},{10,... | collective-permute-start | bytes 1179656 | tf_op jit(solution)/shard_map/ppermute | solution.py:72
  30.3 18.6 %all-to-all-done = bf16[8,96,512]{2,1,0:T(8,128)(2,1)S(1)} async-done(((bf16[8,96,512]{2,1,0:T(8,128)(2,1)}), bf16[8,96,512]{2,1,0:T(8,128)(2,1)S(1)}, u32[]{:S(2)}, u32[]{:S(2)}) %all-to-all-start) | async-done | bytes 786464 | tf_op jit(solution)/shard_map/all_to_all | solution.py:69
  48.9 1.5 %collective-permute-start = (bf16[768,512]{1,0:T(8,128)(2,1)S(1)}, bf16[768,512]{1,0:T(8,128)(2,1)}, u32[]{:S(2)}, u32[]{:S(2)}) collective-permute-start(bf16[768,512]{1,0:T(8,128)(2,1)S(1)} %bitcast.57), channel_id=1, source_target_pairs={{0,2},{1,3},{2,0},{3,1},{4,6},{5,7},{6,4},{7,5},{8,10},{9,11},{10,... | collective-permute-start | bytes 2359304 | tf_op jit(solution)/shard_map/ppermute | solution.py:72
  50.4 0.5 collective-permute-start.5
  50.9 0.2 broadcast_in_dim.46
  51.2 1.0 constant_dynamic-update-slice_fusion.2
  52.2 0.0 collective-permute-done.4
  52.3 1.0 constant_dynamic-update-slice_fusion.1
  53.3 0.2 collective-permute-start.1
  53.5 0.4 broadcast_in_dim.40
  53.9 0.1 constant_dynamic-update-slice_fusion.7
  54.1 12.8 %collective-permute-done = bf16[768,512]{1,0:T(8,128)(2,1)} collective-permute-done((bf16[768,512]{1,0:T(8,128)(2,1)S(1)}, bf16[768,512]{1,0:T(8,128)(2,1)}, u32[]{:S(2)}, u32[]{:S(2)}) %collective-permute-start) | collective-permute-done | bytes 786464 | tf_op jit(solution)/shard_map/ppermute | solution.py:72
  66.9 3.5 %multiply_convert_fusion.2 = (bf16[768,1024]{1,0:T(8,128)(2,1)}, f32[768,1024]{1,0:T(8,128)S(1)}) fusion(bf16[768,1024]{1,0:T(8,128)(2,1)S(1)} %constant_dynamic-update-slice_fusion, bf16[1,1024,1024]{2,1,0:T(8,128)(2,1)S(1)} %copy-done), kind=kOutput, calls=%fused_computation.14 | convolution fusion | flops 1617690624 | bytes 8388608 | tf_op jit(solution)/shard_map/dot_general | solution.py:101
  70.4 1.4 %constant_dynamic-update-slice_fusion.6 = bf16[768,2048]{1,0:T(8,128)(2,1)S(1)} fusion(bf16[768,2048]{1,0:T(8,128)(2,1)S(1)} %constant_dynamic-update-slice_fusion.7, bf16[768,512]{1,0:T(8,128)(2,1)} %collective-permute-done, s32[]{:T(128)S(6)} %select_n.67), kind=kLoop, calls=%fused_computation.61 | loop fusion | bytes 1572868 | tf_op jit(solution)/shard_map/dynamic_update_slice | solution.py:83
  71.8 0.1 constant_dynamic-update-slice_fusion.5
  71.9 0.1 constant_dynamic-update-slice_fusion.4
  72.0 0.8 copy-done.2
  72.8 5.0 %fusion.9 = bf16[768,1024]{1,0:T(8,128)(2,1)S(1)} fusion(f32[768,1024]{1,0:T(8,128)S(1)} %get-tuple-element.12, bf16[768,2048]{1,0:T(8,128)(2,1)S(1)} %constant_dynamic-update-slice_fusion.4, bf16[1,1024,2048]{2,1,0:T(8,128)(2,1)S(1)} %copy-done.2), kind=kOutput, calls=%fused_computation.13 | convolution fusion | flops 3236954112 | bytes 12058624 | tf_op jit(solution)/shard_map/dot_general | solution.py:104
  77.8 1.8 %fusion.12 = f32[768,1024]{1,0:T(8,128)S(1)} fusion(bf16[768,1024]{1,0:T(8,128)(2,1)S(1)} %fusion.9, bf16[1,1024,1024]{2,1,0:T(8,128)(2,1)S(1)} %copy-done), kind=kOutput, calls=%fused_computation.15 | convolution fusion | flops 1610612736 | bytes 6815744 | tf_op jit(solution)/shard_map/dot_general | solution.py:108
  79.7 0.4 dynamic-slice_bitcast_fusion.3
  80.1 0.2 pad_maximum_fusion
  80.3 0.6 collective-permute-start.6
  80.9 3.0 %collective-permute-done.6 = f32[512,768]{0,1:T(8,128)S(1)} collective-permute-done((f32[512,768]{0,1:T(8,128)S(1)}, f32[512,768]{0,1:T(8,128)S(1)}, u32[]{:S(2)}, u32[]{:S(2)}) %collective-permute-start.6) | collective-permute-done | bytes 1572896 | tf_op jit(solution)/shard_map/ppermute | solution.py:35
  83.9 0.3 maximum_add_fusion
  84.2 0.1 slice.46
  84.2 1.6 %collective-permute-start.7 = (bf16[256,768]{0,1:T(8,128)(2,1)S(1)}, bf16[256,768]{0,1:T(8,128)(2,1)S(1)}, u32[]{:S(2)}, u32[]{:S(2)}) collective-permute-start(bf16[256,768]{0,1:T(8,128)(2,1)S(1)} %slice.46), channel_id=1, source_target_pairs={{0,2},{1,3},{2,0},{3,1},{4,6},{5,7},{6,4},{7,5},{8,10},{9,11},{10,... | collective-permute-start | bytes 1179656 | tf_op jit(solution)/shard_map/ppermute | solution.py:37
  85.8 3.2 %fusion.16 = bf16[1,1024,1024]{2,1,0:T(8,128)(2,1)} fusion(bf16[768,1024]{1,0:T(8,128)(2,1)S(1)} %constant_dynamic-update-slice_fusion, bf16[768,1024]{1,0:T(8,128)(2,1)S(1)} %fusion.9), kind=kOutput, calls=%fused_computation.19 | convolution fusion | flops 1612709888 | bytes 5242880 | tf_op jit(solution)/shard_map/dot_general | solution.py:126
  89.0 6.7 %collective-permute-done.7 = bf16[256,768]{0,1:T(8,128)(2,1)S(1)} collective-permute-done((bf16[256,768]{0,1:T(8,128)(2,1)S(1)}, bf16[256,768]{0,1:T(8,128)(2,1)S(1)}, u32[]{:S(2)}, u32[]{:S(2)}) %collective-permute-start.7) | collective-permute-done | bytes 393248 | tf_op jit(solution)/shard_map/ppermute | solution.py:37
  95.7 0.9 fusion.17
  96.6 5.1 %all-to-all-start.2 = ((bf16[256,8,96]{0,2,1:T(8,128)(2,1)}), bf16[256,8,96]{0,2,1:T(8,128)(2,1)S(1)}, u32[]{:S(2)}, u32[]{:S(2)}) async-start(bf16[256,8,96]{0,2,1:T(8,128)(2,1)} %bitcast.20), calls=%async_computation.2 | async-start | bytes 786432 | tf_op jit(solution)/shard_map/all_to_all | solution.py:115
  101.7 7.9 %fusion.2 = bf16[1,1024,2048]{2,1,0:T(8,128)(2,1)} fusion(bf16[768,1024]{1,0:T(8,128)(2,1)} %get-tuple-element.11, bf16[768,2048]{1,0:T(8,128)(2,1)} %copy-done.1), kind=kOutput, calls=%fused_computation.6 | convolution fusion | flops 3225419776 | bytes 8912896 | tf_op jit(solution)/shard_map/dot_general | solution.py:129
  109.6 3.5 %all-to-all-done.2 = bf16[256,8,96]{0,2,1:T(8,128)(2,1)S(1)} async-done(((bf16[256,8,96]{0,2,1:T(8,128)(2,1)}), bf16[256,8,96]{0,2,1:T(8,128)(2,1)S(1)}, u32[]{:S(2)}, u32[]{:S(2)}) %all-to-all-start.2) | async-done | bytes 393248 | tf_op jit(solution)/shard_map/all_to_all | solution.py:115
  113.1 1.1 convolution_convert_fusion.2
  (17 shorter events, 0.2 us)
Async XLA Ops:
  0.6 66.2 %copy-start = (bf16[1,1024,1024]{2,1,0:T(8,128)(2,1)S(1)}, bf16[1,1024,1024]{2,1,0:T(8,128)(2,1)}, u32[]{:S(2)}) copy-start(bf16[1,1024,1024]{2,1,0:T(8,128)(2,1)} %param.10) | copy-start | bytes 6291460
  6.2 19.0 %all-to-all-start.1 = ((bf16[8,96,256]{2,1,0:T(8,128)(2,1)}), bf16[8,96,256]{2,1,0:T(8,128)(2,1)S(1)}, u32[]{:S(2)}, u32[]{:S(2)}) async-start(bf16[8,96,256]{2,1,0:T(8,128)(2,1)} %bitcast.13), calls=%async_computation.1 | async-start | bytes 786432 | tf_op jit(solution)/shard_map/all_to_all | solution.py:69
  25.1 23.8 %all-to-all-start = ((bf16[8,96,512]{2,1,0:T(8,128)(2,1)}), bf16[8,96,512]{2,1,0:T(8,128)(2,1)S(1)}, u32[]{:S(2)}, u32[]{:S(2)}) async-start(bf16[8,96,512]{2,1,0:T(8,128)(2,1)} %bitcast.63), calls=%async_computation | async-start | bytes 1572864 | tf_op jit(solution)/shard_map/all_to_all | solution.py:69
  28.8 21.7 %collective-permute-start.3 = (bf16[768,256]{1,0:T(8,128)(2,1)S(1)}, bf16[768,256]{1,0:T(8,128)(2,1)}, u32[]{:S(2)}, u32[]{:S(2)}) collective-permute-start(bf16[768,256]{1,0:T(8,128)(2,1)S(1)} %bitcast.60), channel_id=1, source_target_pairs={{0,2},{1,3},{2,0},{3,1},{4,6},{5,7},{6,4},{7,5},{8,10},{9,11},{10,... | collective-permute-start | bytes 1179656 | tf_op jit(solution)/shard_map/ppermute | solution.py:72
  48.9 18.0 %collective-permute-start = (bf16[768,512]{1,0:T(8,128)(2,1)S(1)}, bf16[768,512]{1,0:T(8,128)(2,1)}, u32[]{:S(2)}, u32[]{:S(2)}) collective-permute-start(bf16[768,512]{1,0:T(8,128)(2,1)S(1)} %bitcast.57), channel_id=1, source_target_pairs={{0,2},{1,3},{2,0},{3,1},{4,6},{5,7},{6,4},{7,5},{8,10},{9,11},{10,... | collective-permute-start | bytes 2359304 | tf_op jit(solution)/shard_map/ppermute | solution.py:72
  50.4 1.9 %collective-permute-start.4 = (bf16[768,256]{1,0:T(8,128)(2,1)S(1)}, bf16[768,256]{1,0:T(8,128)(2,1)}, u32[]{:S(2)}, u32[]{:S(2)}) collective-permute-start(bf16[768,256]{1,0:T(8,128)(2,1)S(1)} %bitcast.61), channel_id=1, source_target_pairs={{0,1},{1,0},{2,3},{3,2},{4,5},{5,4},{6,7},{7,6},{8,9},{9,8},{10,11... | collective-permute-start | bytes 1179656 | tf_op jit(solution)/shard_map/ppermute | solution.py:76
  50.4 3.6 %collective-permute-start.5 = (bf16[768,256]{1,0:T(8,128)(2,1)}, bf16[768,256]{1,0:T(8,128)(2,1)S(1)}, u32[]{:S(2)}, u32[]{:S(2)}) collective-permute-start(bf16[768,256]{1,0:T(8,128)(2,1)} %collective-permute-done.3), channel_id=1, source_target_pairs={{0,1},{1,0},{2,3},{3,2},{4,5},{5,4},{6,7},{7,6},{8,9},{9,8},{10,11... | collective-permute-start | bytes 1179656 | tf_op jit(solution)/shard_map/ppermute | solution.py:76
  53.3 18.5 %collective-permute-start.1 = (bf16[768,512]{1,0:T(8,128)(2,1)S(1)}, bf16[768,512]{1,0:T(8,128)(2,1)S(1)}, u32[]{:S(2)}, u32[]{:S(2)}) collective-permute-start(bf16[768,512]{1,0:T(8,128)(2,1)S(1)} %bitcast.58), channel_id=1, source_target_pairs={{0,1},{1,0},{2,3},{3,2},{4,5},{5,4},{6,7},{7,6},{8,9},{9,8},{10,11... | collective-permute-start | bytes 2359304 | tf_op jit(solution)/shard_map/ppermute | solution.py:76
  66.9 5.0 %collective-permute-start.2 = (bf16[768,512]{1,0:T(8,128)(2,1)}, bf16[768,512]{1,0:T(8,128)(2,1)S(1)}, u32[]{:S(2)}, u32[]{:S(2)}) collective-permute-start(bf16[768,512]{1,0:T(8,128)(2,1)} %collective-permute-done), channel_id=1, source_target_pairs={{0,1},{1,0},{2,3},{3,2},{4,5},{5,4},{6,7},{7,6},{8,9},{9,8},{10,11... | collective-permute-start | bytes 2359304 | tf_op jit(solution)/shard_map/ppermute | solution.py:76
  70.4 2.4 %copy-start.2 = (bf16[1,1024,2048]{2,1,0:T(8,128)(2,1)S(1)}, bf16[1,1024,2048]{2,1,0:T(8,128)(2,1)}, u32[]{:S(2)}) copy-start(bf16[1,1024,2048]{2,1,0:T(8,128)(2,1)} %param.11) | copy-start | bytes 12582916
  72.0 5.8 %copy-start.1 = (bf16[768,2048]{1,0:T(8,128)(2,1)}, bf16[768,2048]{1,0:T(8,128)(2,1)S(1)}, u32[]{:S(2)}) copy-start(bf16[768,2048]{1,0:T(8,128)(2,1)S(1)} %constant_dynamic-update-slice_fusion.4) | copy-start | bytes 9437188
  80.3 3.6 %collective-permute-start.6 = (f32[512,768]{0,1:T(8,128)S(1)}, f32[512,768]{0,1:T(8,128)S(1)}, u32[]{:S(2)}, u32[]{:S(2)}) collective-permute-start(f32[512,768]{0,1:T(8,128)S(1)} %pad_maximum_fusion), channel_id=1, source_target_pairs={{0,1},{1,0},{2,3},{3,2},{4,5},{5,4},{6,7},{7,6},{8,9},{9,8},{10,11... | collective-permute-start | bytes 4718600 | tf_op jit(solution)/shard_map/ppermute | solution.py:35
  84.2 11.5 %collective-permute-start.7 = (bf16[256,768]{0,1:T(8,128)(2,1)S(1)}, bf16[256,768]{0,1:T(8,128)(2,1)S(1)}, u32[]{:S(2)}, u32[]{:S(2)}) collective-permute-start(bf16[256,768]{0,1:T(8,128)(2,1)S(1)} %slice.46), channel_id=1, source_target_pairs={{0,2},{1,3},{2,0},{3,1},{4,6},{5,7},{6,4},{7,5},{8,10},{9,11},{10,... | collective-permute-start | bytes 1179656 | tf_op jit(solution)/shard_map/ppermute | solution.py:37
  96.6 16.5 %all-to-all-start.2 = ((bf16[256,8,96]{0,2,1:T(8,128)(2,1)}), bf16[256,8,96]{0,2,1:T(8,128)(2,1)S(1)}, u32[]{:S(2)}, u32[]{:S(2)}) async-start(bf16[256,8,96]{0,2,1:T(8,128)(2,1)} %bitcast.20), calls=%async_computation.2 | async-start | bytes 786432 | tf_op jit(solution)/shard_map/all_to_all | solution.py:115

commit v5 on v2

--- a/solution.py
+++ b/solution.py
@@ -58,23 +58,53 @@
     ).astype(jnp.bfloat16)
     tp_size = lax.axis_size("tp")
     tp_index = lax.axis_index("tp")
-    split = 2 if tp_size % 2 == 0 else 1
-    half = tp_index % split
+    split = 4 if tp_size == 4 else (2 if tp_size % 2 == 0 else 1)
 
-    def dispatched(table, selection):
-        width = table.shape[1] // split
-        mine = lax.dynamic_slice_in_dim(table, half * width, width, 1)
-        mine = jnp.dot(selection, mine, preferred_element_type=jnp.float32).astype(jnp.bfloat16)
-        mine = lax.all_to_all(mine, "ep", split_axis=0, concat_axis=0, tiled=True)
-        if split == 1:
-            return mine
-        other = lax.ppermute(mine, "tp", [(i, i ^ 1) for i in range(tp_size)])
-        whole = jnp.zeros((mine.shape[0], table.shape[1]), jnp.bfloat16)
-        whole = lax.dynamic_update_slice_in_dim(whole, mine, half * width, 1)
-        return lax.dynamic_update_slice_in_dim(whole, other, (1 - half) * width, 1)
+    chunks = 2 if capacity % 2 == 0 else 1
 
-    rows_x = dispatched(features, pick)
-    rows_dy = dispatched(cotangent, pick_scaled)
+    def dispatched(tables, selections):
+        part = tp_index % split
+        widths = [table.shape[1] // split for table in tables]
+        mine = jnp.concatenate(
+            [
+                jnp.dot(
+                    selection,
+                    lax.dynamic_slice_in_dim(table, part * width, width, 1),
+                    preferred_element_type=jnp.float32,
+                ).astype(jnp.bfloat16)
+                for table, selection, width in zip(tables, selections, widths)
+            ],
+            axis=1,
+        ).reshape(device_count, capacity, sum(widths))
+        rows = capacity // chunks
+        wholes = [
+            jnp.zeros((device_count, capacity, table.shape[1]), jnp.bfloat16) for table in tables
+        ]
+        for chunk in range(chunks):
+            block = mine[:, chunk * rows:(chunk + 1) * rows].reshape(device_count * rows, -1)
+            block = lax.all_to_all(block, "ep", split_axis=0, concat_axis=0, tiled=True)
+            pieces = [(block, part)]
+            if split == 4:
+                across = lax.ppermute(block, "tp", [(i, i ^ 2) for i in range(tp_size)])
+                pieces.append((across, part ^ 2))
+            if split >= 2:
+                pieces += [
+                    (lax.ppermute(piece, "tp", [(i, i ^ 1) for i in range(tp_size)]), where ^ 1)
+                    for piece, where in pieces
+                ]
+            for piece, where in pieces:
+                piece = piece.reshape(device_count, rows, -1)
+                start = 0
+                for index, width in enumerate(widths):
+                    wholes[index] = lax.dynamic_update_slice(
+                        wholes[index],
+                        piece[:, :, start:start + width],
+                        (0, chunk * rows, where * width),
+                    )
+                    start += width
+        return [whole.reshape(slot_count, -1) for whole in wholes]
+
+    rows_x, rows_dy = dispatched((features, cotangent), (pick, pick_scaled))
     piece_in = w_in[0]
     piece_out = w_out[0]
     span = piece_in.shape[1]

time: 134 us -> 124 us (0.925)
  waiting for transfers between devices: 79 us -> 43.2 us
  blocking collectives: 0 us -> 23.6 us
  local copies, waits for them, and re-layouts: 7.82 us -> 12 us
  starting transfers between devices: 16.4 us -> 14.8 us
  matrix products: 25.6 us -> 24.2 us
    all_to_all x2 -> x1, waiting for transfers between devices: 56.2 us -> 13.7 us  [dispatched(): block = lax.all_to_all(block, 'ep', split_axis=0, concat_axis=0, tiled=True)]
    all_to_all x0 -> x1, blocking collectives: none -> 23.6 us  [dispatched(): block = lax.all_to_all(block, 'ep', split_axis=0, concat_axis=0, tiled=True)]
    all_to_all x2 -> x1, starting transfers between devices: 10.9 us -> 3.54 us  [dispatched(): block = lax.all_to_all(block, 'ep', split_axis=0, concat_axis=0, tiled=True)]
    ppermute x2 -> x6, waiting for transfers between devices: 2.11 us -> 8.59 us  [the longest x2 8.58 us: dispatched(): across = lax.ppermute(block, 'tp', [(i, i ^ 2) for i in range(tp_size)])]
    ppermute x2 -> x6, starting transfers between devices: 0.03 us -> 3.69 us  [the longest x2 3.11 us: dispatched(): across = lax.ppermute(block, 'tp', [(i, i ^ 2) for i in range(tp_size)])]
    unnamed x11 -> x9, local copies, waits for them, and re-layouts: 0.84 us -> 3.59 us
    all_to_all x1, starting transfers between devices: 3.63 us -> 5.38 us  [shards(): lax.all_to_all(summed.astype(jnp.bfloat16), 'ep', split_axis=1, concat_ax...]
    concatenate x0 -> x1, local copies, waits for them, and re-layouts: none -> 1.56 us  [dispatched(): jnp.concatenate([jnp.dot(selection, lax.dynamic_slice_in_dim(table, part...]
  transfers between devices with their start and end apart: 7 -> 10, of which waited for: 6 -> 5; matrix products, arithmetic and copies ran while one was open for 14% -> 13% of each run, Pallas kernels for 0% -> 0%
where the time goes in v5:
time: 124 us
  waiting for transfers between devices  43.2 us (35%)
  matrix products  24.2 us (20%)
  blocking collectives  23.6 us (19%)
  starting transfers between devices  14.8 us (12%)
  local copies, waits for them, and re-layouts  12 us (10%)
  other arithmetic  5.03 us (4%)
    all_to_all x1, blocking collectives, dispatched(): block = lax.all_to_all(block, 'ep', split_axis=0, concat_axis=0, tiled=True)  23.6 us
    ppermute x1, waiting for transfers between devices, chip_then_link_sum(): return mine + lax.ppermute(send, 'tp', [(i, i ^ 2) for i in range(4)])  15.1 us
    all_to_all x1, waiting for transfers between devices, dispatched(): block = lax.all_to_all(block, 'ep', split_axis=0, concat_axis=0, tiled=True)  13.7 us
    dot_general x1, matrix products, span_grads(): lax.dot_general(act_cols, rows_dy, (((0,), (0,)), ((), ())), preferred_el...  8.64 us
    ppermute x2, waiting for transfers between devices, dispatched(): across = lax.ppermute(block, 'tp', [(i, i ^ 2) for i in range(tp_size)])  8.58 us
    all_to_all x1, starting transfers between devices, shards(): lax.all_to_all(summed.astype(jnp.bfloat16), 'ep', split_axis=1, concat_ax...  5.38 us
    dot_general x1, matrix products, shards(): lax.dot_general(rows_dy, weight_out, (((1,), (1,)), ((), ())), preferred_...  5.04 us
    dynamic_update_slice x16, local copies, waits for them, and re-layouts, dispatched(): lax.dynamic_update_slice(wholes[index], piece[:, :, start:start + width],...  4.36 us
  transfers between devices with their start and end apart: 10, of which 5 were waited for; matrix products, arithmetic and copies ran while one was open for 13% of the time, Pallas kernels for 0%

profile of v5, /device:TPU:0, one launch (start us, length us, event | category | flops | bytes accessed | tf_op | source)
XLA Modules:
  0.0 123.8 jit_solution(1223656776460017171)
XLA Ops:
  0.6 0.0 copy-start
  0.7 1.0 copy.17
  1.6 0.1 eq.60
  1.8 1.1 reduce-window.6
  2.9 0.2 slice_reduce_fusion
  3.2 0.1 fusion.37
  3.3 0.1 reduce_sum.12
  3.4 0.1 copy.18
  3.5 0.7 multiply_add_fusion
  4.2 0.7 convert_multiply_fusion
  4.9 1.3 %convolution_convert_fusion.1 = bf16[768,256]{0,1:T(8,128)(2,1)S(1)} fusion(s32[256]{0:T(256)S(1)} %bitcast.83, s32[256]{0:T(256)S(1)} %bitcast.80, bf16[256,1024]{1,0:T(8,128)(2,1)} %param.6, s32[]{:T(128)S(6)} %select_n.70), kind=kOutput, calls=%fused_computation.27 | convolution fusion | flops 101449728 | bytes 526340 | tf_op jit(solution)/shard_map/dot_general | solution.py:70
  6.2 1.4 %convolution_convert_fusion = bf16[768,512]{0,1:T(8,128)(2,1)S(1)} fusion(f32[256]{0:T(256)S(1)} %bitcast.87, f32[256]{0:T(256)S(1)} %bitcast.86, s32[256]{0:T(256)S(1)} %bitcast.84, s32[256]{0:T(256)S(1)} %bitcast.81, bf16[256,2048]{1,0:T(8,128)(2,1)} %param.7, s32[]{:T(128)S(6)} %select_n.73), kind=kOutput, calls=%fused_computation.26 | convolution fusion | flops 202506240 | bytes 1052676 | tf_op jit(solution)/shard_map/dot_general | solution.py:70
  7.6 1.1 pad_maximum_fusion.1
  8.7 1.6 %copy.19 = bf16[768,768]{1,0:T(8,128)(2,1)S(1)} copy(bf16[768,768]{0,1:T(8,128)(2,1)} %pad_maximum_fusion.1) | data formatting | bytes 2359296 | tf_op jit(solution)/shard_map/concatenate | solution.py:68
  10.2 0.9 fusion.45
  11.1 23.6 %all_to_all.30 = bf16[8,48,768]{2,1,0:T(8,128)(2,1)S(1)} all-to-all(bf16[8,48,768]{2,1,0:T(8,128)(2,1)S(1)} %get-tuple-element.8), channel_id=1, replica_groups=mesh['ep'=8,'tp'=4] {'ep'}, dimensions={0} | all-to-all | bytes 1179648 | tf_op jit(solution)/shard_map/all_to_all | solution.py:85
  34.7 3.5 %all-to-all-start.1 = ((bf16[8,48,768]{2,1,0:T(8,128)(2,1)}), bf16[8,48,768]{2,1,0:T(8,128)(2,1)S(1)}, u32[]{:S(2)}, u32[]{:S(2)}) async-start(bf16[8,48,768]{2,1,0:T(8,128)(2,1)} %get-tuple-element.7), calls=%async_computation.1 | async-start | bytes 1179648 | tf_op jit(solution)/shard_map/all_to_all | solution.py:85
  38.3 1.6 %collective-permute-start = (bf16[384,768]{1,0:T(8,128)(2,1)S(1)}, bf16[384,768]{1,0:T(8,128)(2,1)}, u32[]{:S(2)}, u32[]{:S(2)}) collective-permute-start(bf16[384,768]{1,0:T(8,128)(2,1)S(1)} %bitcast.66), channel_id=1, source_target_pairs={{0,2},{1,3},{2,0},{3,1},{4,6},{5,7},{6,4},{7,5},{8,10},{9,11},{10,... | collective-permute-start | bytes 1769480 | tf_op jit(solution)/shard_map/ppermute | solution.py:88
  39.9 0.0 collective-permute-start.1
  39.9 13.7 %all-to-all-done.1 = bf16[8,48,768]{2,1,0:T(8,128)(2,1)S(1)} async-done(((bf16[8,48,768]{2,1,0:T(8,128)(2,1)}), bf16[8,48,768]{2,1,0:T(8,128)(2,1)S(1)}, u32[]{:S(2)}, u32[]{:S(2)}) %all-to-all-start.1) | async-done | bytes 589856 | tf_op jit(solution)/shard_map/all_to_all | solution.py:85
  53.5 1.5 %collective-permute-start.3 = (bf16[384,768]{1,0:T(8,128)(2,1)S(1)}, bf16[384,768]{1,0:T(8,128)(2,1)S(1)}, u32[]{:S(2)}, u32[]{:S(2)}) collective-permute-start(bf16[384,768]{1,0:T(8,128)(2,1)S(1)} %bitcast.64), channel_id=1, source_target_pairs={{0,2},{1,3},{2,0},{3,1},{4,6},{5,7},{6,4},{7,5},{8,10},{9,11},{10,... | collective-permute-start | bytes 1769480 | tf_op jit(solution)/shard_map/ppermute | solution.py:88
  55.1 0.4 broadcast_in_dim.40
  55.5 0.2 broadcast_in_dim.46
  55.7 0.6 collective-permute-start.2
  56.3 0.9 slice_dynamic-update-slice_fusion.14
  57.3 0.9 slice_dynamic-update-slice_fusion.13
  58.2 8.6 %collective-permute-done.3 = bf16[384,768]{1,0:T(8,128)(2,1)S(1)} collective-permute-done((bf16[384,768]{1,0:T(8,128)(2,1)S(1)}, bf16[384,768]{1,0:T(8,128)(2,1)S(1)}, u32[]{:S(2)}, u32[]{:S(2)}) %collective-permute-start.3) | collective-permute-done | bytes 589856 | tf_op jit(solution)/shard_map/ppermute | solution.py:88
  66.8 1.0 slice_dynamic-update-slice_fusion.6
  67.8 1.0 slice_dynamic-update-slice_fusion.5
  69.4 0.0 copy-start.2
  69.4 1.8 %fusion.14 = f32[768,1024]{1,0:T(8,128)S(1)} fusion(bf16[768,1024]{1,0:T(8,128)(2,1)S(1)} %bitcast.68, bf16[1,1024,1024]{2,1,0:T(8,128)(2,1)S(1)} %copy-done), kind=kOutput, calls=%fused_computation.17 | convolution fusion | flops 1610612736 | bytes 6815744 | tf_op jit(solution)/shard_map/dot_general | solution.py:121
  71.2 2.6 %copy-done.2 = bf16[1,1024,2048]{2,1,0:T(8,128)(2,1)S(1)} copy-done((bf16[1,1024,2048]{2,1,0:T(8,128)(2,1)S(1)}, bf16[1,1024,2048]{2,1,0:T(8,128)(2,1)}, u32[]{:S(2)}) %copy-start.2) | copy-done | bytes 4194328
  73.8 5.0 %fusion.9 = bf16[768,1024]{1,0:T(8,128)(2,1)S(1)} fusion(f32[768,1024]{1,0:T(8,128)S(1)} %fusion.14, bf16[768,2048]{1,0:T(8,128)(2,1)S(1)} %bitcast.62, bf16[1,1024,2048]{2,1,0:T(8,128)(2,1)S(1)} %copy-done.2), kind=kOutput, calls=%fused_computation.13 | convolution fusion | flops 3236954112 | bytes 12058624 | tf_op jit(solution)/shard_map/dot_general | solution.py:124
  78.8 1.8 %fusion.12 = f32[768,1024]{1,0:T(8,128)S(1)} fusion(bf16[768,1024]{1,0:T(8,128)(2,1)S(1)} %fusion.9, bf16[1,1024,1024]{2,1,0:T(8,128)(2,1)S(1)} %copy-done), kind=kOutput, calls=%fused_computation.15 | convolution fusion | flops 1610612736 | bytes 6815744 | tf_op jit(solution)/shard_map/dot_general | solution.py:128
  80.7 0.4 dynamic-slice_bitcast_fusion.3
  81.1 0.2 pad_maximum_fusion
  81.3 0.6 collective-permute-start.6
  81.8 3.0 %collective-permute-done.6 = f32[512,768]{0,1:T(8,128)S(1)} collective-permute-done((f32[512,768]{0,1:T(8,128)S(1)}, f32[512,768]{0,1:T(8,128)S(1)}, u32[]{:S(2)}, u32[]{:S(2)}) %collective-permute-start.6) | collective-permute-done | bytes 1572896 | tf_op jit(solution)/shard_map/ppermute | solution.py:35
  84.9 0.3 maximum_add_fusion
  85.1 0.1 slice.128
  85.2 1.6 %collective-permute-start.7 = (f32[256,768]{0,1:T(8,128)S(1)}, f32[256,768]{0,1:T(8,128)S(1)}, u32[]{:S(2)}, u32[]{:S(2)}) collective-permute-start(f32[256,768]{0,1:T(8,128)S(1)} %slice.128), channel_id=1, source_target_pairs={{0,2},{1,3},{2,0},{3,1},{4,6},{5,7},{6,4},{7,5},{8,10},{9,11},{10,... | collective-permute-start | bytes 2359304 | tf_op jit(solution)/shard_map/ppermute | solution.py:37
  86.8 3.2 %fusion.16 = bf16[1,1024,1024]{2,1,0:T(8,128)(2,1)} fusion(bf16[768,1024]{1,0:T(8,128)(2,1)S(1)} %bitcast.69, bf16[768,1024]{1,0:T(8,128)(2,1)S(1)} %fusion.9), kind=kOutput, calls=%fused_computation.19 | convolution fusion | flops 1612709888 | bytes 5242880 | tf_op jit(solution)/shard_map/dot_general | solution.py:146
  90.0 15.1 %collective-permute-done.7 = f32[256,768]{0,1:T(8,128)S(1)} collective-permute-done((f32[256,768]{0,1:T(8,128)S(1)}, f32[256,768]{0,1:T(8,128)S(1)}, u32[]{:S(2)}, u32[]{:S(2)}) %collective-permute-start.7) | collective-permute-done | bytes 786464 | tf_op jit(solution)/shard_map/ppermute | solution.py:37
  105.1 0.8 fusion.21
  105.9 5.4 %all-to-all-start.2 = ((bf16[256,8,96]{0,2,1:T(8,128)(2,1)}), bf16[256,8,96]{0,2,1:T(8,128)(2,1)S(1)}, u32[]{:S(2)}, u32[]{:S(2)}) async-start(bf16[256,8,96]{0,2,1:T(8,128)(2,1)} %bitcast.27), calls=%async_computation.2 | async-start | bytes 786432 | tf_op jit(solution)/shard_map/all_to_all | solution.py:135
  111.3 8.6 %fusion.2 = bf16[1,1024,2048]{2,1,0:T(8,128)(2,1)} fusion(bf16[768,2048]{1,0:T(8,128)(2,1)} %bitcast.63, f32[768,1024]{1,0:T(8,128)} %copy-done.3), kind=kOutput, calls=%fused_computation.6 | convolution fusion | flops 3232497664 | bytes 10485760 | tf_op jit(solution)/shard_map/dot_general | solution.py:149
  120.0 2.8 %all-to-all-done.2 = bf16[256,8,96]{0,2,1:T(8,128)(2,1)S(1)} async-done(((bf16[256,8,96]{0,2,1:T(8,128)(2,1)}), bf16[256,8,96]{0,2,1:T(8,128)(2,1)S(1)}, u32[]{:S(2)}, u32[]{:S(2)}) %all-to-all-start.2) | async-done | bytes 393248 | tf_op jit(solution)/shard_map/all_to_all | solution.py:135
  122.7 1.1 convolution_convert_fusion.2
  (29 shorter events, 0.5 us)
Async XLA Ops:
  0.6 68.7 %copy-start = (bf16[1,1024,1024]{2,1,0:T(8,128)(2,1)S(1)}, bf16[1,1024,1024]{2,1,0:T(8,128)(2,1)}, u32[]{:S(2)}) copy-start(bf16[1,1024,1024]{2,1,0:T(8,128)(2,1)} %param.10) | copy-start | bytes 6291460
  34.7 18.8 %all-to-all-start.1 = ((bf16[8,48,768]{2,1,0:T(8,128)(2,1)}), bf16[8,48,768]{2,1,0:T(8,128)(2,1)S(1)}, u32[]{:S(2)}, u32[]{:S(2)}) async-start(bf16[8,48,768]{2,1,0:T(8,128)(2,1)} %get-tuple-element.7), calls=%async_computation.1 | async-start | bytes 1179648 | tf_op jit(solution)/shard_map/all_to_all | solution.py:85
  38.3 17.5 %collective-permute-start = (bf16[384,768]{1,0:T(8,128)(2,1)S(1)}, bf16[384,768]{1,0:T(8,128)(2,1)}, u32[]{:S(2)}, u32[]{:S(2)}) collective-permute-start(bf16[384,768]{1,0:T(8,128)(2,1)S(1)} %bitcast.66), channel_id=1, source_target_pairs={{0,2},{1,3},{2,0},{3,1},{4,6},{5,7},{6,4},{7,5},{8,10},{9,11},{10,... | collective-permute-start | bytes 1769480 | tf_op jit(solution)/shard_map/ppermute | solution.py:88
  39.9 17.4 %collective-permute-start.1 = (bf16[384,768]{1,0:T(8,128)(2,1)S(1)}, bf16[384,768]{1,0:T(8,128)(2,1)}, u32[]{:S(2)}, u32[]{:S(2)}) collective-permute-start(bf16[384,768]{1,0:T(8,128)(2,1)S(1)} %bitcast.67), channel_id=1, source_target_pairs={{0,1},{1,0},{2,3},{3,2},{4,5},{5,4},{6,7},{7,6},{8,9},{9,8},{10,11... | collective-permute-start | bytes 1769480 | tf_op jit(solution)/shard_map/ppermute | solution.py:92
  53.5 13.3 %collective-permute-start.3 = (bf16[384,768]{1,0:T(8,128)(2,1)S(1)}, bf16[384,768]{1,0:T(8,128)(2,1)S(1)}, u32[]{:S(2)}, u32[]{:S(2)}) collective-permute-start(bf16[384,768]{1,0:T(8,128)(2,1)S(1)} %bitcast.64), channel_id=1, source_target_pairs={{0,2},{1,3},{2,0},{3,1},{4,6},{5,7},{6,4},{7,5},{8,10},{9,11},{10,... | collective-permute-start | bytes 1769480 | tf_op jit(solution)/shard_map/ppermute | solution.py:88
  55.1 14.0 %collective-permute-start.4 = (bf16[384,768]{1,0:T(8,128)(2,1)S(1)}, bf16[384,768]{1,0:T(8,128)(2,1)S(1)}, u32[]{:S(2)}, u32[]{:S(2)}) collective-permute-start(bf16[384,768]{1,0:T(8,128)(2,1)S(1)} %bitcast.65), channel_id=1, source_target_pairs={{0,1},{1,0},{2,3},{3,2},{4,5},{5,4},{6,7},{7,6},{8,9},{9,8},{10,11... | collective-permute-start | bytes 1769480 | tf_op jit(solution)/shard_map/ppermute | solution.py:92
  55.7 13.2 %collective-permute-start.2 = (bf16[384,768]{1,0:T(8,128)(2,1)}, bf16[384,768]{1,0:T(8,128)(2,1)S(1)}, u32[]{:S(2)}, u32[]{:S(2)}) collective-permute-start(bf16[384,768]{1,0:T(8,128)(2,1)} %collective-permute-done), channel_id=1, source_target_pairs={{0,1},{1,0},{2,3},{3,2},{4,5},{5,4},{6,7},{7,6},{8,9},{9,8},{10,11... | collective-permute-start | bytes 1769480 | tf_op jit(solution)/shard_map/ppermute | solution.py:92
  66.8 2.5 %collective-permute-start.5 = (bf16[384,768]{1,0:T(8,128)(2,1)S(1)}, bf16[384,768]{1,0:T(8,128)(2,1)S(1)}, u32[]{:S(2)}, u32[]{:S(2)}) collective-permute-start(bf16[384,768]{1,0:T(8,128)(2,1)S(1)} %collective-permute-done.3), channel_id=1, source_target_pairs={{0,1},{1,0},{2,3},{3,2},{4,5},{5,4},{6,7},{7,6},{8,9},{9,8},{10,11... | collective-permute-start | bytes 1769480 | tf_op jit(solution)/shard_map/ppermute | solution.py:92
  69.3 1.9 %copy-start.1 = (bf16[8,96,2048]{2,1,0:T(8,128)(2,1)}, bf16[8,96,2048]{2,1,0:T(8,128)(2,1)S(1)}, u32[]{:S(2)}) copy-start(bf16[8,96,2048]{2,1,0:T(8,128)(2,1)S(1)} %slice_dynamic-update-slice_fusion) | copy-start | bytes 9437188
  69.4 4.4 %copy-start.2 = (bf16[1,1024,2048]{2,1,0:T(8,128)(2,1)S(1)}, bf16[1,1024,2048]{2,1,0:T(8,128)(2,1)}, u32[]{:S(2)}) copy-start(bf16[1,1024,2048]{2,1,0:T(8,128)(2,1)} %param.11) | copy-start | bytes 12582916
  71.2 7.7 %copy-start.3 = (f32[768,1024]{1,0:T(8,128)}, f32[768,1024]{1,0:T(8,128)S(1)}, u32[]{:S(2)}) copy-start(f32[768,1024]{1,0:T(8,128)S(1)} %fusion.14) | copy-start | bytes 9437188
  81.3 3.6 %collective-permute-start.6 = (f32[512,768]{0,1:T(8,128)S(1)}, f32[512,768]{0,1:T(8,128)S(1)}, u32[]{:S(2)}, u32[]{:S(2)}) collective-permute-start(f32[512,768]{0,1:T(8,128)S(1)} %pad_maximum_fusion), channel_id=1, source_target_pairs={{0,1},{1,0},{2,3},{3,2},{4,5},{5,4},{6,7},{7,6},{8,9},{9,8},{10,11... | collective-permute-start | bytes 4718600 | tf_op jit(solution)/shard_map/ppermute | solution.py:35
  85.2 19.9 %collective-permute-start.7 = (f32[256,768]{0,1:T(8,128)S(1)}, f32[256,768]{0,1:T(8,128)S(1)}, u32[]{:S(2)}, u32[]{:S(2)}) collective-permute-start(f32[256,768]{0,1:T(8,128)S(1)} %slice.128), channel_id=1, source_target_pairs={{0,2},{1,3},{2,0},{3,1},{4,6},{5,7},{6,4},{7,5},{8,10},{9,11},{10,... | collective-permute-start | bytes 2359304 | tf_op jit(solution)/shard_map/ppermute | solution.py:37
  105.9 16.8 %all-to-all-start.2 = ((bf16[256,8,96]{0,2,1:T(8,128)(2,1)}), bf16[256,8,96]{0,2,1:T(8,128)(2,1)S(1)}, u32[]{:S(2)}, u32[]{:S(2)}) async-start(bf16[256,8,96]{0,2,1:T(8,128)(2,1)} %bitcast.27), calls=%async_computation.2 | async-start | bytes 786432 | tf_op jit(solution)/shard_map/all_to_all | solution.py:135

commit v6 on v3

--- a/solution.py
+++ b/solution.py
@@ -111,13 +111,6 @@
         summed = chip_then_link_sum(partial, tp_index)
     else:
         summed = lax.psum_scatter(partial, "tp", scatter_dimension=0, tiled=True)
-    returned = lax.all_to_all(
-        summed.astype(jnp.bfloat16), "ep", split_axis=1, concat_axis=1, tiled=True
-    )
-    grad_in = lax.dot_general(
-        pick, returned, (((0,), (1,)), ((), ())), preferred_element_type=jnp.float32
-    ).astype(jnp.bfloat16)
-
     def span_grads(first_span, span_total):
         width = span_total * span
         act_cols = lax.dynamic_slice_in_dim(act_rows, first_span * span, width, 1)
@@ -138,6 +131,15 @@
     grad_scale = 1.0 / math.sqrt(2.0 * tokens_here * device_count / E)
     grad_w_in = (summed_grads[0] * grad_scale).T.astype(jnp.bfloat16)[None]
     grad_w_out = (summed_grads[1] * grad_scale).astype(jnp.bfloat16)[None]
+    leaving, grad_w_in, grad_w_out = lax.optimization_barrier(
+        (summed.astype(jnp.bfloat16), grad_w_in, grad_w_out)
+    )
+    returned = lax.all_to_all(
+        leaving, "ep", split_axis=1, concat_axis=1, tiled=True
+    )
+    grad_in = lax.dot_general(
+        pick, returned, (((0,), (1,)), ((), ())), preferred_element_type=jnp.float32
+    ).astype(jnp.bfloat16)
     return (grad_in, grad_w_in, grad_w_out)
 
 

time: 123 us -> 121 us (0.984)
  blocking collectives: 0 us -> 16.6 us
  waiting for transfers between devices: 61.2 us -> 53.2 us
  starting transfers between devices: 22 us -> 16.8 us
  matrix products: 25.7 us -> 22.3 us
    all_to_all x0 -> x1, blocking collectives: none -> 16.6 us  [shards(): lax.all_to_all(leaving, 'ep', split_axis=1, concat_axis=1, tiled=True)]
    all_to_all x1 -> x0, starting transfers between devices: 5.11 us -> none  [shards(): lax.all_to_all(summed.astype(jnp.bfloat16), 'ep', split_axis=1, concat_ax...]
    dot_general x1, matrix products: 8.64 us -> 5.24 us  [span_grads(): lax.dot_general(act_cols, rows_dy, (((0,), (0,)), ((), ())), preferred_el...]
    ppermute x1, waiting for transfers between devices: 3.04 us -> 0.01 us  [chip_then_link_sum(): keep = keep + lax.ppermute(give, 'tp', [(i, i ^ 1) for i in range(4)])]
    all_to_all x1 -> x0, waiting for transfers between devices: 2.76 us -> none  [shards(): lax.all_to_all(summed.astype(jnp.bfloat16), 'ep', split_axis=1, concat_ax...]
    ppermute x1, waiting for transfers between devices: 15.1 us -> 12.9 us  [chip_then_link_sum(): return mine + lax.ppermute(send, 'tp', [(i, i ^ 2) for i in range(4)])]
  transfers between devices with their start and end apart: 11 -> 10, of which waited for: 6 -> 4; matrix products, arithmetic and copies ran while one was open for 18% -> 14% of each run, Pallas kernels for 0% -> 0%
where the time goes in v6:
time: 121 us; the launch traced here: 120 us
  waiting for transfers between devices  53.2 us (44%)
  matrix products  22.3 us (18%)
  starting transfers between devices  16.8 us (14%)
  blocking collectives  16.6 us (14%)
  local copies, waits for them, and re-layouts  7.23 us (6%)
  other arithmetic  3.3 us (3%)
    all_to_all x2, waiting for transfers between devices, dispatched(): mine = lax.all_to_all(mine, 'ep', split_axis=0, concat_axis=0, tiled=True)  27.4 us
    all_to_all x1, blocking collectives, shards(): lax.all_to_all(leaving, 'ep', split_axis=1, concat_axis=1, tiled=True)  16.6 us
    ppermute x1, waiting for transfers between devices, chip_then_link_sum(): return mine + lax.ppermute(send, 'tp', [(i, i ^ 2) for i in range(4)])  12.9 us
    ppermute x2, waiting for transfers between devices, dispatched(): across = lax.ppermute(mine, 'tp', [(i, i ^ 2) for i in range(tp_size)])  12.9 us
    all_to_all x2, starting transfers between devices, dispatched(): mine = lax.all_to_all(mine, 'ep', split_axis=0, concat_axis=0, tiled=True)  10.9 us
    dot_general x1, matrix products, span_grads(): lax.dot_general(act_cols, rows_dy, (((0,), (0,)), ((), ())), preferred_el...  5.24 us
    dot_general x1, matrix products, shards(): lax.dot_general(rows_dy, weight_out, (((1,), (1,)), ((), ())), preferred_...  5.05 us
    dot_general x2, matrix products, dispatched(): jnp.dot(selection, mine, preferred_element_type=jnp.float32)  4.14 us
  transfers between devices with their start and end apart: 10, of which 4 were waited for; matrix products, arithmetic and copies ran while one was open for 14% of the time, Pallas kernels for 0%

profile of v6, /device:TPU:0, one launch (start us, length us, event | category | flops | bytes accessed | tf_op | source)
XLA Modules:
  0.0 120.3 jit_solution(16280180784446207559)
XLA Ops:
  0.6 0.0 copy-start
  0.7 1.0 copy.15
  1.6 0.1 eq.61
  1.8 1.1 reduce-window.6
  2.9 0.2 slice_reduce_fusion
  3.2 0.1 fusion.37
  3.3 0.1 reduce_sum.12
  3.4 0.1 copy.16
  3.5 0.7 multiply_add_fusion
  4.2 1.9 %convolution_convert_fusion.1 = bf16[768,256]{1,0:T(8,128)(2,1)} fusion(s32[256]{0:T(256)S(1)} %bitcast.67, s32[256]{0:T(256)S(1)} %bitcast.64, bf16[256,1024]{1,0:T(8,128)(2,1)} %param.6, s32[]{:T(128)S(6)} %select_n.70), kind=kOutput, calls=%fused_computation.27 | convolution fusion | flops 101449728 | bytes 526340 | tf_op jit(solution)/shard_map/dot_general | solution.py:67
  6.2 7.3 %all-to-all-start.1 = ((bf16[8,96,256]{2,1,0:T(8,128)(2,1)}), bf16[8,96,256]{2,1,0:T(8,128)(2,1)S(1)}, u32[]{:S(2)}, u32[]{:S(2)}) async-start(bf16[8,96,256]{2,1,0:T(8,128)(2,1)} %bitcast.13), calls=%async_computation.1 | async-start | bytes 786432 | tf_op jit(solution)/shard_map/all_to_all | solution.py:68
  13.4 0.7 convert_multiply_fusion
  14.1 2.2 %convolution_convert_fusion = bf16[768,512]{1,0:T(8,128)(2,1)} fusion(f32[256]{0:T(256)S(1)} %bitcast.71, f32[256]{0:T(256)S(1)} %bitcast.70, s32[256]{0:T(256)S(1)} %bitcast.68, s32[256]{0:T(256)S(1)} %bitcast.65, bf16[256,2048]{1,0:T(8,128)(2,1)} %param.7, s32[]{:T(128)S(6)} %select_n.66), kind=kOutput, calls=%fused_computation.26 | convolution fusion | flops 202506240 | bytes 1052676 | tf_op jit(solution)/shard_map/dot_general | solution.py:67
  16.3 8.8 %all-to-all-done.1 = bf16[8,96,256]{2,1,0:T(8,128)(2,1)S(1)} async-done(((bf16[8,96,256]{2,1,0:T(8,128)(2,1)}), bf16[8,96,256]{2,1,0:T(8,128)(2,1)S(1)}, u32[]{:S(2)}, u32[]{:S(2)}) %all-to-all-start.1) | async-done | bytes 393248 | tf_op jit(solution)/shard_map/all_to_all | solution.py:68
  25.1 3.6 %all-to-all-start = ((bf16[8,96,512]{2,1,0:T(8,128)(2,1)}), bf16[8,96,512]{2,1,0:T(8,128)(2,1)S(1)}, u32[]{:S(2)}, u32[]{:S(2)}) async-start(bf16[8,96,512]{2,1,0:T(8,128)(2,1)} %bitcast.61), calls=%async_computation | async-start | bytes 1572864 | tf_op jit(solution)/shard_map/all_to_all | solution.py:68
  28.8 1.5 %collective-permute-start.3 = (bf16[768,256]{1,0:T(8,128)(2,1)S(1)}, bf16[768,256]{1,0:T(8,128)(2,1)}, u32[]{:S(2)}, u32[]{:S(2)}) collective-permute-start(bf16[768,256]{1,0:T(8,128)(2,1)S(1)} %bitcast.57), channel_id=1, source_target_pairs={{0,2},{1,3},{2,0},{3,1},{4,6},{5,7},{6,4},{7,5},{8,10},{9,11},{10,... | collective-permute-start | bytes 1179656 | tf_op jit(solution)/shard_map/ppermute | solution.py:71
  30.3 18.6 %all-to-all-done = bf16[8,96,512]{2,1,0:T(8,128)(2,1)S(1)} async-done(((bf16[8,96,512]{2,1,0:T(8,128)(2,1)}), bf16[8,96,512]{2,1,0:T(8,128)(2,1)S(1)}, u32[]{:S(2)}, u32[]{:S(2)}) %all-to-all-start) | async-done | bytes 786464 | tf_op jit(solution)/shard_map/all_to_all | solution.py:68
  48.9 1.5 %collective-permute-start = (bf16[768,512]{1,0:T(8,128)(2,1)S(1)}, bf16[768,512]{1,0:T(8,128)(2,1)}, u32[]{:S(2)}, u32[]{:S(2)}) collective-permute-start(bf16[768,512]{1,0:T(8,128)(2,1)S(1)} %bitcast.54), channel_id=1, source_target_pairs={{0,2},{1,3},{2,0},{3,1},{4,6},{5,7},{6,4},{7,5},{8,10},{9,11},{10,... | collective-permute-start | bytes 2359304 | tf_op jit(solution)/shard_map/ppermute | solution.py:71
  50.4 0.5 collective-permute-start.5
  50.9 0.2 broadcast_in_dim.46
  51.2 1.0 constant_dynamic-update-slice_fusion.2
  52.2 0.0 collective-permute-done.4
  52.3 1.0 constant_dynamic-update-slice_fusion.1
  53.3 0.2 collective-permute-start.1
  53.5 0.4 broadcast_in_dim.40
  53.9 0.1 constant_dynamic-update-slice_fusion.7
  54.0 12.9 %collective-permute-done = bf16[768,512]{1,0:T(8,128)(2,1)} collective-permute-done((bf16[768,512]{1,0:T(8,128)(2,1)S(1)}, bf16[768,512]{1,0:T(8,128)(2,1)}, u32[]{:S(2)}, u32[]{:S(2)}) %collective-permute-start) | collective-permute-done | bytes 786464 | tf_op jit(solution)/shard_map/ppermute | solution.py:71
  66.9 0.0 collective-permute-start.2
  66.9 1.8 %fusion.14 = f32[768,1024]{1,0:T(8,128)S(1)} fusion(bf16[768,1024]{1,0:T(8,128)(2,1)S(1)} %constant_dynamic-update-slice_fusion, bf16[1,1024,1024]{2,1,0:T(8,128)(2,1)S(1)} %copy-done), kind=kOutput, calls=%fused_computation.17 | convolution fusion | flops 1610612736 | bytes 6815744 | tf_op jit(solution)/shard_map/dot_general | solution.py:100
  68.7 0.0 copy-start.1
  68.7 1.4 %constant_dynamic-update-slice_fusion.6 = bf16[768,2048]{1,0:T(8,128)(2,1)S(1)} fusion(bf16[768,2048]{1,0:T(8,128)(2,1)S(1)} %constant_dynamic-update-slice_fusion.7, bf16[768,512]{1,0:T(8,128)(2,1)} %collective-permute-done, s32[]{:T(128)S(6)} %select_n.67), kind=kLoop, calls=%fused_computation.64 | loop fusion | bytes 1572868 | tf_op jit(solution)/shard_map/dynamic_update_slice | solution.py:82
  70.2 0.1 constant_dynamic-update-slice_fusion.5
  70.3 0.1 constant_dynamic-update-slice_fusion.4
  70.4 0.8 copy-done.1
  71.2 5.0 %fusion.9 = bf16[768,1024]{1,0:T(8,128)(2,1)S(1)} fusion(f32[768,1024]{1,0:T(8,128)S(1)} %fusion.14, bf16[768,2048]{1,0:T(8,128)(2,1)S(1)} %constant_dynamic-update-slice_fusion.4, bf16[1,1024,2048]{2,1,0:T(8,128)(2,1)S(1)} %copy-done.1), kind=kOutput, calls=%fused_computation.13 | convolution fusion | flops 3236954112 | bytes 12058624 | tf_op jit(solution)/shard_map/dot_general | solution.py:103
  76.2 1.8 %fusion.12 = f32[768,1024]{1,0:T(8,128)S(1)} fusion(bf16[768,1024]{1,0:T(8,128)(2,1)S(1)} %fusion.9, bf16[1,1024,1024]{2,1,0:T(8,128)(2,1)S(1)} %copy-done), kind=kOutput, calls=%fused_computation.15 | convolution fusion | flops 1610612736 | bytes 6815744 | tf_op jit(solution)/shard_map/dot_general | solution.py:107
  78.0 0.4 dynamic-slice_bitcast_fusion.3
  78.4 0.2 pad_maximum_fusion
  78.7 0.6 collective-permute-start.6
  79.2 3.2 %fusion.16 = bf16[1,1024,1024]{2,1,0:T(8,128)(2,1)} fusion(bf16[768,1024]{1,0:T(8,128)(2,1)S(1)} %constant_dynamic-update-slice_fusion, bf16[768,1024]{1,0:T(8,128)(2,1)S(1)} %fusion.9), kind=kOutput, calls=%fused_computation.19 | convolution fusion | flops 1612709888 | bytes 5242880 | tf_op jit(solution)/shard_map/dot_general | solution.py:118
  82.4 0.3 maximum_add_fusion
  82.7 0.1 slice.38
  82.7 1.6 %collective-permute-start.7 = (f32[256,768]{0,1:T(8,128)S(1)}, f32[256,768]{0,1:T(8,128)S(1)}, u32[]{:S(2)}, u32[]{:S(2)}) collective-permute-start(f32[256,768]{0,1:T(8,128)S(1)} %slice.38), channel_id=1, source_target_pairs={{0,2},{1,3},{2,0},{3,1},{4,6},{5,7},{6,4},{7,5},{8,10},{9,11},{10,... | collective-permute-start | bytes 2359304 | tf_op jit(solution)/shard_map/ppermute | solution.py:37
  84.3 5.2 %fusion.2 = bf16[1,1024,2048]{2,1,0:T(8,128)(2,1)} fusion(bf16[768,2048]{1,0:T(8,128)(2,1)S(1)} %constant_dynamic-update-slice_fusion.4, f32[768,1024]{1,0:T(8,128)S(1)} %fusion.14), kind=kOutput, calls=%fused_computation.6 | convolution fusion | flops 3232497664 | bytes 10485760 | tf_op jit(solution)/shard_map/dot_general | solution.py:121
  89.6 12.9 %collective-permute-done.7 = f32[256,768]{0,1:T(8,128)S(1)} collective-permute-done((f32[256,768]{0,1:T(8,128)S(1)}, f32[256,768]{0,1:T(8,128)S(1)}, u32[]{:S(2)}, u32[]{:S(2)}) %collective-permute-start.7) | collective-permute-done | bytes 786464 | tf_op jit(solution)/shard_map/ppermute | solution.py:37
  102.5 0.2 fusion.21
  102.7 16.6 %all_to_all.36 = bf16[256,8,96]{0,2,1:T(8,128)(2,1)S(1)} all-to-all(bf16[256,8,96]{0,2,1:T(8,128)(2,1)S(1)} %bitcast.60), channel_id=1, replica_groups=mesh['ep'=8,'tp'=4] {'ep'}, dimensions={1} | all-to-all | bytes 786432 | tf_op jit(solution)/shard_map/all_to_all | solution.py:137
  119.2 1.1 convolution_convert_fusion.2
  (14 shorter events, 0.2 us)
Async XLA Ops:
  0.6 66.3 %copy-start = (bf16[1,1024,1024]{2,1,0:T(8,128)(2,1)S(1)}, bf16[1,1024,1024]{2,1,0:T(8,128)(2,1)}, u32[]{:S(2)}) copy-start(bf16[1,1024,1024]{2,1,0:T(8,128)(2,1)} %param.10) | copy-start | bytes 6291460
  6.2 19.0 %all-to-all-start.1 = ((bf16[8,96,256]{2,1,0:T(8,128)(2,1)}), bf16[8,96,256]{2,1,0:T(8,128)(2,1)S(1)}, u32[]{:S(2)}, u32[]{:S(2)}) async-start(bf16[8,96,256]{2,1,0:T(8,128)(2,1)} %bitcast.13), calls=%async_computation.1 | async-start | bytes 786432 | tf_op jit(solution)/shard_map/all_to_all | solution.py:68
  25.1 23.8 %all-to-all-start = ((bf16[8,96,512]{2,1,0:T(8,128)(2,1)}), bf16[8,96,512]{2,1,0:T(8,128)(2,1)S(1)}, u32[]{:S(2)}, u32[]{:S(2)}) async-start(bf16[8,96,512]{2,1,0:T(8,128)(2,1)} %bitcast.61), calls=%async_computation | async-start | bytes 1572864 | tf_op jit(solution)/shard_map/all_to_all | solution.py:68
  28.8 21.7 %collective-permute-start.3 = (bf16[768,256]{1,0:T(8,128)(2,1)S(1)}, bf16[768,256]{1,0:T(8,128)(2,1)}, u32[]{:S(2)}, u32[]{:S(2)}) collective-permute-start(bf16[768,256]{1,0:T(8,128)(2,1)S(1)} %bitcast.57), channel_id=1, source_target_pairs={{0,2},{1,3},{2,0},{3,1},{4,6},{5,7},{6,4},{7,5},{8,10},{9,11},{10,... | collective-permute-start | bytes 1179656 | tf_op jit(solution)/shard_map/ppermute | solution.py:71
  48.9 18.0 %collective-permute-start = (bf16[768,512]{1,0:T(8,128)(2,1)S(1)}, bf16[768,512]{1,0:T(8,128)(2,1)}, u32[]{:S(2)}, u32[]{:S(2)}) collective-permute-start(bf16[768,512]{1,0:T(8,128)(2,1)S(1)} %bitcast.54), channel_id=1, source_target_pairs={{0,2},{1,3},{2,0},{3,1},{4,6},{5,7},{6,4},{7,5},{8,10},{9,11},{10,... | collective-permute-start | bytes 2359304 | tf_op jit(solution)/shard_map/ppermute | solution.py:71
  50.4 1.9 %collective-permute-start.4 = (bf16[768,256]{1,0:T(8,128)(2,1)S(1)}, bf16[768,256]{1,0:T(8,128)(2,1)}, u32[]{:S(2)}, u32[]{:S(2)}) collective-permute-start(bf16[768,256]{1,0:T(8,128)(2,1)S(1)} %bitcast.58), channel_id=1, source_target_pairs={{0,1},{1,0},{2,3},{3,2},{4,5},{5,4},{6,7},{7,6},{8,9},{9,8},{10,11... | collective-permute-start | bytes 1179656 | tf_op jit(solution)/shard_map/ppermute | solution.py:75
  50.4 16.5 %collective-permute-start.5 = (bf16[768,256]{1,0:T(8,128)(2,1)}, bf16[768,256]{1,0:T(8,128)(2,1)S(1)}, u32[]{:S(2)}, u32[]{:S(2)}) collective-permute-start(bf16[768,256]{1,0:T(8,128)(2,1)} %collective-permute-done.3), channel_id=1, source_target_pairs={{0,1},{1,0},{2,3},{3,2},{4,5},{5,4},{6,7},{7,6},{8,9},{9,8},{10,11... | collective-permute-start | bytes 1179656 | tf_op jit(solution)/shard_map/ppermute | solution.py:75
  53.3 16.8 %collective-permute-start.1 = (bf16[768,512]{1,0:T(8,128)(2,1)S(1)}, bf16[768,512]{1,0:T(8,128)(2,1)S(1)}, u32[]{:S(2)}, u32[]{:S(2)}) collective-permute-start(bf16[768,512]{1,0:T(8,128)(2,1)S(1)} %bitcast.55), channel_id=1, source_target_pairs={{0,1},{1,0},{2,3},{3,2},{4,5},{5,4},{6,7},{7,6},{8,9},{9,8},{10,11... | collective-permute-start | bytes 2359304 | tf_op jit(solution)/shard_map/ppermute | solution.py:75
  66.9 3.4 %collective-permute-start.2 = (bf16[768,512]{1,0:T(8,128)(2,1)}, bf16[768,512]{1,0:T(8,128)(2,1)S(1)}, u32[]{:S(2)}, u32[]{:S(2)}) collective-permute-start(bf16[768,512]{1,0:T(8,128)(2,1)} %collective-permute-done), channel_id=1, source_target_pairs={{0,1},{1,0},{2,3},{3,2},{4,5},{5,4},{6,7},{7,6},{8,9},{9,8},{10,11... | collective-permute-start | bytes 2359304 | tf_op jit(solution)/shard_map/ppermute | solution.py:75
  68.7 2.4 %copy-start.1 = (bf16[1,1024,2048]{2,1,0:T(8,128)(2,1)S(1)}, bf16[1,1024,2048]{2,1,0:T(8,128)(2,1)}, u32[]{:S(2)}) copy-start(bf16[1,1024,2048]{2,1,0:T(8,128)(2,1)} %param.11) | copy-start | bytes 12582916
  78.7 3.7 %collective-permute-start.6 = (f32[512,768]{0,1:T(8,128)S(1)}, f32[512,768]{0,1:T(8,128)S(1)}, u32[]{:S(2)}, u32[]{:S(2)}) collective-permute-start(f32[512,768]{0,1:T(8,128)S(1)} %pad_maximum_fusion), channel_id=1, source_target_pairs={{0,1},{1,0},{2,3},{3,2},{4,5},{5,4},{6,7},{7,6},{8,9},{9,8},{10,11... | collective-permute-start | bytes 4718600 | tf_op jit(solution)/shard_map/ppermute | solution.py:35
  82.7 19.8 %collective-permute-start.7 = (f32[256,768]{0,1:T(8,128)S(1)}, f32[256,768]{0,1:T(8,128)S(1)}, u32[]{:S(2)}, u32[]{:S(2)}) collective-permute-start(f32[256,768]{0,1:T(8,128)S(1)} %slice.38), channel_id=1, source_target_pairs={{0,2},{1,3},{2,0},{3,1},{4,6},{5,7},{6,4},{7,5},{8,10},{9,11},{10,... | collective-permute-start | bytes 2359304 | tf_op jit(solution)/shard_map/ppermute | solution.py:37

commit v7 on v2

--- a/solution.py
+++ b/solution.py
@@ -58,23 +58,11 @@
     ).astype(jnp.bfloat16)
     tp_size = lax.axis_size("tp")
     tp_index = lax.axis_index("tp")
-    split = 2 if tp_size % 2 == 0 else 1
-    half = tp_index % split
+    split = 4 if tp_size == 4 else (2 if tp_size % 2 == 0 else 1)
+    part = tp_index % split
+    chunks = 2 if capacity % 2 == 0 else 1
+    rows = capacity // chunks
 
-    def dispatched(table, selection):
-        width = table.shape[1] // split
-        mine = lax.dynamic_slice_in_dim(table, half * width, width, 1)
-        mine = jnp.dot(selection, mine, preferred_element_type=jnp.float32).astype(jnp.bfloat16)
-        mine = lax.all_to_all(mine, "ep", split_axis=0, concat_axis=0, tiled=True)
-        if split == 1:
-            return mine
-        other = lax.ppermute(mine, "tp", [(i, i ^ 1) for i in range(tp_size)])
-        whole = jnp.zeros((mine.shape[0], table.shape[1]), jnp.bfloat16)
-        whole = lax.dynamic_update_slice_in_dim(whole, mine, half * width, 1)
-        return lax.dynamic_update_slice_in_dim(whole, other, (1 - half) * width, 1)
-
-    rows_x = dispatched(features, pick)
-    rows_dy = dispatched(cotangent, pick_scaled)
     piece_in = w_in[0]
     piece_out = w_out[0]
     span = piece_in.shape[1]
@@ -88,49 +76,102 @@
         anchor = (replica - turn_index) % replicas
         weight_in = lax.dynamic_update_slice_in_dim(weight_in, moving[0], anchor * span, 1)
         weight_out = lax.dynamic_update_slice_in_dim(weight_out, moving[1], anchor * span, 0)
-    pre = jnp.dot(rows_x, weight_in, preferred_element_type=jnp.float32)
-    activated, gelu_back = jax.vjp(jax.nn.gelu, pre)
-    act_rows = activated.astype(jnp.bfloat16)
-    back_act = lax.dot_general(
-        rows_dy, weight_out, (((1,), (1,)), ((), ())), preferred_element_type=jnp.float32
-    )
-    back_pre = gelu_back(back_act)[0].astype(jnp.bfloat16)
-    partial = lax.dot_general(
-        weight_in, back_pre, (((1,), (1,)), ((), ())), preferred_element_type=jnp.float32
-    )
-    if tp_size == 4:
-        summed = chip_then_link_sum(partial, tp_index)
-    else:
-        summed = lax.psum_scatter(partial, "tp", scatter_dimension=0, tiled=True)
-    returned = lax.all_to_all(
-        summed.astype(jnp.bfloat16), "ep", split_axis=1, concat_axis=1, tiled=True
-    )
-    grad_in = lax.dot_general(
-        pick, returned, (((0,), (1,)), ((), ())), preferred_element_type=jnp.float32
-    ).astype(jnp.bfloat16)
 
-    def span_grads(first_span, span_total):
-        width = span_total * span
-        act_cols = lax.dynamic_slice_in_dim(act_rows, first_span * span, width, 1)
-        pre_cols = lax.dynamic_slice_in_dim(back_pre, first_span * span, width, 1)
+    tables = (features, cotangent)
+    widths = [table.shape[1] // split for table in tables]
+    mine = jnp.concatenate(
+        [
+            jnp.dot(
+                selection,
+                lax.dynamic_slice_in_dim(table, part * width, width, 1),
+                preferred_element_type=jnp.float32,
+            ).astype(jnp.bfloat16)
+            for table, selection, width in zip(tables, (pick, pick_scaled), widths)
+        ],
+        axis=1,
+    ).reshape(device_count, capacity, sum(widths))
+
+    def chunk_rows(chunk):
+        block = mine[:, chunk * rows:(chunk + 1) * rows].reshape(device_count * rows, -1)
+        block = lax.all_to_all(block, "ep", split_axis=0, concat_axis=0, tiled=True)
+        pieces = [(block, part)]
+        if split == 4:
+            across = lax.ppermute(block, "tp", [(i, i ^ 2) for i in range(tp_size)])
+            pieces.append((across, part ^ 2))
+        if split >= 2:
+            pieces += [
+                (lax.ppermute(piece, "tp", [(i, i ^ 1) for i in range(tp_size)]), where ^ 1)
+                for piece, where in pieces
+            ]
+        wholes = [
+            jnp.zeros((device_count * rows, table.shape[1]), jnp.bfloat16) for table in tables
+        ]
+        for piece, where in pieces:
+            start = 0
+            for index, width in enumerate(widths):
+                wholes[index] = lax.dynamic_update_slice_in_dim(
+                    wholes[index], piece[:, start:start + width], where * width, 1
+                )
+                start += width
+        return wholes
+
+    def expert_rows(rows_x, rows_dy):
+        pre = jnp.dot(rows_x, weight_in, preferred_element_type=jnp.float32)
+        activated, gelu_back = jax.vjp(jax.nn.gelu, pre)
+        act_rows = activated.astype(jnp.bfloat16)
+        back_act = lax.dot_general(
+            rows_dy, weight_out, (((1,), (1,)), ((), ())), preferred_element_type=jnp.float32
+        )
+        back_pre = gelu_back(back_act)[0].astype(jnp.bfloat16)
+        partial = lax.dot_general(
+            weight_in, back_pre, (((1,), (1,)), ((), ())), preferred_element_type=jnp.float32
+        )
+        if tp_size == 4:
+            summed = chip_then_link_sum(partial, tp_index)
+        else:
+            summed = lax.psum_scatter(partial, "tp", scatter_dimension=0, tiled=True)
         grad_first = lax.dot_general(
-            pre_cols, rows_x, (((0,), (0,)), ((), ())), preferred_element_type=jnp.float32
+            back_pre, rows_x, (((0,), (0,)), ((), ())), preferred_element_type=jnp.float32
         )
         grad_second = lax.dot_general(
-            act_cols, rows_dy, (((0,), (0,)), ((), ())), preferred_element_type=jnp.float32
+            act_rows, rows_dy, (((0,), (0,)), ((), ())), preferred_element_type=jnp.float32
         )
-        return (grad_first, grad_second)
+        return summed, grad_first, grad_second
 
-    summed_grads = span_grads((replica - 1) % replicas, 1)
+    selection = pick.reshape(device_count, capacity, tokens_here)
+    grad_in = None
+    totals = None
+    for chunk in range(chunks):
+        rows_x, rows_dy = chunk_rows(chunk)
+        summed, grad_first, grad_second = expert_rows(rows_x, rows_dy)
+        if totals is None:
+            totals = (grad_first, grad_second)
+        else:
+            totals = (totals[0] + grad_first, totals[1] + grad_second)
+        returned = lax.all_to_all(
+            summed.astype(jnp.bfloat16), "ep", split_axis=1, concat_axis=1, tiled=True
+        )
+        chosen = selection[:, chunk * rows:(chunk + 1) * rows].reshape(device_count * rows, -1)
+        term = lax.dot_general(
+            chosen, returned, (((0,), (1,)), ((), ())), preferred_element_type=jnp.float32
+        )
+        grad_in = term if grad_in is None else grad_in + term
+    grad_in = grad_in.astype(jnp.bfloat16)
+
+    def span_of(total, first_span):
+        return lax.dynamic_slice_in_dim(total, first_span * span, span, 0)
+
+    summed_grads = tuple(span_of(total, (replica - 1) % replicas) for total in totals)
     for turn_index in range(1, replicas):
         summed_grads = shifted((summed_grads[0], summed_grads[1]), "ep", E)
-        own_grads = span_grads((replica - turn_index - 1) % replicas, 1)
-        summed_grads = (summed_grads[0] + own_grads[0], summed_grads[1] + own_grads[1])
+        own = (replica - turn_index - 1) % replicas
+        summed_grads = tuple(
+            moved + span_of(total, own) for moved, total in zip(summed_grads, totals)
+        )
     grad_scale = 1.0 / math.sqrt(2.0 * tokens_here * device_count / E)
     grad_w_in = (summed_grads[0] * grad_scale).T.astype(jnp.bfloat16)[None]
     grad_w_out = (summed_grads[1] * grad_scale).astype(jnp.bfloat16)[None]
     return (grad_in, grad_w_in, grad_w_out)
-
 
 def solution(mesh):
     return jax.shard_map(

time: 134 us -> 129 us (0.963)
  waiting for transfers between devices: 79 us -> 32 us
  blocking collectives: 0 us -> 23.7 us
  local copies, waits for them, and re-layouts: 7.82 us -> 14.1 us
  matrix products: 25.6 us -> 31.1 us
  other arithmetic: 4.1 us -> 7.69 us
  starting transfers between devices: 16.4 us -> 18.2 us
    all_to_all x2 -> x1, waiting for transfers between devices: 56.2 us -> 13.5 us  [chunk_rows(): block = lax.all_to_all(block, 'ep', split_axis=0, concat_axis=0, tiled=True)]
    all_to_all x0 -> x1, blocking collectives: none -> 23.7 us  [chunk_rows(): block = lax.all_to_all(block, 'ep', split_axis=0, concat_axis=0, tiled=True)]
    ppermute x1 -> x2, waiting for transfers between devices: 14.9 us -> 4.2 us  [chip_then_link_sum(): return mine + lax.ppermute(send, 'tp', [(i, i ^ 2) for i in range(4)])]
    ppermute x2 -> x6, waiting for transfers between devices: 2.11 us -> 11.3 us  [the longest x2 11.3 us: chunk_rows(): across = lax.ppermute(block, 'tp', [(i, i ^ 2) for i in range(tp_size)])]
    all_to_all x2 -> x1, starting transfers between devices: 10.9 us -> 3.54 us  [chunk_rows(): block = lax.all_to_all(block, 'ep', split_axis=0, concat_axis=0, tiled=True)]
    dot_general x8 -> x14, matrix products: 25.6 us -> 31.1 us  [the longest x2 9.54 us: expert_rows(): lax.dot_general(back_pre, rows_x, (((0,), (0,)), ((), ())), preferred_ele...]
    all_to_all x1 -> x2, starting transfers between devices: 3.63 us -> 8.39 us  [shards(): lax.all_to_all(summed.astype(jnp.bfloat16), 'ep', split_axis=1, concat_ax...]
    ppermute x2 -> x6, starting transfers between devices: 0.03 us -> 3.47 us  [the longest x2 3.1 us: chunk_rows(): across = lax.ppermute(block, 'tp', [(i, i ^ 2) for i in range(tp_size)])]
  transfers between devices with their start and end apart: 7 -> 13, of which waited for: 6 -> 5; matrix products, arithmetic and copies ran while one was open for 14% -> 24% of each run, Pallas kernels for 0% -> 0%
where the time goes in v7:
time: 129 us; the launch traced here: 128 us
  waiting for transfers between devices  32 us (25%)
  matrix products  31.1 us (24%)
  blocking collectives  23.7 us (18%)
  starting transfers between devices  18.2 us (14%)
  local copies, waits for them, and re-layouts  14.1 us (11%)
  other arithmetic  7.69 us (6%)
    all_to_all x1, blocking collectives, chunk_rows(): block = lax.all_to_all(block, 'ep', split_axis=0, concat_axis=0, tiled=True)  23.7 us
    all_to_all x1, waiting for transfers between devices, chunk_rows(): block = lax.all_to_all(block, 'ep', split_axis=0, concat_axis=0, tiled=True)  13.5 us
    ppermute x2, waiting for transfers between devices, chunk_rows(): across = lax.ppermute(block, 'tp', [(i, i ^ 2) for i in range(tp_size)])  11.3 us
    dot_general x2, matrix products, expert_rows(): lax.dot_general(back_pre, rows_x, (((0,), (0,)), ((), ())), preferred_ele...  9.54 us
    all_to_all x2, starting transfers between devices, shards(): lax.all_to_all(summed.astype(jnp.bfloat16), 'ep', split_axis=1, concat_ax...  8.39 us
    dot_general x2, matrix products, expert_rows(): lax.dot_general(act_rows, rows_dy, (((0,), (0,)), ((), ())), preferred_el...  7.52 us
    dynamic_update_slice x16, local copies, waits for them, and re-layouts, chunk_rows(): lax.dynamic_update_slice_in_dim(wholes[index], piece[:, start:start + wid...  6.3 us
    dot_general x2, matrix products, expert_rows(): lax.dot_general(rows_dy, weight_out, (((1,), (1,)), ((), ())), preferred_...  5.29 us
  transfers between devices with their start and end apart: 13, of which 5 were waited for; matrix products, arithmetic and copies ran while one was open for 24% of the time, Pallas kernels for 0%

profile of v7, /device:TPU:0, one launch (start us, length us, event | category | flops | bytes accessed | tf_op | source)
XLA Modules:
  0.0 127.9 jit_solution(14642232032818356780)
XLA Ops:
  0.7 0.8 convert_multiply_fusion
  1.5 0.8 copy.17
  2.5 1.1 reduce-window.6
  4.2 0.7 multiply_add_fusion.1
  4.9 1.3 convolution_convert_fusion.1
  6.2 1.4 %convolution_convert_fusion = bf16[768,512]{0,1:T(8,128)(2,1)S(1)} fusion(f32[256]{0:T(256)S(1)} %bitcast.97, f32[256]{0:T(256)S(1)} %bitcast.96, s32[256]{0:T(256)S(1)} %bitcast.94, s32[256]{0:T(256)S(1)} %bitcast.91, bf16[256,2048]{1,0:T(8,128)(2,1)} %param.7, s32[]{:T(128)S(6)} %select_n.79), kind=kOutput, calls=%fused_computation.36 | convolution fusion | flops 202506240 | bytes 1052676 | tf_op jit(solution)/shard_map/dot_general | solution.py:84
  7.6 1.1 pad_maximum_fusion
  8.7 1.6 %copy.19 = bf16[768,768]{1,0:T(8,128)(2,1)S(1)} copy(bf16[768,768]{0,1:T(8,128)(2,1)} %pad_maximum_fusion) | data formatting | bytes 2359296 | tf_op jit(solution)/shard_map/concatenate | solution.py:82
  10.2 0.9 fusion.71
  11.1 23.7 %all_to_all.36 = bf16[8,48,768]{2,1,0:T(8,128)(2,1)} all-to-all(bf16[8,48,768]{2,1,0:T(8,128)(2,1)S(1)} %get-tuple-element.12), channel_id=1, replica_groups=mesh['ep'=8,'tp'=4] {'ep'}, dimensions={0} | all-to-all | bytes 1179648 | tf_op jit(solution)/shard_map/all_to_all | solution.py:96
  34.8 3.5 %all-to-all-start = ((bf16[8,48,768]{2,1,0:T(8,128)(2,1)}), bf16[8,48,768]{2,1,0:T(8,128)(2,1)S(1)}, u32[]{:S(2)}, u32[]{:S(2)}) async-start(bf16[8,48,768]{2,1,0:T(8,128)(2,1)} %get-tuple-element.11), calls=%async_computation | async-start | bytes 1179648 | tf_op jit(solution)/shard_map/all_to_all | solution.py:96
  38.5 1.6 %collective-permute-start.5 = (bf16[384,768]{1,0:T(8,128)(2,1)}, bf16[384,768]{1,0:T(8,128)(2,1)}, u32[]{:S(2)}, u32[]{:S(2)}) collective-permute-start(bf16[384,768]{1,0:T(8,128)(2,1)} %bitcast.20), channel_id=1, source_target_pairs={{0,2},{1,3},{2,0},{3,1},{4,6},{5,7},{6,4},{7,5},{8,10},{9,11},{10,... | collective-permute-start | bytes 1769480 | tf_op jit(solution)/shard_map/ppermute | solution.py:99
  40.1 13.5 %all-to-all-done = bf16[8,48,768]{2,1,0:T(8,128)(2,1)S(1)} async-done(((bf16[8,48,768]{2,1,0:T(8,128)(2,1)}), bf16[8,48,768]{2,1,0:T(8,128)(2,1)S(1)}, u32[]{:S(2)}, u32[]{:S(2)}) %all-to-all-start) | async-done | bytes 589856 | tf_op jit(solution)/shard_map/all_to_all | solution.py:96
  53.6 1.5 %collective-permute-start = (bf16[384,768]{1,0:T(8,128)(2,1)S(1)}, bf16[384,768]{1,0:T(8,128)(2,1)S(1)}, u32[]{:S(2)}, u32[]{:S(2)}) collective-permute-start(bf16[384,768]{1,0:T(8,128)(2,1)S(1)} %bitcast.86), channel_id=1, source_target_pairs={{0,2},{1,3},{2,0},{3,1},{4,6},{5,7},{6,4},{7,5},{8,10},{9,11},{10,... | collective-permute-start | bytes 1769480 | tf_op jit(solution)/shard_map/ppermute | solution.py:99
  55.3 0.9 slice_dynamic-update-slice_fusion.11
  56.5 1.0 slice_dynamic-update-slice_fusion.3
  58.1 11.3 %collective-permute-done = bf16[384,768]{1,0:T(8,128)(2,1)S(1)} collective-permute-done((bf16[384,768]{1,0:T(8,128)(2,1)S(1)}, bf16[384,768]{1,0:T(8,128)(2,1)S(1)}, u32[]{:S(2)}, u32[]{:S(2)}) %collective-permute-start) | collective-permute-done | bytes 589856 | tf_op jit(solution)/shard_map/ppermute | solution.py:99
  69.4 1.0 slice_dynamic-update-slice_fusion.2
  70.4 0.9 slice_dynamic-update-slice_fusion.10
  71.5 1.0 slice_dynamic-update-slice_fusion.1
  72.5 0.9 slice_dynamic-update-slice_fusion.9
  73.6 1.0 fusion.11
  74.7 1.0 fusion.7
  75.7 1.1 copy-done.8
  76.9 2.6 %fusion.27 = bf16[384,1024]{1,0:T(8,128)(2,1)S(1)} fusion(f32[384,1024]{1,0:T(8,128)S(1)} %fusion.7, bf16[384,2048]{1,0:T(8,128)(2,1)S(1)} %slice_dynamic-update-slice_fusion, bf16[1,1024,2048]{2,1,0:T(8,128)(2,1)S(1)} %copy-done.8), kind=kOutput, calls=%fused_computation.33 | convolution fusion | flops 1618477056 | bytes 8126464 | tf_op jit(solution)/shard_map/dot_general | solution.py:122
  79.5 1.0 fusion.5
  80.6 2.7 %fusion.20 = bf16[384,1024]{1,0:T(8,128)(2,1)S(1)} fusion(f32[384,1024]{1,0:T(8,128)S(1)} %fusion.11, bf16[384,2048]{1,0:T(8,128)(2,1)S(1)} %slice_dynamic-update-slice_fusion.4, bf16[1,1024,2048]{2,1,0:T(8,128)(2,1)S(1)} %copy-done.8), kind=kOutput, calls=%fused_computation.26 | convolution fusion | flops 1618477056 | bytes 8126464 | tf_op jit(solution)/shard_map/dot_general | solution.py:122
  83.3 0.9 copy-done.5
  84.2 1.0 fusion.9
  85.2 0.4 dynamic-slice_bitcast_fusion.3
  85.7 0.6 collective-permute-start.8
  86.3 0.9 compare_or_fusion
  87.3 2.7 %fusion.34 = f32[1024,2048]{1,0:T(8,128)S(1)} fusion(bf16[384,2048]{1,0:T(8,128)(2,1)S(1)} %slice_dynamic-update-slice_fusion, f32[384,1024]{1,0:T(8,128)S(1)} %fusion.7), kind=kOutput, calls=%fused_computation.43 | convolution fusion | flops 1614151680 | bytes 11534336 | tf_op jit(solution)/shard_map/dot_general | solution.py:136
  90.2 1.6 %collective-permute-start.9 = (f32[256,384]{0,1:T(8,128)S(1)}, f32[256,384]{0,1:T(8,128)S(1)}, u32[]{:S(2)}, u32[]{:S(2)}) collective-permute-start(f32[256,384]{0,1:T(8,128)S(1)} %slice.148), channel_id=1, source_target_pairs={{0,2},{1,3},{2,0},{3,1},{4,6},{5,7},{6,4},{7,5},{8,10},{9,11},{10,... | collective-permute-start | bytes 1179656 | tf_op jit(solution)/shard_map/ppermute | solution.py:37
  91.8 4.8 %fusion.4 = bf16[1,1024,2048]{2,1,0:T(8,128)(2,1)} fusion(f32[1024,2048]{1,0:T(8,128)S(1)} %fusion.34, bf16[384,2048]{1,0:T(8,128)(2,1)S(1)} %slice_dynamic-update-slice_fusion.4, f32[384,1024]{1,0:T(8,128)S(1)} %fusion.11), kind=kOutput, calls=%fused_computation.6 | convolution fusion | flops 1620443136 | bytes 15728640 | tf_op jit(solution)/shard_map/dot_general | solution.py:136
  96.7 0.8 slice.136
  97.5 0.5 collective-permute-start.4
  98.1 4.2 %collective-permute-done.9 = f32[256,384]{0,1:T(8,128)S(1)} collective-permute-done((f32[256,384]{0,1:T(8,128)S(1)}, f32[256,384]{0,1:T(8,128)S(1)}, u32[]{:S(2)}, u32[]{:S(2)}) %collective-permute-start.9) | collective-permute-done | bytes 393248 | tf_op jit(solution)/shard_map/ppermute | solution.py:37
  102.3 0.7 fusion.45
  103.0 4.0 %all-to-all-start.3 = ((bf16[256,8,48]{0,2,1:T(8,128)(2,1)}), bf16[256,8,48]{0,2,1:T(8,128)(2,1)}, u32[]{:S(2)}, u32[]{:S(2)}) async-start(bf16[256,8,48]{0,2,1:T(8,128)(2,1)} %bitcast.25), calls=%async_computation.3 | async-start | bytes 393216 | tf_op jit(solution)/shard_map/all_to_all | solution.py:151
  107.0 4.5 %fusion.74 = f32[1024,1024]{1,0:T(8,128)} fusion(bf16[384,1024]{1,0:T(8,128)(2,1)S(1)} %slice_dynamic-update-slice_fusion.8, bf16[384,1024]{1,0:T(8,128)(2,1)} %copy-done.6), kind=kOutput, calls=%fused_computation.125 | convolution fusion | flops 805306368 | bytes 5767168 | tf_op jit(solution)/shard_map/dot_general | solution.py:133
  111.5 1.8 %fusion.46 = bf16[256,384]{0,1:T(8,128)(2,1)} fusion(f32[256,384]{0,1:T(8,128)} %collective-permute-done.4, f32[512,384]{0,1:T(8,128)S(1)} %copy-done.2), kind=kLoop, calls=%fused_computation.68 | loop fusion | flops 196608 | bytes 983040 | tf_op jit(solution)/shard_map/convert_element_type | solution.py:152
  113.3 1.5 %all-to-all-done.3 = bf16[256,8,48]{0,2,1:T(8,128)(2,1)} async-done(((bf16[256,8,48]{0,2,1:T(8,128)(2,1)}), bf16[256,8,48]{0,2,1:T(8,128)(2,1)}, u32[]{:S(2)}, u32[]{:S(2)}) %all-to-all-start.3) | async-done | bytes 196640 | tf_op jit(solution)/shard_map/all_to_all | solution.py:151
  114.8 4.4 %all-to-all-start.1 = ((bf16[256,8,48]{0,2,1:T(8,128)(2,1)}), bf16[256,8,48]{0,2,1:T(8,128)(2,1)S(1)}, u32[]{:S(2)}, u32[]{:S(2)}) async-start(bf16[256,8,48]{0,2,1:T(8,128)(2,1)} %bitcast.18), calls=%async_computation.1 | async-start | bytes 393216 | tf_op jit(solution)/shard_map/all_to_all | solution.py:151
  119.2 5.1 %fusion.13 = bf16[1,1024,1024]{2,1,0:T(8,128)(2,1)} fusion(f32[1024,1024]{1,0:T(8,128)} %fusion.74, bf16[384,1024]{1,0:T(8,128)(2,1)S(1)} %copy-done.4, bf16[384,1024]{1,0:T(8,128)(2,1)} %copy-done.5), kind=kOutput, calls=%fused_computation.19 | convolution fusion | flops 808452096 | bytes 7864320 | tf_op jit(solution)/shard_map/dot_general | solution.py:133
  124.3 1.2 convolution_bitcast_fusion
  125.5 1.5 %all-to-all-done.1 = bf16[256,8,48]{0,2,1:T(8,128)(2,1)S(1)} async-done(((bf16[256,8,48]{0,2,1:T(8,128)(2,1)}), bf16[256,8,48]{0,2,1:T(8,128)(2,1)S(1)}, u32[]{:S(2)}, u32[]{:S(2)}) %all-to-all-start.1) | async-done | bytes 196640 | tf_op jit(solution)/shard_map/all_to_all | solution.py:151
  127.0 0.9 fusion.33
  (59 shorter events, 2.5 us)
Async XLA Ops:
  0.6 73.0 %copy-start = (bf16[1,1024,1024]{2,1,0:T(8,128)(2,1)S(1)}, bf16[1,1024,1024]{2,1,0:T(8,128)(2,1)}, u32[]{:S(2)}) copy-start(bf16[1,1024,1024]{2,1,0:T(8,128)(2,1)} %param.10) | copy-start | bytes 6291460
  34.8 18.8 %all-to-all-start = ((bf16[8,48,768]{2,1,0:T(8,128)(2,1)}), bf16[8,48,768]{2,1,0:T(8,128)(2,1)S(1)}, u32[]{:S(2)}, u32[]{:S(2)}) async-start(bf16[8,48,768]{2,1,0:T(8,128)(2,1)} %get-tuple-element.11), calls=%async_computation | async-start | bytes 1179648 | tf_op jit(solution)/shard_map/all_to_all | solution.py:96
  38.5 33.0 %collective-permute-start.6 = (bf16[384,768]{1,0:T(8,128)(2,1)}, bf16[384,768]{1,0:T(8,128)(2,1)}, u32[]{:S(2)}, u32[]{:S(2)}) collective-permute-start(bf16[384,768]{1,0:T(8,128)(2,1)} %bitcast.20), channel_id=1, source_target_pairs={{0,1},{1,0},{2,3},{3,2},{4,5},{5,4},{6,7},{7,6},{8,9},{9,8},{10,11... | collective-permute-start | bytes 1769480 | tf_op jit(solution)/shard_map/ppermute | solution.py:103
  38.5 19.3 %collective-permute-start.5 = (bf16[384,768]{1,0:T(8,128)(2,1)}, bf16[384,768]{1,0:T(8,128)(2,1)}, u32[]{:S(2)}, u32[]{:S(2)}) collective-permute-start(bf16[384,768]{1,0:T(8,128)(2,1)} %bitcast.20), channel_id=1, source_target_pairs={{0,2},{1,3},{2,0},{3,1},{4,6},{5,7},{6,4},{7,5},{8,10},{9,11},{10,... | collective-permute-start | bytes 1769480 | tf_op jit(solution)/shard_map/ppermute | solution.py:99
  53.6 19.8 %collective-permute-start.1 = (bf16[384,768]{1,0:T(8,128)(2,1)S(1)}, bf16[384,768]{1,0:T(8,128)(2,1)S(1)}, u32[]{:S(2)}, u32[]{:S(2)}) collective-permute-start(bf16[384,768]{1,0:T(8,128)(2,1)S(1)} %bitcast.85), channel_id=1, source_target_pairs={{0,1},{1,0},{2,3},{3,2},{4,5},{5,4},{6,7},{7,6},{8,9},{9,8},{10,11... | collective-permute-start | bytes 1769480 | tf_op jit(solution)/shard_map/ppermute | solution.py:103
  53.6 15.7 %collective-permute-start = (bf16[384,768]{1,0:T(8,128)(2,1)S(1)}, bf16[384,768]{1,0:T(8,128)(2,1)S(1)}, u32[]{:S(2)}, u32[]{:S(2)}) collective-permute-start(bf16[384,768]{1,0:T(8,128)(2,1)S(1)} %bitcast.86), channel_id=1, source_target_pairs={{0,2},{1,3},{2,0},{3,1},{4,6},{5,7},{6,4},{7,5},{8,10},{9,11},{10,... | collective-permute-start | bytes 1769480 | tf_op jit(solution)/shard_map/ppermute | solution.py:99
  57.8 16.8 %collective-permute-start.7 = (bf16[384,768]{1,0:T(8,128)(2,1)}, bf16[384,768]{1,0:T(8,128)(2,1)S(1)}, u32[]{:S(2)}, u32[]{:S(2)}) collective-permute-start(bf16[384,768]{1,0:T(8,128)(2,1)} %collective-permute-done.5), channel_id=1, source_target_pairs={{0,1},{1,0},{2,3},{3,2},{4,5},{5,4},{6,7},{7,6},{8,9},{9,8},{10,11... | collective-permute-start | bytes 1769480 | tf_op jit(solution)/shard_map/ppermute | solution.py:103
  69.4 4.2 %collective-permute-start.2 = (bf16[384,768]{1,0:T(8,128)(2,1)S(1)}, bf16[384,768]{1,0:T(8,128)(2,1)S(1)}, u32[]{:S(2)}, u32[]{:S(2)}) collective-permute-start(bf16[384,768]{1,0:T(8,128)(2,1)S(1)} %collective-permute-done), channel_id=1, source_target_pairs={{0,1},{1,0},{2,3},{3,2},{4,5},{5,4},{6,7},{7,6},{8,9},{9,8},{10,11... | collective-permute-start | bytes 1769480 | tf_op jit(solution)/shard_map/ppermute | solution.py:103
  73.6 1.0 copy-start.3
  74.7 2.2 %copy-start.8 = (bf16[1,1024,2048]{2,1,0:T(8,128)(2,1)S(1)}, bf16[1,1024,2048]{2,1,0:T(8,128)(2,1)}, u32[]{:S(2)}) copy-start(bf16[1,1024,2048]{2,1,0:T(8,128)(2,1)} %param.11) | copy-start | bytes 12582916
  79.5 1.0 copy-start.6
  83.3 0.9 copy-start.5
  85.7 4.4 %collective-permute-start.8 = (f32[512,384]{0,1:T(8,128)S(1)}, f32[512,384]{0,1:T(8,128)S(1)}, u32[]{:S(2)}, u32[]{:S(2)}) collective-permute-start(f32[512,384]{0,1:T(8,128)S(1)} %pad_maximum_fusion.2), channel_id=1, source_target_pairs={{0,1},{1,0},{2,3},{3,2},{4,5},{5,4},{6,7},{7,6},{8,9},{9,8},{10,11... | collective-permute-start | bytes 2359304 | tf_op jit(solution)/shard_map/ppermute | solution.py:35
  87.2 9.3 %collective-permute-start.3 = (f32[512,384]{0,1:T(8,128)S(1)}, f32[512,384]{0,1:T(8,128)S(1)}, u32[]{:S(2)}, u32[]{:S(2)}) collective-permute-start(f32[512,384]{0,1:T(8,128)S(1)} %pad_maximum_fusion.1), channel_id=1, source_target_pairs={{0,1},{1,0},{2,3},{3,2},{4,5},{5,4},{6,7},{7,6},{8,9},{9,8},{10,11... | collective-permute-start | bytes 2359304 | tf_op jit(solution)/shard_map/ppermute | solution.py:35
  90.2 12.1 %collective-permute-start.9 = (f32[256,384]{0,1:T(8,128)S(1)}, f32[256,384]{0,1:T(8,128)S(1)}, u32[]{:S(2)}, u32[]{:S(2)}) collective-permute-start(f32[256,384]{0,1:T(8,128)S(1)} %slice.148), channel_id=1, source_target_pairs={{0,2},{1,3},{2,0},{3,1},{4,6},{5,7},{6,4},{7,5},{8,10},{9,11},{10,... | collective-permute-start | bytes 1179656 | tf_op jit(solution)/shard_map/ppermute | solution.py:37
  96.7 6.3 %copy-start.1 = (f32[512,384]{0,1:T(8,128)}, f32[512,384]{0,1:T(8,128)S(1)}, u32[]{:S(2)}) copy-start(f32[512,384]{0,1:T(8,128)S(1)} %maximum_add_fusion) | copy-start | bytes 2359300
  97.5 13.9 %collective-permute-start.4 = (f32[256,384]{0,1:T(8,128)}, f32[256,384]{0,1:T(8,128)}, u32[]{:S(2)}, u32[]{:S(2)}) collective-permute-start(f32[256,384]{0,1:T(8,128)} %slice.136), channel_id=1, source_target_pairs={{0,2},{1,3},{2,0},{3,1},{4,6},{5,7},{6,4},{7,5},{8,10},{9,11},{10,... | collective-permute-start | bytes 1179656 | tf_op jit(solution)/shard_map/ppermute | solution.py:37
  103.0 11.8 %all-to-all-start.3 = ((bf16[256,8,48]{0,2,1:T(8,128)(2,1)}), bf16[256,8,48]{0,2,1:T(8,128)(2,1)}, u32[]{:S(2)}, u32[]{:S(2)}) async-start(bf16[256,8,48]{0,2,1:T(8,128)(2,1)} %bitcast.25), calls=%async_computation.3 | async-start | bytes 393216 | tf_op jit(solution)/shard_map/all_to_all | solution.py:151
  107.0 4.5 %copy-start.2 = (f32[512,384]{0,1:T(8,128)S(1)}, f32[512,384]{0,1:T(8,128)}, u32[]{:S(2)}) copy-start(f32[512,384]{0,1:T(8,128)} %copy-done.1) | copy-start | bytes 2359300
  111.5 7.7 %copy-start.4 = (bf16[384,1024]{1,0:T(8,128)(2,1)S(1)}, bf16[384,1024]{1,0:T(8,128)(2,1)}, u32[]{:S(2)}) copy-start(bf16[384,1024]{1,0:T(8,128)(2,1)} %copy-done.3) | copy-start | bytes 2359300
  114.8 12.2 %all-to-all-start.1 = ((bf16[256,8,48]{0,2,1:T(8,128)(2,1)}), bf16[256,8,48]{0,2,1:T(8,128)(2,1)S(1)}, u32[]{:S(2)}, u32[]{:S(2)}) async-start(bf16[256,8,48]{0,2,1:T(8,128)(2,1)} %bitcast.18), calls=%async_computation.1 | async-start | bytes 393216 | tf_op jit(solution)/shard_map/all_to_all | solution.py:151
  119.2 5.1 %copy-start.7 = (pred[8,96,256]{2,1,0:T(8,128)(4,1)S(1)}, pred[8,96,256]{2,1,0:T(8,128)(4,1)}, u32[]{:S(2)}) copy-start(pred[8,96,256]{2,1,0:T(8,128)(4,1)} %compare_or_fusion) | copy-start | bytes 589828

commit v8 on v6

--- a/solution.py
+++ b/solution.py
@@ -60,12 +60,15 @@
     tp_index = lax.axis_index("tp")
     split = 4 if tp_size == 4 else (2 if tp_size % 2 == 0 else 1)
 
-    def dispatched(table, selection):
+    part = tp_index % split
+
+    def local_columns(table, selection):
         width = table.shape[1] // split
-        part = tp_index % split
         mine = lax.dynamic_slice_in_dim(table, part * width, width, 1)
-        mine = jnp.dot(selection, mine, preferred_element_type=jnp.float32).astype(jnp.bfloat16)
-        mine = lax.all_to_all(mine, "ep", split_axis=0, concat_axis=0, tiled=True)
+        return jnp.dot(selection, mine, preferred_element_type=jnp.float32).astype(jnp.bfloat16)
+
+    def spread(mine, columns):
+        width = columns // split
         pieces = [(mine, part)]
         if split == 4:
             across = lax.ppermute(mine, "tp", [(i, i ^ 2) for i in range(tp_size)])
@@ -77,13 +80,19 @@
             ]
         if split == 1:
             return mine
-        whole = jnp.zeros((mine.shape[0], table.shape[1]), jnp.bfloat16)
+        whole = jnp.zeros((mine.shape[0], columns), jnp.bfloat16)
         for piece, where in pieces:
             whole = lax.dynamic_update_slice_in_dim(whole, piece, where * width, 1)
         return whole
 
-    rows_x = dispatched(features, pick)
-    rows_dy = dispatched(cotangent, pick_scaled)
+    def over_ep(piece):
+        return lax.all_to_all(piece, "ep", split_axis=0, concat_axis=0, tiled=True)
+
+    moved_dy = over_ep(local_columns(cotangent, pick_scaled))
+    local_x, moved_dy = lax.optimization_barrier((local_columns(features, pick), moved_dy))
+    moved_x = over_ep(local_x)
+    rows_dy = spread(moved_dy, cotangent.shape[1])
+    rows_x = spread(moved_x, features.shape[1])
     piece_in = w_in[0]
     piece_out = w_out[0]
     span = piece_in.shape[1]

time: 121 us -> 122 us (level)
  waiting for transfers between devices: 53.2 us -> 55 us
  transfers between devices with their start and end apart: 10 -> 10, of which waited for: 4 -> 5; matrix products, arithmetic and copies ran while one was open for 14% -> 14% of each run, Pallas kernels for 0% -> 0%
where the time goes in v8:
time: 122 us; the launch traced here: 121 us
  waiting for transfers between devices  55 us (45%)
  matrix products  22.3 us (18%)
  blocking collectives  17.2 us (14%)
  starting transfers between devices  16.1 us (13%)
  local copies, waits for them, and re-layouts  6.72 us (6%)
  other arithmetic  3.3 us (3%)
    all_to_all x2, waiting for transfers between devices, over_ep(): return lax.all_to_all(piece, 'ep', split_axis=0, concat_axis=0, tiled=True)  28.6 us
    all_to_all x1, blocking collectives, shards(): lax.all_to_all(leaving, 'ep', split_axis=1, concat_axis=1, tiled=True)  17.2 us
    ppermute x2, waiting for transfers between devices, spread(): across = lax.ppermute(mine, 'tp', [(i, i ^ 2) for i in range(tp_size)])  13.5 us
    ppermute x1, waiting for transfers between devices, chip_then_link_sum(): return mine + lax.ppermute(send, 'tp', [(i, i ^ 2) for i in range(4)])  12.9 us
    all_to_all x2, starting transfers between devices, over_ep(): return lax.all_to_all(piece, 'ep', split_axis=0, concat_axis=0, tiled=True)  10.8 us
    dot_general x1, matrix products, span_grads(): lax.dot_general(act_cols, rows_dy, (((0,), (0,)), ((), ())), preferred_el...  5.24 us
    dot_general x1, matrix products, shards(): lax.dot_general(rows_dy, weight_out, (((1,), (1,)), ((), ())), preferred_...  5.04 us
    dot_general x2, matrix products, local_columns(): jnp.dot(selection, mine, preferred_element_type=jnp.float32)  4.14 us
  transfers between devices with their start and end apart: 10, of which 5 were waited for; matrix products, arithmetic and copies ran while one was open for 14% of the time, Pallas kernels for 0%

profile of v8, /device:TPU:0, one launch (start us, length us, event | category | flops | bytes accessed | tf_op | source)
XLA Modules:
  0.0 121.5 jit_solution(7866999439480182389)
XLA Ops:
  0.6 0.0 copy-start
  0.7 1.0 copy.15
  1.6 0.1 eq.60
  1.8 1.1 reduce-window.6
  2.9 0.2 slice_reduce_fusion
  3.2 0.1 fusion.37
  3.3 0.1 reduce_sum.12
  3.4 0.1 copy.16
  3.5 0.7 multiply_add_fusion
  4.2 0.7 convert_multiply_fusion
  4.9 2.2 %convolution_convert_fusion = bf16[768,512]{1,0:T(8,128)(2,1)} fusion(f32[256]{0:T(256)S(1)} %bitcast.72, f32[256]{0:T(256)S(1)} %bitcast.71, s32[256]{0:T(256)S(1)} %bitcast.68, s32[256]{0:T(256)S(1)} %bitcast.65, bf16[256,2048]{1,0:T(8,128)(2,1)} %param.7, s32[]{:T(128)S(6)} %select_n.65), kind=kOutput, calls=%fused_computation.26 | convolution fusion | flops 202506240 | bytes 1052676 | tf_op jit(solution)/shard_map/dot_general | solution.py:68
  7.1 7.3 %all-to-all-start = ((bf16[8,96,512]{2,1,0:T(8,128)(2,1)}), bf16[8,96,512]{2,1,0:T(8,128)(2,1)S(1)}, u32[]{:S(2)}, u32[]{:S(2)}) async-start(bf16[8,96,512]{2,1,0:T(8,128)(2,1)} %bitcast.61), calls=%async_computation | async-start | bytes 1572864 | tf_op jit(solution)/shard_map/all_to_all | solution.py:89
  14.4 1.9 %convolution_convert_fusion.1 = bf16[768,256]{1,0:T(8,128)(2,1)} fusion(s32[256]{0:T(256)S(1)} %bitcast.69, s32[256]{0:T(256)S(1)} %bitcast.66, bf16[256,1024]{1,0:T(8,128)(2,1)} %param.6, s32[]{:T(128)S(6)} %select_n.62), kind=kOutput, calls=%fused_computation.27 | convolution fusion | flops 101449728 | bytes 526340 | tf_op jit(solution)/shard_map/dot_general | solution.py:68
  16.3 18.2 %all-to-all-done = bf16[8,96,512]{2,1,0:T(8,128)(2,1)S(1)} async-done(((bf16[8,96,512]{2,1,0:T(8,128)(2,1)}), bf16[8,96,512]{2,1,0:T(8,128)(2,1)S(1)}, u32[]{:S(2)}, u32[]{:S(2)}) %all-to-all-start) | async-done | bytes 786464 | tf_op jit(solution)/shard_map/all_to_all | solution.py:89
  34.6 3.6 %all-to-all-start.1 = ((bf16[8,96,256]{2,1,0:T(8,128)(2,1)}), bf16[8,96,256]{2,1,0:T(8,128)(2,1)S(1)}, u32[]{:S(2)}, u32[]{:S(2)}) async-start(bf16[8,96,256]{2,1,0:T(8,128)(2,1)} %bitcast.62), calls=%async_computation.1 | async-start | bytes 786432 | tf_op jit(solution)/shard_map/all_to_all | solution.py:89
  38.1 1.5 %collective-permute-start = (bf16[768,512]{1,0:T(8,128)(2,1)S(1)}, bf16[768,512]{1,0:T(8,128)(2,1)}, u32[]{:S(2)}, u32[]{:S(2)}) collective-permute-start(bf16[768,512]{1,0:T(8,128)(2,1)S(1)} %bitcast.54), channel_id=1, source_target_pairs={{0,2},{1,3},{2,0},{3,1},{4,6},{5,7},{6,4},{7,5},{8,10},{9,11},{10,... | collective-permute-start | bytes 2359304 | tf_op jit(solution)/shard_map/ppermute | solution.py:74
  39.7 0.0 collective-permute-start.1
  39.7 10.3 %all-to-all-done.1 = bf16[8,96,256]{2,1,0:T(8,128)(2,1)S(1)} async-done(((bf16[8,96,256]{2,1,0:T(8,128)(2,1)}), bf16[8,96,256]{2,1,0:T(8,128)(2,1)S(1)}, u32[]{:S(2)}, u32[]{:S(2)}) %all-to-all-start.1) | async-done | bytes 393248 | tf_op jit(solution)/shard_map/all_to_all | solution.py:89
  50.0 1.5 %collective-permute-start.3 = (bf16[768,256]{1,0:T(8,128)(2,1)S(1)}, bf16[768,256]{1,0:T(8,128)(2,1)}, u32[]{:S(2)}, u32[]{:S(2)}) collective-permute-start(bf16[768,256]{1,0:T(8,128)(2,1)S(1)} %bitcast.57), channel_id=1, source_target_pairs={{0,2},{1,3},{2,0},{3,1},{4,6},{5,7},{6,4},{7,5},{8,10},{9,11},{10,... | collective-permute-start | bytes 1179656 | tf_op jit(solution)/shard_map/ppermute | solution.py:74
  51.5 0.4 broadcast_in_dim.40
  51.9 0.1 constant_dynamic-update-slice_fusion.7
  52.0 0.1 collective-permute-start.4
  52.1 0.2 broadcast_in_dim.46
  52.3 6.3 %collective-permute-done = bf16[768,512]{1,0:T(8,128)(2,1)} collective-permute-done((bf16[768,512]{1,0:T(8,128)(2,1)S(1)}, bf16[768,512]{1,0:T(8,128)(2,1)}, u32[]{:S(2)}, u32[]{:S(2)}) %collective-permute-start) | collective-permute-done | bytes 786464 | tf_op jit(solution)/shard_map/ppermute | solution.py:74
  58.7 7.2 %collective-permute-done.3 = bf16[768,256]{1,0:T(8,128)(2,1)} collective-permute-done((bf16[768,256]{1,0:T(8,128)(2,1)S(1)}, bf16[768,256]{1,0:T(8,128)(2,1)}, u32[]{:S(2)}, u32[]{:S(2)}) %collective-permute-start.3) | collective-permute-done | bytes 393248 | tf_op jit(solution)/shard_map/ppermute | solution.py:74
  65.8 0.0 collective-permute-start.5
  65.8 1.2 %constant_dynamic-update-slice_fusion.6 = bf16[768,2048]{1,0:T(8,128)(2,1)S(1)} fusion(bf16[768,2048]{1,0:T(8,128)(2,1)S(1)} %constant_dynamic-update-slice_fusion.7, bf16[768,512]{1,0:T(8,128)(2,1)} %collective-permute-done, s32[]{:T(128)S(6)} %select_n.66), kind=kLoop, calls=%fused_computation.63 | loop fusion | bytes 1572868 | tf_op jit(solution)/shard_map/dynamic_update_slice | solution.py:85
  67.1 0.0 collective-permute-done.1
  67.1 1.2 %constant_dynamic-update-slice_fusion.5 = bf16[768,2048]{1,0:T(8,128)(2,1)S(1)} fusion(bf16[768,2048]{1,0:T(8,128)(2,1)S(1)} %constant_dynamic-update-slice_fusion.6, bf16[768,512]{1,0:T(8,128)(2,1)} %collective-permute-done.1, s32[]{:T(128)S(6)} %select_n.67), kind=kLoop, calls=%fused_computation.62 | loop fusion | bytes 1572868 | tf_op jit(solution)/shard_map/dynamic_update_slice | solution.py:85
  68.4 1.0 constant_dynamic-update-slice_fusion.2
  69.5 0.0 copy-start.1
  69.6 1.8 %fusion.14 = f32[768,1024]{1,0:T(8,128)S(1)} fusion(bf16[768,1024]{1,0:T(8,128)(2,1)S(1)} %constant_dynamic-update-slice_fusion, bf16[1,1024,1024]{2,1,0:T(8,128)(2,1)S(1)} %copy-done), kind=kOutput, calls=%fused_computation.17 | convolution fusion | flops 1610612736 | bytes 6815744 | tf_op jit(solution)/shard_map/dot_general | solution.py:109
  71.4 0.1 constant_dynamic-update-slice_fusion.4
  71.5 0.3 copy-done.1
  71.7 5.0 %fusion.9 = bf16[768,1024]{1,0:T(8,128)(2,1)S(1)} fusion(f32[768,1024]{1,0:T(8,128)S(1)} %fusion.14, bf16[768,2048]{1,0:T(8,128)(2,1)S(1)} %constant_dynamic-update-slice_fusion.4, bf16[1,1024,2048]{2,1,0:T(8,128)(2,1)S(1)} %copy-done.1), kind=kOutput, calls=%fused_computation.13 | convolution fusion | flops 3236954112 | bytes 12058624 | tf_op jit(solution)/shard_map/dot_general | solution.py:112
  76.8 1.8 %fusion.12 = f32[768,1024]{1,0:T(8,128)S(1)} fusion(bf16[768,1024]{1,0:T(8,128)(2,1)S(1)} %fusion.9, bf16[1,1024,1024]{2,1,0:T(8,128)(2,1)S(1)} %copy-done), kind=kOutput, calls=%fused_computation.15 | convolution fusion | flops 1610612736 | bytes 6815744 | tf_op jit(solution)/shard_map/dot_general | solution.py:116
  78.6 0.4 dynamic-slice_bitcast_fusion.3
  79.0 0.2 pad_maximum_fusion
  79.2 0.6 collective-permute-start.6
  79.8 3.2 %fusion.16 = bf16[1,1024,1024]{2,1,0:T(8,128)(2,1)} fusion(bf16[768,1024]{1,0:T(8,128)(2,1)S(1)} %constant_dynamic-update-slice_fusion, bf16[768,1024]{1,0:T(8,128)(2,1)S(1)} %fusion.9), kind=kOutput, calls=%fused_computation.19 | convolution fusion | flops 1612709888 | bytes 5242880 | tf_op jit(solution)/shard_map/dot_general | solution.py:127
  83.0 0.3 maximum_add_fusion
  83.2 0.1 slice.38
  83.3 1.6 %collective-permute-start.7 = (f32[256,768]{0,1:T(8,128)S(1)}, f32[256,768]{0,1:T(8,128)S(1)}, u32[]{:S(2)}, u32[]{:S(2)}) collective-permute-start(f32[256,768]{0,1:T(8,128)S(1)} %slice.38), channel_id=1, source_target_pairs={{0,2},{1,3},{2,0},{3,1},{4,6},{5,7},{6,4},{7,5},{8,10},{9,11},{10,... | collective-permute-start | bytes 2359304 | tf_op jit(solution)/shard_map/ppermute | solution.py:37
  84.9 5.2 %fusion.2 = bf16[1,1024,2048]{2,1,0:T(8,128)(2,1)} fusion(bf16[768,2048]{1,0:T(8,128)(2,1)S(1)} %constant_dynamic-update-slice_fusion.4, f32[768,1024]{1,0:T(8,128)S(1)} %fusion.14), kind=kOutput, calls=%fused_computation.6 | convolution fusion | flops 3232497664 | bytes 10485760 | tf_op jit(solution)/shard_map/dot_general | solution.py:130
  90.1 12.9 %collective-permute-done.7 = f32[256,768]{0,1:T(8,128)S(1)} collective-permute-done((f32[256,768]{0,1:T(8,128)S(1)}, f32[256,768]{0,1:T(8,128)S(1)}, u32[]{:S(2)}, u32[]{:S(2)}) %collective-permute-start.7) | collective-permute-done | bytes 786464 | tf_op jit(solution)/shard_map/ppermute | solution.py:37
  103.1 0.2 fusion.21
  103.2 17.2 %all_to_all.36 = bf16[256,8,96]{0,2,1:T(8,128)(2,1)S(1)} all-to-all(bf16[256,8,96]{0,2,1:T(8,128)(2,1)S(1)} %bitcast.60), channel_id=1, replica_groups=mesh['ep'=8,'tp'=4] {'ep'}, dimensions={1} | all-to-all | bytes 786432 | tf_op jit(solution)/shard_map/all_to_all | solution.py:146
  120.4 1.1 convolution_convert_fusion.2
  (14 shorter events, 0.2 us)
Async XLA Ops:
  0.6 68.9 %copy-start = (bf16[1,1024,1024]{2,1,0:T(8,128)(2,1)S(1)}, bf16[1,1024,1024]{2,1,0:T(8,128)(2,1)}, u32[]{:S(2)}) copy-start(bf16[1,1024,1024]{2,1,0:T(8,128)(2,1)} %param.10) | copy-start | bytes 6291460
  7.1 27.5 %all-to-all-start = ((bf16[8,96,512]{2,1,0:T(8,128)(2,1)}), bf16[8,96,512]{2,1,0:T(8,128)(2,1)S(1)}, u32[]{:S(2)}, u32[]{:S(2)}) async-start(bf16[8,96,512]{2,1,0:T(8,128)(2,1)} %bitcast.61), calls=%async_computation | async-start | bytes 1572864 | tf_op jit(solution)/shard_map/all_to_all | solution.py:89
  34.6 15.4 %all-to-all-start.1 = ((bf16[8,96,256]{2,1,0:T(8,128)(2,1)}), bf16[8,96,256]{2,1,0:T(8,128)(2,1)S(1)}, u32[]{:S(2)}, u32[]{:S(2)}) async-start(bf16[8,96,256]{2,1,0:T(8,128)(2,1)} %bitcast.62), calls=%async_computation.1 | async-start | bytes 786432 | tf_op jit(solution)/shard_map/all_to_all | solution.py:89
  38.1 20.5 %collective-permute-start = (bf16[768,512]{1,0:T(8,128)(2,1)S(1)}, bf16[768,512]{1,0:T(8,128)(2,1)}, u32[]{:S(2)}, u32[]{:S(2)}) collective-permute-start(bf16[768,512]{1,0:T(8,128)(2,1)S(1)} %bitcast.54), channel_id=1, source_target_pairs={{0,2},{1,3},{2,0},{3,1},{4,6},{5,7},{6,4},{7,5},{8,10},{9,11},{10,... | collective-permute-start | bytes 2359304 | tf_op jit(solution)/shard_map/ppermute | solution.py:74
  39.7 27.4 %collective-permute-start.1 = (bf16[768,512]{1,0:T(8,128)(2,1)S(1)}, bf16[768,512]{1,0:T(8,128)(2,1)}, u32[]{:S(2)}, u32[]{:S(2)}) collective-permute-start(bf16[768,512]{1,0:T(8,128)(2,1)S(1)} %bitcast.55), channel_id=1, source_target_pairs={{0,1},{1,0},{2,3},{3,2},{4,5},{5,4},{6,7},{7,6},{8,9},{9,8},{10,11... | collective-permute-start | bytes 2359304 | tf_op jit(solution)/shard_map/ppermute | solution.py:78
  50.0 15.9 %collective-permute-start.3 = (bf16[768,256]{1,0:T(8,128)(2,1)S(1)}, bf16[768,256]{1,0:T(8,128)(2,1)}, u32[]{:S(2)}, u32[]{:S(2)}) collective-permute-start(bf16[768,256]{1,0:T(8,128)(2,1)S(1)} %bitcast.57), channel_id=1, source_target_pairs={{0,2},{1,3},{2,0},{3,1},{4,6},{5,7},{6,4},{7,5},{8,10},{9,11},{10,... | collective-permute-start | bytes 1179656 | tf_op jit(solution)/shard_map/ppermute | solution.py:74
  52.0 17.4 %collective-permute-start.4 = (bf16[768,256]{1,0:T(8,128)(2,1)S(1)}, bf16[768,256]{1,0:T(8,128)(2,1)S(1)}, u32[]{:S(2)}, u32[]{:S(2)}) collective-permute-start(bf16[768,256]{1,0:T(8,128)(2,1)S(1)} %bitcast.58), channel_id=1, source_target_pairs={{0,1},{1,0},{2,3},{3,2},{4,5},{5,4},{6,7},{7,6},{8,9},{9,8},{10,11... | collective-permute-start | bytes 1179656 | tf_op jit(solution)/shard_map/ppermute | solution.py:78
  58.7 12.7 %collective-permute-start.2 = (bf16[768,512]{1,0:T(8,128)(2,1)}, bf16[768,512]{1,0:T(8,128)(2,1)S(1)}, u32[]{:S(2)}, u32[]{:S(2)}) collective-permute-start(bf16[768,512]{1,0:T(8,128)(2,1)} %collective-permute-done), channel_id=1, source_target_pairs={{0,1},{1,0},{2,3},{3,2},{4,5},{5,4},{6,7},{7,6},{8,9},{9,8},{10,11... | collective-permute-start | bytes 2359304 | tf_op jit(solution)/shard_map/ppermute | solution.py:78
  65.8 3.6 %collective-permute-start.5 = (bf16[768,256]{1,0:T(8,128)(2,1)}, bf16[768,256]{1,0:T(8,128)(2,1)S(1)}, u32[]{:S(2)}, u32[]{:S(2)}) collective-permute-start(bf16[768,256]{1,0:T(8,128)(2,1)} %collective-permute-done.3), channel_id=1, source_target_pairs={{0,1},{1,0},{2,3},{3,2},{4,5},{5,4},{6,7},{7,6},{8,9},{9,8},{10,11... | collective-permute-start | bytes 1179656 | tf_op jit(solution)/shard_map/ppermute | solution.py:78
  69.5 2.2 %copy-start.1 = (bf16[1,1024,2048]{2,1,0:T(8,128)(2,1)S(1)}, bf16[1,1024,2048]{2,1,0:T(8,128)(2,1)}, u32[]{:S(2)}) copy-start(bf16[1,1024,2048]{2,1,0:T(8,128)(2,1)} %param.11) | copy-start | bytes 12582916
  79.2 3.7 %collective-permute-start.6 = (f32[512,768]{0,1:T(8,128)S(1)}, f32[512,768]{0,1:T(8,128)S(1)}, u32[]{:S(2)}, u32[]{:S(2)}) collective-permute-start(f32[512,768]{0,1:T(8,128)S(1)} %pad_maximum_fusion), channel_id=1, source_target_pairs={{0,1},{1,0},{2,3},{3,2},{4,5},{5,4},{6,7},{7,6},{8,9},{9,8},{10,11... | collective-permute-start | bytes 4718600 | tf_op jit(solution)/shard_map/ppermute | solution.py:35
  83.3 19.8 %collective-permute-start.7 = (f32[256,768]{0,1:T(8,128)S(1)}, f32[256,768]{0,1:T(8,128)S(1)}, u32[]{:S(2)}, u32[]{:S(2)}) collective-permute-start(f32[256,768]{0,1:T(8,128)S(1)} %slice.38), channel_id=1, source_target_pairs={{0,2},{1,3},{2,0},{3,1},{4,6},{5,7},{6,4},{7,5},{8,10},{9,11},{10,... | collective-permute-start | bytes 2359304 | tf_op jit(solution)/shard_map/ppermute | solution.py:37

commit v9 on v6

--- a/solution.py
+++ b/solution.py
@@ -22,6 +22,22 @@
     within = jnp.sum(one_hot * earlier, axis=2)
     block_ids = jnp.arange(blocks, dtype=jnp.int32)[:, None]
     return ((block_ids * experts + flattened) * capacity + within).reshape(-1)
+
+
+def exchange(value, axis, dimension):
+    peers = lax.axis_size(axis)
+    if peers > 8:
+        return lax.all_to_all(value, axis, split_axis=dimension, concat_axis=dimension, tiled=True)
+    me = lax.axis_index(axis)
+    block = value.shape[dimension] // peers
+    result = value
+    for shift in range(1, peers):
+        target = (me + shift) % peers
+        source = (me + peers - shift) % peers
+        outgoing = lax.dynamic_slice_in_dim(value, target * block, block, dimension)
+        incoming = lax.ppermute(outgoing, axis, [(i, (i + shift) % peers) for i in range(peers)])
+        result = lax.dynamic_update_slice_in_dim(result, incoming, source * block, dimension)
+    return result
 
 
 def chip_then_link_sum(partial, j):
@@ -65,7 +81,7 @@
         part = tp_index % split
         mine = lax.dynamic_slice_in_dim(table, part * width, width, 1)
         mine = jnp.dot(selection, mine, preferred_element_type=jnp.float32).astype(jnp.bfloat16)
-        mine = lax.all_to_all(mine, "ep", split_axis=0, concat_axis=0, tiled=True)
+        mine = exchange(mine, "ep", 0)
         pieces = [(mine, part)]
         if split == 4:
             across = lax.ppermute(mine, "tp", [(i, i ^ 2) for i in range(tp_size)])
@@ -134,9 +150,7 @@
     leaving, grad_w_in, grad_w_out = lax.optimization_barrier(
         (summed.astype(jnp.bfloat16), grad_w_in, grad_w_out)
     )
-    returned = lax.all_to_all(
-        leaving, "ep", split_axis=1, concat_axis=1, tiled=True
-    )
+    returned = exchange(leaving, "ep", 1)
     grad_in = lax.dot_general(
         pick, returned, (((0,), (1,)), ((), ())), preferred_element_type=jnp.float32
     ).astype(jnp.bfloat16)

time: 121 us -> 118 us (0.975)
  starting transfers between devices: 16.8 us -> 42.3 us
  blocking collectives: 16.6 us -> 0 us
  waiting for transfers between devices: 53.2 us -> 42 us
  matrix products: 22.3 us -> 20.7 us
    ppermute x0 -> x21, starting transfers between devices: none -> 34.6 us  [exchange(): lax.ppermute(outgoing, axis, [(i, (i + shift) % peers) for i in range(pee...]
    all_to_all x2 -> x0, waiting for transfers between devices: 27.4 us -> none  [dispatched(): mine = lax.all_to_all(mine, 'ep', split_axis=0, concat_axis=0, tiled=True)]
    all_to_all x1 -> x0, blocking collectives: 16.6 us -> none  [shards(): lax.all_to_all(leaving, 'ep', split_axis=1, concat_axis=1, tiled=True)]
    ppermute x0 -> x21, waiting for transfers between devices: none -> 13.1 us  [exchange(): lax.ppermute(outgoing, axis, [(i, (i + shift) % peers) for i in range(pee...]
    all_to_all x2 -> x0, starting transfers between devices: 10.9 us -> none  [dispatched(): mine = lax.all_to_all(mine, 'ep', split_axis=0, concat_axis=0, tiled=True)]
    ppermute x2, waiting for transfers between devices: 12.9 us -> 15.9 us  [dispatched(): across = lax.ppermute(mine, 'tp', [(i, i ^ 2) for i in range(tp_size)])]
    ppermute x2, starting transfers between devices: 3.06 us -> 4.95 us  [dispatched(): across = lax.ppermute(mine, 'tp', [(i, i ^ 2) for i in range(tp_size)])]
    dot_general x2, matrix products: 4.14 us -> 2.5 us  [dispatched(): jnp.dot(selection, mine, preferred_element_type=jnp.float32)]
  transfers between devices with their start and end apart: 10 -> 29, of which waited for: 4 -> 8; matrix products, arithmetic and copies ran while one was open for 14% -> 15% of each run, Pallas kernels for 0% -> 0%
where the time goes in v9:
time: 118 us
  starting transfers between devices  42.3 us (36%)
  waiting for transfers between devices  42 us (36%)
  matrix products  20.7 us (18%)
  local copies, waits for them, and re-layouts  8.35 us (7%)
  other arithmetic  3.33 us (3%)
    ppermute x21, starting transfers between devices, exchange(): lax.ppermute(outgoing, axis, [(i, (i + shift) % peers) for i in range(pee...  34.6 us
    ppermute x2, waiting for transfers between devices, dispatched(): across = lax.ppermute(mine, 'tp', [(i, i ^ 2) for i in range(tp_size)])  15.9 us
    ppermute x21, waiting for transfers between devices, exchange(): lax.ppermute(outgoing, axis, [(i, (i + shift) % peers) for i in range(pee...  13.1 us
    ppermute x1, waiting for transfers between devices, chip_then_link_sum(): return mine + lax.ppermute(send, 'tp', [(i, i ^ 2) for i in range(4)])  12.9 us
    dot_general x1, matrix products, span_grads(): lax.dot_general(act_cols, rows_dy, (((0,), (0,)), ((), ())), preferred_el...  5.24 us
    dot_general x1, matrix products, shards(): lax.dot_general(rows_dy, weight_out, (((1,), (1,)), ((), ())), preferred_...  5.05 us
    ppermute x2, starting transfers between devices, dispatched(): across = lax.ppermute(mine, 'tp', [(i, i ^ 2) for i in range(tp_size)])  4.95 us
    dynamic_update_slice x8, local copies, waits for them, and re-layouts, dispatched(): whole = lax.dynamic_update_slice_in_dim(whole, piece, where * width, 1)  3.88 us
  transfers between devices with their start and end apart: 29, of which 8 were waited for; matrix products, arithmetic and copies ran while one was open for 15% of the time, Pallas kernels for 0%

profile of v9, /device:TPU:0, one launch (start us, length us, event | category | flops | bytes accessed | tf_op | source)
XLA Modules:
  0.0 117.7 jit_solution(10720549951821358910)
XLA Ops:
  0.7 1.0 copy.15
  1.8 1.1 reduce-window.6
  3.5 0.7 multiply_add_fusion
  4.2 1.2 %convolution_convert_fusion.1 = bf16[768,256]{1,0:T(8,128)(2,1)S(1)} fusion(s32[256]{0:T(256)S(1)} %bitcast.52, s32[256]{0:T(256)S(1)} %bitcast.49, bf16[256,1024]{1,0:T(8,128)(2,1)} %param.6, s32[]{:T(128)S(6)} %select_n.238), kind=kOutput, calls=%fused_computation.27 | convolution fusion | flops 101449728 | bytes 526340 | tf_op jit(solution)/shard_map/dot_general | solution.py:83
  5.4 3.0 %collective-permute-start.10 = (bf16[96,256]{1,0:T(8,128)(2,1)S(1)}, bf16[96,256]{1,0:T(8,128)(2,1)}, u32[]{:S(2)}, u32[]{:S(2)}) collective-permute-start(bf16[96,256]{1,0:T(8,128)(2,1)S(1)} %constant_dynamic-slice_fusion.13), channel_id=1, source_target_pairs={{0,4},{4,8},{8,12},{12,16},{16,20},{20,24},{24,28},{28,0},{1,5},{5... | collective-permute-start | bytes 147464 | tf_op jit(solution)/shard_map/ppermute | solution.py:38
  8.5 0.7 convert_multiply_fusion
  9.1 1.3 %convolution_convert_fusion = bf16[768,512]{1,0:T(8,128)(2,1)S(1)} fusion(f32[256]{0:T(256)S(1)} %bitcast.56, f32[256]{0:T(256)S(1)} %bitcast.55, s32[256]{0:T(256)S(1)} %bitcast.53, s32[256]{0:T(256)S(1)} %bitcast.50, bf16[256,2048]{1,0:T(8,128)(2,1)} %param.7, s32[]{:T(128)S(6)} %select_n.220), kind=kOutput, calls=%fused_computation.26 | convolution fusion | flops 202506240 | bytes 1052676 | tf_op jit(solution)/shard_map/dot_general | solution.py:83
  10.5 1.6 %collective-permute-start = (bf16[96,512]{1,0:T(8,128)(2,1)S(1)}, bf16[96,512]{1,0:T(8,128)(2,1)S(1)}, u32[]{:S(2)}, u32[]{:S(2)}) collective-permute-start(bf16[96,512]{1,0:T(8,128)(2,1)S(1)} %constant_dynamic-slice_fusion.20), channel_id=1, source_target_pairs={{0,4},{4,8},{8,12},{12,16},{16,20},{20,24},{24,28},{28,0},{1,5},{5... | collective-permute-start | bytes 294920 | tf_op jit(solution)/shard_map/ppermute | solution.py:38
  12.1 1.6 %collective-permute-done.10 = bf16[96,256]{1,0:T(8,128)(2,1)} collective-permute-done((bf16[96,256]{1,0:T(8,128)(2,1)S(1)}, bf16[96,256]{1,0:T(8,128)(2,1)}, u32[]{:S(2)}, u32[]{:S(2)}) %collective-permute-start.10) | collective-permute-done | bytes 49184 | tf_op jit(solution)/shard_map/ppermute | solution.py:38
  13.7 0.8 constant_dynamic-slice_fusion.7
  14.6 2.5 %collective-permute-start.12 = (bf16[96,256]{1,0:T(8,128)(2,1)S(1)}, bf16[96,256]{1,0:T(8,128)(2,1)S(1)}, u32[]{:S(2)}, u32[]{:S(2)}) collective-permute-start(bf16[96,256]{1,0:T(8,128)(2,1)S(1)} %get-tuple-element.31), channel_id=1, source_target_pairs={{0,12},{4,16},{8,20},{12,24},{16,28},{20,0},{24,4},{28,8},{1,13},{... | collective-permute-start | bytes 147464 | tf_op jit(solution)/shard_map/ppermute | solution.py:38
  17.1 1.2 %collective-permute-start.13 = (bf16[96,256]{1,0:T(8,128)(2,1)S(1)}, bf16[96,256]{1,0:T(8,128)(2,1)S(1)}, u32[]{:S(2)}, u32[]{:S(2)}) collective-permute-start(bf16[96,256]{1,0:T(8,128)(2,1)S(1)} %get-tuple-element.30), channel_id=1, source_target_pairs={{0,16},{4,20},{8,24},{12,28},{16,0},{20,4},{24,8},{28,12},{1,17},{... | collective-permute-start | bytes 147464 | tf_op jit(solution)/shard_map/ppermute | solution.py:38
  18.3 2.6 %collective-permute-start.14 = (bf16[96,256]{1,0:T(8,128)(2,1)S(1)}, bf16[96,256]{1,0:T(8,128)(2,1)S(1)}, u32[]{:S(2)}, u32[]{:S(2)}) collective-permute-start(bf16[96,256]{1,0:T(8,128)(2,1)S(1)} %get-tuple-element.29), channel_id=1, source_target_pairs={{0,20},{4,24},{8,28},{12,0},{16,4},{20,8},{24,12},{28,16},{1,21},{... | collective-permute-start | bytes 147464 | tf_op jit(solution)/shard_map/ppermute | solution.py:38
  20.9 1.4 %collective-permute-start.15 = (bf16[96,256]{1,0:T(8,128)(2,1)S(1)}, bf16[96,256]{1,0:T(8,128)(2,1)S(1)}, u32[]{:S(2)}, u32[]{:S(2)}) collective-permute-start(bf16[96,256]{1,0:T(8,128)(2,1)S(1)} %get-tuple-element.28), channel_id=1, source_target_pairs={{0,24},{4,28},{8,0},{12,4},{16,8},{20,12},{24,16},{28,20},{1,25},{... | collective-permute-start | bytes 147464 | tf_op jit(solution)/shard_map/ppermute | solution.py:38
  22.4 1.4 %collective-permute-start.16 = (bf16[96,256]{1,0:T(8,128)(2,1)S(1)}, bf16[96,256]{1,0:T(8,128)(2,1)S(1)}, u32[]{:S(2)}, u32[]{:S(2)}) collective-permute-start(bf16[96,256]{1,0:T(8,128)(2,1)S(1)} %get-tuple-element.27), channel_id=1, source_target_pairs={{0,28},{4,0},{8,4},{12,8},{16,12},{20,16},{24,20},{28,24},{1,29},{... | collective-permute-start | bytes 147464 | tf_op jit(solution)/shard_map/ppermute | solution.py:38
  23.8 0.7 collective-permute-start.1
  24.6 1.9 %collective-permute-start.2 = (bf16[96,512]{1,0:T(8,128)(2,1)S(1)}, bf16[96,512]{1,0:T(8,128)(2,1)S(1)}, u32[]{:S(2)}, u32[]{:S(2)}) collective-permute-start(bf16[96,512]{1,0:T(8,128)(2,1)S(1)} %get-tuple-element.17), channel_id=1, source_target_pairs={{0,12},{4,16},{8,20},{12,24},{16,28},{20,0},{24,4},{28,8},{1,13},{... | collective-permute-start | bytes 294920 | tf_op jit(solution)/shard_map/ppermute | solution.py:38
  26.5 2.0 %collective-permute-start.3 = (bf16[96,512]{1,0:T(8,128)(2,1)S(1)}, bf16[96,512]{1,0:T(8,128)(2,1)S(1)}, u32[]{:S(2)}, u32[]{:S(2)}) collective-permute-start(bf16[96,512]{1,0:T(8,128)(2,1)S(1)} %get-tuple-element.16), channel_id=1, source_target_pairs={{0,16},{4,20},{8,24},{12,28},{16,0},{20,4},{24,8},{28,12},{1,17},{... | collective-permute-start | bytes 294920 | tf_op jit(solution)/shard_map/ppermute | solution.py:38
  28.5 2.3 %collective-permute-start.4 = (bf16[96,512]{1,0:T(8,128)(2,1)S(1)}, bf16[96,512]{1,0:T(8,128)(2,1)S(1)}, u32[]{:S(2)}, u32[]{:S(2)}) collective-permute-start(bf16[96,512]{1,0:T(8,128)(2,1)S(1)} %get-tuple-element.15), channel_id=1, source_target_pairs={{0,20},{4,24},{8,28},{12,0},{16,4},{20,8},{24,12},{28,16},{1,21},{... | collective-permute-start | bytes 294920 | tf_op jit(solution)/shard_map/ppermute | solution.py:38
  30.8 2.0 %collective-permute-start.5 = (bf16[96,512]{1,0:T(8,128)(2,1)S(1)}, bf16[96,512]{1,0:T(8,128)(2,1)S(1)}, u32[]{:S(2)}, u32[]{:S(2)}) collective-permute-start(bf16[96,512]{1,0:T(8,128)(2,1)S(1)} %get-tuple-element.14), channel_id=1, source_target_pairs={{0,24},{4,28},{8,0},{12,4},{16,8},{20,12},{24,16},{28,20},{1,25},{... | collective-permute-start | bytes 294920 | tf_op jit(solution)/shard_map/ppermute | solution.py:38
  32.8 0.6 collective-permute-start.6
  33.3 2.3 %collective-permute-done.2 = bf16[96,512]{1,0:T(8,128)(2,1)S(1)} collective-permute-done((bf16[96,512]{1,0:T(8,128)(2,1)S(1)}, bf16[96,512]{1,0:T(8,128)(2,1)S(1)}, u32[]{:S(2)}, u32[]{:S(2)}) %collective-permute-start.2) | collective-permute-done | bytes 98336 | tf_op jit(solution)/shard_map/ppermute | solution.py:38
  35.7 2.9 %collective-permute-start.17 = (bf16[768,256]{1,0:T(8,128)(2,1)S(1)}, bf16[768,256]{1,0:T(8,128)(2,1)}, u32[]{:S(2)}, u32[]{:S(2)}) collective-permute-start(bf16[768,256]{1,0:T(8,128)(2,1)S(1)} %constant_dynamic-update-slice_fusion.11), channel_id=1, source_target_pairs={{0,2},{1,3},{2,0},{3,1},{4,6},{5,7},{6,4},{7,5},{8,10},{9,11},{10,... | collective-permute-start | bytes 1179656 | tf_op jit(solution)/shard_map/ppermute | solution.py:87
  38.7 2.1 %collective-permute-start.7 = (bf16[768,512]{1,0:T(8,128)(2,1)S(1)}, bf16[768,512]{1,0:T(8,128)(2,1)}, u32[]{:S(2)}, u32[]{:S(2)}) collective-permute-start(bf16[768,512]{1,0:T(8,128)(2,1)S(1)} %constant_dynamic-update-slice_fusion.22), channel_id=1, source_target_pairs={{0,2},{1,3},{2,0},{3,1},{4,6},{5,7},{6,4},{7,5},{8,10},{9,11},{10,... | collective-permute-start | bytes 2359304 | tf_op jit(solution)/shard_map/ppermute | solution.py:87
  40.8 7.9 %collective-permute-done.17 = bf16[768,256]{1,0:T(8,128)(2,1)} collective-permute-done((bf16[768,256]{1,0:T(8,128)(2,1)S(1)}, bf16[768,256]{1,0:T(8,128)(2,1)}, u32[]{:S(2)}, u32[]{:S(2)}) %collective-permute-start.17) | collective-permute-done | bytes 393248 | tf_op jit(solution)/shard_map/ppermute | solution.py:87
  48.9 0.6 collective-permute-start.8
  50.0 1.0 constant_dynamic-update-slice_fusion.9
  51.0 1.0 constant_dynamic-update-slice_fusion.8
  52.1 8.0 %collective-permute-done.7 = bf16[768,512]{1,0:T(8,128)(2,1)} collective-permute-done((bf16[768,512]{1,0:T(8,128)(2,1)S(1)}, bf16[768,512]{1,0:T(8,128)(2,1)}, u32[]{:S(2)}, u32[]{:S(2)}) %collective-permute-start.7) | collective-permute-done | bytes 786464 | tf_op jit(solution)/shard_map/ppermute | solution.py:87
  60.2 1.8 %fusion.14 = f32[768,1024]{1,0:T(8,128)S(1)} fusion(bf16[768,1024]{1,0:T(8,128)(2,1)S(1)} %constant_dynamic-update-slice_fusion.7, bf16[1,1024,1024]{2,1,0:T(8,128)(2,1)S(1)} %copy-done), kind=kOutput, calls=%fused_computation.17 | convolution fusion | flops 1610612736 | bytes 6815744 | tf_op jit(solution)/shard_map/dot_general | solution.py:116
  62.0 1.4 %constant_dynamic-update-slice_fusion.20 = bf16[768,2048]{1,0:T(8,128)(2,1)S(1)} fusion(bf16[768,2048]{1,0:T(8,128)(2,1)S(1)} %constant_dynamic-update-slice_fusion.21, bf16[768,512]{1,0:T(8,128)(2,1)} %collective-permute-done.7, s32[]{:T(128)S(6)} %select_n.235), kind=kLoop, calls=%fused_computation.92 | loop fusion | bytes 1572868 | tf_op jit(solution)/shard_map/dynamic_update_slice | solution.py:98
  63.6 0.8 copy-done.1
  64.4 5.0 %fusion.9 = bf16[768,1024]{1,0:T(8,128)(2,1)S(1)} fusion(f32[768,1024]{1,0:T(8,128)S(1)} %fusion.14, bf16[768,2048]{1,0:T(8,128)(2,1)S(1)} %constant_dynamic-update-slice_fusion.18, bf16[1,1024,2048]{2,1,0:T(8,128)(2,1)S(1)} %copy-done.1), kind=kOutput, calls=%fused_computation.13 | convolution fusion | flops 3236954112 | bytes 12058624 | tf_op jit(solution)/shard_map/dot_general | solution.py:119
  69.5 1.8 %fusion.12 = f32[768,1024]{1,0:T(8,128)S(1)} fusion(bf16[768,1024]{1,0:T(8,128)(2,1)S(1)} %fusion.9, bf16[1,1024,1024]{2,1,0:T(8,128)(2,1)S(1)} %copy-done), kind=kOutput, calls=%fused_computation.15 | convolution fusion | flops 1610612736 | bytes 6815744 | tf_op jit(solution)/shard_map/dot_general | solution.py:123
  71.3 0.4 dynamic-slice_bitcast_fusion.3
  71.9 0.6 collective-permute-start.20
  72.5 3.2 %fusion.16 = bf16[1,1024,1024]{2,1,0:T(8,128)(2,1)} fusion(bf16[768,1024]{1,0:T(8,128)(2,1)S(1)} %constant_dynamic-update-slice_fusion.7, bf16[768,1024]{1,0:T(8,128)(2,1)S(1)} %fusion.9), kind=kOutput, calls=%fused_computation.19 | convolution fusion | flops 1612709888 | bytes 5242880 | tf_op jit(solution)/shard_map/dot_general | solution.py:134
  76.0 1.6 %collective-permute-start.21 = (f32[256,768]{0,1:T(8,128)S(1)}, f32[256,768]{0,1:T(8,128)S(1)}, u32[]{:S(2)}, u32[]{:S(2)}) collective-permute-start(f32[256,768]{0,1:T(8,128)S(1)} %slice.38), channel_id=1, source_target_pairs={{0,2},{1,3},{2,0},{3,1},{4,6},{5,7},{6,4},{7,5},{8,10},{9,11},{10,... | collective-permute-start | bytes 2359304 | tf_op jit(solution)/shard_map/ppermute | solution.py:53
  77.6 5.2 %fusion.2 = bf16[1,1024,2048]{2,1,0:T(8,128)(2,1)} fusion(bf16[768,2048]{1,0:T(8,128)(2,1)S(1)} %constant_dynamic-update-slice_fusion.18, f32[768,1024]{1,0:T(8,128)S(1)} %fusion.14), kind=kOutput, calls=%fused_computation.6 | convolution fusion | flops 3232497664 | bytes 10485760 | tf_op jit(solution)/shard_map/dot_general | solution.py:137
  82.8 12.9 %collective-permute-done.21 = f32[256,768]{0,1:T(8,128)S(1)} collective-permute-done((f32[256,768]{0,1:T(8,128)S(1)}, f32[256,768]{0,1:T(8,128)S(1)}, u32[]{:S(2)}, u32[]{:S(2)}) %collective-permute-start.21) | collective-permute-done | bytes 786464 | tf_op jit(solution)/shard_map/ppermute | solution.py:53
  96.2 6.6 %collective-permute-done.22 = bf16[256,96]{0,1:T(8,128)(2,1)S(1)} collective-permute-done((bf16[256,96]{0,1:T(8,128)(2,1)S(1)}, bf16[256,96]{0,1:T(8,128)(2,1)S(1)}, u32[]{:S(2)}, u32[]{:S(2)}) %collective-permute-start.22) | collective-permute-done | bytes 49184 | tf_op jit(solution)/shard_map/ppermute | solution.py:38
  102.8 2.3 %collective-permute-start.23 = (bf16[256,96]{0,1:T(8,128)(2,1)S(1)}, bf16[256,96]{0,1:T(8,128)(2,1)S(1)}, u32[]{:S(2)}, u32[]{:S(2)}) collective-permute-start(bf16[256,96]{0,1:T(8,128)(2,1)S(1)} %get-tuple-element.25), channel_id=1, source_target_pairs={{0,8},{4,12},{8,16},{12,20},{16,24},{20,28},{24,0},{28,4},{1,9},{5... | collective-permute-start | bytes 147464 | tf_op jit(solution)/shard_map/ppermute | solution.py:38
  105.1 1.6 %collective-permute-start.24 = (bf16[256,96]{0,1:T(8,128)(2,1)S(1)}, bf16[256,96]{0,1:T(8,128)(2,1)S(1)}, u32[]{:S(2)}, u32[]{:S(2)}) collective-permute-start(bf16[256,96]{0,1:T(8,128)(2,1)S(1)} %get-tuple-element.24), channel_id=1, source_target_pairs={{0,12},{4,16},{8,20},{12,24},{16,28},{20,0},{24,4},{28,8},{1,13},{... | collective-permute-start | bytes 147464 | tf_op jit(solution)/shard_map/ppermute | solution.py:38
  106.7 1.9 %collective-permute-start.25 = (bf16[256,96]{0,1:T(8,128)(2,1)S(1)}, bf16[256,96]{0,1:T(8,128)(2,1)S(1)}, u32[]{:S(2)}, u32[]{:S(2)}) collective-permute-start(bf16[256,96]{0,1:T(8,128)(2,1)S(1)} %get-tuple-element.23), channel_id=1, source_target_pairs={{0,16},{4,20},{8,24},{12,28},{16,0},{20,4},{24,8},{28,12},{1,17},{... | collective-permute-start | bytes 147464 | tf_op jit(solution)/shard_map/ppermute | solution.py:38
  108.6 3.8 %collective-permute-start.26 = (bf16[256,96]{0,1:T(8,128)(2,1)S(1)}, bf16[256,96]{0,1:T(8,128)(2,1)S(1)}, u32[]{:S(2)}, u32[]{:S(2)}) collective-permute-start(bf16[256,96]{0,1:T(8,128)(2,1)S(1)} %get-tuple-element.22), channel_id=1, source_target_pairs={{0,20},{4,24},{8,28},{12,0},{16,4},{20,8},{24,12},{28,16},{1,21},{... | collective-permute-start | bytes 147464 | tf_op jit(solution)/shard_map/ppermute | solution.py:38
  112.5 1.5 %collective-permute-start.28 = (bf16[256,96]{0,1:T(8,128)(2,1)S(1)}, bf16[256,96]{0,1:T(8,128)(2,1)S(1)}, u32[]{:S(2)}, u32[]{:S(2)}) collective-permute-start(bf16[256,96]{0,1:T(8,128)(2,1)S(1)} %get-tuple-element.20), channel_id=1, source_target_pairs={{0,28},{4,0},{8,4},{12,8},{16,12},{20,16},{24,20},{28,24},{1,29},{... | collective-permute-start | bytes 147464 | tf_op jit(solution)/shard_map/ppermute | solution.py:38
  114.2 2.3 %collective-permute-done.27 = bf16[256,96]{0,1:T(8,128)(2,1)S(1)} collective-permute-done((bf16[256,96]{0,1:T(8,128)(2,1)S(1)}, bf16[256,96]{0,1:T(8,128)(2,1)S(1)}, u32[]{:S(2)}, u32[]{:S(2)}) %collective-permute-start.27) | collective-permute-done | bytes 49184 | tf_op jit(solution)/shard_map/ppermute | solution.py:38
  116.6 1.1 convolution_convert_fusion.2
  (75 shorter events, 3.3 us)
Async XLA Ops:
  0.6 59.5 %copy-start = (bf16[1,1024,1024]{2,1,0:T(8,128)(2,1)S(1)}, bf16[1,1024,1024]{2,1,0:T(8,128)(2,1)}, u32[]{:S(2)}) copy-start(bf16[1,1024,1024]{2,1,0:T(8,128)(2,1)} %param.10) | copy-start | bytes 6291460
  5.4 8.2 %collective-permute-start.10 = (bf16[96,256]{1,0:T(8,128)(2,1)S(1)}, bf16[96,256]{1,0:T(8,128)(2,1)}, u32[]{:S(2)}, u32[]{:S(2)}) collective-permute-start(bf16[96,256]{1,0:T(8,128)(2,1)S(1)} %constant_dynamic-slice_fusion.13), channel_id=1, source_target_pairs={{0,4},{4,8},{8,12},{12,16},{16,20},{20,24},{24,28},{28,0},{1,5},{5... | collective-permute-start | bytes 147464 | tf_op jit(solution)/shard_map/ppermute | solution.py:38
  10.5 10.4 %collective-permute-start = (bf16[96,512]{1,0:T(8,128)(2,1)S(1)}, bf16[96,512]{1,0:T(8,128)(2,1)S(1)}, u32[]{:S(2)}, u32[]{:S(2)}) collective-permute-start(bf16[96,512]{1,0:T(8,128)(2,1)S(1)} %constant_dynamic-slice_fusion.20), channel_id=1, source_target_pairs={{0,4},{4,8},{8,12},{12,16},{16,20},{20,24},{24,28},{28,0},{1,5},{5... | collective-permute-start | bytes 294920 | tf_op jit(solution)/shard_map/ppermute | solution.py:38
  14.5 7.9 %collective-permute-start.11 = (bf16[96,256]{1,0:T(8,128)(2,1)S(1)}, bf16[96,256]{1,0:T(8,128)(2,1)S(1)}, u32[]{:S(2)}, u32[]{:S(2)}) collective-permute-start(bf16[96,256]{1,0:T(8,128)(2,1)S(1)} %get-tuple-element.32), channel_id=1, source_target_pairs={{0,8},{4,12},{8,16},{12,20},{16,24},{20,28},{24,0},{28,4},{1,9},{5... | collective-permute-start | bytes 147464 | tf_op jit(solution)/shard_map/ppermute | solution.py:38
  14.6 9.3 %collective-permute-start.12 = (bf16[96,256]{1,0:T(8,128)(2,1)S(1)}, bf16[96,256]{1,0:T(8,128)(2,1)S(1)}, u32[]{:S(2)}, u32[]{:S(2)}) collective-permute-start(bf16[96,256]{1,0:T(8,128)(2,1)S(1)} %get-tuple-element.31), channel_id=1, source_target_pairs={{0,12},{4,16},{8,20},{12,24},{16,28},{20,0},{24,4},{28,8},{1,13},{... | collective-permute-start | bytes 147464 | tf_op jit(solution)/shard_map/ppermute | solution.py:38
  17.1 7.5 %collective-permute-start.13 = (bf16[96,256]{1,0:T(8,128)(2,1)S(1)}, bf16[96,256]{1,0:T(8,128)(2,1)S(1)}, u32[]{:S(2)}, u32[]{:S(2)}) collective-permute-start(bf16[96,256]{1,0:T(8,128)(2,1)S(1)} %get-tuple-element.30), channel_id=1, source_target_pairs={{0,16},{4,20},{8,24},{12,28},{16,0},{20,4},{24,8},{28,12},{1,17},{... | collective-permute-start | bytes 147464 | tf_op jit(solution)/shard_map/ppermute | solution.py:38
  18.3 8.2 %collective-permute-start.14 = (bf16[96,256]{1,0:T(8,128)(2,1)S(1)}, bf16[96,256]{1,0:T(8,128)(2,1)S(1)}, u32[]{:S(2)}, u32[]{:S(2)}) collective-permute-start(bf16[96,256]{1,0:T(8,128)(2,1)S(1)} %get-tuple-element.29), channel_id=1, source_target_pairs={{0,20},{4,24},{8,28},{12,0},{16,4},{20,8},{24,12},{28,16},{1,21},{... | collective-permute-start | bytes 147464 | tf_op jit(solution)/shard_map/ppermute | solution.py:38
  20.9 7.6 %collective-permute-start.15 = (bf16[96,256]{1,0:T(8,128)(2,1)S(1)}, bf16[96,256]{1,0:T(8,128)(2,1)S(1)}, u32[]{:S(2)}, u32[]{:S(2)}) collective-permute-start(bf16[96,256]{1,0:T(8,128)(2,1)S(1)} %get-tuple-element.28), channel_id=1, source_target_pairs={{0,24},{4,28},{8,0},{12,4},{16,8},{20,12},{24,16},{28,20},{1,25},{... | collective-permute-start | bytes 147464 | tf_op jit(solution)/shard_map/ppermute | solution.py:38
  22.4 8.4 %collective-permute-start.16 = (bf16[96,256]{1,0:T(8,128)(2,1)S(1)}, bf16[96,256]{1,0:T(8,128)(2,1)S(1)}, u32[]{:S(2)}, u32[]{:S(2)}) collective-permute-start(bf16[96,256]{1,0:T(8,128)(2,1)S(1)} %get-tuple-element.27), channel_id=1, source_target_pairs={{0,28},{4,0},{8,4},{12,8},{16,12},{20,16},{24,20},{28,24},{1,29},{... | collective-permute-start | bytes 147464 | tf_op jit(solution)/shard_map/ppermute | solution.py:38
  23.8 8.9 %collective-permute-start.1 = (bf16[96,512]{1,0:T(8,128)(2,1)S(1)}, bf16[96,512]{1,0:T(8,128)(2,1)S(1)}, u32[]{:S(2)}, u32[]{:S(2)}) collective-permute-start(bf16[96,512]{1,0:T(8,128)(2,1)S(1)} %get-tuple-element.18), channel_id=1, source_target_pairs={{0,8},{4,12},{8,16},{12,20},{16,24},{20,28},{24,0},{28,4},{1,9},{5... | collective-permute-start | bytes 294920 | tf_op jit(solution)/shard_map/ppermute | solution.py:38
  24.6 11.1 %collective-permute-start.2 = (bf16[96,512]{1,0:T(8,128)(2,1)S(1)}, bf16[96,512]{1,0:T(8,128)(2,1)S(1)}, u32[]{:S(2)}, u32[]{:S(2)}) collective-permute-start(bf16[96,512]{1,0:T(8,128)(2,1)S(1)} %get-tuple-element.17), channel_id=1, source_target_pairs={{0,12},{4,16},{8,20},{12,24},{16,28},{20,0},{24,4},{28,8},{1,13},{... | collective-permute-start | bytes 294920 | tf_op jit(solution)/shard_map/ppermute | solution.py:38
  26.5 12.1 %collective-permute-start.3 = (bf16[96,512]{1,0:T(8,128)(2,1)S(1)}, bf16[96,512]{1,0:T(8,128)(2,1)S(1)}, u32[]{:S(2)}, u32[]{:S(2)}) collective-permute-start(bf16[96,512]{1,0:T(8,128)(2,1)S(1)} %get-tuple-element.16), channel_id=1, source_target_pairs={{0,16},{4,20},{8,24},{12,28},{16,0},{20,4},{24,8},{28,12},{1,17},{... | collective-permute-start | bytes 294920 | tf_op jit(solution)/shard_map/ppermute | solution.py:38
  28.5 10.1 %collective-permute-start.4 = (bf16[96,512]{1,0:T(8,128)(2,1)S(1)}, bf16[96,512]{1,0:T(8,128)(2,1)S(1)}, u32[]{:S(2)}, u32[]{:S(2)}) collective-permute-start(bf16[96,512]{1,0:T(8,128)(2,1)S(1)} %get-tuple-element.15), channel_id=1, source_target_pairs={{0,20},{4,24},{8,28},{12,0},{16,4},{20,8},{24,12},{28,16},{1,21},{... | collective-permute-start | bytes 294920 | tf_op jit(solution)/shard_map/ppermute | solution.py:38
  30.8 7.9 %collective-permute-start.5 = (bf16[96,512]{1,0:T(8,128)(2,1)S(1)}, bf16[96,512]{1,0:T(8,128)(2,1)S(1)}, u32[]{:S(2)}, u32[]{:S(2)}) collective-permute-start(bf16[96,512]{1,0:T(8,128)(2,1)S(1)} %get-tuple-element.14), channel_id=1, source_target_pairs={{0,24},{4,28},{8,0},{12,4},{16,8},{20,12},{24,16},{28,20},{1,25},{... | collective-permute-start | bytes 294920 | tf_op jit(solution)/shard_map/ppermute | solution.py:38
  32.8 5.9 %collective-permute-start.6 = (bf16[96,512]{1,0:T(8,128)(2,1)S(1)}, bf16[96,512]{1,0:T(8,128)(2,1)S(1)}, u32[]{:S(2)}, u32[]{:S(2)}) collective-permute-start(bf16[96,512]{1,0:T(8,128)(2,1)S(1)} %get-tuple-element.13), channel_id=1, source_target_pairs={{0,28},{4,0},{8,4},{12,8},{16,12},{20,16},{24,20},{28,24},{1,29},{... | collective-permute-start | bytes 294920 | tf_op jit(solution)/shard_map/ppermute | solution.py:38
  35.7 13.0 %collective-permute-start.17 = (bf16[768,256]{1,0:T(8,128)(2,1)S(1)}, bf16[768,256]{1,0:T(8,128)(2,1)}, u32[]{:S(2)}, u32[]{:S(2)}) collective-permute-start(bf16[768,256]{1,0:T(8,128)(2,1)S(1)} %constant_dynamic-update-slice_fusion.11), channel_id=1, source_target_pairs={{0,2},{1,3},{2,0},{3,1},{4,6},{5,7},{6,4},{7,5},{8,10},{9,11},{10,... | collective-permute-start | bytes 1179656 | tf_op jit(solution)/shard_map/ppermute | solution.py:87
  38.7 21.4 %collective-permute-start.7 = (bf16[768,512]{1,0:T(8,128)(2,1)S(1)}, bf16[768,512]{1,0:T(8,128)(2,1)}, u32[]{:S(2)}, u32[]{:S(2)}) collective-permute-start(bf16[768,512]{1,0:T(8,128)(2,1)S(1)} %constant_dynamic-update-slice_fusion.22), channel_id=1, source_target_pairs={{0,2},{1,3},{2,0},{3,1},{4,6},{5,7},{6,4},{7,5},{8,10},{9,11},{10,... | collective-permute-start | bytes 2359304 | tf_op jit(solution)/shard_map/ppermute | solution.py:87
  40.8 10.3 %collective-permute-start.18 = (bf16[768,256]{1,0:T(8,128)(2,1)S(1)}, bf16[768,256]{1,0:T(8,128)(2,1)}, u32[]{:S(2)}, u32[]{:S(2)}) collective-permute-start(bf16[768,256]{1,0:T(8,128)(2,1)S(1)} %constant_dynamic-update-slice_fusion.11), channel_id=1, source_target_pairs={{0,1},{1,0},{2,3},{3,2},{4,5},{5,4},{6,7},{7,6},{8,9},{9,8},{10,11... | collective-permute-start | bytes 1179656 | tf_op jit(solution)/shard_map/ppermute | solution.py:91
  48.7 11.5 %collective-permute-start.19 = (bf16[768,256]{1,0:T(8,128)(2,1)}, bf16[768,256]{1,0:T(8,128)(2,1)S(1)}, u32[]{:S(2)}, u32[]{:S(2)}) collective-permute-start(bf16[768,256]{1,0:T(8,128)(2,1)} %collective-permute-done.17), channel_id=1, source_target_pairs={{0,1},{1,0},{2,3},{3,2},{4,5},{5,4},{6,7},{7,6},{8,9},{9,8},{10,11... | collective-permute-start | bytes 1179656 | tf_op jit(solution)/shard_map/ppermute | solution.py:91
  48.9 14.5 %collective-permute-start.8 = (bf16[768,512]{1,0:T(8,128)(2,1)S(1)}, bf16[768,512]{1,0:T(8,128)(2,1)S(1)}, u32[]{:S(2)}, u32[]{:S(2)}) collective-permute-start(bf16[768,512]{1,0:T(8,128)(2,1)S(1)} %constant_dynamic-update-slice_fusion.22), channel_id=1, source_target_pairs={{0,1},{1,0},{2,3},{3,2},{4,5},{5,4},{6,7},{7,6},{8,9},{9,8},{10,11... | collective-permute-start | bytes 2359304 | tf_op jit(solution)/shard_map/ppermute | solution.py:91
  60.1 3.4 %collective-permute-start.9 = (bf16[768,512]{1,0:T(8,128)(2,1)}, bf16[768,512]{1,0:T(8,128)(2,1)S(1)}, u32[]{:S(2)}, u32[]{:S(2)}) collective-permute-start(bf16[768,512]{1,0:T(8,128)(2,1)} %collective-permute-done.7), channel_id=1, source_target_pairs={{0,1},{1,0},{2,3},{3,2},{4,5},{5,4},{6,7},{7,6},{8,9},{9,8},{10,11... | collective-permute-start | bytes 2359304 | tf_op jit(solution)/shard_map/ppermute | solution.py:91
  62.0 2.4 %copy-start.1 = (bf16[1,1024,2048]{2,1,0:T(8,128)(2,1)S(1)}, bf16[1,1024,2048]{2,1,0:T(8,128)(2,1)}, u32[]{:S(2)}) copy-start(bf16[1,1024,2048]{2,1,0:T(8,128)(2,1)} %param.11) | copy-start | bytes 12582916
  71.9 3.7 %collective-permute-start.20 = (f32[512,768]{0,1:T(8,128)S(1)}, f32[512,768]{0,1:T(8,128)S(1)}, u32[]{:S(2)}, u32[]{:S(2)}) collective-permute-start(f32[512,768]{0,1:T(8,128)S(1)} %pad_maximum_fusion), channel_id=1, source_target_pairs={{0,1},{1,0},{2,3},{3,2},{4,5},{5,4},{6,7},{7,6},{8,9},{9,8},{10,11... | collective-permute-start | bytes 4718600 | tf_op jit(solution)/shard_map/ppermute | solution.py:51
  76.0 19.8 %collective-permute-start.21 = (f32[256,768]{0,1:T(8,128)S(1)}, f32[256,768]{0,1:T(8,128)S(1)}, u32[]{:S(2)}, u32[]{:S(2)}) collective-permute-start(f32[256,768]{0,1:T(8,128)S(1)} %slice.38), channel_id=1, source_target_pairs={{0,2},{1,3},{2,0},{3,1},{4,6},{5,7},{6,4},{7,5},{8,10},{9,11},{10,... | collective-permute-start | bytes 2359304 | tf_op jit(solution)/shard_map/ppermute | solution.py:53
  95.9 6.8 %collective-permute-start.22 = (bf16[256,96]{0,1:T(8,128)(2,1)S(1)}, bf16[256,96]{0,1:T(8,128)(2,1)S(1)}, u32[]{:S(2)}, u32[]{:S(2)}) collective-permute-start(bf16[256,96]{0,1:T(8,128)(2,1)S(1)} %constant_dynamic-slice_fusion.6), channel_id=1, source_target_pairs={{0,4},{4,8},{8,12},{12,16},{16,20},{20,24},{24,28},{28,0},{1,5},{5... | collective-permute-start | bytes 147464 | tf_op jit(solution)/shard_map/ppermute | solution.py:38
  102.8 9.7 %collective-permute-start.23 = (bf16[256,96]{0,1:T(8,128)(2,1)S(1)}, bf16[256,96]{0,1:T(8,128)(2,1)S(1)}, u32[]{:S(2)}, u32[]{:S(2)}) collective-permute-start(bf16[256,96]{0,1:T(8,128)(2,1)S(1)} %get-tuple-element.25), channel_id=1, source_target_pairs={{0,8},{4,12},{8,16},{12,20},{16,24},{20,28},{24,0},{28,4},{1,9},{5... | collective-permute-start | bytes 147464 | tf_op jit(solution)/shard_map/ppermute | solution.py:38
  105.1 8.8 %collective-permute-start.24 = (bf16[256,96]{0,1:T(8,128)(2,1)S(1)}, bf16[256,96]{0,1:T(8,128)(2,1)S(1)}, u32[]{:S(2)}, u32[]{:S(2)}) collective-permute-start(bf16[256,96]{0,1:T(8,128)(2,1)S(1)} %get-tuple-element.24), channel_id=1, source_target_pairs={{0,12},{4,16},{8,20},{12,24},{16,28},{20,0},{24,4},{28,8},{1,13},{... | collective-permute-start | bytes 147464 | tf_op jit(solution)/shard_map/ppermute | solution.py:38
  106.7 7.2 %collective-permute-start.25 = (bf16[256,96]{0,1:T(8,128)(2,1)S(1)}, bf16[256,96]{0,1:T(8,128)(2,1)S(1)}, u32[]{:S(2)}, u32[]{:S(2)}) collective-permute-start(bf16[256,96]{0,1:T(8,128)(2,1)S(1)} %get-tuple-element.23), channel_id=1, source_target_pairs={{0,16},{4,20},{8,24},{12,28},{16,0},{20,4},{24,8},{28,12},{1,17},{... | collective-permute-start | bytes 147464 | tf_op jit(solution)/shard_map/ppermute | solution.py:38
  108.6 5.6 %collective-permute-start.26 = (bf16[256,96]{0,1:T(8,128)(2,1)S(1)}, bf16[256,96]{0,1:T(8,128)(2,1)S(1)}, u32[]{:S(2)}, u32[]{:S(2)}) collective-permute-start(bf16[256,96]{0,1:T(8,128)(2,1)S(1)} %get-tuple-element.22), channel_id=1, source_target_pairs={{0,20},{4,24},{8,28},{12,0},{16,4},{20,8},{24,12},{28,16},{1,21},{... | collective-permute-start | bytes 147464 | tf_op jit(solution)/shard_map/ppermute | solution.py:38
  112.5 4.1 %collective-permute-start.27 = (bf16[256,96]{0,1:T(8,128)(2,1)S(1)}, bf16[256,96]{0,1:T(8,128)(2,1)S(1)}, u32[]{:S(2)}, u32[]{:S(2)}) collective-permute-start(bf16[256,96]{0,1:T(8,128)(2,1)S(1)} %get-tuple-element.21), channel_id=1, source_target_pairs={{0,24},{4,28},{8,0},{12,4},{16,8},{20,12},{24,16},{28,20},{1,25},{... | collective-permute-start | bytes 147464 | tf_op jit(solution)/shard_map/ppermute | solution.py:38
  112.5 4.1 %collective-permute-start.28 = (bf16[256,96]{0,1:T(8,128)(2,1)S(1)}, bf16[256,96]{0,1:T(8,128)(2,1)S(1)}, u32[]{:S(2)}, u32[]{:S(2)}) collective-permute-start(bf16[256,96]{0,1:T(8,128)(2,1)S(1)} %get-tuple-element.20), channel_id=1, source_target_pairs={{0,28},{4,0},{8,4},{12,8},{16,12},{20,16},{24,20},{28,24},{1,29},{... | collective-permute-start | bytes 147464 | tf_op jit(solution)/shard_map/ppermute | solution.py:38

commit v10 on v9

--- a/solution.py
+++ b/solution.py
@@ -76,30 +76,39 @@
     tp_index = lax.axis_index("tp")
     split = 4 if tp_size == 4 else (2 if tp_size % 2 == 0 else 1)
 
-    def dispatched(table, selection):
-        width = table.shape[1] // split
-        part = tp_index % split
-        mine = lax.dynamic_slice_in_dim(table, part * width, width, 1)
-        mine = jnp.dot(selection, mine, preferred_element_type=jnp.float32).astype(jnp.bfloat16)
-        mine = exchange(mine, "ep", 0)
-        pieces = [(mine, part)]
-        if split == 4:
-            across = lax.ppermute(mine, "tp", [(i, i ^ 2) for i in range(tp_size)])
-            pieces.append((across, part ^ 2))
-        if split >= 2:
-            pieces += [
-                (lax.ppermute(piece, "tp", [(i, i ^ 1) for i in range(tp_size)]), where ^ 1)
-                for piece, where in pieces
-            ]
-        if split == 1:
-            return mine
-        whole = jnp.zeros((mine.shape[0], table.shape[1]), jnp.bfloat16)
-        for piece, where in pieces:
-            whole = lax.dynamic_update_slice_in_dim(whole, piece, where * width, 1)
-        return whole
-
-    rows_x = dispatched(features, pick)
-    rows_dy = dispatched(cotangent, pick_scaled)
+    part = tp_index % split
+    tables = (features, cotangent)
+    widths = [table.shape[1] // split for table in tables]
+    mine = jnp.concatenate(
+        [
+            jnp.dot(
+                selection,
+                lax.dynamic_slice_in_dim(table, part * width, width, 1),
+                preferred_element_type=jnp.float32,
+            ).astype(jnp.bfloat16)
+            for table, selection, width in zip(tables, (pick, pick_scaled), widths)
+        ],
+        axis=1,
+    )
+    mine = exchange(mine, "ep", 0)
+    pieces = [(mine, part)]
+    if split == 4:
+        across = lax.ppermute(mine, "tp", [(i, i ^ 2) for i in range(tp_size)])
+        pieces.append((across, part ^ 2))
+    if split >= 2:
+        pieces += [
+            (lax.ppermute(piece, "tp", [(i, i ^ 1) for i in range(tp_size)]), where ^ 1)
+            for piece, where in pieces
+        ]
+    wholes = [jnp.zeros((slot_count, table.shape[1]), jnp.bfloat16) for table in tables]
+    for piece, where in pieces:
+        start = 0
+        for index, width in enumerate(widths):
+            wholes[index] = lax.dynamic_update_slice_in_dim(
+                wholes[index], piece[:, start:start + width], where * width, 1
+            )
+            start += width
+    rows_x, rows_dy = wholes
     piece_in = w_in[0]
     piece_out = w_out[0]
     span = piece_in.shape[1]

time: 118 us -> 150 us (1.27)
  local copies, waits for them, and re-layouts: 8.35 us -> 33 us
  waiting for transfers between devices: 42 us -> 55.5 us
  starting transfers between devices: 42.3 us -> 29.2 us
  other arithmetic: 3.33 us -> 8.11 us
    dynamic_update_slice x18 -> x13, local copies, waits for them, and re-layouts: 0.16 us -> 25.8 us  [exchange(): lax.dynamic_update_slice_in_dim(result, incoming, source * block, dimension)]
    ppermute x6 -> x3, waiting for transfers between devices: 15.9 us -> 26.3 us  [the longest x1 26.3 us: shards(): across = lax.ppermute(mine, 'tp', [(i, i ^ 2) for i in range(tp_size)])]
    ppermute x21 -> x14, starting transfers between devices: 34.6 us -> 25.5 us  [exchange(): lax.ppermute(outgoing, axis, [(i, (i + shift) % peers) for i in range(pee...]
    concatenate x0 -> x3, other arithmetic: none -> 4.8 us  [shards(): jnp.concatenate([jnp.dot(selection, lax.dynamic_slice_in_dim(table, part...]
    ppermute x6 -> x3, starting transfers between devices: 5.53 us -> 1.53 us  [the longest x1 1.52 us: shards(): across = lax.ppermute(mine, 'tp', [(i, i ^ 2) for i in range(tp_size)])]
    ppermute x21 -> x14, waiting for transfers between devices: 13.1 us -> 16.8 us  [exchange(): lax.ppermute(outgoing, axis, [(i, (i + shift) % peers) for i in range(pee...]
  transfers between devices with their start and end apart: 29 -> 19, of which waited for: 8 -> 8; matrix products, arithmetic and copies ran while one was open for 15% -> 26% of each run, Pallas kernels for 0% -> 0%
where the time goes in v10:
time: 150 us; the launch traced here: 148 us
  waiting for transfers between devices  55.5 us (37%)
  local copies, waits for them, and re-layouts  33 us (22%)
  starting transfers between devices  29.2 us (19%)
  matrix products  21.6 us (14%)
  other arithmetic  8.11 us (5%)
    ppermute x1, waiting for transfers between devices, shards(): across = lax.ppermute(mine, 'tp', [(i, i ^ 2) for i in range(tp_size)])  26.3 us
    dynamic_update_slice x13, local copies, waits for them, and re-layouts, exchange(): lax.dynamic_update_slice_in_dim(result, incoming, source * block, dimension)  25.8 us
    ppermute x14, starting transfers between devices, exchange(): lax.ppermute(outgoing, axis, [(i, (i + shift) % peers) for i in range(pee...  25.5 us
    ppermute x14, waiting for transfers between devices, exchange(): lax.ppermute(outgoing, axis, [(i, (i + shift) % peers) for i in range(pee...  16.8 us
    ppermute x1, waiting for transfers between devices, chip_then_link_sum(): return mine + lax.ppermute(send, 'tp', [(i, i ^ 2) for i in range(4)])  12.4 us
    dot_general x1, matrix products, span_grads(): lax.dot_general(act_cols, rows_dy, (((0,), (0,)), ((), ())), preferred_el...  5.84 us
    dot_general x1, matrix products, shards(): lax.dot_general(rows_dy, weight_out, (((1,), (1,)), ((), ())), preferred_...  5.19 us
    concatenate x3, other arithmetic, shards(): jnp.concatenate([jnp.dot(selection, lax.dynamic_slice_in_dim(table, part...  4.8 us
  transfers between devices with their start and end apart: 19, of which 8 were waited for; matrix products, arithmetic and copies ran while one was open for 26% of the time, Pallas kernels for 0%

profile of v10, /device:TPU:0, one launch (start us, length us, event | category | flops | bytes accessed | tf_op | source)
XLA Modules:
  0.0 148.4 jit_solution(13625196925761311955)
XLA Ops:
  0.7 0.9 copy.15
  1.8 1.1 reduce-window.6
  3.6 0.7 multiply_add_fusion
  4.3 0.7 convert_multiply_fusion
  5.0 1.3 convolution_convert_fusion.1
  6.2 1.4 convolution_convert_fusion
  7.6 2.7 %fusion.41 = (bf16[96,768]{0,1:T(8,128)(2,1)S(1)}, bf16[96,768]{0,1:T(8,128)(2,1)}, bf16[96,768]{0,1:T(8,128)(2,1)}, bf16[96,768]{0,1:T(8,128)(2,1)}, bf16[96,768]{0,1:T(8,128)(2,1)}, /*index=5*/bf16[96,768]{0,1:T(8,128)(2,1)}) fusion(s32[]{:T(128)S(6)} %select_n.181, bf16[768,512]{0,1:T(8,128)(2,1)S(1)} %convolution_convert_fusion, ...), kind=kLoop, calls=%fused_computation.78 | loop fusion | flops 1769472 | bytes 2064408 | tf_op jit(solution)/shard_map/concatenate | solution.py:82
  10.3 3.0 %collective-permute-start = (bf16[96,768]{0,1:T(8,128)(2,1)}, bf16[96,768]{0,1:T(8,128)(2,1)}, u32[]{:S(2)}, u32[]{:S(2)}) collective-permute-start(bf16[96,768]{0,1:T(8,128)(2,1)} %get-tuple-element.14), channel_id=1, source_target_pairs={{0,4},{4,8},{8,12},{12,16},{16,20},{20,24},{24,28},{28,0},{1,5},{5... | collective-permute-start | bytes 442376 | tf_op jit(solution)/shard_map/ppermute | solution.py:38
  13.3 1.6 %collective-permute-start.1 = (bf16[96,768]{0,1:T(8,128)(2,1)}, bf16[96,768]{0,1:T(8,128)(2,1)}, u32[]{:S(2)}, u32[]{:S(2)}) collective-permute-start(bf16[96,768]{0,1:T(8,128)(2,1)} %get-tuple-element.15), channel_id=1, source_target_pairs={{0,8},{4,12},{8,16},{12,20},{16,24},{20,28},{24,0},{28,4},{1,9},{5... | collective-permute-start | bytes 442376 | tf_op jit(solution)/shard_map/ppermute | solution.py:38
  14.9 2.6 %collective-permute-start.2 = (bf16[96,768]{0,1:T(8,128)(2,1)}, bf16[96,768]{0,1:T(8,128)(2,1)}, u32[]{:S(2)}, u32[]{:S(2)}) collective-permute-start(bf16[96,768]{0,1:T(8,128)(2,1)} %get-tuple-element.16), channel_id=1, source_target_pairs={{0,12},{4,16},{8,20},{12,24},{16,28},{20,0},{24,4},{28,8},{1,13},{... | collective-permute-start | bytes 442376 | tf_op jit(solution)/shard_map/ppermute | solution.py:38
  17.5 1.2 collective-permute-start.3
  18.7 2.6 %collective-permute-start.4 = (bf16[96,768]{0,1:T(8,128)(2,1)}, bf16[96,768]{0,1:T(8,128)(2,1)}, u32[]{:S(2)}, u32[]{:S(2)}) collective-permute-start(bf16[96,768]{0,1:T(8,128)(2,1)} %get-tuple-element.18), channel_id=1, source_target_pairs={{0,20},{4,24},{8,28},{12,0},{16,4},{20,8},{24,12},{28,16},{1,21},{... | collective-permute-start | bytes 442376 | tf_op jit(solution)/shard_map/ppermute | solution.py:38
  21.3 1.0 fusion.40
  22.6 1.8 %collective-permute-start.5 = (bf16[96,768]{0,1:T(8,128)(2,1)}, bf16[96,768]{0,1:T(8,128)(2,1)}, u32[]{:S(2)}, u32[]{:S(2)}) collective-permute-start(bf16[96,768]{0,1:T(8,128)(2,1)} %fusion.40), channel_id=1, source_target_pairs={{0,24},{4,28},{8,0},{12,4},{16,8},{20,12},{24,16},{28,20},{1,25},{... | collective-permute-start | bytes 442376 | tf_op jit(solution)/shard_map/ppermute | solution.py:38
  24.4 3.5 %collective-permute-start.6 = (bf16[96,768]{0,1:T(8,128)(2,1)S(1)}, bf16[96,768]{0,1:T(8,128)(2,1)}, u32[]{:S(2)}, u32[]{:S(2)}) collective-permute-start(bf16[96,768]{0,1:T(8,128)(2,1)S(1)} %get-tuple-element.13), channel_id=1, source_target_pairs={{0,28},{4,0},{8,4},{12,8},{16,12},{20,16},{24,20},{28,24},{1,29},{... | collective-permute-start | bytes 442376 | tf_op jit(solution)/shard_map/ppermute | solution.py:38
  27.9 1.1 pad_maximum_fusion
  29.0 3.2 %dynamic_update_slice.68 = bf16[768,768]{0,1:T(8,128)(2,1)} dynamic-update-slice(bf16[768,768]{0,1:T(8,128)(2,1)} %pad_maximum_fusion, bf16[96,768]{0,1:T(8,128)(2,1)} %collective-permute-done, s32[]{:T(128)S(6)} %select_n.181, s32[]{:T(128)} %constant.165.clone.1) | dynamic-update-slice | bytes 294916 | tf_op jit(solution)/shard_map/dynamic_update_slice | solution.py:39
  32.2 3.8 %dynamic_update_slice.69 = bf16[768,768]{0,1:T(8,128)(2,1)} dynamic-update-slice(bf16[768,768]{0,1:T(8,128)(2,1)} %dynamic_update_slice.68, bf16[96,768]{0,1:T(8,128)(2,1)} %collective-permute-done.1, s32[]{:T(128)S(6)} %select_n.185, s32[]{:T(128)} %constant.165.clone.1) | dynamic-update-slice | bytes 294916 | tf_op jit(solution)/shard_map/dynamic_update_slice | solution.py:39
  36.0 2.6 %collective-permute-done.2 = bf16[96,768]{0,1:T(8,128)(2,1)} collective-permute-done((bf16[96,768]{0,1:T(8,128)(2,1)}, bf16[96,768]{0,1:T(8,128)(2,1)}, u32[]{:S(2)}, u32[]{:S(2)}) %collective-permute-start.2) | collective-permute-done | bytes 147488 | tf_op jit(solution)/shard_map/ppermute | solution.py:38
  38.6 3.8 %dynamic_update_slice.70 = bf16[768,768]{0,1:T(8,128)(2,1)} dynamic-update-slice(bf16[768,768]{0,1:T(8,128)(2,1)} %dynamic_update_slice.69, bf16[96,768]{0,1:T(8,128)(2,1)} %collective-permute-done.2, s32[]{:T(128)S(6)} %select_n.189, s32[]{:T(128)} %constant.165.clone.1) | dynamic-update-slice | bytes 294916 | tf_op jit(solution)/shard_map/dynamic_update_slice | solution.py:39
  42.4 3.4 %dynamic_update_slice.71 = bf16[768,768]{0,1:T(8,128)(2,1)} dynamic-update-slice(bf16[768,768]{0,1:T(8,128)(2,1)} %dynamic_update_slice.70, bf16[96,768]{0,1:T(8,128)(2,1)} %collective-permute-done.3, s32[]{:T(128)S(6)} %select_n.191, s32[]{:T(128)} %constant.165.clone.1) | dynamic-update-slice | bytes 294916 | tf_op jit(solution)/shard_map/dynamic_update_slice | solution.py:39
  45.8 3.8 %dynamic_update_slice.72 = bf16[768,768]{0,1:T(8,128)(2,1)} dynamic-update-slice(bf16[768,768]{0,1:T(8,128)(2,1)} %dynamic_update_slice.71, bf16[96,768]{0,1:T(8,128)(2,1)} %collective-permute-done.4, s32[]{:T(128)S(6)} %select_n.187, s32[]{:T(128)} %constant.165.clone.1) | dynamic-update-slice | bytes 294916 | tf_op jit(solution)/shard_map/dynamic_update_slice | solution.py:39
  49.6 3.8 %dynamic_update_slice.73 = bf16[768,768]{0,1:T(8,128)(2,1)} dynamic-update-slice(bf16[768,768]{0,1:T(8,128)(2,1)} %dynamic_update_slice.72, bf16[96,768]{0,1:T(8,128)(2,1)} %collective-permute-done.5, s32[]{:T(128)S(6)} %select_n.183, s32[]{:T(128)} %constant.165.clone.1) | dynamic-update-slice | bytes 294916 | tf_op jit(solution)/shard_map/dynamic_update_slice | solution.py:39
  53.4 3.8 %dynamic_update_slice.74 = bf16[768,768]{0,1:T(8,128)(2,1)} dynamic-update-slice(bf16[768,768]{0,1:T(8,128)(2,1)} %dynamic_update_slice.73, bf16[96,768]{0,1:T(8,128)(2,1)} %collective-permute-done.6, s32[]{:T(128)S(6)} %select_n.179, s32[]{:T(128)} %constant.165.clone.1) | dynamic-update-slice | bytes 294916 | tf_op jit(solution)/shard_map/dynamic_update_slice | solution.py:39
  57.3 1.5 %collective-permute-start.7 = (bf16[768,768]{0,1:T(8,128)(2,1)}, bf16[768,768]{0,1:T(8,128)(2,1)}, u32[]{:S(2)}, u32[]{:S(2)}) collective-permute-start(bf16[768,768]{0,1:T(8,128)(2,1)} %dynamic_update_slice.74), channel_id=1, source_target_pairs={{0,2},{1,3},{2,0},{3,1},{4,6},{5,7},{6,4},{7,5},{8,10},{9,11},{10,... | collective-permute-start | bytes 3538952 | tf_op jit(solution)/shard_map/ppermute | solution.py:96
  59.1 26.3 %collective-permute-done.7 = bf16[768,768]{0,1:T(8,128)(2,1)} collective-permute-done((bf16[768,768]{0,1:T(8,128)(2,1)}, bf16[768,768]{0,1:T(8,128)(2,1)}, u32[]{:S(2)}, u32[]{:S(2)}) %collective-permute-start.7) | collective-permute-done | bytes 1179680 | tf_op jit(solution)/shard_map/ppermute | solution.py:96
  85.5 1.0 slice_dynamic-update-slice_fusion.6
  86.6 1.0 slice_dynamic-update-slice_fusion.5
  87.6 1.2 slice_dynamic-update-slice_fusion.2
  88.8 1.2 slice_dynamic-update-slice_fusion.1
  90.1 1.9 %fusion.14 = f32[768,1024]{1,0:T(8,128)S(1)} fusion(bf16[768,1024]{0,1:T(8,128)(2,1)S(1)} %slice_dynamic-update-slice_fusion.4, bf16[1,1024,1024]{2,1,0:T(8,128)(2,1)S(1)} %copy-done), kind=kOutput, calls=%fused_computation.25 | convolution fusion | flops 1610612736 | bytes 6815744 | tf_op jit(solution)/shard_map/dot_general | solution.py:125
  92.3 5.2 %fusion.9 = bf16[768,1024]{1,0:T(8,128)(2,1)S(1)} fusion(f32[768,1024]{1,0:T(8,128)S(1)} %fusion.14, bf16[768,2048]{0,1:T(8,128)(2,1)S(1)} %slice_dynamic-update-slice_fusion, bf16[1,1024,2048]{2,1,0:T(8,128)(2,1)S(1)} %copy-done.2), kind=kOutput, calls=%fused_computation.13 | convolution fusion | flops 3236954112 | bytes 12058624 | tf_op jit(solution)/shard_map/dot_general | solution.py:128
  97.5 1.9 %fusion.12 = f32[768,1024]{1,0:T(8,128)S(1)} fusion(bf16[768,1024]{1,0:T(8,128)(2,1)S(1)} %fusion.9, bf16[1,1024,1024]{2,1,0:T(8,128)(2,1)S(1)} %copy-done), kind=kOutput, calls=%fused_computation.23 | convolution fusion | flops 1610612736 | bytes 6815744 | tf_op jit(solution)/shard_map/dot_general | solution.py:132
  100.0 0.6 collective-permute-start.10
  100.5 3.1 %fusion.16 = bf16[1,1024,1024]{2,1,0:T(8,128)(2,1)} fusion(bf16[768,1024]{0,1:T(8,128)(2,1)S(1)} %slice_dynamic-update-slice_fusion.4, bf16[768,1024]{1,0:T(8,128)(2,1)S(1)} %fusion.9), kind=kOutput, calls=%fused_computation.27 | convolution fusion | flops 1612709888 | bytes 5242880 | tf_op jit(solution)/shard_map/dot_general | solution.py:143
  104.0 1.6 %collective-permute-start.11 = (f32[256,768]{0,1:T(8,128)S(1)}, f32[256,768]{0,1:T(8,128)S(1)}, u32[]{:S(2)}, u32[]{:S(2)}) collective-permute-start(f32[256,768]{0,1:T(8,128)S(1)} %slice.78), channel_id=1, source_target_pairs={{0,2},{1,3},{2,0},{3,1},{4,6},{5,7},{6,4},{7,5},{8,10},{9,11},{10,... | collective-permute-start | bytes 2359304 | tf_op jit(solution)/shard_map/ppermute | solution.py:53
  105.6 5.8 %fusion.2 = bf16[1,1024,2048]{2,1,0:T(8,128)(2,1)} fusion(bf16[768,2048]{0,1:T(8,128)(2,1)S(1)} %slice_dynamic-update-slice_fusion, f32[768,1024]{1,0:T(8,128)S(1)} %fusion.14), kind=kOutput, calls=%fused_computation.6 | convolution fusion | flops 3232497664 | bytes 10485760 | tf_op jit(solution)/shard_map/dot_general | solution.py:146
  111.4 12.4 %collective-permute-done.11 = f32[256,768]{0,1:T(8,128)S(1)} collective-permute-done((f32[256,768]{0,1:T(8,128)S(1)}, f32[256,768]{0,1:T(8,128)S(1)}, u32[]{:S(2)}, u32[]{:S(2)}) %collective-permute-start.11) | collective-permute-done | bytes 786464 | tf_op jit(solution)/shard_map/ppermute | solution.py:53
  124.0 1.0 collective-permute-start.12
  125.0 10.5 %collective-permute-done.12 = bf16[256,96]{0,1:T(8,128)(2,1)S(1)} collective-permute-done((bf16[256,96]{0,1:T(8,128)(2,1)S(1)}, bf16[256,96]{0,1:T(8,128)(2,1)S(1)}, u32[]{:S(2)}, u32[]{:S(2)}) %collective-permute-start.12) | collective-permute-done | bytes 49184 | tf_op jit(solution)/shard_map/ppermute | solution.py:38
  135.5 0.9 collective-permute-start.14
  136.5 1.8 %collective-permute-start.15 = (bf16[256,96]{0,1:T(8,128)(2,1)S(1)}, bf16[256,96]{0,1:T(8,128)(2,1)S(1)}, u32[]{:S(2)}, u32[]{:S(2)}) collective-permute-start(bf16[256,96]{0,1:T(8,128)(2,1)S(1)} %get-tuple-element.22), channel_id=1, source_target_pairs={{0,16},{4,20},{8,24},{12,28},{16,0},{20,4},{24,8},{28,12},{1,17},{... | collective-permute-start | bytes 147464 | tf_op jit(solution)/shard_map/ppermute | solution.py:38
  138.2 3.8 %collective-permute-start.16 = (bf16[256,96]{0,1:T(8,128)(2,1)S(1)}, bf16[256,96]{0,1:T(8,128)(2,1)S(1)}, u32[]{:S(2)}, u32[]{:S(2)}) collective-permute-start(bf16[256,96]{0,1:T(8,128)(2,1)S(1)} %get-tuple-element.21), channel_id=1, source_target_pairs={{0,20},{4,24},{8,28},{12,0},{16,4},{20,8},{24,12},{28,16},{1,21},{... | collective-permute-start | bytes 147464 | tf_op jit(solution)/shard_map/ppermute | solution.py:38
  142.1 1.1 collective-permute-start.17
  143.2 0.6 collective-permute-start.18
  144.1 2.1 %collective-permute-done.17 = bf16[256,96]{0,1:T(8,128)(2,1)S(1)} collective-permute-done((bf16[256,96]{0,1:T(8,128)(2,1)S(1)}, bf16[256,96]{0,1:T(8,128)(2,1)S(1)}, u32[]{:S(2)}, u32[]{:S(2)}) %collective-permute-start.17) | collective-permute-done | bytes 49184 | tf_op jit(solution)/shard_map/ppermute | solution.py:38
  146.2 1.1 collective-permute-done.18
  147.3 1.1 convolution_convert_fusion.2
  (51 shorter events, 3.3 us)
Async XLA Ops:
  0.6 89.4 %copy-start = (bf16[1,1024,1024]{2,1,0:T(8,128)(2,1)S(1)}, bf16[1,1024,1024]{2,1,0:T(8,128)(2,1)}, u32[]{:S(2)}) copy-start(bf16[1,1024,1024]{2,1,0:T(8,128)(2,1)} %param.10) | copy-start | bytes 6291460
  10.3 12.3 %collective-permute-start = (bf16[96,768]{0,1:T(8,128)(2,1)}, bf16[96,768]{0,1:T(8,128)(2,1)}, u32[]{:S(2)}, u32[]{:S(2)}) collective-permute-start(bf16[96,768]{0,1:T(8,128)(2,1)} %get-tuple-element.14), channel_id=1, source_target_pairs={{0,4},{4,8},{8,12},{12,16},{16,20},{20,24},{24,28},{28,0},{1,5},{5... | collective-permute-start | bytes 442376 | tf_op jit(solution)/shard_map/ppermute | solution.py:38
  13.3 11.1 %collective-permute-start.1 = (bf16[96,768]{0,1:T(8,128)(2,1)}, bf16[96,768]{0,1:T(8,128)(2,1)}, u32[]{:S(2)}, u32[]{:S(2)}) collective-permute-start(bf16[96,768]{0,1:T(8,128)(2,1)} %get-tuple-element.15), channel_id=1, source_target_pairs={{0,8},{4,12},{8,16},{12,20},{16,24},{20,28},{24,0},{28,4},{1,9},{5... | collective-permute-start | bytes 442376 | tf_op jit(solution)/shard_map/ppermute | solution.py:38
  14.9 23.7 %collective-permute-start.2 = (bf16[96,768]{0,1:T(8,128)(2,1)}, bf16[96,768]{0,1:T(8,128)(2,1)}, u32[]{:S(2)}, u32[]{:S(2)}) collective-permute-start(bf16[96,768]{0,1:T(8,128)(2,1)} %get-tuple-element.16), channel_id=1, source_target_pairs={{0,12},{4,16},{8,20},{12,24},{16,28},{20,0},{24,4},{28,8},{1,13},{... | collective-permute-start | bytes 442376 | tf_op jit(solution)/shard_map/ppermute | solution.py:38
  17.5 24.9 %collective-permute-start.3 = (bf16[96,768]{0,1:T(8,128)(2,1)}, bf16[96,768]{0,1:T(8,128)(2,1)}, u32[]{:S(2)}, u32[]{:S(2)}) collective-permute-start(bf16[96,768]{0,1:T(8,128)(2,1)} %get-tuple-element.17), channel_id=1, source_target_pairs={{0,16},{4,20},{8,24},{12,28},{16,0},{20,4},{24,8},{28,12},{1,17},{... | collective-permute-start | bytes 442376 | tf_op jit(solution)/shard_map/ppermute | solution.py:38
  18.7 27.1 %collective-permute-start.4 = (bf16[96,768]{0,1:T(8,128)(2,1)}, bf16[96,768]{0,1:T(8,128)(2,1)}, u32[]{:S(2)}, u32[]{:S(2)}) collective-permute-start(bf16[96,768]{0,1:T(8,128)(2,1)} %get-tuple-element.18), channel_id=1, source_target_pairs={{0,20},{4,24},{8,28},{12,0},{16,4},{20,8},{24,12},{28,16},{1,21},{... | collective-permute-start | bytes 442376 | tf_op jit(solution)/shard_map/ppermute | solution.py:38
  22.6 27.0 %collective-permute-start.5 = (bf16[96,768]{0,1:T(8,128)(2,1)}, bf16[96,768]{0,1:T(8,128)(2,1)}, u32[]{:S(2)}, u32[]{:S(2)}) collective-permute-start(bf16[96,768]{0,1:T(8,128)(2,1)} %fusion.40), channel_id=1, source_target_pairs={{0,24},{4,28},{8,0},{12,4},{16,8},{20,12},{24,16},{28,20},{1,25},{... | collective-permute-start | bytes 442376 | tf_op jit(solution)/shard_map/ppermute | solution.py:38
  24.4 29.0 %collective-permute-start.6 = (bf16[96,768]{0,1:T(8,128)(2,1)S(1)}, bf16[96,768]{0,1:T(8,128)(2,1)}, u32[]{:S(2)}, u32[]{:S(2)}) collective-permute-start(bf16[96,768]{0,1:T(8,128)(2,1)S(1)} %get-tuple-element.13), channel_id=1, source_target_pairs={{0,28},{4,0},{8,4},{12,8},{16,12},{20,16},{24,20},{28,24},{1,29},{... | collective-permute-start | bytes 442376 | tf_op jit(solution)/shard_map/ppermute | solution.py:38
  57.3 1.7 %copy-start.1 = (bf16[768,768]{0,1:T(8,128)(2,1)S(1)}, bf16[768,768]{0,1:T(8,128)(2,1)}, u32[]{:S(2)}) copy-start(bf16[768,768]{0,1:T(8,128)(2,1)} %dynamic_update_slice.74) | copy-start | bytes 3538948
  57.3 28.1 %collective-permute-start.7 = (bf16[768,768]{0,1:T(8,128)(2,1)}, bf16[768,768]{0,1:T(8,128)(2,1)}, u32[]{:S(2)}, u32[]{:S(2)}) collective-permute-start(bf16[768,768]{0,1:T(8,128)(2,1)} %dynamic_update_slice.74), channel_id=1, source_target_pairs={{0,2},{1,3},{2,0},{3,1},{4,6},{5,7},{6,4},{7,5},{8,10},{9,11},{10,... | collective-permute-start | bytes 3538952 | tf_op jit(solution)/shard_map/ppermute | solution.py:96
  58.8 27.8 %collective-permute-start.8 = (bf16[768,768]{0,1:T(8,128)(2,1)}, bf16[768,768]{0,1:T(8,128)(2,1)}, u32[]{:S(2)}, u32[]{:S(2)}) collective-permute-start(bf16[768,768]{0,1:T(8,128)(2,1)} %dynamic_update_slice.74), channel_id=1, source_target_pairs={{0,1},{1,0},{2,3},{3,2},{4,5},{5,4},{6,7},{7,6},{8,9},{9,8},{10,11... | collective-permute-start | bytes 3538952 | tf_op jit(solution)/shard_map/ppermute | solution.py:100
  85.4 4.6 %collective-permute-start.9 = (bf16[768,768]{0,1:T(8,128)(2,1)}, bf16[768,768]{0,1:T(8,128)(2,1)S(1)}, u32[]{:S(2)}, u32[]{:S(2)}) collective-permute-start(bf16[768,768]{0,1:T(8,128)(2,1)} %collective-permute-done.7), channel_id=1, source_target_pairs={{0,1},{1,0},{2,3},{3,2},{4,5},{5,4},{6,7},{7,6},{8,9},{9,8},{10,11... | collective-permute-start | bytes 3538952 | tf_op jit(solution)/shard_map/ppermute | solution.py:100
  90.1 2.2 %copy-start.2 = (bf16[1,1024,2048]{2,1,0:T(8,128)(2,1)S(1)}, bf16[1,1024,2048]{2,1,0:T(8,128)(2,1)}, u32[]{:S(2)}) copy-start(bf16[1,1024,2048]{2,1,0:T(8,128)(2,1)} %param.11) | copy-start | bytes 12582916
  100.0 3.7 %collective-permute-start.10 = (f32[512,768]{0,1:T(8,128)S(1)}, f32[512,768]{0,1:T(8,128)S(1)}, u32[]{:S(2)}, u32[]{:S(2)}) collective-permute-start(f32[512,768]{0,1:T(8,128)S(1)} %pad_maximum_fusion.1), channel_id=1, source_target_pairs={{0,1},{1,0},{2,3},{3,2},{4,5},{5,4},{6,7},{7,6},{8,9},{9,8},{10,11... | collective-permute-start | bytes 4718600 | tf_op jit(solution)/shard_map/ppermute | solution.py:51
  104.0 19.8 %collective-permute-start.11 = (f32[256,768]{0,1:T(8,128)S(1)}, f32[256,768]{0,1:T(8,128)S(1)}, u32[]{:S(2)}, u32[]{:S(2)}) collective-permute-start(f32[256,768]{0,1:T(8,128)S(1)} %slice.78), channel_id=1, source_target_pairs={{0,2},{1,3},{2,0},{3,1},{4,6},{5,7},{6,4},{7,5},{8,10},{9,11},{10,... | collective-permute-start | bytes 2359304 | tf_op jit(solution)/shard_map/ppermute | solution.py:53
  124.0 11.5 %collective-permute-start.12 = (bf16[256,96]{0,1:T(8,128)(2,1)S(1)}, bf16[256,96]{0,1:T(8,128)(2,1)S(1)}, u32[]{:S(2)}, u32[]{:S(2)}) collective-permute-start(bf16[256,96]{0,1:T(8,128)(2,1)S(1)} %constant_dynamic-slice_fusion.6), channel_id=1, source_target_pairs={{0,4},{4,8},{8,12},{12,16},{16,20},{20,24},{24,28},{28,0},{1,5},{5... | collective-permute-start | bytes 147464 | tf_op jit(solution)/shard_map/ppermute | solution.py:38
  135.5 7.7 %collective-permute-start.13 = (bf16[256,96]{0,1:T(8,128)(2,1)S(1)}, bf16[256,96]{0,1:T(8,128)(2,1)S(1)}, u32[]{:S(2)}, u32[]{:S(2)}) collective-permute-start(bf16[256,96]{0,1:T(8,128)(2,1)S(1)} %get-tuple-element.24), channel_id=1, source_target_pairs={{0,8},{4,12},{8,16},{12,20},{16,24},{20,28},{24,0},{28,4},{1,9},{5... | collective-permute-start | bytes 147464 | tf_op jit(solution)/shard_map/ppermute | solution.py:38
  135.5 8.2 %collective-permute-start.14 = (bf16[256,96]{0,1:T(8,128)(2,1)S(1)}, bf16[256,96]{0,1:T(8,128)(2,1)S(1)}, u32[]{:S(2)}, u32[]{:S(2)}) collective-permute-start(bf16[256,96]{0,1:T(8,128)(2,1)S(1)} %get-tuple-element.23), channel_id=1, source_target_pairs={{0,12},{4,16},{8,20},{12,24},{16,28},{20,0},{24,4},{28,8},{1,13},{... | collective-permute-start | bytes 147464 | tf_op jit(solution)/shard_map/ppermute | solution.py:38
  136.5 7.6 %collective-permute-start.15 = (bf16[256,96]{0,1:T(8,128)(2,1)S(1)}, bf16[256,96]{0,1:T(8,128)(2,1)S(1)}, u32[]{:S(2)}, u32[]{:S(2)}) collective-permute-start(bf16[256,96]{0,1:T(8,128)(2,1)S(1)} %get-tuple-element.22), channel_id=1, source_target_pairs={{0,16},{4,20},{8,24},{12,28},{16,0},{20,4},{24,8},{28,12},{1,17},{... | collective-permute-start | bytes 147464 | tf_op jit(solution)/shard_map/ppermute | solution.py:38
  138.2 5.8 %collective-permute-start.16 = (bf16[256,96]{0,1:T(8,128)(2,1)S(1)}, bf16[256,96]{0,1:T(8,128)(2,1)S(1)}, u32[]{:S(2)}, u32[]{:S(2)}) collective-permute-start(bf16[256,96]{0,1:T(8,128)(2,1)S(1)} %get-tuple-element.21), channel_id=1, source_target_pairs={{0,20},{4,24},{8,28},{12,0},{16,4},{20,8},{24,12},{28,16},{1,21},{... | collective-permute-start | bytes 147464 | tf_op jit(solution)/shard_map/ppermute | solution.py:38
  142.1 4.1 %collective-permute-start.17 = (bf16[256,96]{0,1:T(8,128)(2,1)S(1)}, bf16[256,96]{0,1:T(8,128)(2,1)S(1)}, u32[]{:S(2)}, u32[]{:S(2)}) collective-permute-start(bf16[256,96]{0,1:T(8,128)(2,1)S(1)} %get-tuple-element.20), channel_id=1, source_target_pairs={{0,24},{4,28},{8,0},{12,4},{16,8},{20,12},{24,16},{28,20},{1,25},{... | collective-permute-start | bytes 147464 | tf_op jit(solution)/shard_map/ppermute | solution.py:38
  143.2 4.1 %collective-permute-start.18 = (bf16[256,96]{0,1:T(8,128)(2,1)S(1)}, bf16[256,96]{0,1:T(8,128)(2,1)S(1)}, u32[]{:S(2)}, u32[]{:S(2)}) collective-permute-start(bf16[256,96]{0,1:T(8,128)(2,1)S(1)} %get-tuple-element.19), channel_id=1, source_target_pairs={{0,28},{4,0},{8,4},{12,8},{16,12},{20,16},{24,20},{28,24},{1,29},{... | collective-permute-start | bytes 147464 | tf_op jit(solution)/shard_map/ppermute | solution.py:38

commit v11 on v9

--- a/solution.py
+++ b/solution.py
@@ -150,7 +150,7 @@
     leaving, grad_w_in, grad_w_out = lax.optimization_barrier(
         (summed.astype(jnp.bfloat16), grad_w_in, grad_w_out)
     )
-    returned = exchange(leaving, "ep", 1)
+    returned = lax.all_to_all(leaving, "ep", split_axis=1, concat_axis=1, tiled=True)
     grad_in = lax.dot_general(
         pick, returned, (((0,), (1,)), ((), ())), preferred_element_type=jnp.float32
     ).astype(jnp.bfloat16)

time: 118 us -> 117 us (level)
  blocking collectives: 0 us -> 19.5 us
  starting transfers between devices: 42.3 us -> 31 us
  waiting for transfers between devices: 42 us -> 32.8 us
    all_to_all x0 -> x1, blocking collectives: none -> 19.5 us  [shards(): lax.all_to_all(leaving, 'ep', split_axis=1, concat_axis=1, tiled=True)]
    ppermute x21 -> x14, starting transfers between devices: 34.6 us -> 23.3 us  [exchange(): lax.ppermute(outgoing, axis, [(i, (i + shift) % peers) for i in range(pee...]
    ppermute x21 -> x14, waiting for transfers between devices: 13.1 us -> 3.95 us  [exchange(): lax.ppermute(outgoing, axis, [(i, (i + shift) % peers) for i in range(pee...]
  transfers between devices with their start and end apart: 29 -> 22, of which waited for: 8 -> 5; matrix products, arithmetic and copies ran while one was open for 15% -> 15% of each run, Pallas kernels for 0% -> 0%
where the time goes in v11:
time: 117 us; the launch traced here: 116 us
  waiting for transfers between devices  32.8 us (28%)
  starting transfers between devices  31 us (26%)
  matrix products  20.7 us (18%)
  blocking collectives  19.5 us (17%)
  local copies, waits for them, and re-layouts  8.26 us (7%)
  other arithmetic  3.33 us (3%)
    ppermute x14, starting transfers between devices, exchange(): lax.ppermute(outgoing, axis, [(i, (i + shift) % peers) for i in range(pee...  23.3 us
    all_to_all x1, blocking collectives, shards(): lax.all_to_all(leaving, 'ep', split_axis=1, concat_axis=1, tiled=True)  19.5 us
    ppermute x2, waiting for transfers between devices, dispatched(): across = lax.ppermute(mine, 'tp', [(i, i ^ 2) for i in range(tp_size)])  15.9 us
    ppermute x1, waiting for transfers between devices, chip_then_link_sum(): return mine + lax.ppermute(send, 'tp', [(i, i ^ 2) for i in range(4)])  12.9 us
    dot_general x1, matrix products, span_grads(): lax.dot_general(act_cols, rows_dy, (((0,), (0,)), ((), ())), preferred_el...  5.24 us
    dot_general x1, matrix products, shards(): lax.dot_general(rows_dy, weight_out, (((1,), (1,)), ((), ())), preferred_...  5.05 us
    ppermute x2, starting transfers between devices, dispatched(): across = lax.ppermute(mine, 'tp', [(i, i ^ 2) for i in range(tp_size)])  4.95 us
    ppermute x14, waiting for transfers between devices, exchange(): lax.ppermute(outgoing, axis, [(i, (i + shift) % peers) for i in range(pee...  3.95 us
  transfers between devices with their start and end apart: 22, of which 5 were waited for; matrix products, arithmetic and copies ran while one was open for 15% of the time, Pallas kernels for 0%

profile of v11, /device:TPU:0, one launch (start us, length us, event | category | flops | bytes accessed | tf_op | source)
XLA Modules:
  0.0 116.5 jit_solution(12069976820331975977)
XLA Ops:
  0.7 1.0 copy.15
  1.8 1.1 reduce-window.6
  2.9 0.2 slice_reduce_fusion
  3.5 0.7 multiply_add_fusion
  4.2 1.2 %convolution_convert_fusion.1 = bf16[768,256]{1,0:T(8,128)(2,1)S(1)} fusion(s32[256]{0:T(256)S(1)} %bitcast.56, s32[256]{0:T(256)S(1)} %bitcast.53, bf16[256,1024]{1,0:T(8,128)(2,1)} %param.6, s32[]{:T(128)S(6)} %select_n.196), kind=kOutput, calls=%fused_computation.27 | convolution fusion | flops 101449728 | bytes 526340 | tf_op jit(solution)/shard_map/dot_general | solution.py:83
  5.4 3.0 %collective-permute-start.10 = (bf16[96,256]{1,0:T(8,128)(2,1)S(1)}, bf16[96,256]{1,0:T(8,128)(2,1)}, u32[]{:S(2)}, u32[]{:S(2)}) collective-permute-start(bf16[96,256]{1,0:T(8,128)(2,1)S(1)} %constant_dynamic-slice_fusion.6), channel_id=1, source_target_pairs={{0,4},{4,8},{8,12},{12,16},{16,20},{20,24},{24,28},{28,0},{1,5},{5... | collective-permute-start | bytes 147464 | tf_op jit(solution)/shard_map/ppermute | solution.py:38
  8.5 0.7 convert_multiply_fusion
  9.1 1.3 %convolution_convert_fusion = bf16[768,512]{1,0:T(8,128)(2,1)S(1)} fusion(f32[256]{0:T(256)S(1)} %bitcast.60, f32[256]{0:T(256)S(1)} %bitcast.59, s32[256]{0:T(256)S(1)} %bitcast.57, s32[256]{0:T(256)S(1)} %bitcast.54, bf16[256,2048]{1,0:T(8,128)(2,1)} %param.7, s32[]{:T(128)S(6)} %select_n.178), kind=kOutput, calls=%fused_computation.26 | convolution fusion | flops 202506240 | bytes 1052676 | tf_op jit(solution)/shard_map/dot_general | solution.py:83
  10.5 1.6 %collective-permute-start = (bf16[96,512]{1,0:T(8,128)(2,1)S(1)}, bf16[96,512]{1,0:T(8,128)(2,1)S(1)}, u32[]{:S(2)}, u32[]{:S(2)}) collective-permute-start(bf16[96,512]{1,0:T(8,128)(2,1)S(1)} %constant_dynamic-slice_fusion.13), channel_id=1, source_target_pairs={{0,4},{4,8},{8,12},{12,16},{16,20},{20,24},{24,28},{28,0},{1,5},{5... | collective-permute-start | bytes 294920 | tf_op jit(solution)/shard_map/ppermute | solution.py:38
  12.1 1.6 %collective-permute-done.10 = bf16[96,256]{1,0:T(8,128)(2,1)} collective-permute-done((bf16[96,256]{1,0:T(8,128)(2,1)S(1)}, bf16[96,256]{1,0:T(8,128)(2,1)}, u32[]{:S(2)}, u32[]{:S(2)}) %collective-permute-start.10) | collective-permute-done | bytes 49184 | tf_op jit(solution)/shard_map/ppermute | solution.py:38
  13.7 0.8 constant_dynamic-slice_fusion
  14.6 2.5 %collective-permute-start.12 = (bf16[96,256]{1,0:T(8,128)(2,1)S(1)}, bf16[96,256]{1,0:T(8,128)(2,1)S(1)}, u32[]{:S(2)}, u32[]{:S(2)}) collective-permute-start(bf16[96,256]{1,0:T(8,128)(2,1)S(1)} %get-tuple-element.24), channel_id=1, source_target_pairs={{0,12},{4,16},{8,20},{12,24},{16,28},{20,0},{24,4},{28,8},{1,13},{... | collective-permute-start | bytes 147464 | tf_op jit(solution)/shard_map/ppermute | solution.py:38
  17.1 1.2 %collective-permute-start.13 = (bf16[96,256]{1,0:T(8,128)(2,1)S(1)}, bf16[96,256]{1,0:T(8,128)(2,1)S(1)}, u32[]{:S(2)}, u32[]{:S(2)}) collective-permute-start(bf16[96,256]{1,0:T(8,128)(2,1)S(1)} %get-tuple-element.23), channel_id=1, source_target_pairs={{0,16},{4,20},{8,24},{12,28},{16,0},{20,4},{24,8},{28,12},{1,17},{... | collective-permute-start | bytes 147464 | tf_op jit(solution)/shard_map/ppermute | solution.py:38
  18.3 2.6 %collective-permute-start.14 = (bf16[96,256]{1,0:T(8,128)(2,1)S(1)}, bf16[96,256]{1,0:T(8,128)(2,1)S(1)}, u32[]{:S(2)}, u32[]{:S(2)}) collective-permute-start(bf16[96,256]{1,0:T(8,128)(2,1)S(1)} %get-tuple-element.22), channel_id=1, source_target_pairs={{0,20},{4,24},{8,28},{12,0},{16,4},{20,8},{24,12},{28,16},{1,21},{... | collective-permute-start | bytes 147464 | tf_op jit(solution)/shard_map/ppermute | solution.py:38
  20.9 1.4 %collective-permute-start.15 = (bf16[96,256]{1,0:T(8,128)(2,1)S(1)}, bf16[96,256]{1,0:T(8,128)(2,1)S(1)}, u32[]{:S(2)}, u32[]{:S(2)}) collective-permute-start(bf16[96,256]{1,0:T(8,128)(2,1)S(1)} %get-tuple-element.21), channel_id=1, source_target_pairs={{0,24},{4,28},{8,0},{12,4},{16,8},{20,12},{24,16},{28,20},{1,25},{... | collective-permute-start | bytes 147464 | tf_op jit(solution)/shard_map/ppermute | solution.py:38
  22.4 1.4 %collective-permute-start.16 = (bf16[96,256]{1,0:T(8,128)(2,1)S(1)}, bf16[96,256]{1,0:T(8,128)(2,1)S(1)}, u32[]{:S(2)}, u32[]{:S(2)}) collective-permute-start(bf16[96,256]{1,0:T(8,128)(2,1)S(1)} %get-tuple-element.20), channel_id=1, source_target_pairs={{0,28},{4,0},{8,4},{12,8},{16,12},{20,16},{24,20},{28,24},{1,29},{... | collective-permute-start | bytes 147464 | tf_op jit(solution)/shard_map/ppermute | solution.py:38
  23.8 0.7 collective-permute-start.1
  24.6 1.9 %collective-permute-start.2 = (bf16[96,512]{1,0:T(8,128)(2,1)S(1)}, bf16[96,512]{1,0:T(8,128)(2,1)S(1)}, u32[]{:S(2)}, u32[]{:S(2)}) collective-permute-start(bf16[96,512]{1,0:T(8,128)(2,1)S(1)} %get-tuple-element.17), channel_id=1, source_target_pairs={{0,12},{4,16},{8,20},{12,24},{16,28},{20,0},{24,4},{28,8},{1,13},{... | collective-permute-start | bytes 294920 | tf_op jit(solution)/shard_map/ppermute | solution.py:38
  26.5 2.0 %collective-permute-start.3 = (bf16[96,512]{1,0:T(8,128)(2,1)S(1)}, bf16[96,512]{1,0:T(8,128)(2,1)S(1)}, u32[]{:S(2)}, u32[]{:S(2)}) collective-permute-start(bf16[96,512]{1,0:T(8,128)(2,1)S(1)} %get-tuple-element.16), channel_id=1, source_target_pairs={{0,16},{4,20},{8,24},{12,28},{16,0},{20,4},{24,8},{28,12},{1,17},{... | collective-permute-start | bytes 294920 | tf_op jit(solution)/shard_map/ppermute | solution.py:38
  28.5 2.3 %collective-permute-start.4 = (bf16[96,512]{1,0:T(8,128)(2,1)S(1)}, bf16[96,512]{1,0:T(8,128)(2,1)S(1)}, u32[]{:S(2)}, u32[]{:S(2)}) collective-permute-start(bf16[96,512]{1,0:T(8,128)(2,1)S(1)} %get-tuple-element.15), channel_id=1, source_target_pairs={{0,20},{4,24},{8,28},{12,0},{16,4},{20,8},{24,12},{28,16},{1,21},{... | collective-permute-start | bytes 294920 | tf_op jit(solution)/shard_map/ppermute | solution.py:38
  30.8 2.0 %collective-permute-start.5 = (bf16[96,512]{1,0:T(8,128)(2,1)S(1)}, bf16[96,512]{1,0:T(8,128)(2,1)S(1)}, u32[]{:S(2)}, u32[]{:S(2)}) collective-permute-start(bf16[96,512]{1,0:T(8,128)(2,1)S(1)} %get-tuple-element.14), channel_id=1, source_target_pairs={{0,24},{4,28},{8,0},{12,4},{16,8},{20,12},{24,16},{28,20},{1,25},{... | collective-permute-start | bytes 294920 | tf_op jit(solution)/shard_map/ppermute | solution.py:38
  32.8 0.6 collective-permute-start.6
  33.3 2.3 %collective-permute-done.2 = bf16[96,512]{1,0:T(8,128)(2,1)S(1)} collective-permute-done((bf16[96,512]{1,0:T(8,128)(2,1)S(1)}, bf16[96,512]{1,0:T(8,128)(2,1)S(1)}, u32[]{:S(2)}, u32[]{:S(2)}) %collective-permute-start.2) | collective-permute-done | bytes 98336 | tf_op jit(solution)/shard_map/ppermute | solution.py:38
  35.7 2.9 %collective-permute-start.17 = (bf16[768,256]{1,0:T(8,128)(2,1)S(1)}, bf16[768,256]{1,0:T(8,128)(2,1)}, u32[]{:S(2)}, u32[]{:S(2)}) collective-permute-start(bf16[768,256]{1,0:T(8,128)(2,1)S(1)} %constant_dynamic-update-slice_fusion.4), channel_id=1, source_target_pairs={{0,2},{1,3},{2,0},{3,1},{4,6},{5,7},{6,4},{7,5},{8,10},{9,11},{10,... | collective-permute-start | bytes 1179656 | tf_op jit(solution)/shard_map/ppermute | solution.py:87
  38.7 2.1 %collective-permute-start.7 = (bf16[768,512]{1,0:T(8,128)(2,1)S(1)}, bf16[768,512]{1,0:T(8,128)(2,1)}, u32[]{:S(2)}, u32[]{:S(2)}) collective-permute-start(bf16[768,512]{1,0:T(8,128)(2,1)S(1)} %constant_dynamic-update-slice_fusion.15), channel_id=1, source_target_pairs={{0,2},{1,3},{2,0},{3,1},{4,6},{5,7},{6,4},{7,5},{8,10},{9,11},{10,... | collective-permute-start | bytes 2359304 | tf_op jit(solution)/shard_map/ppermute | solution.py:87
  40.8 7.9 %collective-permute-done.17 = bf16[768,256]{1,0:T(8,128)(2,1)} collective-permute-done((bf16[768,256]{1,0:T(8,128)(2,1)S(1)}, bf16[768,256]{1,0:T(8,128)(2,1)}, u32[]{:S(2)}, u32[]{:S(2)}) %collective-permute-start.17) | collective-permute-done | bytes 393248 | tf_op jit(solution)/shard_map/ppermute | solution.py:87
  48.7 0.2 broadcast_in_dim.46
  48.9 0.6 collective-permute-start.8
  49.5 0.4 broadcast_in_dim.40
  50.0 1.0 constant_dynamic-update-slice_fusion.2
  51.0 1.0 constant_dynamic-update-slice_fusion.1
  52.1 8.0 %collective-permute-done.7 = bf16[768,512]{1,0:T(8,128)(2,1)} collective-permute-done((bf16[768,512]{1,0:T(8,128)(2,1)S(1)}, bf16[768,512]{1,0:T(8,128)(2,1)}, u32[]{:S(2)}, u32[]{:S(2)}) %collective-permute-start.7) | collective-permute-done | bytes 786464 | tf_op jit(solution)/shard_map/ppermute | solution.py:87
  60.2 1.8 %fusion.14 = f32[768,1024]{1,0:T(8,128)S(1)} fusion(bf16[768,1024]{1,0:T(8,128)(2,1)S(1)} %constant_dynamic-update-slice_fusion, bf16[1,1024,1024]{2,1,0:T(8,128)(2,1)S(1)} %copy-done), kind=kOutput, calls=%fused_computation.17 | convolution fusion | flops 1610612736 | bytes 6815744 | tf_op jit(solution)/shard_map/dot_general | solution.py:116
  62.0 1.4 %constant_dynamic-update-slice_fusion.13 = bf16[768,2048]{1,0:T(8,128)(2,1)S(1)} fusion(bf16[768,2048]{1,0:T(8,128)(2,1)S(1)} %constant_dynamic-update-slice_fusion.14, bf16[768,512]{1,0:T(8,128)(2,1)} %collective-permute-done.7, s32[]{:T(128)S(6)} %select_n.193), kind=kLoop, calls=%fused_computation.78 | loop fusion | bytes 1572868 | tf_op jit(solution)/shard_map/dynamic_update_slice | solution.py:98
  63.6 0.8 copy-done.1
  64.4 5.0 %fusion.9 = bf16[768,1024]{1,0:T(8,128)(2,1)S(1)} fusion(f32[768,1024]{1,0:T(8,128)S(1)} %fusion.14, bf16[768,2048]{1,0:T(8,128)(2,1)S(1)} %constant_dynamic-update-slice_fusion.11, bf16[1,1024,2048]{2,1,0:T(8,128)(2,1)S(1)} %copy-done.1), kind=kOutput, calls=%fused_computation.13 | convolution fusion | flops 3236954112 | bytes 12058624 | tf_op jit(solution)/shard_map/dot_general | solution.py:119
  69.5 1.8 %fusion.12 = f32[768,1024]{1,0:T(8,128)S(1)} fusion(bf16[768,1024]{1,0:T(8,128)(2,1)S(1)} %fusion.9, bf16[1,1024,1024]{2,1,0:T(8,128)(2,1)S(1)} %copy-done), kind=kOutput, calls=%fused_computation.15 | convolution fusion | flops 1610612736 | bytes 6815744 | tf_op jit(solution)/shard_map/dot_general | solution.py:123
  71.3 0.4 dynamic-slice_bitcast_fusion.3
  71.7 0.2 pad_maximum_fusion
  71.9 0.6 collective-permute-start.20
  72.5 3.2 %fusion.16 = bf16[1,1024,1024]{2,1,0:T(8,128)(2,1)} fusion(bf16[768,1024]{1,0:T(8,128)(2,1)S(1)} %constant_dynamic-update-slice_fusion, bf16[768,1024]{1,0:T(8,128)(2,1)S(1)} %fusion.9), kind=kOutput, calls=%fused_computation.19 | convolution fusion | flops 1612709888 | bytes 5242880 | tf_op jit(solution)/shard_map/dot_general | solution.py:134
  75.6 0.3 maximum_add_fusion
  76.0 1.6 %collective-permute-start.21 = (f32[256,768]{0,1:T(8,128)S(1)}, f32[256,768]{0,1:T(8,128)S(1)}, u32[]{:S(2)}, u32[]{:S(2)}) collective-permute-start(f32[256,768]{0,1:T(8,128)S(1)} %slice.38), channel_id=1, source_target_pairs={{0,2},{1,3},{2,0},{3,1},{4,6},{5,7},{6,4},{7,5},{8,10},{9,11},{10,... | collective-permute-start | bytes 2359304 | tf_op jit(solution)/shard_map/ppermute | solution.py:53
  77.6 5.2 %fusion.2 = bf16[1,1024,2048]{2,1,0:T(8,128)(2,1)} fusion(bf16[768,2048]{1,0:T(8,128)(2,1)S(1)} %constant_dynamic-update-slice_fusion.11, f32[768,1024]{1,0:T(8,128)S(1)} %fusion.14), kind=kOutput, calls=%fused_computation.6 | convolution fusion | flops 3232497664 | bytes 10485760 | tf_op jit(solution)/shard_map/dot_general | solution.py:137
  82.8 12.9 %collective-permute-done.21 = f32[256,768]{0,1:T(8,128)S(1)} collective-permute-done((f32[256,768]{0,1:T(8,128)S(1)}, f32[256,768]{0,1:T(8,128)S(1)}, u32[]{:S(2)}, u32[]{:S(2)}) %collective-permute-start.21) | collective-permute-done | bytes 786464 | tf_op jit(solution)/shard_map/ppermute | solution.py:53
  95.8 0.2 fusion.21
  95.9 19.5 %all_to_all.12 = bf16[256,8,96]{0,2,1:T(8,128)(2,1)S(1)} all-to-all(bf16[256,8,96]{0,2,1:T(8,128)(2,1)S(1)} %bitcast.50), channel_id=1, replica_groups=mesh['ep'=8,'tp'=4] {'ep'}, dimensions={1} | all-to-all | bytes 786432 | tf_op jit(solution)/shard_map/all_to_all | solution.py:153
  115.4 1.1 convolution_convert_fusion.2
  (54 shorter events, 1.3 us)
Async XLA Ops:
  0.6 59.5 %copy-start = (bf16[1,1024,1024]{2,1,0:T(8,128)(2,1)S(1)}, bf16[1,1024,1024]{2,1,0:T(8,128)(2,1)}, u32[]{:S(2)}) copy-start(bf16[1,1024,1024]{2,1,0:T(8,128)(2,1)} %param.10) | copy-start | bytes 6291460
  5.4 8.2 %collective-permute-start.10 = (bf16[96,256]{1,0:T(8,128)(2,1)S(1)}, bf16[96,256]{1,0:T(8,128)(2,1)}, u32[]{:S(2)}, u32[]{:S(2)}) collective-permute-start(bf16[96,256]{1,0:T(8,128)(2,1)S(1)} %constant_dynamic-slice_fusion.6), channel_id=1, source_target_pairs={{0,4},{4,8},{8,12},{12,16},{16,20},{20,24},{24,28},{28,0},{1,5},{5... | collective-permute-start | bytes 147464 | tf_op jit(solution)/shard_map/ppermute | solution.py:38
  10.5 10.4 %collective-permute-start = (bf16[96,512]{1,0:T(8,128)(2,1)S(1)}, bf16[96,512]{1,0:T(8,128)(2,1)S(1)}, u32[]{:S(2)}, u32[]{:S(2)}) collective-permute-start(bf16[96,512]{1,0:T(8,128)(2,1)S(1)} %constant_dynamic-slice_fusion.13), channel_id=1, source_target_pairs={{0,4},{4,8},{8,12},{12,16},{16,20},{20,24},{24,28},{28,0},{1,5},{5... | collective-permute-start | bytes 294920 | tf_op jit(solution)/shard_map/ppermute | solution.py:38
  14.5 7.9 %collective-permute-start.11 = (bf16[96,256]{1,0:T(8,128)(2,1)S(1)}, bf16[96,256]{1,0:T(8,128)(2,1)S(1)}, u32[]{:S(2)}, u32[]{:S(2)}) collective-permute-start(bf16[96,256]{1,0:T(8,128)(2,1)S(1)} %get-tuple-element.25), channel_id=1, source_target_pairs={{0,8},{4,12},{8,16},{12,20},{16,24},{20,28},{24,0},{28,4},{1,9},{5... | collective-permute-start | bytes 147464 | tf_op jit(solution)/shard_map/ppermute | solution.py:38
  14.6 9.3 %collective-permute-start.12 = (bf16[96,256]{1,0:T(8,128)(2,1)S(1)}, bf16[96,256]{1,0:T(8,128)(2,1)S(1)}, u32[]{:S(2)}, u32[]{:S(2)}) collective-permute-start(bf16[96,256]{1,0:T(8,128)(2,1)S(1)} %get-tuple-element.24), channel_id=1, source_target_pairs={{0,12},{4,16},{8,20},{12,24},{16,28},{20,0},{24,4},{28,8},{1,13},{... | collective-permute-start | bytes 147464 | tf_op jit(solution)/shard_map/ppermute | solution.py:38
  17.1 7.5 %collective-permute-start.13 = (bf16[96,256]{1,0:T(8,128)(2,1)S(1)}, bf16[96,256]{1,0:T(8,128)(2,1)S(1)}, u32[]{:S(2)}, u32[]{:S(2)}) collective-permute-start(bf16[96,256]{1,0:T(8,128)(2,1)S(1)} %get-tuple-element.23), channel_id=1, source_target_pairs={{0,16},{4,20},{8,24},{12,28},{16,0},{20,4},{24,8},{28,12},{1,17},{... | collective-permute-start | bytes 147464 | tf_op jit(solution)/shard_map/ppermute | solution.py:38
  18.3 8.2 %collective-permute-start.14 = (bf16[96,256]{1,0:T(8,128)(2,1)S(1)}, bf16[96,256]{1,0:T(8,128)(2,1)S(1)}, u32[]{:S(2)}, u32[]{:S(2)}) collective-permute-start(bf16[96,256]{1,0:T(8,128)(2,1)S(1)} %get-tuple-element.22), channel_id=1, source_target_pairs={{0,20},{4,24},{8,28},{12,0},{16,4},{20,8},{24,12},{28,16},{1,21},{... | collective-permute-start | bytes 147464 | tf_op jit(solution)/shard_map/ppermute | solution.py:38
  20.9 7.6 %collective-permute-start.15 = (bf16[96,256]{1,0:T(8,128)(2,1)S(1)}, bf16[96,256]{1,0:T(8,128)(2,1)S(1)}, u32[]{:S(2)}, u32[]{:S(2)}) collective-permute-start(bf16[96,256]{1,0:T(8,128)(2,1)S(1)} %get-tuple-element.21), channel_id=1, source_target_pairs={{0,24},{4,28},{8,0},{12,4},{16,8},{20,12},{24,16},{28,20},{1,25},{... | collective-permute-start | bytes 147464 | tf_op jit(solution)/shard_map/ppermute | solution.py:38
  22.4 8.4 %collective-permute-start.16 = (bf16[96,256]{1,0:T(8,128)(2,1)S(1)}, bf16[96,256]{1,0:T(8,128)(2,1)S(1)}, u32[]{:S(2)}, u32[]{:S(2)}) collective-permute-start(bf16[96,256]{1,0:T(8,128)(2,1)S(1)} %get-tuple-element.20), channel_id=1, source_target_pairs={{0,28},{4,0},{8,4},{12,8},{16,12},{20,16},{24,20},{28,24},{1,29},{... | collective-permute-start | bytes 147464 | tf_op jit(solution)/shard_map/ppermute | solution.py:38
  23.8 8.9 %collective-permute-start.1 = (bf16[96,512]{1,0:T(8,128)(2,1)S(1)}, bf16[96,512]{1,0:T(8,128)(2,1)S(1)}, u32[]{:S(2)}, u32[]{:S(2)}) collective-permute-start(bf16[96,512]{1,0:T(8,128)(2,1)S(1)} %get-tuple-element.18), channel_id=1, source_target_pairs={{0,8},{4,12},{8,16},{12,20},{16,24},{20,28},{24,0},{28,4},{1,9},{5... | collective-permute-start | bytes 294920 | tf_op jit(solution)/shard_map/ppermute | solution.py:38
  24.6 11.1 %collective-permute-start.2 = (bf16[96,512]{1,0:T(8,128)(2,1)S(1)}, bf16[96,512]{1,0:T(8,128)(2,1)S(1)}, u32[]{:S(2)}, u32[]{:S(2)}) collective-permute-start(bf16[96,512]{1,0:T(8,128)(2,1)S(1)} %get-tuple-element.17), channel_id=1, source_target_pairs={{0,12},{4,16},{8,20},{12,24},{16,28},{20,0},{24,4},{28,8},{1,13},{... | collective-permute-start | bytes 294920 | tf_op jit(solution)/shard_map/ppermute | solution.py:38
  26.5 12.1 %collective-permute-start.3 = (bf16[96,512]{1,0:T(8,128)(2,1)S(1)}, bf16[96,512]{1,0:T(8,128)(2,1)S(1)}, u32[]{:S(2)}, u32[]{:S(2)}) collective-permute-start(bf16[96,512]{1,0:T(8,128)(2,1)S(1)} %get-tuple-element.16), channel_id=1, source_target_pairs={{0,16},{4,20},{8,24},{12,28},{16,0},{20,4},{24,8},{28,12},{1,17},{... | collective-permute-start | bytes 294920 | tf_op jit(solution)/shard_map/ppermute | solution.py:38
  28.5 10.1 %collective-permute-start.4 = (bf16[96,512]{1,0:T(8,128)(2,1)S(1)}, bf16[96,512]{1,0:T(8,128)(2,1)S(1)}, u32[]{:S(2)}, u32[]{:S(2)}) collective-permute-start(bf16[96,512]{1,0:T(8,128)(2,1)S(1)} %get-tuple-element.15), channel_id=1, source_target_pairs={{0,20},{4,24},{8,28},{12,0},{16,4},{20,8},{24,12},{28,16},{1,21},{... | collective-permute-start | bytes 294920 | tf_op jit(solution)/shard_map/ppermute | solution.py:38
  30.8 7.9 %collective-permute-start.5 = (bf16[96,512]{1,0:T(8,128)(2,1)S(1)}, bf16[96,512]{1,0:T(8,128)(2,1)S(1)}, u32[]{:S(2)}, u32[]{:S(2)}) collective-permute-start(bf16[96,512]{1,0:T(8,128)(2,1)S(1)} %get-tuple-element.14), channel_id=1, source_target_pairs={{0,24},{4,28},{8,0},{12,4},{16,8},{20,12},{24,16},{28,20},{1,25},{... | collective-permute-start | bytes 294920 | tf_op jit(solution)/shard_map/ppermute | solution.py:38
  32.8 5.9 %collective-permute-start.6 = (bf16[96,512]{1,0:T(8,128)(2,1)S(1)}, bf16[96,512]{1,0:T(8,128)(2,1)S(1)}, u32[]{:S(2)}, u32[]{:S(2)}) collective-permute-start(bf16[96,512]{1,0:T(8,128)(2,1)S(1)} %get-tuple-element.13), channel_id=1, source_target_pairs={{0,28},{4,0},{8,4},{12,8},{16,12},{20,16},{24,20},{28,24},{1,29},{... | collective-permute-start | bytes 294920 | tf_op jit(solution)/shard_map/ppermute | solution.py:38
  35.7 13.0 %collective-permute-start.17 = (bf16[768,256]{1,0:T(8,128)(2,1)S(1)}, bf16[768,256]{1,0:T(8,128)(2,1)}, u32[]{:S(2)}, u32[]{:S(2)}) collective-permute-start(bf16[768,256]{1,0:T(8,128)(2,1)S(1)} %constant_dynamic-update-slice_fusion.4), channel_id=1, source_target_pairs={{0,2},{1,3},{2,0},{3,1},{4,6},{5,7},{6,4},{7,5},{8,10},{9,11},{10,... | collective-permute-start | bytes 1179656 | tf_op jit(solution)/shard_map/ppermute | solution.py:87
  38.7 21.4 %collective-permute-start.7 = (bf16[768,512]{1,0:T(8,128)(2,1)S(1)}, bf16[768,512]{1,0:T(8,128)(2,1)}, u32[]{:S(2)}, u32[]{:S(2)}) collective-permute-start(bf16[768,512]{1,0:T(8,128)(2,1)S(1)} %constant_dynamic-update-slice_fusion.15), channel_id=1, source_target_pairs={{0,2},{1,3},{2,0},{3,1},{4,6},{5,7},{6,4},{7,5},{8,10},{9,11},{10,... | collective-permute-start | bytes 2359304 | tf_op jit(solution)/shard_map/ppermute | solution.py:87
  40.8 10.3 %collective-permute-start.18 = (bf16[768,256]{1,0:T(8,128)(2,1)S(1)}, bf16[768,256]{1,0:T(8,128)(2,1)}, u32[]{:S(2)}, u32[]{:S(2)}) collective-permute-start(bf16[768,256]{1,0:T(8,128)(2,1)S(1)} %constant_dynamic-update-slice_fusion.4), channel_id=1, source_target_pairs={{0,1},{1,0},{2,3},{3,2},{4,5},{5,4},{6,7},{7,6},{8,9},{9,8},{10,11... | collective-permute-start | bytes 1179656 | tf_op jit(solution)/shard_map/ppermute | solution.py:91
  48.7 11.5 %collective-permute-start.19 = (bf16[768,256]{1,0:T(8,128)(2,1)}, bf16[768,256]{1,0:T(8,128)(2,1)S(1)}, u32[]{:S(2)}, u32[]{:S(2)}) collective-permute-start(bf16[768,256]{1,0:T(8,128)(2,1)} %collective-permute-done.17), channel_id=1, source_target_pairs={{0,1},{1,0},{2,3},{3,2},{4,5},{5,4},{6,7},{7,6},{8,9},{9,8},{10,11... | collective-permute-start | bytes 1179656 | tf_op jit(solution)/shard_map/ppermute | solution.py:91
  48.9 14.5 %collective-permute-start.8 = (bf16[768,512]{1,0:T(8,128)(2,1)S(1)}, bf16[768,512]{1,0:T(8,128)(2,1)S(1)}, u32[]{:S(2)}, u32[]{:S(2)}) collective-permute-start(bf16[768,512]{1,0:T(8,128)(2,1)S(1)} %constant_dynamic-update-slice_fusion.15), channel_id=1, source_target_pairs={{0,1},{1,0},{2,3},{3,2},{4,5},{5,4},{6,7},{7,6},{8,9},{9,8},{10,11... | collective-permute-start | bytes 2359304 | tf_op jit(solution)/shard_map/ppermute | solution.py:91
  60.1 3.4 %collective-permute-start.9 = (bf16[768,512]{1,0:T(8,128)(2,1)}, bf16[768,512]{1,0:T(8,128)(2,1)S(1)}, u32[]{:S(2)}, u32[]{:S(2)}) collective-permute-start(bf16[768,512]{1,0:T(8,128)(2,1)} %collective-permute-done.7), channel_id=1, source_target_pairs={{0,1},{1,0},{2,3},{3,2},{4,5},{5,4},{6,7},{7,6},{8,9},{9,8},{10,11... | collective-permute-start | bytes 2359304 | tf_op jit(solution)/shard_map/ppermute | solution.py:91
  62.0 2.4 %copy-start.1 = (bf16[1,1024,2048]{2,1,0:T(8,128)(2,1)S(1)}, bf16[1,1024,2048]{2,1,0:T(8,128)(2,1)}, u32[]{:S(2)}) copy-start(bf16[1,1024,2048]{2,1,0:T(8,128)(2,1)} %param.11) | copy-start | bytes 12582916
  71.9 3.7 %collective-permute-start.20 = (f32[512,768]{0,1:T(8,128)S(1)}, f32[512,768]{0,1:T(8,128)S(1)}, u32[]{:S(2)}, u32[]{:S(2)}) collective-permute-start(f32[512,768]{0,1:T(8,128)S(1)} %pad_maximum_fusion), channel_id=1, source_target_pairs={{0,1},{1,0},{2,3},{3,2},{4,5},{5,4},{6,7},{7,6},{8,9},{9,8},{10,11... | collective-permute-start | bytes 4718600 | tf_op jit(solution)/shard_map/ppermute | solution.py:51
  76.0 19.8 %collective-permute-start.21 = (f32[256,768]{0,1:T(8,128)S(1)}, f32[256,768]{0,1:T(8,128)S(1)}, u32[]{:S(2)}, u32[]{:S(2)}) collective-permute-start(f32[256,768]{0,1:T(8,128)S(1)} %slice.38), channel_id=1, source_target_pairs={{0,2},{1,3},{2,0},{3,1},{4,6},{5,7},{6,4},{7,5},{8,10},{9,11},{10,... | collective-permute-start | bytes 2359304 | tf_op jit(solution)/shard_map/ppermute | solution.py:53

commit v12 on v11

--- a/solution.py
+++ b/solution.py
@@ -76,12 +76,15 @@
     tp_index = lax.axis_index("tp")
     split = 4 if tp_size == 4 else (2 if tp_size % 2 == 0 else 1)
 
-    def dispatched(table, selection):
+    part = tp_index % split
+
+    def local_columns(table, selection):
         width = table.shape[1] // split
-        part = tp_index % split
         mine = lax.dynamic_slice_in_dim(table, part * width, width, 1)
-        mine = jnp.dot(selection, mine, preferred_element_type=jnp.float32).astype(jnp.bfloat16)
-        mine = exchange(mine, "ep", 0)
+        return jnp.dot(selection, mine, preferred_element_type=jnp.float32).astype(jnp.bfloat16)
+
+    def spread(mine, columns):
+        width = columns // split
         pieces = [(mine, part)]
         if split == 4:
             across = lax.ppermute(mine, "tp", [(i, i ^ 2) for i in range(tp_size)])
@@ -93,13 +96,16 @@
             ]
         if split == 1:
             return mine
-        whole = jnp.zeros((mine.shape[0], table.shape[1]), jnp.bfloat16)
+        whole = jnp.zeros((mine.shape[0], columns), jnp.bfloat16)
         for piece, where in pieces:
             whole = lax.dynamic_update_slice_in_dim(whole, piece, where * width, 1)
         return whole
 
-    rows_x = dispatched(features, pick)
-    rows_dy = dispatched(cotangent, pick_scaled)
+    local_x = local_columns(features, pick)
+    local_dy = local_columns(cotangent, pick_scaled)
+    moved = exchange(jnp.concatenate([local_x, local_dy], axis=1), "ep", 0)
+    rows_x = spread(moved[:, :local_x.shape[1]], features.shape[1])
+    rows_dy = spread(moved[:, local_x.shape[1]:], cotangent.shape[1])
     piece_in = w_in[0]
     piece_out = w_out[0]
     span = piece_in.shape[1]

time: 117 us -> 157 us (1.34)
  local copies, waits for them, and re-layouts: 8.26 us -> 39.9 us
  starting transfers between devices: 31 us -> 21.3 us
  waiting for transfers between devices: 32.8 us -> 38.2 us
  other arithmetic: 3.33 us -> 8.11 us
  matrix products: 20.7 us -> 24.5 us
  blocking collectives: 19.5 us -> 22.3 us
    dynamic_update_slice x12 -> x7, local copies, waits for them, and re-layouts: 0.11 us -> 25.7 us  [exchange(): lax.dynamic_update_slice_in_dim(result, incoming, source * block, dimension)]
    ppermute x14 -> x7, starting transfers between devices: 23.3 us -> 16.2 us  [exchange(): lax.ppermute(outgoing, axis, [(i, (i + shift) % peers) for i in range(pee...]
    ppermute x6, waiting for transfers between devices: 15.9 us -> 22.7 us  [the longest x2 22.7 us: spread(): across = lax.ppermute(mine, 'tp', [(i, i ^ 2) for i in range(tp_size)])]
    concatenate x0 -> x3, other arithmetic: none -> 4.8 us  [shards(): moved = exchange(jnp.concatenate([local_x, local_dy], axis=1), 'ep', 0)]
    dynamic_update_slice x8 -> x6, local copies, waits for them, and re-layouts: 3.88 us -> 8.53 us  [spread(): whole = lax.dynamic_update_slice_in_dim(whole, piece, where * width, 1)]
    all_to_all x1, blocking collectives: 19.5 us -> 22.3 us  [shards(): lax.all_to_all(leaving, 'ep', split_axis=1, concat_axis=1, tiled=True)]
    ppermute x6, starting transfers between devices: 5.53 us -> 3.47 us  [the longest x2 2.45 us: spread(): across = lax.ppermute(mine, 'tp', [(i, i ^ 2) for i in range(tp_size)])]
    dot_general x1, matrix products: 1.79 us -> 3.39 us  [shards(): pre = jnp.dot(rows_x, weight_in, preferred_element_type=jnp.float32)]
  transfers between devices with their start and end apart: 22 -> 15, of which waited for: 5 -> 4; matrix products, arithmetic and copies ran while one was open for 15% -> 31% of each run, Pallas kernels for 0% -> 0%
where the time goes in v12:
time: 157 us; the launch traced here: 155 us
  local copies, waits for them, and re-layouts  39.9 us (25%)
  waiting for transfers between devices  38.2 us (24%)
  matrix products  24.5 us (16%)
  blocking collectives  22.3 us (14%)
  starting transfers between devices  21.3 us (14%)
  other arithmetic  8.11 us (5%)
    dynamic_update_slice x7, local copies, waits for them, and re-layouts, exchange(): lax.dynamic_update_slice_in_dim(result, incoming, source * block, dimension)  25.7 us
    ppermute x2, waiting for transfers between devices, spread(): across = lax.ppermute(mine, 'tp', [(i, i ^ 2) for i in range(tp_size)])  22.7 us
    all_to_all x1, blocking collectives, shards(): lax.all_to_all(leaving, 'ep', split_axis=1, concat_axis=1, tiled=True)  22.3 us
    ppermute x7, starting transfers between devices, exchange(): lax.ppermute(outgoing, axis, [(i, (i + shift) % peers) for i in range(pee...  16.2 us
    ppermute x1, waiting for transfers between devices, chip_then_link_sum(): return mine + lax.ppermute(send, 'tp', [(i, i ^ 2) for i in range(4)])  12.5 us
    dynamic_update_slice x6, local copies, waits for them, and re-layouts, spread(): whole = lax.dynamic_update_slice_in_dim(whole, piece, where * width, 1)  8.53 us
    dot_general x1, matrix products, span_grads(): lax.dot_general(act_cols, rows_dy, (((0,), (0,)), ((), ())), preferred_el...  5.87 us
    dot_general x1, matrix products, shards(): lax.dot_general(rows_dy, weight_out, (((1,), (1,)), ((), ())), preferred_...  5.19 us
  transfers between devices with their start and end apart: 15, of which 4 were waited for; matrix products, arithmetic and copies ran while one was open for 31% of the time, Pallas kernels for 0%

profile of v12, /device:TPU:0, one launch (start us, length us, event | category | flops | bytes accessed | tf_op | source)
XLA Modules:
  0.0 155.3 jit_solution(14485170498254629412)
XLA Ops:
  0.7 0.9 copy.15
  1.8 1.1 reduce-window.6
  3.6 0.7 multiply_add_fusion
  4.3 0.7 convert_multiply_fusion
  5.0 1.3 convolution_convert_fusion.1
  6.2 1.4 convolution_convert_fusion
  7.6 2.7 %fusion.41 = (bf16[96,768]{0,1:T(8,128)(2,1)S(1)}, bf16[96,768]{0,1:T(8,128)(2,1)}, bf16[96,768]{0,1:T(8,128)(2,1)}, bf16[96,768]{0,1:T(8,128)(2,1)}, bf16[96,768]{0,1:T(8,128)(2,1)}, /*index=5*/bf16[96,768]{0,1:T(8,128)(2,1)}) fusion(s32[]{:T(128)S(6)} %select_n.139, bf16[768,512]{0,1:T(8,128)(2,1)S(1)} %convolution_convert_fusion, ...), kind=kLoop, calls=%fused_computation.70 | loop fusion | flops 1769472 | bytes 2064408 | tf_op jit(solution)/shard_map/concatenate | solution.py:106
  10.3 3.0 %collective-permute-start = (bf16[96,768]{0,1:T(8,128)(2,1)}, bf16[96,768]{0,1:T(8,128)(2,1)}, u32[]{:S(2)}, u32[]{:S(2)}) collective-permute-start(bf16[96,768]{0,1:T(8,128)(2,1)} %get-tuple-element.18), channel_id=1, source_target_pairs={{0,4},{4,8},{8,12},{12,16},{16,20},{20,24},{24,28},{28,0},{1,5},{5... | collective-permute-start | bytes 442376 | tf_op jit(solution)/shard_map/ppermute | solution.py:38
  13.3 1.6 %collective-permute-start.1 = (bf16[96,768]{0,1:T(8,128)(2,1)}, bf16[96,768]{0,1:T(8,128)(2,1)}, u32[]{:S(2)}, u32[]{:S(2)}) collective-permute-start(bf16[96,768]{0,1:T(8,128)(2,1)} %get-tuple-element.19), channel_id=1, source_target_pairs={{0,8},{4,12},{8,16},{12,20},{16,24},{20,28},{24,0},{28,4},{1,9},{5... | collective-permute-start | bytes 442376 | tf_op jit(solution)/shard_map/ppermute | solution.py:38
  14.9 2.6 %collective-permute-start.2 = (bf16[96,768]{0,1:T(8,128)(2,1)}, bf16[96,768]{0,1:T(8,128)(2,1)}, u32[]{:S(2)}, u32[]{:S(2)}) collective-permute-start(bf16[96,768]{0,1:T(8,128)(2,1)} %get-tuple-element.20), channel_id=1, source_target_pairs={{0,12},{4,16},{8,20},{12,24},{16,28},{20,0},{24,4},{28,8},{1,13},{... | collective-permute-start | bytes 442376 | tf_op jit(solution)/shard_map/ppermute | solution.py:38
  17.5 1.2 collective-permute-start.3
  18.7 2.6 %collective-permute-start.4 = (bf16[96,768]{0,1:T(8,128)(2,1)}, bf16[96,768]{0,1:T(8,128)(2,1)}, u32[]{:S(2)}, u32[]{:S(2)}) collective-permute-start(bf16[96,768]{0,1:T(8,128)(2,1)} %get-tuple-element.22), channel_id=1, source_target_pairs={{0,20},{4,24},{8,28},{12,0},{16,4},{20,8},{24,12},{28,16},{1,21},{... | collective-permute-start | bytes 442376 | tf_op jit(solution)/shard_map/ppermute | solution.py:38
  21.3 1.0 fusion.40
  22.3 0.3 collective-permute-done
  22.6 1.8 %collective-permute-start.5 = (bf16[96,768]{0,1:T(8,128)(2,1)}, bf16[96,768]{0,1:T(8,128)(2,1)}, u32[]{:S(2)}, u32[]{:S(2)}) collective-permute-start(bf16[96,768]{0,1:T(8,128)(2,1)} %fusion.40), channel_id=1, source_target_pairs={{0,24},{4,28},{8,0},{12,4},{16,8},{20,12},{24,16},{28,20},{1,25},{... | collective-permute-start | bytes 442376 | tf_op jit(solution)/shard_map/ppermute | solution.py:38
  24.4 3.5 %collective-permute-start.6 = (bf16[96,768]{0,1:T(8,128)(2,1)S(1)}, bf16[96,768]{0,1:T(8,128)(2,1)}, u32[]{:S(2)}, u32[]{:S(2)}) collective-permute-start(bf16[96,768]{0,1:T(8,128)(2,1)S(1)} %get-tuple-element.17), channel_id=1, source_target_pairs={{0,28},{4,0},{8,4},{12,8},{16,12},{20,16},{24,20},{28,24},{1,29},{... | collective-permute-start | bytes 442376 | tf_op jit(solution)/shard_map/ppermute | solution.py:38
  27.9 1.1 pad_maximum_fusion
  29.0 3.2 %dynamic_update_slice.47 = bf16[768,768]{0,1:T(8,128)(2,1)} dynamic-update-slice(bf16[768,768]{0,1:T(8,128)(2,1)} %pad_maximum_fusion, bf16[96,768]{0,1:T(8,128)(2,1)} %collective-permute-done, s32[]{:T(128)S(6)} %select_n.139, s32[]{:T(128)} %constant.137.clone.1) | dynamic-update-slice | bytes 294916 | tf_op jit(solution)/shard_map/dynamic_update_slice | solution.py:39
  32.2 3.8 %dynamic_update_slice.48 = bf16[768,768]{0,1:T(8,128)(2,1)} dynamic-update-slice(bf16[768,768]{0,1:T(8,128)(2,1)} %dynamic_update_slice.47, bf16[96,768]{0,1:T(8,128)(2,1)} %collective-permute-done.1, s32[]{:T(128)S(6)} %select_n.143, s32[]{:T(128)} %constant.137.clone.1) | dynamic-update-slice | bytes 294916 | tf_op jit(solution)/shard_map/dynamic_update_slice | solution.py:39
  36.0 2.6 %collective-permute-done.2 = bf16[96,768]{0,1:T(8,128)(2,1)} collective-permute-done((bf16[96,768]{0,1:T(8,128)(2,1)}, bf16[96,768]{0,1:T(8,128)(2,1)}, u32[]{:S(2)}, u32[]{:S(2)}) %collective-permute-start.2) | collective-permute-done | bytes 147488 | tf_op jit(solution)/shard_map/ppermute | solution.py:38
  38.6 3.8 %dynamic_update_slice.49 = bf16[768,768]{0,1:T(8,128)(2,1)} dynamic-update-slice(bf16[768,768]{0,1:T(8,128)(2,1)} %dynamic_update_slice.48, bf16[96,768]{0,1:T(8,128)(2,1)} %collective-permute-done.2, s32[]{:T(128)S(6)} %select_n.147, s32[]{:T(128)} %constant.137.clone.1) | dynamic-update-slice | bytes 294916 | tf_op jit(solution)/shard_map/dynamic_update_slice | solution.py:39
  42.4 3.4 %dynamic_update_slice.50 = bf16[768,768]{0,1:T(8,128)(2,1)} dynamic-update-slice(bf16[768,768]{0,1:T(8,128)(2,1)} %dynamic_update_slice.49, bf16[96,768]{0,1:T(8,128)(2,1)} %collective-permute-done.3, s32[]{:T(128)S(6)} %select_n.149, s32[]{:T(128)} %constant.137.clone.1) | dynamic-update-slice | bytes 294916 | tf_op jit(solution)/shard_map/dynamic_update_slice | solution.py:39
  45.8 3.8 %dynamic_update_slice.51 = bf16[768,768]{0,1:T(8,128)(2,1)} dynamic-update-slice(bf16[768,768]{0,1:T(8,128)(2,1)} %dynamic_update_slice.50, bf16[96,768]{0,1:T(8,128)(2,1)} %collective-permute-done.4, s32[]{:T(128)S(6)} %select_n.145, s32[]{:T(128)} %constant.137.clone.1) | dynamic-update-slice | bytes 294916 | tf_op jit(solution)/shard_map/dynamic_update_slice | solution.py:39
  49.6 3.8 %dynamic_update_slice.52 = bf16[768,768]{0,1:T(8,128)(2,1)} dynamic-update-slice(bf16[768,768]{0,1:T(8,128)(2,1)} %dynamic_update_slice.51, bf16[96,768]{0,1:T(8,128)(2,1)} %collective-permute-done.5, s32[]{:T(128)S(6)} %select_n.141, s32[]{:T(128)} %constant.137.clone.1) | dynamic-update-slice | bytes 294916 | tf_op jit(solution)/shard_map/dynamic_update_slice | solution.py:39
  53.4 3.8 %dynamic_update_slice.53 = bf16[768,768]{0,1:T(8,128)(2,1)} dynamic-update-slice(bf16[768,768]{0,1:T(8,128)(2,1)} %dynamic_update_slice.52, bf16[96,768]{0,1:T(8,128)(2,1)} %collective-permute-done.6, s32[]{:T(128)S(6)} %select_n.137, s32[]{:T(128)} %constant.137.clone.1) | dynamic-update-slice | bytes 294916 | tf_op jit(solution)/shard_map/dynamic_update_slice | solution.py:39
  57.5 1.1 copy-done.1
  58.6 1.6 %collective-permute-start.7 = (bf16[768,512]{0,1:T(8,128)(2,1)S(1)}, bf16[768,512]{0,1:T(8,128)(2,1)}, u32[]{:S(2)}, u32[]{:S(2)}) collective-permute-start(bf16[768,512]{0,1:T(8,128)(2,1)S(1)} %get-tuple-element.13), channel_id=1, source_target_pairs={{0,2},{1,3},{2,0},{3,1},{4,6},{5,7},{6,4},{7,5},{8,10},{9,11},{10,... | collective-permute-start | bytes 2359304 | tf_op jit(solution)/shard_map/ppermute | solution.py:90
  60.2 1.3 broadcast_in_dim.46
  61.5 0.9 fusion.53
  62.4 0.9 collective-permute-start.10
  63.3 0.5 collective-permute-start.11
  63.8 22.7 %collective-permute-done.10 = bf16[768,256]{0,1:T(8,128)(2,1)S(1)} collective-permute-done((bf16[768,256]{0,1:T(8,128)(2,1)}, bf16[768,256]{0,1:T(8,128)(2,1)S(1)}, u32[]{:S(2)}, u32[]{:S(2)}) %collective-permute-start.10) | collective-permute-done | bytes 393248 | tf_op jit(solution)/shard_map/ppermute | solution.py:90
  86.5 0.8 constant_dynamic-update-slice_fusion.2
  87.3 1.8 %constant_dynamic-update-slice_fusion.1 = bf16[768,1024]{0,1:T(8,128)(2,1)} fusion(bf16[768,1024]{0,1:T(8,128)(2,1)} %constant_dynamic-update-slice_fusion.2, bf16[768,256]{0,1:T(8,128)(2,1)} %collective-permute-done.11, s32[]{:T(128)S(6)} %select_n.154), kind=kLoop, calls=%fused_computation.80 | loop fusion | bytes 786436 | tf_op jit(solution)/shard_map/dynamic_update_slice | solution.py:101
  89.1 0.5 collective-permute-start.9
  89.6 1.8 %constant_dynamic-update-slice_fusion = bf16[768,1024]{0,1:T(8,128)(2,1)} fusion(bf16[768,1024]{0,1:T(8,128)(2,1)} %constant_dynamic-update-slice_fusion.1, bf16[768,256]{0,1:T(8,128)(2,1)} %collective-permute-done.12, s32[]{:T(128)S(6)} %select_n.155), kind=kLoop, calls=%fused_computation.79 | loop fusion | bytes 786436 | tf_op jit(solution)/shard_map/dynamic_update_slice | solution.py:101
  91.4 2.1 %constant_dynamic-update-slice_fusion.6 = bf16[768,2048]{0,1:T(8,128)(2,1)} fusion(bf16[768,2048]{0,1:T(8,128)(2,1)} %copy-done.2, bf16[768,512]{0,1:T(8,128)(2,1)} %collective-permute-done.7, s32[]{:T(128)S(6)} %select_n.150), kind=kLoop, calls=%fused_computation.85 | loop fusion | bytes 1572868 | tf_op jit(solution)/shard_map/dynamic_update_slice | solution.py:101
  93.4 2.1 %constant_dynamic-update-slice_fusion.5 = bf16[768,2048]{0,1:T(8,128)(2,1)} fusion(bf16[768,2048]{0,1:T(8,128)(2,1)} %constant_dynamic-update-slice_fusion.6, bf16[768,512]{0,1:T(8,128)(2,1)} %collective-permute-done.8, s32[]{:T(128)S(6)} %select_n.151), kind=kLoop, calls=%fused_computation.84 | loop fusion | bytes 1572868 | tf_op jit(solution)/shard_map/dynamic_update_slice | solution.py:101
  95.5 3.4 %fusion.14 = f32[768,1024]{1,0:T(8,128)S(1)} fusion(bf16[768,1024]{0,1:T(8,128)(2,1)} %constant_dynamic-update-slice_fusion, bf16[1,1024,1024]{2,1,0:T(8,128)(2,1)S(1)} %copy-done), kind=kOutput, calls=%fused_computation.25 | convolution fusion | flops 1610612736 | bytes 6815744 | tf_op jit(solution)/shard_map/dot_general | solution.py:122
  99.1 5.2 %fusion.9 = bf16[768,1024]{1,0:T(8,128)(2,1)S(1)} fusion(f32[768,1024]{1,0:T(8,128)S(1)} %fusion.14, bf16[768,2048]{0,1:T(8,128)(2,1)S(1)} %constant_dynamic-update-slice_fusion.4, bf16[1,1024,2048]{2,1,0:T(8,128)(2,1)S(1)} %copy-done.4), kind=kOutput, calls=%fused_computation.13 | convolution fusion | flops 3236954112 | bytes 12058624 | tf_op jit(solution)/shard_map/dot_general | solution.py:125
  104.3 1.8 %fusion.12 = f32[768,1024]{1,0:T(8,128)S(1)} fusion(bf16[768,1024]{1,0:T(8,128)(2,1)S(1)} %fusion.9, bf16[1,1024,1024]{2,1,0:T(8,128)(2,1)S(1)} %copy-done), kind=kOutput, calls=%fused_computation.23 | convolution fusion | flops 1610612736 | bytes 6815744 | tf_op jit(solution)/shard_map/dot_general | solution.py:129
  106.2 0.4 dynamic-slice_bitcast_fusion.3
  106.9 4.5 %fusion.16 = bf16[1,1024,1024]{2,1,0:T(8,128)(2,1)} fusion(bf16[768,1024]{0,1:T(8,128)(2,1)} %constant_dynamic-update-slice_fusion, bf16[768,1024]{1,0:T(8,128)(2,1)S(1)} %fusion.9), kind=kOutput, calls=%fused_computation.27 | convolution fusion | flops 1612709888 | bytes 5242880 | tf_op jit(solution)/shard_map/dot_general | solution.py:140
  111.7 1.6 %collective-permute-start.14 = (f32[256,768]{0,1:T(8,128)S(1)}, f32[256,768]{0,1:T(8,128)S(1)}, u32[]{:S(2)}, u32[]{:S(2)}) collective-permute-start(f32[256,768]{0,1:T(8,128)S(1)} %slice.48), channel_id=1, source_target_pairs={{0,2},{1,3},{2,0},{3,1},{4,6},{5,7},{6,4},{7,5},{8,10},{9,11},{10,... | collective-permute-start | bytes 2359304 | tf_op jit(solution)/shard_map/ppermute | solution.py:53
  113.3 5.9 %fusion.2 = bf16[1,1024,2048]{2,1,0:T(8,128)(2,1)} fusion(bf16[768,2048]{0,1:T(8,128)(2,1)S(1)} %constant_dynamic-update-slice_fusion.4, f32[768,1024]{1,0:T(8,128)S(1)} %fusion.14), kind=kOutput, calls=%fused_computation.6 | convolution fusion | flops 3232497664 | bytes 10485760 | tf_op jit(solution)/shard_map/dot_general | solution.py:143
  119.2 12.5 %collective-permute-done.14 = f32[256,768]{0,1:T(8,128)S(1)} collective-permute-done((f32[256,768]{0,1:T(8,128)S(1)}, f32[256,768]{0,1:T(8,128)S(1)}, u32[]{:S(2)}, u32[]{:S(2)}) %collective-permute-start.14) | collective-permute-done | bytes 786464 | tf_op jit(solution)/shard_map/ppermute | solution.py:53
  131.9 22.3 %all_to_all.12 = bf16[256,8,96]{0,2,1:T(8,128)(2,1)S(1)} all-to-all(bf16[256,8,96]{0,2,1:T(8,128)(2,1)S(1)} %bitcast.50), channel_id=1, replica_groups=mesh['ep'=8,'tp'=4] {'ep'}, dimensions={1} | all-to-all | bytes 786432 | tf_op jit(solution)/shard_map/all_to_all | solution.py:159
  154.2 1.1 convolution_convert_fusion.2
  (40 shorter events, 2.1 us)
Async XLA Ops:
  0.6 94.9 %copy-start = (bf16[1,1024,1024]{2,1,0:T(8,128)(2,1)S(1)}, bf16[1,1024,1024]{2,1,0:T(8,128)(2,1)}, u32[]{:S(2)}) copy-start(bf16[1,1024,1024]{2,1,0:T(8,128)(2,1)} %param.10) | copy-start | bytes 6291460
  10.3 12.3 %collective-permute-start = (bf16[96,768]{0,1:T(8,128)(2,1)}, bf16[96,768]{0,1:T(8,128)(2,1)}, u32[]{:S(2)}, u32[]{:S(2)}) collective-permute-start(bf16[96,768]{0,1:T(8,128)(2,1)} %get-tuple-element.18), channel_id=1, source_target_pairs={{0,4},{4,8},{8,12},{12,16},{16,20},{20,24},{24,28},{28,0},{1,5},{5... | collective-permute-start | bytes 442376 | tf_op jit(solution)/shard_map/ppermute | solution.py:38
  13.3 11.1 %collective-permute-start.1 = (bf16[96,768]{0,1:T(8,128)(2,1)}, bf16[96,768]{0,1:T(8,128)(2,1)}, u32[]{:S(2)}, u32[]{:S(2)}) collective-permute-start(bf16[96,768]{0,1:T(8,128)(2,1)} %get-tuple-element.19), channel_id=1, source_target_pairs={{0,8},{4,12},{8,16},{12,20},{16,24},{20,28},{24,0},{28,4},{1,9},{5... | collective-permute-start | bytes 442376 | tf_op jit(solution)/shard_map/ppermute | solution.py:38
  14.9 23.7 %collective-permute-start.2 = (bf16[96,768]{0,1:T(8,128)(2,1)}, bf16[96,768]{0,1:T(8,128)(2,1)}, u32[]{:S(2)}, u32[]{:S(2)}) collective-permute-start(bf16[96,768]{0,1:T(8,128)(2,1)} %get-tuple-element.20), channel_id=1, source_target_pairs={{0,12},{4,16},{8,20},{12,24},{16,28},{20,0},{24,4},{28,8},{1,13},{... | collective-permute-start | bytes 442376 | tf_op jit(solution)/shard_map/ppermute | solution.py:38
  17.5 24.9 %collective-permute-start.3 = (bf16[96,768]{0,1:T(8,128)(2,1)}, bf16[96,768]{0,1:T(8,128)(2,1)}, u32[]{:S(2)}, u32[]{:S(2)}) collective-permute-start(bf16[96,768]{0,1:T(8,128)(2,1)} %get-tuple-element.21), channel_id=1, source_target_pairs={{0,16},{4,20},{8,24},{12,28},{16,0},{20,4},{24,8},{28,12},{1,17},{... | collective-permute-start | bytes 442376 | tf_op jit(solution)/shard_map/ppermute | solution.py:38
  18.7 27.1 %collective-permute-start.4 = (bf16[96,768]{0,1:T(8,128)(2,1)}, bf16[96,768]{0,1:T(8,128)(2,1)}, u32[]{:S(2)}, u32[]{:S(2)}) collective-permute-start(bf16[96,768]{0,1:T(8,128)(2,1)} %get-tuple-element.22), channel_id=1, source_target_pairs={{0,20},{4,24},{8,28},{12,0},{16,4},{20,8},{24,12},{28,16},{1,21},{... | collective-permute-start | bytes 442376 | tf_op jit(solution)/shard_map/ppermute | solution.py:38
  22.6 27.0 %collective-permute-start.5 = (bf16[96,768]{0,1:T(8,128)(2,1)}, bf16[96,768]{0,1:T(8,128)(2,1)}, u32[]{:S(2)}, u32[]{:S(2)}) collective-permute-start(bf16[96,768]{0,1:T(8,128)(2,1)} %fusion.40), channel_id=1, source_target_pairs={{0,24},{4,28},{8,0},{12,4},{16,8},{20,12},{24,16},{28,20},{1,25},{... | collective-permute-start | bytes 442376 | tf_op jit(solution)/shard_map/ppermute | solution.py:38
  24.4 29.0 %collective-permute-start.6 = (bf16[96,768]{0,1:T(8,128)(2,1)S(1)}, bf16[96,768]{0,1:T(8,128)(2,1)}, u32[]{:S(2)}, u32[]{:S(2)}) collective-permute-start(bf16[96,768]{0,1:T(8,128)(2,1)S(1)} %get-tuple-element.17), channel_id=1, source_target_pairs={{0,28},{4,0},{8,4},{12,8},{16,12},{20,16},{24,20},{28,24},{1,29},{... | collective-permute-start | bytes 442376 | tf_op jit(solution)/shard_map/ppermute | solution.py:38
  57.3 1.3 copy-start.1
  58.6 3.8 %copy-start.2 = (bf16[768,2048]{0,1:T(8,128)(2,1)}, bf16[768,2048]{0,1:T(8,128)(2,1)S(1)}, u32[]{:S(2)}) copy-start(bf16[768,2048]{0,1:T(8,128)(2,1)S(1)} %get-tuple-element.14) | copy-start | bytes 9437188
  58.6 30.4 %collective-permute-start.7 = (bf16[768,512]{0,1:T(8,128)(2,1)S(1)}, bf16[768,512]{0,1:T(8,128)(2,1)}, u32[]{:S(2)}, u32[]{:S(2)}) collective-permute-start(bf16[768,512]{0,1:T(8,128)(2,1)S(1)} %get-tuple-element.13), channel_id=1, source_target_pairs={{0,2},{1,3},{2,0},{3,1},{4,6},{5,7},{6,4},{7,5},{8,10},{9,11},{10,... | collective-permute-start | bytes 2359304 | tf_op jit(solution)/shard_map/ppermute | solution.py:90
  62.4 24.1 %collective-permute-start.10 = (bf16[768,256]{0,1:T(8,128)(2,1)}, bf16[768,256]{0,1:T(8,128)(2,1)S(1)}, u32[]{:S(2)}, u32[]{:S(2)}) collective-permute-start(bf16[768,256]{0,1:T(8,128)(2,1)} %get-tuple-element.15), channel_id=1, source_target_pairs={{0,2},{1,3},{2,0},{3,1},{4,6},{5,7},{6,4},{7,5},{8,10},{9,11},{10,... | collective-permute-start | bytes 1179656 | tf_op jit(solution)/shard_map/ppermute | solution.py:90
  63.3 30.1 %collective-permute-start.8 = (bf16[768,512]{0,1:T(8,128)(2,1)S(1)}, bf16[768,512]{0,1:T(8,128)(2,1)}, u32[]{:S(2)}, u32[]{:S(2)}) collective-permute-start(bf16[768,512]{0,1:T(8,128)(2,1)S(1)} %get-tuple-element.13), channel_id=1, source_target_pairs={{0,1},{1,0},{2,3},{3,2},{4,5},{5,4},{6,7},{7,6},{8,9},{9,8},{10,11... | collective-permute-start | bytes 2359304 | tf_op jit(solution)/shard_map/ppermute | solution.py:94
  63.3 24.0 %collective-permute-start.11 = (bf16[768,256]{0,1:T(8,128)(2,1)}, bf16[768,256]{0,1:T(8,128)(2,1)}, u32[]{:S(2)}, u32[]{:S(2)}) collective-permute-start(bf16[768,256]{0,1:T(8,128)(2,1)} %get-tuple-element.15), channel_id=1, source_target_pairs={{0,1},{1,0},{2,3},{3,2},{4,5},{5,4},{6,7},{7,6},{8,9},{9,8},{10,11... | collective-permute-start | bytes 1179656 | tf_op jit(solution)/shard_map/ppermute | solution.py:94
  86.5 3.1 %collective-permute-start.12 = (bf16[768,256]{0,1:T(8,128)(2,1)S(1)}, bf16[768,256]{0,1:T(8,128)(2,1)}, u32[]{:S(2)}, u32[]{:S(2)}) collective-permute-start(bf16[768,256]{0,1:T(8,128)(2,1)S(1)} %collective-permute-done.10), channel_id=1, source_target_pairs={{0,1},{1,0},{2,3},{3,2},{4,5},{5,4},{6,7},{7,6},{8,9},{9,8},{10,11... | collective-permute-start | bytes 1179656 | tf_op jit(solution)/shard_map/ppermute | solution.py:94
  89.1 9.8 %collective-permute-start.9 = (bf16[768,512]{0,1:T(8,128)(2,1)}, bf16[768,512]{0,1:T(8,128)(2,1)S(1)}, u32[]{:S(2)}, u32[]{:S(2)}) collective-permute-start(bf16[768,512]{0,1:T(8,128)(2,1)} %collective-permute-done.7), channel_id=1, source_target_pairs={{0,1},{1,0},{2,3},{3,2},{4,5},{5,4},{6,7},{7,6},{8,9},{9,8},{10,11... | collective-permute-start | bytes 2359304 | tf_op jit(solution)/shard_map/ppermute | solution.py:94
  95.5 3.4 %copy-start.3 = (bf16[768,2048]{0,1:T(8,128)(2,1)S(1)}, bf16[768,2048]{0,1:T(8,128)(2,1)}, u32[]{:S(2)}) copy-start(bf16[768,2048]{0,1:T(8,128)(2,1)} %constant_dynamic-update-slice_fusion.5) | copy-start | bytes 9437188
  95.5 3.6 %copy-start.4 = (bf16[1,1024,2048]{2,1,0:T(8,128)(2,1)S(1)}, bf16[1,1024,2048]{2,1,0:T(8,128)(2,1)}, u32[]{:S(2)}) copy-start(bf16[1,1024,2048]{2,1,0:T(8,128)(2,1)} %param.11) | copy-start | bytes 12582916
  106.8 4.6 %collective-permute-start.13 = (f32[512,768]{0,1:T(8,128)S(1)}, f32[512,768]{0,1:T(8,128)S(1)}, u32[]{:S(2)}, u32[]{:S(2)}) collective-permute-start(f32[512,768]{0,1:T(8,128)S(1)} %pad_maximum_fusion.1), channel_id=1, source_target_pairs={{0,1},{1,0},{2,3},{3,2},{4,5},{5,4},{6,7},{7,6},{8,9},{9,8},{10,11... | collective-permute-start | bytes 4718600 | tf_op jit(solution)/shard_map/ppermute | solution.py:51
  111.7 20.0 %collective-permute-start.14 = (f32[256,768]{0,1:T(8,128)S(1)}, f32[256,768]{0,1:T(8,128)S(1)}, u32[]{:S(2)}, u32[]{:S(2)}) collective-permute-start(f32[256,768]{0,1:T(8,128)S(1)} %slice.48), channel_id=1, source_target_pairs={{0,2},{1,3},{2,0},{3,1},{4,6},{5,7},{6,4},{7,5},{8,10},{9,11},{10,... | collective-permute-start | bytes 2359304 | tf_op jit(solution)/shard_map/ppermute | solution.py:53

commit v13 on v12

--- a/solution.py
+++ b/solution.py
@@ -38,6 +38,19 @@
         incoming = lax.ppermute(outgoing, axis, [(i, (i + shift) % peers) for i in range(peers)])
         result = lax.dynamic_update_slice_in_dim(result, incoming, source * block, dimension)
     return result
+
+
+def exchange_rotated(value, axis):
+    peers = lax.axis_size(axis)
+    me = lax.axis_index(axis)
+    block = value.shape[0] // peers
+    pieces = [lax.dynamic_slice_in_dim(value, me * block, block, 0)]
+    for shift in range(1, peers):
+        target = (me + peers - shift) % peers
+        outgoing = lax.dynamic_slice_in_dim(value, target * block, block, 0)
+        pairs = [(i, (i + peers - shift) % peers) for i in range(peers)]
+        pieces.append(lax.ppermute(outgoing, axis, pairs))
+    return jnp.concatenate(pieces, axis=0)
 
 
 def chip_then_link_sum(partial, j):
@@ -103,7 +116,12 @@
 
     local_x = local_columns(features, pick)
     local_dy = local_columns(cotangent, pick_scaled)
-    moved = exchange(jnp.concatenate([local_x, local_dy], axis=1), "ep", 0)
+    rotated = device_count <= 8
+    joined = jnp.concatenate([local_x, local_dy], axis=1)
+    if rotated:
+        moved = exchange_rotated(joined, "ep")
+    else:
+        moved = lax.all_to_all(joined, "ep", split_axis=0, concat_axis=0, tiled=True)
     rows_x = spread(moved[:, :local_x.shape[1]], features.shape[1])
     rows_dy = spread(moved[:, local_x.shape[1]:], cotangent.shape[1])
     piece_in = w_in[0]
@@ -156,6 +174,9 @@
     leaving, grad_w_in, grad_w_out = lax.optimization_barrier(
         (summed.astype(jnp.bfloat16), grad_w_in, grad_w_out)
     )
+    if rotated:
+        blocks = leaving.reshape(leaving.shape[0], device_count, capacity)
+        leaving = jnp.roll(blocks, lax.axis_index("ep"), axis=1).reshape(leaving.shape)
     returned = lax.all_to_all(leaving, "ep", split_axis=1, concat_axis=1, tiled=True)
     grad_in = lax.dot_general(
         pick, returned, (((0,), (1,)), ((), ())), preferred_element_type=jnp.float32

time: 157 us -> 148 us (0.943)
  waiting for transfers between devices: 38.2 us -> 63.8 us
  local copies, waits for them, and re-layouts: 39.9 us -> 17.8 us
  blocking collectives: 22.3 us -> 14.9 us
  starting transfers between devices: 21.3 us -> 15.3 us
    dynamic_update_slice x7 -> x0, local copies, waits for them, and re-layouts: 25.7 us -> none  [exchange(): lax.dynamic_update_slice_in_dim(result, incoming, source * block, dimension)]
    ppermute x7, waiting for transfers between devices: 2.89 us -> 28.5 us  [exchange_rotated(): pieces.append(lax.ppermute(outgoing, axis, pairs))]
    all_to_all x1, blocking collectives: 22.3 us -> 14.9 us  [shards(): lax.all_to_all(leaving, 'ep', split_axis=1, concat_axis=1, tiled=True)]
    ppermute x7, starting transfers between devices: 16.2 us -> 10.2 us  [exchange_rotated(): pieces.append(lax.ppermute(outgoing, axis, pairs))]
    concatenate x0 -> x1, local copies, waits for them, and re-layouts: none -> 2.52 us  [exchange_rotated(): return jnp.concatenate(pieces, axis=0)]
    add x1, other arithmetic: 0.26 us -> 1.84 us  [chip_then_link_sum(): keep = keep + lax.ppermute(give, 'tp', [(i, i ^ 1) for i in range(4)])]
  transfers between devices with their start and end apart: 15 -> 15, of which waited for: 4 -> 6; matrix products, arithmetic and copies ran while one was open for 31% -> 18% of each run, Pallas kernels for 0% -> 0%
where the time goes in v13:
time: 148 us; the launch traced here: 147 us
  waiting for transfers between devices  63.8 us (43%)
  matrix products  25.1 us (17%)
  local copies, waits for them, and re-layouts  17.8 us (12%)
  starting transfers between devices  15.3 us (10%)
  blocking collectives  14.9 us (10%)
  other arithmetic  9.35 us (6%)
    ppermute x7, waiting for transfers between devices, exchange_rotated(): pieces.append(lax.ppermute(outgoing, axis, pairs))  28.5 us
    ppermute x2, waiting for transfers between devices, spread(): across = lax.ppermute(mine, 'tp', [(i, i ^ 2) for i in range(tp_size)])  22.8 us
    all_to_all x1, blocking collectives, shards(): lax.all_to_all(leaving, 'ep', split_axis=1, concat_axis=1, tiled=True)  14.9 us
    ppermute x1, waiting for transfers between devices, chip_then_link_sum(): return mine + lax.ppermute(send, 'tp', [(i, i ^ 2) for i in range(4)])  12.5 us
    ppermute x7, starting transfers between devices, exchange_rotated(): pieces.append(lax.ppermute(outgoing, axis, pairs))  10.2 us
    dynamic_update_slice x6, local copies, waits for them, and re-layouts, spread(): whole = lax.dynamic_update_slice_in_dim(whole, piece, where * width, 1)  7.42 us
    dot_general x1, matrix products, span_grads(): lax.dot_general(act_cols, rows_dy, (((0,), (0,)), ((), ())), preferred_el...  5.85 us
    dot_general x1, matrix products, shards(): lax.dot_general(rows_dy, weight_out, (((1,), (1,)), ((), ())), preferred_...  5.18 us
  transfers between devices with their start and end apart: 15, of which 6 were waited for; matrix products, arithmetic and copies ran while one was open for 18% of the time, Pallas kernels for 0%

profile of v13, /device:TPU:0, one launch (start us, length us, event | category | flops | bytes accessed | tf_op | source)
XLA Modules:
  0.0 147.2 jit_solution(8200513341938059719)
XLA Ops:
  0.7 0.9 copy.15
  1.8 1.1 reduce-window.6
  3.0 0.2 slice_reduce_fusion
  3.5 0.7 multiply_add_fusion
  4.2 0.7 convert_multiply_fusion
  4.9 1.3 convolution_convert_fusion.1
  6.2 1.4 convolution_convert_fusion
  7.6 1.3 fusion.43
  8.9 4.0 %collective-permute-start.4 = (bf16[96,768]{0,1:T(8,128)(2,1)}, bf16[96,768]{0,1:T(8,128)(2,1)}, u32[]{:S(2)}, u32[]{:S(2)}) collective-permute-start(bf16[96,768]{0,1:T(8,128)(2,1)} %get-tuple-element.24), channel_id=1, source_target_pairs={{0,12},{4,16},{8,20},{12,24},{16,28},{20,0},{24,4},{28,8},{1,13},{... | collective-permute-start | bytes 442376 | tf_op jit(solution)/shard_map/ppermute | solution.py:52
  12.9 1.6 %collective-permute-start.5 = (bf16[96,768]{0,1:T(8,128)(2,1)}, bf16[96,768]{0,1:T(8,128)(2,1)}, u32[]{:S(2)}, u32[]{:S(2)}) collective-permute-start(bf16[96,768]{0,1:T(8,128)(2,1)} %get-tuple-element.23), channel_id=1, source_target_pairs={{0,8},{4,12},{8,16},{12,20},{16,24},{20,28},{24,0},{28,4},{1,9},{5... | collective-permute-start | bytes 442376 | tf_op jit(solution)/shard_map/ppermute | solution.py:52
  14.5 1.8 %fusion.36 = (bf16[96,768]{0,1:T(8,128)(2,1)S(1)}, bf16[96,768]{0,1:T(8,128)(2,1)S(1)}, bf16[96,768]{0,1:T(8,128)(2,1)S(1)}, bf16[96,768]{0,1:T(8,128)(2,1)S(1)}...) fusion(s32[]{:T(128)S(6)} %select_n.144, bf16[768,512]{0,1:T(8,128)(2,1)S(1)} %convolution_convert_fusion, ...), kind=kLoop, calls=%fused_computation.68 | loop fusion | flops 1769472 | bytes 2064408 | tf_op jit(solution)/shard_map/concatenate | solution.py:120
  16.3 3.3 %collective-permute-start = (bf16[96,768]{0,1:T(8,128)(2,1)S(1)}, bf16[96,768]{0,1:T(8,128)(2,1)S(1)}, u32[]{:S(2)}, u32[]{:S(2)}) collective-permute-start(bf16[96,768]{0,1:T(8,128)(2,1)S(1)} %get-tuple-element.19), channel_id=1, source_target_pairs={{0,28},{4,0},{8,4},{12,8},{16,12},{20,16},{24,20},{28,24},{1,29},{... | collective-permute-start | bytes 442376 | tf_op jit(solution)/shard_map/ppermute | solution.py:52
  19.6 1.3 collective-permute-start.2
  20.9 7.6 %collective-permute-done.4 = bf16[96,768]{0,1:T(8,128)(2,1)} collective-permute-done((bf16[96,768]{0,1:T(8,128)(2,1)}, bf16[96,768]{0,1:T(8,128)(2,1)}, u32[]{:S(2)}, u32[]{:S(2)}) %collective-permute-start.4) | collective-permute-done | bytes 147488 | tf_op jit(solution)/shard_map/ppermute | solution.py:52
  28.6 4.1 %collective-permute-done.1 = bf16[96,768]{0,1:T(8,128)(2,1)S(1)} collective-permute-done((bf16[96,768]{0,1:T(8,128)(2,1)S(1)}, bf16[96,768]{0,1:T(8,128)(2,1)S(1)}, u32[]{:S(2)}, u32[]{:S(2)}) %collective-permute-start.1) | collective-permute-done | bytes 147488 | tf_op jit(solution)/shard_map/ppermute | solution.py:52
  32.7 2.7 %collective-permute-done.2 = bf16[96,768]{0,1:T(8,128)(2,1)S(1)} collective-permute-done((bf16[96,768]{0,1:T(8,128)(2,1)S(1)}, bf16[96,768]{0,1:T(8,128)(2,1)S(1)}, u32[]{:S(2)}, u32[]{:S(2)}) %collective-permute-start.2) | collective-permute-done | bytes 147488 | tf_op jit(solution)/shard_map/ppermute | solution.py:52
  35.3 14.2 %collective-permute-done.3 = bf16[96,768]{0,1:T(8,128)(2,1)S(1)} collective-permute-done((bf16[96,768]{0,1:T(8,128)(2,1)S(1)}, bf16[96,768]{0,1:T(8,128)(2,1)S(1)}, u32[]{:S(2)}, u32[]{:S(2)}) %collective-permute-start.3) | collective-permute-done | bytes 147488 | tf_op jit(solution)/shard_map/ppermute | solution.py:52
  49.5 0.6 copy-done.11
  50.1 0.7 copy-done.12
  50.8 2.5 %concatenate.17 = bf16[768,768]{0,1:T(8,128)(2,1)S(1)} concatenate(bf16[96,768]{0,1:T(8,128)(2,1)S(1)} %get-tuple-element.18, bf16[96,768]{0,1:T(8,128)(2,1)} %copy-done.8, bf16[96,768]{0,1:T(8,128)(2,1)} %copy-done.9, bf16[96,768]{0,1:T(8,128)(2,1)} %copy-done.10, bf16[96,768]{0,1:T(8,128)(2,1)} %copy-done.11, bf16[96,768]{0,1:T(8,128)(2,1)} %collective-permute-done.4, ...), dimensions={0} | concatenate | bytes 2359296 | tf_op jit(solution)/shard_map/concatenate | solution.py:53
  53.3 0.2 broadcast_in_dim.40
  53.6 1.0 fusion.54
  54.6 1.5 %collective-permute-start.7 = (bf16[768,512]{0,1:T(8,128)(2,1)}, bf16[768,512]{0,1:T(8,128)(2,1)}, u32[]{:S(2)}, u32[]{:S(2)}) collective-permute-start(bf16[768,512]{0,1:T(8,128)(2,1)} %get-tuple-element.13), channel_id=1, source_target_pairs={{0,2},{1,3},{2,0},{3,1},{4,6},{5,7},{6,4},{7,5},{8,10},{9,11},{10,... | collective-permute-start | bytes 2359304 | tf_op jit(solution)/shard_map/ppermute | solution.py:103
  56.1 1.4 broadcast_in_dim.46
  57.4 1.0 fusion.55
  58.4 0.9 collective-permute-start.10
  59.3 0.5 collective-permute-start.11
  59.9 22.8 %collective-permute-done.10 = bf16[768,256]{0,1:T(8,128)(2,1)S(1)} collective-permute-done((bf16[768,256]{0,1:T(8,128)(2,1)}, bf16[768,256]{0,1:T(8,128)(2,1)S(1)}, u32[]{:S(2)}, u32[]{:S(2)}) %collective-permute-start.10) | collective-permute-done | bytes 393248 | tf_op jit(solution)/shard_map/ppermute | solution.py:103
  82.7 0.8 constant_dynamic-update-slice_fusion.2
  83.5 1.8 %constant_dynamic-update-slice_fusion.1 = bf16[768,1024]{0,1:T(8,128)(2,1)} fusion(bf16[768,1024]{0,1:T(8,128)(2,1)} %constant_dynamic-update-slice_fusion.2, bf16[768,256]{0,1:T(8,128)(2,1)} %collective-permute-done.11, s32[]{:T(128)S(6)} %select_n.149), kind=kLoop, calls=%fused_computation.85 | loop fusion | bytes 786436 | tf_op jit(solution)/shard_map/dynamic_update_slice | solution.py:114
  85.3 0.5 collective-permute-start.9
  85.8 1.8 %constant_dynamic-update-slice_fusion = bf16[768,1024]{0,1:T(8,128)(2,1)} fusion(bf16[768,1024]{0,1:T(8,128)(2,1)} %constant_dynamic-update-slice_fusion.1, bf16[768,256]{0,1:T(8,128)(2,1)} %collective-permute-done.12, s32[]{:T(128)S(6)} %select_n.150), kind=kLoop, calls=%fused_computation.84 | loop fusion | bytes 786436 | tf_op jit(solution)/shard_map/dynamic_update_slice | solution.py:114
  87.5 2.1 %constant_dynamic-update-slice_fusion.6 = bf16[768,2048]{0,1:T(8,128)(2,1)} fusion(bf16[768,2048]{0,1:T(8,128)(2,1)} %copy-done.1, bf16[768,512]{0,1:T(8,128)(2,1)} %collective-permute-done.7, s32[]{:T(128)S(6)} %select_n.145), kind=kLoop, calls=%fused_computation.90 | loop fusion | bytes 1572868 | tf_op jit(solution)/shard_map/dynamic_update_slice | solution.py:114
  89.6 0.9 constant_dynamic-update-slice_fusion.5
  90.5 3.4 %fusion.14 = f32[768,1024]{1,0:T(8,128)S(1)} fusion(bf16[768,1024]{0,1:T(8,128)(2,1)} %constant_dynamic-update-slice_fusion, bf16[1,1024,1024]{2,1,0:T(8,128)(2,1)S(1)} %copy-done), kind=kOutput, calls=%fused_computation.25 | convolution fusion | flops 1610612736 | bytes 6815744 | tf_op jit(solution)/shard_map/dot_general | solution.py:140
  94.1 5.2 %fusion.9 = bf16[768,1024]{1,0:T(8,128)(2,1)S(1)} fusion(f32[768,1024]{1,0:T(8,128)S(1)} %fusion.14, bf16[768,2048]{0,1:T(8,128)(2,1)S(1)} %constant_dynamic-update-slice_fusion.4, bf16[1,1024,2048]{2,1,0:T(8,128)(2,1)S(1)} %copy-done.13), kind=kOutput, calls=%fused_computation.13 | convolution fusion | flops 3236954112 | bytes 12058624 | tf_op jit(solution)/shard_map/dot_general | solution.py:143
  99.4 1.8 %fusion.12 = f32[768,1024]{1,0:T(8,128)S(1)} fusion(bf16[768,1024]{1,0:T(8,128)(2,1)S(1)} %fusion.9, bf16[1,1024,1024]{2,1,0:T(8,128)(2,1)S(1)} %copy-done), kind=kOutput, calls=%fused_computation.23 | convolution fusion | flops 1610612736 | bytes 6815744 | tf_op jit(solution)/shard_map/dot_general | solution.py:147
  101.2 1.3 dynamic-slice_bitcast_fusion.3
  102.5 1.4 pad_maximum_fusion
  103.9 5.1 %fusion.16 = bf16[1,1024,1024]{2,1,0:T(8,128)(2,1)} fusion(bf16[768,1024]{0,1:T(8,128)(2,1)} %constant_dynamic-update-slice_fusion, bf16[768,1024]{1,0:T(8,128)(2,1)} %copy-done.14), kind=kOutput, calls=%fused_computation.27 | convolution fusion | flops 1612709888 | bytes 5242880 | tf_op jit(solution)/shard_map/dot_general | solution.py:158
  109.0 1.8 %maximum_add_fusion = f32[512,768]{0,1:T(8,128)S(1)} fusion(f32[512,768]{0,1:T(8,128)} %collective-permute-done.13, f32[256,768]{0,1:T(8,128)S(1)} %copy-done.7, f32[256,768]{0,1:T(8,128)S(1)} %get-tuple-element.9), kind=kLoop, calls=%fused_computation.36 | loop fusion | flops 786432 | bytes 4718592 | tf_op jit(solution)/shard_map/add | solution.py:64
  110.9 1.6 %collective-permute-start.14 = (f32[256,768]{0,1:T(8,128)S(1)}, f32[256,768]{0,1:T(8,128)S(1)}, u32[]{:S(2)}, u32[]{:S(2)}) collective-permute-start(f32[256,768]{0,1:T(8,128)S(1)} %slice.48), channel_id=1, source_target_pairs={{0,2},{1,3},{2,0},{3,1},{4,6},{5,7},{6,4},{7,5},{8,10},{9,11},{10,... | collective-permute-start | bytes 2359304 | tf_op jit(solution)/shard_map/ppermute | solution.py:66
  112.6 5.8 %fusion.2 = bf16[1,1024,2048]{2,1,0:T(8,128)(2,1)} fusion(bf16[768,2048]{0,1:T(8,128)(2,1)S(1)} %copy-done.4, f32[768,1024]{1,0:T(8,128)S(1)} %copy-done.6), kind=kOutput, calls=%fused_computation.6 | convolution fusion | flops 3232497664 | bytes 10485760 | tf_op jit(solution)/shard_map/dot_general | solution.py:161
  118.4 12.5 %collective-permute-done.14 = f32[256,768]{0,1:T(8,128)S(1)} collective-permute-done((f32[256,768]{0,1:T(8,128)S(1)}, f32[256,768]{0,1:T(8,128)S(1)}, u32[]{:S(2)}, u32[]{:S(2)}) %collective-permute-start.14) | collective-permute-done | bytes 786464 | tf_op jit(solution)/shard_map/ppermute | solution.py:66
  130.9 0.2 fusion.21
  131.1 0.2 fusion.25
  131.2 14.9 %all_to_all.9 = bf16[256,8,96]{0,2,1:T(8,128)(2,1)S(1)} all-to-all(bf16[256,8,96]{0,2,1:T(8,128)(2,1)S(1)} %fusion.25), channel_id=1, replica_groups=mesh['ep'=8,'tp'=4] {'ep'}, dimensions={1} | all-to-all | bytes 786432 | tf_op jit(solution)/shard_map/all_to_all | solution.py:180
  146.1 1.1 convolution_convert_fusion.2
  (54 shorter events, 1.0 us)
Async XLA Ops:
  0.6 89.9 %copy-start = (bf16[1,1024,1024]{2,1,0:T(8,128)(2,1)S(1)}, bf16[1,1024,1024]{2,1,0:T(8,128)(2,1)}, u32[]{:S(2)}) copy-start(bf16[1,1024,1024]{2,1,0:T(8,128)(2,1)} %param.10) | copy-start | bytes 6291460
  8.9 19.5 %collective-permute-start.4 = (bf16[96,768]{0,1:T(8,128)(2,1)}, bf16[96,768]{0,1:T(8,128)(2,1)}, u32[]{:S(2)}, u32[]{:S(2)}) collective-permute-start(bf16[96,768]{0,1:T(8,128)(2,1)} %get-tuple-element.24), channel_id=1, source_target_pairs={{0,12},{4,16},{8,20},{12,24},{16,28},{20,0},{24,4},{28,8},{1,13},{... | collective-permute-start | bytes 442376 | tf_op jit(solution)/shard_map/ppermute | solution.py:52
  12.9 15.6 %collective-permute-start.5 = (bf16[96,768]{0,1:T(8,128)(2,1)}, bf16[96,768]{0,1:T(8,128)(2,1)}, u32[]{:S(2)}, u32[]{:S(2)}) collective-permute-start(bf16[96,768]{0,1:T(8,128)(2,1)} %get-tuple-element.23), channel_id=1, source_target_pairs={{0,8},{4,12},{8,16},{12,20},{16,24},{20,28},{24,0},{28,4},{1,9},{5... | collective-permute-start | bytes 442376 | tf_op jit(solution)/shard_map/ppermute | solution.py:52
  16.3 12.3 %collective-permute-start = (bf16[96,768]{0,1:T(8,128)(2,1)S(1)}, bf16[96,768]{0,1:T(8,128)(2,1)S(1)}, u32[]{:S(2)}, u32[]{:S(2)}) collective-permute-start(bf16[96,768]{0,1:T(8,128)(2,1)S(1)} %get-tuple-element.19), channel_id=1, source_target_pairs={{0,28},{4,0},{8,4},{12,8},{16,12},{20,16},{24,20},{28,24},{1,29},{... | collective-permute-start | bytes 442376 | tf_op jit(solution)/shard_map/ppermute | solution.py:52
  19.6 13.1 %collective-permute-start.1 = (bf16[96,768]{0,1:T(8,128)(2,1)S(1)}, bf16[96,768]{0,1:T(8,128)(2,1)S(1)}, u32[]{:S(2)}, u32[]{:S(2)}) collective-permute-start(bf16[96,768]{0,1:T(8,128)(2,1)S(1)} %get-tuple-element.20), channel_id=1, source_target_pairs={{0,24},{4,28},{8,0},{12,4},{16,8},{20,12},{24,16},{28,20},{1,25},{... | collective-permute-start | bytes 442376 | tf_op jit(solution)/shard_map/ppermute | solution.py:52
  19.6 15.7 %collective-permute-start.2 = (bf16[96,768]{0,1:T(8,128)(2,1)S(1)}, bf16[96,768]{0,1:T(8,128)(2,1)S(1)}, u32[]{:S(2)}, u32[]{:S(2)}) collective-permute-start(bf16[96,768]{0,1:T(8,128)(2,1)S(1)} %get-tuple-element.21), channel_id=1, source_target_pairs={{0,20},{4,24},{8,28},{12,0},{16,4},{20,8},{24,12},{28,16},{1,21},{... | collective-permute-start | bytes 442376 | tf_op jit(solution)/shard_map/ppermute | solution.py:52
  28.5 21.0 %collective-permute-start.3 = (bf16[96,768]{0,1:T(8,128)(2,1)S(1)}, bf16[96,768]{0,1:T(8,128)(2,1)S(1)}, u32[]{:S(2)}, u32[]{:S(2)}) collective-permute-start(bf16[96,768]{0,1:T(8,128)(2,1)S(1)} %get-tuple-element.22), channel_id=1, source_target_pairs={{0,16},{4,20},{8,24},{12,28},{16,0},{20,4},{24,8},{28,12},{1,17},{... | collective-permute-start | bytes 442376 | tf_op jit(solution)/shard_map/ppermute | solution.py:52
  28.5 21.0 %collective-permute-start.6 = (bf16[96,768]{0,1:T(8,128)(2,1)S(1)}, bf16[96,768]{0,1:T(8,128)(2,1)S(1)}, u32[]{:S(2)}, u32[]{:S(2)}) collective-permute-start(bf16[96,768]{0,1:T(8,128)(2,1)S(1)} %get-tuple-element.17), channel_id=1, source_target_pairs={{0,4},{4,8},{8,12},{12,16},{16,20},{20,24},{24,28},{28,0},{1,5},{5... | collective-permute-start | bytes 442376 | tf_op jit(solution)/shard_map/ppermute | solution.py:52
  28.6 20.9 %copy-start.8 = (bf16[96,768]{0,1:T(8,128)(2,1)}, bf16[96,768]{0,1:T(8,128)(2,1)S(1)}, u32[]{:S(2)}) copy-start(bf16[96,768]{0,1:T(8,128)(2,1)S(1)} %collective-permute-done) | copy-start | bytes 442372
  32.7 16.8 %copy-start.9 = (bf16[96,768]{0,1:T(8,128)(2,1)}, bf16[96,768]{0,1:T(8,128)(2,1)S(1)}, u32[]{:S(2)}) copy-start(bf16[96,768]{0,1:T(8,128)(2,1)S(1)} %collective-permute-done.1) | copy-start | bytes 442372
  35.3 14.2 %copy-start.10 = (bf16[96,768]{0,1:T(8,128)(2,1)}, bf16[96,768]{0,1:T(8,128)(2,1)S(1)}, u32[]{:S(2)}) copy-start(bf16[96,768]{0,1:T(8,128)(2,1)S(1)} %collective-permute-done.2) | copy-start | bytes 442372
  49.5 0.7 copy-start.11
  50.1 0.7 copy-start.12
  54.5 3.9 %copy-start.1 = (bf16[768,2048]{0,1:T(8,128)(2,1)}, bf16[768,2048]{0,1:T(8,128)(2,1)S(1)}, u32[]{:S(2)}) copy-start(bf16[768,2048]{0,1:T(8,128)(2,1)S(1)} %get-tuple-element.14) | copy-start | bytes 9437188
  54.6 30.7 %collective-permute-start.7 = (bf16[768,512]{0,1:T(8,128)(2,1)}, bf16[768,512]{0,1:T(8,128)(2,1)}, u32[]{:S(2)}, u32[]{:S(2)}) collective-permute-start(bf16[768,512]{0,1:T(8,128)(2,1)} %get-tuple-element.13), channel_id=1, source_target_pairs={{0,2},{1,3},{2,0},{3,1},{4,6},{5,7},{6,4},{7,5},{8,10},{9,11},{10,... | collective-permute-start | bytes 2359304 | tf_op jit(solution)/shard_map/ppermute | solution.py:103
  58.4 24.2 %collective-permute-start.10 = (bf16[768,256]{0,1:T(8,128)(2,1)}, bf16[768,256]{0,1:T(8,128)(2,1)S(1)}, u32[]{:S(2)}, u32[]{:S(2)}) collective-permute-start(bf16[768,256]{0,1:T(8,128)(2,1)} %get-tuple-element.15), channel_id=1, source_target_pairs={{0,2},{1,3},{2,0},{3,1},{4,6},{5,7},{6,4},{7,5},{8,10},{9,11},{10,... | collective-permute-start | bytes 1179656 | tf_op jit(solution)/shard_map/ppermute | solution.py:103
  59.3 30.2 %collective-permute-start.8 = (bf16[768,512]{0,1:T(8,128)(2,1)}, bf16[768,512]{0,1:T(8,128)(2,1)S(1)}, u32[]{:S(2)}, u32[]{:S(2)}) collective-permute-start(bf16[768,512]{0,1:T(8,128)(2,1)} %get-tuple-element.13), channel_id=1, source_target_pairs={{0,1},{1,0},{2,3},{3,2},{4,5},{5,4},{6,7},{7,6},{8,9},{9,8},{10,11... | collective-permute-start | bytes 2359304 | tf_op jit(solution)/shard_map/ppermute | solution.py:107
  59.3 24.1 %collective-permute-start.11 = (bf16[768,256]{0,1:T(8,128)(2,1)}, bf16[768,256]{0,1:T(8,128)(2,1)}, u32[]{:S(2)}, u32[]{:S(2)}) collective-permute-start(bf16[768,256]{0,1:T(8,128)(2,1)} %get-tuple-element.15), channel_id=1, source_target_pairs={{0,1},{1,0},{2,3},{3,2},{4,5},{5,4},{6,7},{7,6},{8,9},{9,8},{10,11... | collective-permute-start | bytes 1179656 | tf_op jit(solution)/shard_map/ppermute | solution.py:107
  82.7 3.1 %collective-permute-start.12 = (bf16[768,256]{0,1:T(8,128)(2,1)S(1)}, bf16[768,256]{0,1:T(8,128)(2,1)}, u32[]{:S(2)}, u32[]{:S(2)}) collective-permute-start(bf16[768,256]{0,1:T(8,128)(2,1)S(1)} %collective-permute-done.10), channel_id=1, source_target_pairs={{0,1},{1,0},{2,3},{3,2},{4,5},{5,4},{6,7},{7,6},{8,9},{9,8},{10,11... | collective-permute-start | bytes 1179656 | tf_op jit(solution)/shard_map/ppermute | solution.py:107
  85.3 8.7 %collective-permute-start.9 = (bf16[768,512]{0,1:T(8,128)(2,1)}, bf16[768,512]{0,1:T(8,128)(2,1)S(1)}, u32[]{:S(2)}, u32[]{:S(2)}) collective-permute-start(bf16[768,512]{0,1:T(8,128)(2,1)} %collective-permute-done.7), channel_id=1, source_target_pairs={{0,1},{1,0},{2,3},{3,2},{4,5},{5,4},{6,7},{7,6},{8,9},{9,8},{10,11... | collective-permute-start | bytes 2359304 | tf_op jit(solution)/shard_map/ppermute | solution.py:107
  90.5 3.4 %copy-start.2 = (bf16[768,2048]{0,1:T(8,128)(2,1)S(1)}, bf16[768,2048]{0,1:T(8,128)(2,1)}, u32[]{:S(2)}) copy-start(bf16[768,2048]{0,1:T(8,128)(2,1)} %constant_dynamic-update-slice_fusion.5) | copy-start | bytes 9437188
  90.5 3.6 %copy-start.13 = (bf16[1,1024,2048]{2,1,0:T(8,128)(2,1)S(1)}, bf16[1,1024,2048]{2,1,0:T(8,128)(2,1)}, u32[]{:S(2)}) copy-start(bf16[1,1024,2048]{2,1,0:T(8,128)(2,1)} %param.11) | copy-start | bytes 12582916
  93.9 5.4 %copy-start.5 = (f32[768,1024]{1,0:T(8,128)}, f32[768,1024]{1,0:T(8,128)S(1)}, u32[]{:S(2)}) copy-start(f32[768,1024]{1,0:T(8,128)S(1)} %fusion.14) | copy-start | bytes 9437188
  94.1 5.2 %copy-start.3 = (bf16[768,2048]{0,1:T(8,128)(2,1)}, bf16[768,2048]{0,1:T(8,128)(2,1)S(1)}, u32[]{:S(2)}) copy-start(bf16[768,2048]{0,1:T(8,128)(2,1)S(1)} %constant_dynamic-update-slice_fusion.4) | copy-start | bytes 9437188
  99.4 1.8 %copy-start.14 = (bf16[768,1024]{1,0:T(8,128)(2,1)}, bf16[768,1024]{1,0:T(8,128)(2,1)S(1)}, u32[]{:S(2)}) copy-start(bf16[768,1024]{1,0:T(8,128)(2,1)S(1)} %fusion.9) | copy-start | bytes 4718596
  103.9 5.1 %collective-permute-start.13 = (f32[512,768]{0,1:T(8,128)}, f32[512,768]{0,1:T(8,128)}, u32[]{:S(2)}, u32[]{:S(2)}) collective-permute-start(f32[512,768]{0,1:T(8,128)} %pad_maximum_fusion), channel_id=1, source_target_pairs={{0,1},{1,0},{2,3},{3,2},{4,5},{5,4},{6,7},{7,6},{8,9},{9,8},{10,11... | collective-permute-start | bytes 4718600 | tf_op jit(solution)/shard_map/ppermute | solution.py:64
  103.9 5.1 %copy-start.7 = (f32[256,768]{0,1:T(8,128)S(1)}, f32[256,768]{0,1:T(8,128)}, u32[]{:S(2)}) copy-start(f32[256,768]{0,1:T(8,128)} %get-tuple-element.12) | copy-start | bytes 2359300
  109.0 3.6 %copy-start.4 = (bf16[768,2048]{0,1:T(8,128)(2,1)S(1)}, bf16[768,2048]{0,1:T(8,128)(2,1)}, u32[]{:S(2)}) copy-start(bf16[768,2048]{0,1:T(8,128)(2,1)} %copy-done.3) | copy-start | bytes 9437188
  109.0 3.6 %copy-start.6 = (f32[768,1024]{1,0:T(8,128)S(1)}, f32[768,1024]{1,0:T(8,128)}, u32[]{:S(2)}) copy-start(f32[768,1024]{1,0:T(8,128)} %copy-done.5) | copy-start | bytes 9437188
  110.9 20.0 %collective-permute-start.14 = (f32[256,768]{0,1:T(8,128)S(1)}, f32[256,768]{0,1:T(8,128)S(1)}, u32[]{:S(2)}, u32[]{:S(2)}) collective-permute-start(f32[256,768]{0,1:T(8,128)S(1)} %slice.48), channel_id=1, source_target_pairs={{0,2},{1,3},{2,0},{3,1},{4,6},{5,7},{6,4},{7,5},{8,10},{9,11},{10,... | collective-permute-start | bytes 2359304 | tf_op jit(solution)/shard_map/ppermute | solution.py:66
